TPU v7x, 32 devices: a whole 2x2x4 slice. The times are simulated.
32 devices in a mesh: kv: 2 (over x), ep: 16 (over z, y, core).
Axes of the slice: x: 2, y: 2, z: 4, core: 2. Of those that a mesh axis runs over, the one named last changes fastest.
Arguments:
- resid: bfloat16 [16, 256, 2048], P('ep', 'kv'), may hold values from -6 to 6
- queries: bfloat16 [16, 256, 1024], P('ep', 'kv'), may hold values from -6 to 6
- new_keys: bfloat16 [16, 256, 1024], P('ep', 'kv'), may hold values from -6 to 6
- new_values: bfloat16 [16, 256, 1024], P('ep', 'kv'), may hold values from -6 to 6
- cache_keys: bfloat16 [16, 2048, 1024], P('ep', 'kv'), may hold values from -6 to 6
- cache_values: bfloat16 [16, 2048, 1024], P('ep', 'kv'), may hold values from -6 to 6
- cached_len: int32 [16], replicated, may hold values from 64 to 2048, as said below
- group_request: int32 [16], P('ep'), may hold values from 0 to 15, each once
- w_out: bfloat16 [1024, 2048], replicated, may hold values from -0.1875 to 0.1875
- norm_gain: bfloat16 [2048], replicated, may hold values from 0.099609375 to 1.8984375
- route_ids: int32 [16, 256, 8], P('ep', 'kv'), may hold values from 0 to 15, all different within a row; in each aligned block of 128 rows (0 to 127, 128 to 255, ..., all dimensions but the last counted through in order) at most 96 rows name the same one
- route_weights: float32 [16, 256, 8], P('ep', 'kv'), may hold values from 0.1 to 0.5
- gate_w: bfloat16 [16, 2048, 512], P('ep', None, 'kv'), may hold values from -0.125 to 0.125
- up_w: bfloat16 [16, 2048, 512], P('ep', None, 'kv'), may hold values from -0.125 to 0.125
- down_w: bfloat16 [16, 512, 2048], P('ep', 'kv'), may hold values from -0.25 to 0.25
Outputs:
- layer_out: bfloat16 [16, 256, 2048], P('ep', 'kv')
Inputs may be any that keep to these rules, and one draw needn't show every extreme that they name: `route_ids`: among the 128 tokens of one device no expert is named more than 96 times, a bound that some block reaches. `cached_len`: some request has exactly 2048 cached positions. `group_request`: every request is held by exactly one group.
All inputs are finite; a program needn't handle non-finite values.
Results may differ from a plain program's by a relative error of at most 0.015.
Values may be sent and summed in bfloat16 or wider, within the bound.
No kernel may reach another device: no remote copies, remote signals or barrier semaphores. Data moves between devices by JAX's collectives and lax.ppermute only.
A program may use at most 128 MiB of HBM per device.

v0:
```python
import math

import jax
import jax.numpy as jnp
from jax import lax
from jax.sharding import PartitionSpec as P

D = 2048
HEAD_DIM = 128
TOP = 8
EXP_DEV = 1


def combined_all(shard, axis, join):
    gathered = jax.tree.map(
        lambda a, kind: lax.all_gather(a.astype(kind), axis),
        shard,
        (jnp.bfloat16, jnp.bfloat16, jnp.bfloat16),
    )

    def take(source):
        return jax.tree.map(
            lambda a, own: lax.dynamic_index_in_dim(a, source, 0, False).astype(own.dtype),
            gathered,
            shard,
        )

    return lax.fori_loop(
        1, lax.axis_size(axis), lambda source, state: join(state, take(source)), take(0)
    )


def expert_full(row_block, gate_part, up_part, down_part):
    gate_val = jnp.einsum(
        "sjkd,jdf->sjkf", row_block, gate_part, preferred_element_type=jnp.float32
    )
    up_val = jnp.einsum("sjkd,jdf->sjkf", row_block, up_part, preferred_element_type=jnp.float32)
    act = (jax.nn.silu(gate_val) * up_val).astype(jnp.bfloat16)
    return jnp.einsum("sjkf,jfd->sjkd", act, down_part, preferred_element_type=jnp.float32)


def shards(
    resid,
    queries,
    new_keys,
    new_values,
    cache_keys,
    cache_values,
    cached_len,
    group_request,
    w_out,
    norm_gain,
    route_ids,
    route_weights,
    gate_w,
    up_w,
    down_w,
):
    kv_rank = lax.axis_index("kv")
    ep_count = lax.axis_size("ep")
    tok_dev = resid.shape[1]
    cl_dev = cache_keys.shape[1]
    feat = queries.shape[2]
    head_count = feat // HEAD_DIM
    score_scale = 1.0 / math.sqrt(HEAD_DIM)
    request_index = jnp.arange(cached_len.shape[0], dtype=jnp.int32)
    length = jnp.sum(jnp.where(request_index == group_request[0], cached_len, 0))
    every_query = lax.all_gather(queries[0], "kv", axis=0, tiled=True)
    new_total = every_query.shape[0]
    query_heads = every_query.reshape(new_total, head_count, HEAD_DIM)
    key_cache = cache_keys[0].reshape(cl_dev, head_count, HEAD_DIM)
    value_cache = cache_values[0].reshape(cl_dev, head_count, HEAD_DIM)
    key_new = new_keys[0].reshape(tok_dev, head_count, HEAD_DIM)
    value_new = new_values[0].reshape(tok_dev, head_count, HEAD_DIM)
    score_cache = (
        jnp.einsum("qhd,khd->qhk", query_heads, key_cache, preferred_element_type=jnp.float32)
        * score_scale
    )
    position = kv_rank * cl_dev + jnp.arange(cl_dev, dtype=jnp.int32)
    score_cache = jnp.where((position < length)[None, None, :], score_cache, -jnp.inf)
    score_new = (
        jnp.einsum("qhd,khd->qhk", query_heads, key_new, preferred_element_type=jnp.float32)
        * score_scale
    )
    local_top = jnp.maximum(jnp.max(score_cache, axis=-1), jnp.max(score_new, axis=-1))
    expo_cache = jnp.exp(score_cache - local_top[..., None])
    expo_new = jnp.exp(score_new - local_top[..., None])
    denom = jnp.sum(expo_cache, axis=-1) + jnp.sum(expo_new, axis=-1)
    summed = jnp.einsum(
        "qhk,khd->qhd",
        expo_cache.astype(jnp.bfloat16),
        value_cache,
        preferred_element_type=jnp.float32,
    )
    summed = summed + jnp.einsum(
        "qhk,khd->qhd", expo_new.astype(jnp.bfloat16), value_new, preferred_element_type=jnp.float32
    )
    summed, denom = (summed.reshape(new_total, feat), denom)

    def join(first, second):
        first_top, first_denom, first_sum = first
        second_top, second_denom, second_sum = second
        joint_top = jnp.maximum(first_top, second_top)
        first_factor = jnp.exp(first_top - joint_top)
        second_factor = jnp.exp(second_top - joint_top)
        rows_here = first_sum.shape[0]
        joint_sum = (
            first_sum.reshape(rows_here, head_count, HEAD_DIM) * first_factor[..., None]
            + second_sum.reshape(rows_here, head_count, HEAD_DIM) * second_factor[..., None]
        )
        return (
            joint_top,
            first_denom * first_factor + second_denom * second_factor,
            joint_sum.reshape(rows_here, feat),
        )

    joint_top, joint_denom, joint_sum = combined_all((local_top, denom, summed), "kv", join)
    row_start = kv_rank * tok_dev
    own_sum = lax.dynamic_slice_in_dim(joint_sum, row_start, tok_dev, 0)
    own_denom = lax.dynamic_slice_in_dim(joint_denom, row_start, tok_dev, 0)
    attended = (
        (own_sum.reshape(tok_dev, head_count, HEAD_DIM) / own_denom[..., None])
        .reshape(tok_dev, feat)
        .astype(jnp.bfloat16)
    )
    proj = jnp.dot(attended, w_out, preferred_element_type=jnp.float32)
    hidden = (resid[0].astype(jnp.float32) + proj).astype(jnp.bfloat16)
    hidden_f = hidden.astype(jnp.float32)
    normed = (
        hidden_f
        * lax.rsqrt(jnp.mean(hidden_f * hidden_f, axis=-1, keepdims=True) + 1e-06)
        * norm_gain.astype(jnp.float32)
    ).astype(jnp.bfloat16)
    expert_count = EXP_DEV * ep_count
    capacity = min(tok_dev, max(2, tok_dev * TOP * 3 // (2 * expert_count)))
    route_flat = route_ids[0].reshape(-1)
    one_hot = (route_flat[:, None] == jnp.arange(expert_count, dtype=jnp.int32)[None, :]).astype(
        jnp.int32
    )
    rank_in = jnp.sum((jnp.cumsum(one_hot, axis=0) - 1) * one_hot, axis=1)
    slot_of = route_flat * capacity + rank_in
    slot_index = jnp.arange(expert_count * capacity, dtype=jnp.int32)
    placing = jnp.sum(
        (slot_of.reshape(tok_dev, TOP)[None, :, :] == slot_index[:, None, None]).astype(jnp.int32),
        axis=-1,
    ).astype(jnp.bfloat16)
    outgoing = jnp.dot(placing, normed, preferred_element_type=jnp.float32).astype(jnp.bfloat16)
    outgoing = outgoing.reshape(ep_count, EXP_DEV, capacity, D)
    full_gate, full_up, full_down = (
        lax.all_gather(gate_w, "kv", axis=2, tiled=True),
        lax.all_gather(up_w, "kv", axis=2, tiled=True),
        lax.all_gather(down_w, "kv", axis=1, tiled=True),
    )
    expert_out = expert_full(
        lax.all_to_all(outgoing, "ep", split_axis=0, concat_axis=0, tiled=True),
        full_gate,
        full_up,
        full_down,
    ).astype(jnp.bfloat16)
    returned = lax.all_to_all(expert_out, "ep", split_axis=0, concat_axis=0, tiled=True).reshape(
        expert_count * capacity, D
    )
    picked = jnp.take(returned, slot_of, axis=0).reshape(tok_dev, TOP, D)
    moe_sum = jnp.sum(picked.astype(jnp.float32) * route_weights[0][..., None], axis=1)
    return (hidden_f + moe_sum).astype(jnp.bfloat16)[None]


def solution(mesh):
    placed = (
        P("ep", "kv", None),
        P("ep", "kv", None),
        P("ep", "kv", None),
        P("ep", "kv", None),
        P("ep", "kv", None),
        P("ep", "kv", None),
        P(),
        P("ep"),
        P(),
        P(),
        P("ep", "kv", None),
        P("ep", "kv", None),
        P("ep", None, "kv"),
        P("ep", None, "kv"),
        P("ep", "kv", None),
    )
    return jax.shard_map(
        shards, mesh=mesh, in_specs=placed, out_specs=P("ep", "kv", None), check_vma=False
    )
```

profile of v0, /device:TPU:15, one launch (start us, length us, event | category | flops | bytes accessed | tf_op | source)
XLA Modules:
  0.0 406.2 jit_solution(18352279872972079744)
XLA Ops:
  7.2 1.1 copy.85
  8.4 7.9 %all-gather = bf16[1,256,1024]{1,2,0:T(8,128)(2,1)S(1)} all-gather(bf16[1,128,1024]{1,2,0:T(8,128)(2,1)S(1)} %copy.85), channel_id=2, replica_groups=mesh['kv'=2,'ep'=16] {'kv'}, dimensions={1}, use_global_device_ids=true | all-gather | bytes 786432 | tf_op jit(solution)/shard_map/all_gather | solution.py:68
  16.3 3.6 copy.115
  20.0 3.9 copy.113
  24.1 0.6 fusion.60
  24.7 0.6 add_compare_fusion
  25.7 3.2 bitcast_reduce_fusion
  28.9 1.9 fusion.7
  30.8 1.3 copy-done
  32.4 1.0 copy.94
  33.5 4.5 %fusion.1 = f32[256,8]{0,1:T(8,128)S(1)} fusion(f32[8,1024,256]{2,1,0:T(8,128)} %copy-done, f32[256,8]{0,1:T(8,128)S(1)} %get-tuple-element.20, pred[1024]{0:T(1024)(128)(4,1)S(1)} %add_compare_fusion), kind=kLoop, calls=%fused_computation.7 | loop fusion | flops 8386560 | bytes 8406016 | tf_op jit(solution)/shard_map/reduce_sum | solution.py:88
  38.5 3.2 all-gather.2
  41.7 3.7 all-gather.1
  45.8 4.5 %reduce-window.6 = s32[16,8,128]{2,1,0:T(8,128)S(1)} reduce-window(s32[16,8,128]{2,1,0:T(8,128)S(1)} %fusion.55, s32[]{:T(128)} %constant.63.clone.1), window={size=1x1x128 pad=0_0x0_0x127_0}, to_apply=%region_5.6 | reduce-window | flops 2080768 | bytes 131076 | tf_op jit(solution)/shard_map/reduce-window
  50.9 8.0 %convert_reduce_fusion = s32[1536,128]{1,0:T(8,128)S(1)} fusion(s32[128,8]{0,1:T(8,128)S(1)} %get-tuple-element.38), kind=kLoop, calls=%fused_computation.14 | loop fusion | flops 4521984 | bytes 790528 | tf_op jit(solution)/shard_map/reduce_sum | solution.py:143
  58.9 0.3 mul.128
  59.6 1.5 copy_bitcast_fusion
  61.0 1.3 slice_bitcast_fusion.1
  62.5 3.3 multiply_reduce_fusion.1
  65.8 4.5 %convolution_convert_fusion = bf16[1536,2048]{1,0:T(8,128)(2,1)} fusion(f32[128,2048]{1,0:T(8,128)S(1)} %get-tuple-element.44, f32[2048]{0:T(1024)S(1)} %convert_element_type.190, f32[128]{0:T(128)S(1)} %add_rsqrt_fusion, s32[1536,128]{1,0:T(8,128)S(1)} %convert_reduce_fusion), kind=kOutput, calls=%fused_computation.6 | convolution fusion | flops 809435136 | bytes 8135168 | tf_op jit(solution)/shard_map/dot_general | solution.py:147
  70.4 9.4 %all-to-all-start = ((bf16[16,1,96,2048]{3,2,1,0:T(8,128)(2,1)}), bf16[16,1,96,2048]{3,2,1,0:T(8,128)(2,1)}, u32[]{:S(2)}, u32[]{:S(2)}) async-start(bf16[16,1,96,2048]{3,2,1,0:T(8,128)(2,1)} %bitcast.162), calls=%async_computation | async-start | bytes 12582912 | tf_op jit(solution)/shard_map/all_to_all | solution.py:155
  79.8 0.7 all-gather.12.cloned.1.call-update
  80.6 0.7 all-gather.10.cloned.1.call-update
  81.9 33.1 %all-gather.12.cloned.1.call-done = bf16[1,2048,512]{2,1,0:T(8,128)(2,1)} async-done(((bf16[1,2048,256]{2,1,0:T(8,128)(2,1)}), bf16[1,2048,512]{2,1,0:T(8,128)(2,1)}) %all-gather.12.cloned.1.call-update) | async-done | bytes 2097168 | tf_op jit(solution)/shard_map/all_gather | solution.py:151
  114.9 102.3 %all-to-all-done = bf16[16,1,96,2048]{3,2,1,0:T(8,128)(2,1)} async-done(((bf16[16,1,96,2048]{3,2,1,0:T(8,128)(2,1)}), bf16[16,1,96,2048]{3,2,1,0:T(8,128)(2,1)}, u32[]{:S(2)}, u32[]{:S(2)}) %all-to-all-start) | async-done | bytes 6291488 | tf_op jit(solution)/shard_map/all_to_all | solution.py:155
  217.2 8.5 %fusion.3 = f32[16,96,512]{2,1,0:T(8,128)} fusion(bf16[16,1,96,2048]{3,2,1,0:T(8,128)(2,1)} %all-to-all-done, bf16[1,2048,512]{2,1,0:T(8,128)(2,1)} %all-gather.12.cloned.1.call-done), kind=kOutput, calls=%fused_computation.9 | convolution fusion | flops 3221225472 | bytes 11534336 | tf_op jit(solution)/shard_map/sjkd,jdf->sjkf/dot_general | solution.py:37
  225.7 12.6 %convert_bitcast_fusion = bf16[16,1,96,2048]{3,2,1,0:T(8,128)(2,1)} fusion(bf16[1,512,2048]{2,1,0:T(8,128)(2,1)} %all-gather.14.cloned.1.call-done, f32[16,96,512]{2,1,0:T(8,128)} %fusion.3, bf16[1,2048,512]{2,1,0:T(8,128)(2,1)} %all-gather.10.cloned.1.call-done, bf16[16,1,96,2048]{3,2,1,0:T(8,128)(2,1)} %all-to-all-done), kind=kOutput, calls=%fused_computation.13 | convolution fusion | flops 6450315264 | bytes 19922944 | tf_op jit(solution)/shard_map/sjkf,jfd->sjkd/dot_general | solution.py:39
  238.3 5.0 %all-to-all-start.1 = ((bf16[16,1,96,2048]{3,2,1,0:T(8,128)(2,1)}), bf16[16,1,96,2048]{3,2,1,0:T(8,128)(2,1)}, u32[]{:S(2)}, u32[]{:S(2)}) async-start(bf16[16,1,96,2048]{3,2,1,0:T(8,128)(2,1)} %convert_bitcast_fusion), calls=%async_computation.1 | async-start | bytes 12582912 | tf_op jit(solution)/shard_map/all_to_all | solution.py:160
  244.0 136.8 %all-to-all-done.1 = bf16[16,1,96,2048]{3,2,1,0:T(8,128)(2,1)} async-done(((bf16[16,1,96,2048]{3,2,1,0:T(8,128)(2,1)}), bf16[16,1,96,2048]{3,2,1,0:T(8,128)(2,1)}, u32[]{:S(2)}, u32[]{:S(2)}) %all-to-all-start.1) | async-done | bytes 6291488 | tf_op jit(solution)/shard_map/all_to_all | solution.py:160
  380.8 12.4 %gather_fusion = bf16[1024,2048]{1,0:T(8,128)(2,1)} fusion(bf16[1536,2048]{1,0:T(8,128)(2,1)} %bitcast.37, s32[1024]{0:T(1024)S(1)} %broadcast_clamp_fusion), kind=kCustom, calls=%fused_computation | custom fusion | bytes 8392704 | tf_op jit(solution)/shard_map/jit(_take)/gather | solution.py:163
  393.1 5.6 %multiply_reduce_fusion = f32[128,2048]{1,0:T(8,128)S(1)} fusion(bf16[1024,2048]{1,0:T(8,128)(2,1)} %gather_fusion, f32[128,8]{1,0:T(8,128)S(1)} %copy.108, pred[128,8]{1,0:T(8,128)(4,1)S(1)} %copy.103), kind=kLoop, calls=%fused_computation.4 | loop fusion | flops 8126464 | bytes 5248000 | tf_op jit(solution)/shard_map/reduce_sum | solution.py:164
  398.8 0.9 fusion.42
  (66 shorter events, 4.0 us)
Async XLA Ops:
  6.5 13.4 %copy-start.3 = (bf16[1,128,1024]{2,1,0:T(8,128)(2,1)S(1)}, bf16[1,128,1024]{2,1,0:T(8,128)(2,1)}, u32[]{:S(2)}) copy-start(bf16[1,128,1024]{2,1,0:T(8,128)(2,1)} %param.17) | copy-start | bytes 786436
  6.5 54.5 %all-gather.8.cloned.1.call-start = ((), (), s32[]{:S(2)}) async-start(), calls=%async_computation.2 | async-start | bytes 1572864 | tf_op jit(solution)/shard_map/all_gather | solution.py:16
  16.3 7.6 %copy-start.4 = (bf16[1,128,1024]{2,1,0:T(8,128)(2,1)S(1)}, bf16[1,128,1024]{2,1,0:T(8,128)(2,1)}, u32[]{:S(2)}) copy-start(bf16[1,128,1024]{2,1,0:T(8,128)(2,1)} %param.18) | copy-start | bytes 786436
  16.3 7.8 %copy-start.8 = (s32[16]{0:T(128)S(1)}, s32[16]{0:T(128)}, u32[]{:S(2)}) copy-start(s32[16]{0:T(128)} %param.21) | copy-start | bytes 196
  25.7 3.2 copy-start.1
  28.9 3.2 copy-start
  33.4 4.7 %copy-start.5 = (s32[1,128,8]{1,2,0:T(8,128)S(1)}, s32[1,128,8]{1,2,0:T(8,128)}, u32[]{:S(2)}) copy-start(s32[1,128,8]{1,2,0:T(8,128)} %param.25) | copy-start | bytes 12292
  33.4 17.4 %copy-start.6 = (bf16[2048]{0:T(1024)(128)(2,1)S(1)}, bf16[2048]{0:T(1024)(128)(2,1)}, u32[]{:S(2)}) copy-start(bf16[2048]{0:T(1024)(128)(2,1)} %param.24) | copy-start | bytes 12292
  59.2 3.3 copy-start.2
  70.4 146.8 %all-to-all-start = ((bf16[16,1,96,2048]{3,2,1,0:T(8,128)(2,1)}), bf16[16,1,96,2048]{3,2,1,0:T(8,128)(2,1)}, u32[]{:S(2)}, u32[]{:S(2)}) async-start(bf16[16,1,96,2048]{3,2,1,0:T(8,128)(2,1)} %bitcast.162), calls=%async_computation | async-start | bytes 12582912 | tf_op jit(solution)/shard_map/all_to_all | solution.py:155
  79.8 35.1 %all-gather.12.cloned.1.call-start = ((), (), s32[]{:S(2)}) async-start(), calls=%async_computation.4 | async-start | bytes 3145728 | tf_op jit(solution)/shard_map/all_gather | solution.py:151
  80.5 145.2 %all-gather.10.cloned.1.call-start = ((), (), s32[]{:S(2)}) async-start(), calls=%async_computation.3 | async-start | bytes 3145728 | tf_op jit(solution)/shard_map/all_gather | solution.py:150
  81.3 144.4 %all-gather.14.cloned.1.call-start = ((), (), s32[]{:S(2)}) async-start(), calls=%async_computation.5 | async-start | bytes 3145728 | tf_op jit(solution)/shard_map/all_gather | solution.py:152
  238.3 5.5 %copy-start.7 = (f32[1,128,8]{1,2,0:T(8,128)S(1)}, f32[1,128,8]{1,2,0:T(8,128)}, u32[]{:S(2)}) copy-start(f32[1,128,8]{1,2,0:T(8,128)} %param.26) | copy-start | bytes 12292
  238.3 142.4 %all-to-all-start.1 = ((bf16[16,1,96,2048]{3,2,1,0:T(8,128)(2,1)}), bf16[16,1,96,2048]{3,2,1,0:T(8,128)(2,1)}, u32[]{:S(2)}, u32[]{:S(2)}) async-start(bf16[16,1,96,2048]{3,2,1,0:T(8,128)(2,1)} %convert_bitcast_fusion), calls=%async_computation.1 | async-start | bytes 12582912 | tf_op jit(solution)/shard_map/all_to_all | solution.py:160
Sparse Core Ops, SparseCore 0:
  33.6 22.3 all-gather.7
  82.2 32.7 all-gather.11
  116.5 33.0 all-gather.9
  151.0 33.1 all-gather.13
where the time goes:
time: 407 us; the launch traced here: 406 us
  waiting for transfers between devices  274 us (67%)
  matrix products  34.7 us (9%)
  local copies, waits for them, and re-layouts  28.8 us (7%)
  other arithmetic  25.2 us (6%)
  starting transfers between devices  14.8 us (4%)
  blocking collectives  14.8 us (4%)
  between operations  14.1 us (3%)
    all_to_all x1, waiting for transfers between devices, shards(): lax.all_to_all(expert_out, 'ep', split_axis=0, concat_axis=0, tiled=True)  137 us
    all_to_all x1, waiting for transfers between devices, shards(): lax.all_to_all(outgoing, 'ep', split_axis=0, concat_axis=0, tiled=True)  102 us
    all_gather x1, waiting for transfers between devices, shards(): lax.all_gather(up_w, 'kv', axis=2, tiled=True)  33.1 us
    dot_general x1, matrix products, expert_full(): jnp.einsum('sjkf,jfd->sjkd', act, down_part, preferred_element_type=jnp.f...  12.6 us
    gather x1, local copies, waits for them, and re-layouts, shards(): picked = jnp.take(returned, slot_of, axis=0).reshape(tok_dev, TOP, D)  12.4 us
    all_to_all x1, starting transfers between devices, shards(): lax.all_to_all(outgoing, 'ep', split_axis=0, concat_axis=0, tiled=True)  9.41 us
    dot_general x1, matrix products, expert_full(): jnp.einsum('sjkd,jdf->sjkf', row_block, up_part, preferred_element_type=j...  8.51 us
  transfers between devices with their start and end apart: 6, of which 3 were waited for; matrix products, arithmetic and copies ran while one was open for 7% of the time, Pallas kernels for 0%

commit v1 on v0

--- a/solution.py
+++ b/solution.py
@@ -1,3 +1,4 @@
+import functools
 import math
 
 import jax
@@ -39,7 +40,87 @@
     return jnp.einsum("sjkf,jfd->sjkd", act, down_part, preferred_element_type=jnp.float32)
 
 
+def gather_stage(block, pairs_list):
+    parts = [block] + [lax.ppermute(block, "ep", pairs) for pairs in pairs_list]
+    return jax.tree.map(lambda *leaves: jnp.stack(leaves), *parts)
+
+
+def scatter_stage(block, pairs_list):
+    total = block[0]
+    for index, pairs in enumerate(pairs_list, 1):
+        back = [(target, source) for source, target in pairs]
+        sent = lax.ppermute(block[index].astype(jnp.bfloat16), "ep", back)
+        total = total + sent.astype(jnp.float32)
+    return total
+
+
+def dense_moe(plan, normed, route_ids, route_weights, gate_w, up_w, down_w):
+    expert_count = EXP_DEV * lax.axis_size("ep")
+    experts = jnp.arange(expert_count, dtype=jnp.int32)
+    chosen = route_ids[:, :, None] == experts[None, None, :]
+    weight_table = jnp.sum(jnp.where(chosen, route_weights[:, :, None], 0.0), axis=1)
+    block = (normed, weight_table)
+    for pairs_list in plan:
+        block = gather_stage(block, pairs_list)
+    rows, weights = block
+    lead = rows.shape[:-2]
+    rows = rows.reshape(-1, D)
+    own = lax.axis_index("ep")
+    weights = jnp.sum(jnp.where(experts == own, weights.reshape(-1, expert_count), 0.0), axis=1)
+    full_gate = lax.all_gather(gate_w[0], "kv", axis=1, tiled=True)
+    full_up = lax.all_gather(up_w[0], "kv", axis=1, tiled=True)
+    full_down = lax.all_gather(down_w[0], "kv", axis=0, tiled=True)
+    gate_val = jnp.dot(rows, full_gate, preferred_element_type=jnp.float32)
+    up_val = jnp.dot(rows, full_up, preferred_element_type=jnp.float32)
+    act = (jax.nn.silu(gate_val) * up_val).astype(jnp.bfloat16)
+    out_rows = jnp.dot(act, full_down, preferred_element_type=jnp.float32).astype(jnp.bfloat16)
+    partial = (out_rows.astype(jnp.float32) * weights[:, None]).reshape(*lead, -1, D)
+    for pairs_list in reversed(plan):
+        partial = scatter_stage(partial, pairs_list)
+    return partial
+
+
+def gather_plan(mesh, shapes):
+    kv_count, ep_count = mesh.devices.shape
+    rows = ep_count * shapes[0][1] // kv_count
+    if EXP_DEV != 1 or shapes[12][0] != ep_count or rows > 4096:
+        return None
+    places = []
+    for device in mesh.devices[0]:
+        coords = getattr(device, "coords", None)
+        core = getattr(device, "core_on_chip", None)
+        if coords is None or core is None:
+            return None
+        places.append(tuple(coords) + (core,))
+    width = len(places[0])
+    values = [sorted({p[a] for p in places}) for a in range(width)]
+    varying = [a for a in range(width) if len(values[a]) > 1]
+    total = 1
+    for a in varying:
+        total *= len(values[a])
+    if total != ep_count or len(set(places)) != ep_count:
+        return None
+    rank_of = {p: r for r, p in enumerate(places)}
+    core_axis = width - 1
+    order = sorted((a for a in varying if a != core_axis), key=lambda a: -len(values[a]))
+    order += [a for a in varying if a == core_axis]
+    plan = []
+    for a in order:
+        size = len(values[a])
+        stage = []
+        for shift in range(1, size):
+            pairs = []
+            for r, p in enumerate(places):
+                moved = list(p)
+                moved[a] = values[a][(values[a].index(p[a]) + shift) % size]
+                pairs.append((r, rank_of[tuple(moved)]))
+            stage.append(pairs)
+        plan.append(stage)
+    return plan
+
+
 def shards(
+    plan,
     resid,
     queries,
     new_keys,
@@ -131,6 +212,9 @@
         * lax.rsqrt(jnp.mean(hidden_f * hidden_f, axis=-1, keepdims=True) + 1e-06)
         * norm_gain.astype(jnp.float32)
     ).astype(jnp.bfloat16)
+    if plan is not None:
+        moe_sum = dense_moe(plan, normed, route_ids[0], route_weights[0], gate_w, up_w, down_w)
+        return (hidden_f + moe_sum).astype(jnp.bfloat16)[None]
     expert_count = EXP_DEV * ep_count
     capacity = min(tok_dev, max(2, tok_dev * TOP * 3 // (2 * expert_count)))
     route_flat = route_ids[0].reshape(-1)
@@ -183,6 +267,12 @@
         P("ep", None, "kv"),
         P("ep", "kv", None),
     )
-    return jax.shard_map(
-        shards, mesh=mesh, in_specs=placed, out_specs=P("ep", "kv", None), check_vma=False
-    )
+
+    def run(*args):
+        plan = gather_plan(mesh, [a.shape for a in args])
+        body = functools.partial(shards, plan)
+        return jax.shard_map(
+            body, mesh=mesh, in_specs=placed, out_specs=P("ep", "kv", None), check_vma=False
+        )(*args)
+
+    return run

time: 407 us -> 370 us (0.909)
  the two profiles are of different devices: /device:TPU:15 before, /device:TPU:24 now
where the time goes in v1:
time: 370 us; the launch traced here: 367 us
  waiting for transfers between devices  213 us (58%)
  matrix products  36.4 us (10%)
  local copies, waits for them, and re-layouts  29.6 us (8%)
  other arithmetic  29.6 us (8%)
  starting transfers between devices  26.9 us (7%)
  blocking collectives  17.5 us (5%)
  between operations  14.1 us (4%)
    ppermute x5, waiting for transfers between devices, scatter_stage(): sent = lax.ppermute(block[index].astype(jnp.bfloat16), 'ep', back)  92.9 us
    ppermute x10, waiting for transfers between devices, gather_stage(): parts = [block] + [lax.ppermute(block, 'ep', pairs) for pairs in pairs_list]  85 us
    all_gather x1, waiting for transfers between devices, dense_moe(): full_down = lax.all_gather(down_w[0], 'kv', axis=0, tiled=True)  24.1 us
    ppermute x10, starting transfers between devices, gather_stage(): parts = [block] + [lax.ppermute(block, 'ep', pairs) for pairs in pairs_list]  21.4 us
    another operation x6, other arithmetic, gather_stage(): return jax.tree.map(lambda *leaves: jnp.stack(leaves), *parts)  14.2 us
    unnamed x18, local copies, waits for them, and re-layouts  12.2 us
    dot_general x1, matrix products, dense_moe(): gate_val = jnp.dot(rows, full_gate, preferred_element_type=jnp.float32)  10.5 us
    dot_general x1, matrix products, dense_moe(): up_val = jnp.dot(rows, full_up, preferred_element_type=jnp.float32)  10.4 us
  transfers between devices with their start and end apart: 19, of which 14 were waited for; matrix products, arithmetic and copies ran while one was open for 12% of the time, Pallas kernels for 0%

profile of v1, /device:TPU:24, one launch (start us, length us, event | category | flops | bytes accessed | tf_op | source)
XLA Modules:
  0.0 367.3 jit_solution(14168955525180943776)
XLA Ops:
  8.3 8.7 %all-gather = bf16[1,256,1024]{1,2,0:T(8,128)(2,1)S(1)} all-gather(bf16[1,128,1024]{1,2,0:T(8,128)(2,1)S(1)} %copy.50), channel_id=2, replica_groups=mesh['kv'=2,'ep'=16] {'kv'}, dimensions={1}, use_global_device_ids=true | all-gather | bytes 786432 | tf_op jit(solution)/shard_map/all_gather | solution.py:149
  19.2 3.6 copy.69
  22.8 4.0 %copy.67 = bf16[1,1024,1024]{1,2,0:T(8,128)(2,1)} copy(bf16[1,1024,1024]{2,1,0:T(8,128)(2,1)} %param.20) | data formatting | bytes 4194304 | tf_op jit(solution)/shard_map/reshape;squeeze | solution.py:153
  28.4 3.2 bitcast_reduce_fusion
  36.3 4.5 %fusion.1 = f32[256,8]{0,1:T(8,128)S(1)} fusion(f32[8,1024,256]{2,1,0:T(8,128)} %copy-done.1, f32[256,8]{0,1:T(8,128)S(1)} %get-tuple-element.22, pred[1024]{0:T(1024)(128)(4,1)S(1)} %add_compare_fusion), kind=kLoop, calls=%fused_computation.8 | loop fusion | flops 8386560 | bytes 8406016 | tf_op jit(solution)/shard_map/reduce_sum | solution.py:169
  40.9 4.3 %all-gather.1 = bf16[512,8]{0,1:T(8,128)(2,1)S(1)} all-gather(bf16[256,8]{0,1:T(8,128)(2,1)S(1)} %get-tuple-element.21), channel_id=3, replica_groups=mesh['kv'=2,'ep'=16] {'kv'}, dimensions={0}, use_global_device_ids=true | all-gather | bytes 12288 | tf_op jit(solution)/shard_map/all_gather | solution.py:17
  45.7 4.4 %all-gather.2 = bf16[512,8]{0,1:T(8,128)(2,1)S(1)} all-gather(bf16[256,8]{0,1:T(8,128)(2,1)S(1)} %add_convert_fusion), channel_id=4, replica_groups=mesh['kv'=2,'ep'=16] {'kv'}, dimensions={0}, use_global_device_ids=true | all-gather | bytes 12288 | tf_op jit(solution)/shard_map/all_gather | solution.py:17
  51.3 7.4 %all-gather.11.cloned.1.call-done = bf16[2,256,1024]{2,1,0:T(8,128)(2,1)} async-done(((bf16[1,256,1024]{2,1,0:T(8,128)(2,1)}), bf16[2,256,1024]{2,1,0:T(8,128)(2,1)}) %all-gather.11.cloned.1.call-update) | async-done | bytes 1048592 | tf_op jit(solution)/shard_map/all_gather | solution.py:17
  60.2 3.3 multiply_reduce_fusion
  66.8 24.0 %collective-permute-done.1 = bf16[128,2048]{1,0:T(8,128)(2,1)S(1)} collective-permute-done((bf16[128,2048]{1,0:T(8,128)(2,1)S(1)}, bf16[128,2048]{1,0:T(8,128)(2,1)S(1)}, u32[]{:S(2)}, u32[]{:S(2)}) %collective-permute-start.1) | collective-permute-done | bytes 524320 | tf_op jit(solution)/shard_map/ppermute | solution.py:44
  90.8 10.1 %collective-permute-done.2 = bf16[128,2048]{1,0:T(8,128)(2,1)S(1)} collective-permute-done((bf16[128,2048]{1,0:T(8,128)(2,1)S(1)}, bf16[128,2048]{1,0:T(8,128)(2,1)S(1)}, u32[]{:S(2)}, u32[]{:S(2)}) %collective-permute-start.2) | collective-permute-done | bytes 524320 | tf_op jit(solution)/shard_map/ppermute | solution.py:44
  104.1 45.2 %collective-permute-done.3 = bf16[4,128,2048]{2,1,0:T(8,128)(2,1)} collective-permute-done((bf16[4,128,2048]{2,1,0:T(8,128)(2,1)}, bf16[4,128,2048]{2,1,0:T(8,128)(2,1)}, u32[]{:S(2)}, u32[]{:S(2)}) %collective-permute-start.3) | collective-permute-done | bytes 2097184 | tf_op jit(solution)/shard_map/ppermute | solution.py:44
  149.3 4.8 %fusion.47 = (bf16[1,2,4,128,2048]{4,3,2,1,0:T(8,128)(2,1)}, bf16[2,4,128,2048]{3,2,1,0:T(8,128)(2,1)}) fusion(bf16[1,4,128,2048]{3,2,1,0:T(8,128)(2,1)} %bitcast.16, bf16[1,4,128,2048]{3,2,1,0:T(8,128)(2,1)S(1)} %get-tuple-element.38), kind=kLoop, calls=%fused_computation.87 | loop fusion | flops 2097152 | bytes 12582912 | tf_op jit(solution)/shard_map/stack | solution.py:45
  154.2 12.8 %collective-permute-start.7 = (f32[128,16]{0,1:T(8,128)S(1)}, f32[128,16]{0,1:T(8,128)S(1)}, u32[]{:S(2)}, u32[]{:S(2)}) collective-permute-start(f32[128,16]{0,1:T(8,128)S(1)} %select_reduce_fusion), channel_id=1, source_target_pairs={{0,12},{1,13},{2,14},{3,15},{4,0},{5,1},{6,2},{7,3},{8,4},{9,5},{1... | collective-permute-start | bytes 24584 | tf_op jit(solution)/shard_map/ppermute | solution.py:44
  177.0 7.6 %pad_maximum_fusion = bf16[2,2,4,128,2048]{4,3,2,1,0:T(8,128)(2,1)} fusion(bf16[1,2,4,128,2048]{4,3,2,1,0:T(8,128)(2,1)} %bitcast.18, bf16[1,2,4,128,2048]{4,3,2,1,0:T(8,128)(2,1)} %get-tuple-element.23), kind=kLoop, calls=%fused_computation.2 | loop fusion | flops 4194304 | bytes 16777216 | tf_op jit(solution)/shard_map/stack | solution.py:45
  184.6 10.5 %fusion.15 = f32[2048,512]{1,0:T(8,128)} fusion(bf16[2048,2048]{1,0:T(8,128)(2,1)} %bitcast.123, bf16[1,2048,512]{2,1,0:T(8,128)(2,1)} %all-gather.13.cloned.1.call-done), kind=kOutput, calls=%fused_computation.27 | convolution fusion | flops 4294967296 | bytes 14680064 | tf_op jit(solution)/shard_map/dot_general | solution.py:73
  195.1 3.8 %all-gather.15.cloned.1.call-done = bf16[1,2048,512]{2,1,0:T(8,128)(2,1)} async-done(((bf16[1,2048,256]{2,1,0:T(8,128)(2,1)}), bf16[1,2048,512]{2,1,0:T(8,128)(2,1)}) %all-gather.15.cloned.1.call-update) | async-done | bytes 2097168 | tf_op jit(solution)/shard_map/all_gather | solution.py:71
  198.9 10.4 %multiply_convert_fusion = bf16[2048,512]{1,0:T(8,128)(2,1)S(1)} fusion(f32[2048,512]{1,0:T(8,128)} %fusion.15, bf16[2048,2048]{1,0:T(8,128)(2,1)} %bitcast.124, bf16[1,2048,512]{2,1,0:T(8,128)(2,1)} %all-gather.15.cloned.1.call-done), kind=kOutput, calls=%fused_computation.15 | convolution fusion | flops 4301258752 | bytes 16777216 | tf_op jit(solution)/shard_map/dot_general | solution.py:74
  209.3 24.1 %all-gather.17.cloned.1.call-done = bf16[1,512,2048]{2,1,0:T(8,128)(2,1)} async-done(((bf16[1,256,2048]{2,1,0:T(8,128)(2,1)}), bf16[1,512,2048]{2,1,0:T(8,128)(2,1)}) %all-gather.17.cloned.1.call-update) | async-done | bytes 2097168 | tf_op jit(solution)/shard_map/all_gather | solution.py:72
  233.4 6.5 %convert_multiply_fusion = f32[2048,2048]{1,0:T(8,128)S(1)} fusion(f32[2048]{0:T(1024)S(1)} %bitcast.144, bf16[2048,512]{1,0:T(8,128)(2,1)S(1)} %multiply_convert_fusion, bf16[1,512,2048]{2,1,0:T(8,128)(2,1)} %all-gather.17.cloned.1.call-done), kind=kOutput, calls=%fused_computation | convolution fusion | flops 4307550208 | bytes 20979712 | tf_op jit(solution)/shard_map/dot_general | solution.py:76
  240.0 3.0 slice.88
  243.0 4.0 %copy-done = f32[2048,2048]{1,0:T(8,128)} copy-done((f32[2048,2048]{1,0:T(8,128)}, f32[2048,2048]{1,0:T(8,128)S(1)}, u32[]{:S(2)}) %copy-start) | copy-done | bytes 16777240
  246.9 4.0 %slice.53 = f32[1024,2048]{1,0:T(8,128)S(1)} slice(f32[2048,2048]{1,0:T(8,128)} %copy-done), slice={[0:1024], [0:2048]} | slice | bytes 16777216 | tf_op jit(solution)/shard_map/slice | solution.py:49
  250.9 3.4 collective-permute-done.10
  254.3 4.7 %convert_add_fusion = f32[2,4,128,2048]{3,2,1,0:T(8,128)} fusion(f32[2,4,128,2048]{3,2,1,0:T(8,128)S(1)} %bitcast.122, bf16[2,4,128,2048]{3,2,1,0:T(8,128)(2,1)S(1)} %collective-permute-done.10), kind=kLoop, calls=%fused_computation.6 | loop fusion | flops 4194304 | bytes 20971520 | tf_op jit(solution)/shard_map/add | solution.py:53
  259.0 2.5 fusion.12
  263.0 46.2 %collective-permute-done.11 = bf16[4,128,2048]{2,1,0:T(8,128)(2,1)S(1)} collective-permute-done((bf16[4,128,2048]{2,1,0:T(8,128)(2,1)S(1)}, bf16[4,128,2048]{2,1,0:T(8,128)(2,1)S(1)}, u32[]{:S(2)}, u32[]{:S(2)}) %collective-permute-start.11) | collective-permute-done | bytes 2097184 | tf_op jit(solution)/shard_map/ppermute | solution.py:52
  309.2 3.1 fusion.49
  313.1 3.3 collective-permute-start.14
  316.4 12.8 %collective-permute-done.12 = bf16[128,2048]{1,0:T(8,128)(2,1)S(1)} collective-permute-done((bf16[128,2048]{1,0:T(8,128)(2,1)S(1)}, bf16[128,2048]{1,0:T(8,128)(2,1)S(1)}, u32[]{:S(2)}, u32[]{:S(2)}) %collective-permute-start.12) | collective-permute-done | bytes 524320 | tf_op jit(solution)/shard_map/ppermute | solution.py:52
  329.2 9.1 %collective-permute-done.14 = bf16[128,2048]{1,0:T(8,128)(2,1)S(1)} collective-permute-done((bf16[128,2048]{1,0:T(8,128)(2,1)S(1)}, bf16[128,2048]{1,0:T(8,128)(2,1)S(1)}, u32[]{:S(2)}, u32[]{:S(2)}) %collective-permute-start.14) | collective-permute-done | bytes 524320 | tf_op jit(solution)/shard_map/ppermute | solution.py:52
  338.3 21.3 %collective-permute-done.13 = bf16[128,2048]{1,0:T(8,128)(2,1)S(1)} collective-permute-done((bf16[128,2048]{1,0:T(8,128)(2,1)S(1)}, bf16[128,2048]{1,0:T(8,128)(2,1)S(1)}, u32[]{:S(2)}, u32[]{:S(2)}) %collective-permute-start.13) | collective-permute-done | bytes 524320 | tf_op jit(solution)/shard_map/ppermute | solution.py:52
  (77 shorter events, 32.7 us)
Async XLA Ops:
  6.5 52.2 %all-gather.11.cloned.1.call-start = ((), (), s32[]{:S(2)}) async-start(), calls=%async_computation | async-start | bytes 1572864 | tf_op jit(solution)/shard_map/all_gather | solution.py:17
  19.2 7.5 %copy-start.6 = (s32[16]{0:T(128)S(1)}, s32[16]{0:T(128)}, u32[]{:S(2)}) copy-start(s32[16]{0:T(128)} %param.21) | copy-start | bytes 196
  28.4 3.2 copy-start.2
  31.6 3.2 copy-start.1
  36.3 4.6 %copy-start.3 = (bf16[2048]{0:T(1024)(128)(2,1)S(1)}, bf16[2048]{0:T(1024)(128)(2,1)}, u32[]{:S(2)}) copy-start(bf16[2048]{0:T(1024)(128)(2,1)} %param.24) | copy-start | bytes 12292
  36.3 148.4 %all-gather.13.cloned.1.call-start = ((), (), s32[]{:S(2)}) async-start(), calls=%async_computation.1 | async-start | bytes 3145728 | tf_op jit(solution)/shard_map/all_gather | solution.py:70
  63.7 27.1 %collective-permute-start.1 = (bf16[128,2048]{1,0:T(8,128)(2,1)S(1)}, bf16[128,2048]{1,0:T(8,128)(2,1)S(1)}, u32[]{:S(2)}, u32[]{:S(2)}) collective-permute-start(bf16[128,2048]{1,0:T(8,128)(2,1)S(1)} %multiply_convert_fusion.1), channel_id=1, source_target_pairs={{0,8},{1,9},{2,10},{3,11},{4,12},{5,13},{6,14},{7,15},{8,0},{9,1},... | collective-permute-start | bytes 1572872 | tf_op jit(solution)/shard_map/ppermute | solution.py:44
  64.2 26.5 %collective-permute-start = (bf16[128,2048]{1,0:T(8,128)(2,1)S(1)}, bf16[128,2048]{1,0:T(8,128)(2,1)S(1)}, u32[]{:S(2)}, u32[]{:S(2)}) collective-permute-start(bf16[128,2048]{1,0:T(8,128)(2,1)S(1)} %multiply_convert_fusion.1), channel_id=1, source_target_pairs={{0,4},{1,5},{2,6},{3,7},{4,8},{5,9},{6,10},{7,11},{8,12},{9,13},{1... | collective-permute-start | bytes 1572872 | tf_op jit(solution)/shard_map/ppermute | solution.py:44
  66.6 34.3 %collective-permute-start.2 = (bf16[128,2048]{1,0:T(8,128)(2,1)S(1)}, bf16[128,2048]{1,0:T(8,128)(2,1)S(1)}, u32[]{:S(2)}, u32[]{:S(2)}) collective-permute-start(bf16[128,2048]{1,0:T(8,128)(2,1)S(1)} %multiply_convert_fusion.1), channel_id=1, source_target_pairs={{0,12},{1,13},{2,14},{3,15},{4,0},{5,1},{6,2},{7,3},{8,4},{9,5},{1... | collective-permute-start | bytes 1572872 | tf_op jit(solution)/shard_map/ppermute | solution.py:44
  102.6 46.8 %collective-permute-start.3 = (bf16[4,128,2048]{2,1,0:T(8,128)(2,1)}, bf16[4,128,2048]{2,1,0:T(8,128)(2,1)}, u32[]{:S(2)}, u32[]{:S(2)}) collective-permute-start(bf16[4,128,2048]{2,1,0:T(8,128)(2,1)} %get-tuple-element.39), channel_id=1, source_target_pairs={{0,2},{1,3},{2,0},{3,1},{4,6},{5,7},{6,4},{7,5},{8,10},{9,11},{10,... | collective-permute-start | bytes 6291464 | tf_op jit(solution)/shard_map/ppermute | solution.py:44
  104.1 94.8 %all-gather.15.cloned.1.call-start = ((), (), s32[]{:S(2)}) async-start(), calls=%async_computation.2 | async-start | bytes 3145728 | tf_op jit(solution)/shard_map/all_gather | solution.py:71
  149.3 4.9 %copy-start.4 = (f32[1,128,8]{1,2,0:T(8,128)S(1)}, f32[1,128,8]{1,2,0:T(8,128)}, u32[]{:S(2)}) copy-start(f32[1,128,8]{1,2,0:T(8,128)} %param.26) | copy-start | bytes 12292
  149.3 4.9 %copy-start.5 = (s32[1,128,8]{1,2,0:T(8,128)S(1)}, s32[1,128,8]{1,2,0:T(8,128)}, u32[]{:S(2)}) copy-start(s32[1,128,8]{1,2,0:T(8,128)} %param.25) | copy-start | bytes 12292
  154.1 22.9 %collective-permute-start.4 = (bf16[2,4,128,2048]{3,2,1,0:T(8,128)(2,1)}, bf16[2,4,128,2048]{3,2,1,0:T(8,128)(2,1)}, u32[]{:S(2)}, u32[]{:S(2)}) collective-permute-start(bf16[2,4,128,2048]{3,2,1,0:T(8,128)(2,1)} %get-tuple-element.32), channel_id=1, source_target_pairs={{0,1},{1,0},{2,3},{3,2},{4,5},{5,4},{6,7},{7,6},{8,9},{9,8},{10,11... | collective-permute-start | bytes 12582920 | tf_op jit(solution)/shard_map/ppermute | solution.py:44
  154.1 79.3 %all-gather.17.cloned.1.call-start = ((), (), s32[]{:S(2)}) async-start(), calls=%async_computation.3 | async-start | bytes 3145728 | tf_op jit(solution)/shard_map/all_gather | solution.py:72
  154.2 15.3 %collective-permute-start.7 = (f32[128,16]{0,1:T(8,128)S(1)}, f32[128,16]{0,1:T(8,128)S(1)}, u32[]{:S(2)}, u32[]{:S(2)}) collective-permute-start(f32[128,16]{0,1:T(8,128)S(1)} %select_reduce_fusion), channel_id=1, source_target_pairs={{0,12},{1,13},{2,14},{3,15},{4,0},{5,1},{6,2},{7,3},{8,4},{9,5},{1... | collective-permute-start | bytes 24584 | tf_op jit(solution)/shard_map/ppermute | solution.py:44
  167.0 4.5 %collective-permute-start.6 = (f32[128,16]{0,1:T(8,128)S(1)}, f32[128,16]{0,1:T(8,128)S(1)}, u32[]{:S(2)}, u32[]{:S(2)}) collective-permute-start(f32[128,16]{0,1:T(8,128)S(1)} %select_reduce_fusion), channel_id=1, source_target_pairs={{0,8},{1,9},{2,10},{3,11},{4,12},{5,13},{6,14},{7,15},{8,0},{9,1},... | collective-permute-start | bytes 24584 | tf_op jit(solution)/shard_map/ppermute | solution.py:44
  167.0 4.5 %collective-permute-start.5 = (f32[128,16]{0,1:T(8,128)S(1)}, f32[128,16]{0,1:T(8,128)S(1)}, u32[]{:S(2)}, u32[]{:S(2)}) collective-permute-start(f32[128,16]{0,1:T(8,128)S(1)} %select_reduce_fusion), channel_id=1, source_target_pairs={{0,4},{1,5},{2,6},{3,7},{4,8},{5,9},{6,10},{7,11},{8,12},{9,13},{1... | collective-permute-start | bytes 24584 | tf_op jit(solution)/shard_map/ppermute | solution.py:44
  171.6 4.0 %collective-permute-start.8 = (f32[4,128,16]{1,2,0:T(8,128)S(1)}, f32[4,128,16]{1,2,0:T(8,128)S(1)}, u32[]{:S(2)}, u32[]{:S(2)}) collective-permute-start(f32[4,128,16]{1,2,0:T(8,128)S(1)} %get-tuple-element.45), channel_id=1, source_target_pairs={{0,2},{1,3},{2,0},{3,1},{4,6},{5,7},{6,4},{7,5},{8,10},{9,11},{10,... | collective-permute-start | bytes 98312 | tf_op jit(solution)/shard_map/ppermute | solution.py:44
  175.6 1.3 collective-permute-start.9
  239.9 7.0 %copy-start = (f32[2048,2048]{1,0:T(8,128)}, f32[2048,2048]{1,0:T(8,128)S(1)}, u32[]{:S(2)}) copy-start(f32[2048,2048]{1,0:T(8,128)S(1)} %convert_multiply_fusion) | copy-start | bytes 50331652
  246.9 7.4 %collective-permute-start.10 = (bf16[2,4,128,2048]{3,2,1,0:T(8,128)(2,1)}, bf16[2,4,128,2048]{3,2,1,0:T(8,128)(2,1)S(1)}, u32[]{:S(2)}, u32[]{:S(2)}) collective-permute-start(bf16[2,4,128,2048]{3,2,1,0:T(8,128)(2,1)} %bitcast.125), channel_id=1, source_target_pairs={{1,0},{0,1},{3,2},{2,3},{5,4},{4,5},{7,6},{6,7},{9,8},{8,9},{11,10... | collective-permute-start | bytes 12582920 | tf_op jit(solution)/shard_map/ppermute | solution.py:52
  261.5 47.7 %collective-permute-start.11 = (bf16[4,128,2048]{2,1,0:T(8,128)(2,1)S(1)}, bf16[4,128,2048]{2,1,0:T(8,128)(2,1)S(1)}, u32[]{:S(2)}, u32[]{:S(2)}) collective-permute-start(bf16[4,128,2048]{2,1,0:T(8,128)(2,1)S(1)} %fusion.12), channel_id=1, source_target_pairs={{2,0},{3,1},{0,2},{1,3},{6,4},{7,5},{4,6},{5,7},{10,8},{11,9},{8,1... | collective-permute-start | bytes 6291464 | tf_op jit(solution)/shard_map/ppermute | solution.py:52
  312.5 16.7 %collective-permute-start.12 = (bf16[128,2048]{1,0:T(8,128)(2,1)S(1)}, bf16[128,2048]{1,0:T(8,128)(2,1)S(1)}, u32[]{:S(2)}, u32[]{:S(2)}) collective-permute-start(bf16[128,2048]{1,0:T(8,128)(2,1)S(1)} %get-tuple-element.34), channel_id=1, source_target_pairs={{4,0},{5,1},{6,2},{7,3},{8,4},{9,5},{10,6},{11,7},{12,8},{13,9},{1... | collective-permute-start | bytes 1572872 | tf_op jit(solution)/shard_map/ppermute | solution.py:52
  313.1 25.2 %collective-permute-start.14 = (bf16[128,2048]{1,0:T(8,128)(2,1)S(1)}, bf16[128,2048]{1,0:T(8,128)(2,1)S(1)}, u32[]{:S(2)}, u32[]{:S(2)}) collective-permute-start(bf16[128,2048]{1,0:T(8,128)(2,1)S(1)} %get-tuple-element.36), channel_id=1, source_target_pairs={{12,0},{13,1},{14,2},{15,3},{0,4},{1,5},{2,6},{3,7},{4,8},{5,9},{6... | collective-permute-start | bytes 1572872 | tf_op jit(solution)/shard_map/ppermute | solution.py:52
  316.4 43.3 %collective-permute-start.13 = (bf16[128,2048]{1,0:T(8,128)(2,1)S(1)}, bf16[128,2048]{1,0:T(8,128)(2,1)S(1)}, u32[]{:S(2)}, u32[]{:S(2)}) collective-permute-start(bf16[128,2048]{1,0:T(8,128)(2,1)S(1)} %get-tuple-element.37), channel_id=1, source_target_pairs={{8,0},{9,1},{10,2},{11,3},{12,4},{13,5},{14,6},{15,7},{0,8},{1,9},... | collective-permute-start | bytes 1572872 | tf_op jit(solution)/shard_map/ppermute | solution.py:52
Sparse Core Ops, SparseCore 0:
  36.4 22.3 all-gather.10
  104.2 42.3 all-gather.12
  154.2 44.5 all-gather.14
  200.3 33.1 all-gather.16

commit v2 on v1

--- a/solution.py
+++ b/solution.py
@@ -40,44 +40,68 @@
     return jnp.einsum("sjkf,jfd->sjkd", act, down_part, preferred_element_type=jnp.float32)
 
 
-def gather_stage(block, pairs_list):
-    parts = [block] + [lax.ppermute(block, "ep", pairs) for pairs in pairs_list]
-    return jax.tree.map(lambda *leaves: jnp.stack(leaves), *parts)
-
-
-def scatter_stage(block, pairs_list):
-    total = block[0]
-    for index, pairs in enumerate(pairs_list, 1):
-        back = [(target, source) for source, target in pairs]
-        sent = lax.ppermute(block[index].astype(jnp.bfloat16), "ep", back)
-        total = total + sent.astype(jnp.float32)
-    return total
+def full_weights(gate_w, up_w, down_w):
+    kv_count = lax.axis_size("kv")
+    if kv_count != 2:
+        return (
+            lax.all_gather(gate_w[0], "kv", axis=1, tiled=True),
+            lax.all_gather(up_w[0], "kv", axis=1, tiled=True),
+            lax.all_gather(down_w[0], "kv", axis=0, tiled=True),
+        )
+    mine = (gate_w[0], up_w[0], down_w[0])
+    other = lax.ppermute(mine, "kv", [(0, 1), (1, 0)])
+    first = lax.axis_index("kv") == 0
+    joined = []
+    for own, far, axis in zip(mine, other, (1, 1, 0)):
+        low = jnp.where(first, own, far)
+        high = jnp.where(first, far, own)
+        joined.append(jnp.concatenate([low, high], axis=axis))
+    return tuple(joined)
 
 
 def dense_moe(plan, normed, route_ids, route_weights, gate_w, up_w, down_w):
     expert_count = EXP_DEV * lax.axis_size("ep")
     experts = jnp.arange(expert_count, dtype=jnp.int32)
+    own_expert = lax.axis_index("ep")
     chosen = route_ids[:, :, None] == experts[None, None, :]
     weight_table = jnp.sum(jnp.where(chosen, route_weights[:, :, None], 0.0), axis=1)
-    block = (normed, weight_table)
+    full_gate, full_up, full_down = full_weights(gate_w, up_w, down_w)
+
+    def expert(block):
+        rows, table = block
+        lead = rows.shape[:-1]
+        rows = rows.reshape(-1, D)
+        weights = jnp.sum(
+            jnp.where(experts == own_expert, table.reshape(-1, expert_count), 0.0), axis=1
+        )
+        gate_val = jnp.dot(rows, full_gate, preferred_element_type=jnp.float32)
+        up_val = jnp.dot(rows, full_up, preferred_element_type=jnp.float32)
+        act = (jax.nn.silu(gate_val) * up_val).astype(jnp.bfloat16)
+        out_rows = jnp.dot(act, full_down, preferred_element_type=jnp.float32)
+        out_rows = out_rows.astype(jnp.bfloat16).astype(jnp.float32)
+        return (out_rows * weights[:, None]).reshape(*lead, D)
+
+    current = (normed, weight_table)
+    arrived = []
     for pairs_list in plan:
-        block = gather_stage(block, pairs_list)
-    rows, weights = block
-    lead = rows.shape[:-2]
-    rows = rows.reshape(-1, D)
-    own = lax.axis_index("ep")
-    weights = jnp.sum(jnp.where(experts == own, weights.reshape(-1, expert_count), 0.0), axis=1)
-    full_gate = lax.all_gather(gate_w[0], "kv", axis=1, tiled=True)
-    full_up = lax.all_gather(up_w[0], "kv", axis=1, tiled=True)
-    full_down = lax.all_gather(down_w[0], "kv", axis=0, tiled=True)
-    gate_val = jnp.dot(rows, full_gate, preferred_element_type=jnp.float32)
-    up_val = jnp.dot(rows, full_up, preferred_element_type=jnp.float32)
-    act = (jax.nn.silu(gate_val) * up_val).astype(jnp.bfloat16)
-    out_rows = jnp.dot(act, full_down, preferred_element_type=jnp.float32).astype(jnp.bfloat16)
-    partial = (out_rows.astype(jnp.float32) * weights[:, None]).reshape(*lead, -1, D)
-    for pairs_list in reversed(plan):
-        partial = scatter_stage(partial, pairs_list)
-    return partial
+        received = [lax.ppermute(current, "ep", pairs) for pairs in pairs_list]
+        arrived.append(jax.tree.map(lambda *leaves: jnp.stack(leaves), *received))
+        current = jax.tree.map(lambda *leaves: jnp.stack(leaves), current, *received)
+    own_part = expert((normed, weight_table))
+    new_parts = [expert(block) for block in arrived]
+    pending = None
+    for stage in reversed(range(len(plan))):
+        pairs_list = plan[stage]
+        total = None if pending is None else pending[0]
+        for index, pairs in enumerate(pairs_list, 1):
+            outgoing = new_parts[stage][index - 1]
+            if pending is not None:
+                outgoing = outgoing + pending[index]
+            back = [(target, source) for source, target in pairs]
+            sent = lax.ppermute(outgoing.astype(jnp.bfloat16), "ep", back).astype(jnp.float32)
+            total = sent if total is None else total + sent
+        pending = total
+    return own_part + pending
 
 
 def gather_plan(mesh, shapes):

time: 370 us -> 382 us (1.032)
  matrix products: 36.4 us -> 49.5 us
  starting transfers between devices: 26.9 us -> 39 us
  local copies, waits for them, and re-layouts: 29.6 us -> 19.4 us
    ppermute x15 -> x18, waiting for transfers between devices: 178 us -> 208 us  [the longest x5 82.5 us: dense_moe(): lax.ppermute(outgoing.astype(jnp.bfloat16), 'ep', back).astype(jnp.float32)]
    all_gather x3 -> x0, waiting for transfers between devices: 27.9 us -> none  [the longest x1 24.1 us: dense_moe(): full_down = lax.all_gather(down_w[0], 'kv', axis=0, tiled=True)]
    another operation x7 -> x6, other arithmetic: 17.3 us -> 3.06 us  [the longest x5 2.89 us: dense_moe(): jnp.stack(leaves)]
    dot_general x3 -> x8, matrix products: 27.4 us -> 40.6 us  [the longest x4 28.6 us: expert(): out_rows = jnp.dot(act, full_down, preferred_element_type=jnp.float32)]
    ppermute x15 -> x18, starting transfers between devices: 26.8 us -> 39 us  [the longest x10 20.9 us: dense_moe(): received = [lax.ppermute(current, 'ep', pairs) for pairs in pairs_list]]
    select_n x0 -> x3, other arithmetic: none -> 7.67 us  [full_weights(): low = jnp.where(first, own, far)]
    slice x2 -> x0, local copies, waits for them, and re-layouts: 6.97 us -> none  [the longest x1 3.96 us: scatter_stage(): total = block[0]]
    convert_element_type x0 -> x3, other arithmetic: none -> 6.12 us  [the longest x1 3.41 us: dense_moe(): lax.ppermute(outgoing.astype(jnp.bfloat16), 'ep', back).astype(jnp.float32)]
  transfers between devices with their start and end apart: 19 -> 19, of which waited for: 14 -> 13; matrix products, arithmetic and copies ran while one was open for 12% -> 9% of each run, Pallas kernels for 0% -> 0%
where the time goes in v2:
time: 382 us
  waiting for transfers between devices  216 us (57%)
  matrix products  49.5 us (13%)
  starting transfers between devices  39 us (10%)
  other arithmetic  26.4 us (7%)
  local copies, waits for them, and re-layouts  19.4 us (5%)
  blocking collectives  17.5 us (5%)
  between operations  14.5 us (4%)
    ppermute x5, waiting for transfers between devices, dense_moe(): lax.ppermute(outgoing.astype(jnp.bfloat16), 'ep', back).astype(jnp.float32)  82.5 us
    ppermute x10, waiting for transfers between devices, dense_moe(): received = [lax.ppermute(current, 'ep', pairs) for pairs in pairs_list]  81.7 us
    ppermute x3, waiting for transfers between devices, full_weights(): other = lax.ppermute(mine, 'kv', [(0, 1), (1, 0)])  44 us
    dot_general x4, matrix products, expert(): out_rows = jnp.dot(act, full_down, preferred_element_type=jnp.float32)  28.6 us
    ppermute x10, starting transfers between devices, dense_moe(): received = [lax.ppermute(current, 'ep', pairs) for pairs in pairs_list]  20.9 us
    ppermute x5, starting transfers between devices, dense_moe(): lax.ppermute(outgoing.astype(jnp.bfloat16), 'ep', back).astype(jnp.float32)  14.5 us
    unnamed x68, local copies, waits for them, and re-layouts  12.5 us
    dot_general x4, matrix products, expert(): gate_val = jnp.dot(rows, full_gate, preferred_element_type=jnp.float32)  12 us
  transfers between devices with their start and end apart: 19, of which 13 were waited for; matrix products, arithmetic and copies ran while one was open for 9% of the time, Pallas kernels for 0%

profile of v2, /device:TPU:24, one launch (start us, length us, event | category | flops | bytes accessed | tf_op | source)
XLA Modules:
  0.0 381.9 jit_solution(4575156648553950076)
XLA Ops:
  8.3 8.7 %all-gather = bf16[1,256,1024]{1,2,0:T(8,128)(2,1)S(1)} all-gather(bf16[1,128,1024]{1,2,0:T(8,128)(2,1)S(1)} %copy.50), channel_id=2, replica_groups=mesh['kv'=2,'ep'=16] {'kv'}, dimensions={1}, use_global_device_ids=true | all-gather | bytes 786432 | tf_op jit(solution)/shard_map/all_gather | solution.py:173
  17.1 3.6 copy.69
  20.8 4.0 %copy.67 = bf16[1,1024,1024]{1,2,0:T(8,128)(2,1)} copy(bf16[1,1024,1024]{2,1,0:T(8,128)(2,1)} %param.20) | data formatting | bytes 4194304 | tf_op jit(solution)/shard_map/reshape;squeeze | solution.py:177
  26.6 3.2 bitcast_reduce_fusion
  34.5 4.5 %fusion.1 = f32[256,8]{0,1:T(8,128)S(1)} fusion(f32[8,1024,256]{2,1,0:T(8,128)} %copy-done.2, f32[256,8]{0,1:T(8,128)S(1)} %get-tuple-element.20, pred[1024]{0:T(1024)(128)(4,1)S(1)} %add_compare_fusion), kind=kLoop, calls=%fused_computation.5 | loop fusion | flops 8386560 | bytes 8406016 | tf_op jit(solution)/shard_map/reduce_sum | solution.py:193
  39.0 4.3 %all-gather.1 = bf16[512,8]{0,1:T(8,128)(2,1)S(1)} all-gather(bf16[256,8]{0,1:T(8,128)(2,1)S(1)} %get-tuple-element.19), channel_id=3, replica_groups=mesh['kv'=2,'ep'=16] {'kv'}, dimensions={0}, use_global_device_ids=true | all-gather | bytes 12288 | tf_op jit(solution)/shard_map/all_gather | solution.py:17
  43.8 4.4 %all-gather.2 = bf16[512,8]{0,1:T(8,128)(2,1)S(1)} all-gather(bf16[256,8]{0,1:T(8,128)(2,1)S(1)} %add_convert_fusion), channel_id=4, replica_groups=mesh['kv'=2,'ep'=16] {'kv'}, dimensions={0}, use_global_device_ids=true | all-gather | bytes 12288 | tf_op jit(solution)/shard_map/all_gather | solution.py:17
  49.5 7.5 %all-gather.5.cloned.1.call-done = bf16[2,256,1024]{2,1,0:T(8,128)(2,1)} async-done(((bf16[1,256,1024]{2,1,0:T(8,128)(2,1)}), bf16[2,256,1024]{2,1,0:T(8,128)(2,1)}) %all-gather.5.cloned.1.call-update) | async-done | bytes 1048592 | tf_op jit(solution)/shard_map/all_gather | solution.py:17
  58.5 3.2 multiply_reduce_fusion
  63.0 2.8 collective-permute-start.3
  65.9 12.7 %collective-permute-done.5 = bf16[128,2048]{1,0:T(8,128)(2,1)S(1)} collective-permute-done((bf16[128,2048]{1,0:T(8,128)(2,1)S(1)}, bf16[128,2048]{1,0:T(8,128)(2,1)S(1)}, u32[]{:S(2)}, u32[]{:S(2)}) %collective-permute-start.5) | collective-permute-done | bytes 524320 | tf_op jit(solution)/shard_map/ppermute | solution.py:87
  78.6 21.4 %collective-permute-done.4 = bf16[128,2048]{1,0:T(8,128)(2,1)S(1)} collective-permute-done((bf16[128,2048]{1,0:T(8,128)(2,1)S(1)}, bf16[128,2048]{1,0:T(8,128)(2,1)S(1)}, u32[]{:S(2)}, u32[]{:S(2)}) %collective-permute-start.4) | collective-permute-done | bytes 524320 | tf_op jit(solution)/shard_map/ppermute | solution.py:87
  102.5 44.6 %collective-permute-done.6 = bf16[4,128,2048]{2,1,0:T(8,128)(2,1)S(1)} collective-permute-done((bf16[4,128,2048]{2,1,0:T(8,128)(2,1)S(1)}, bf16[4,128,2048]{2,1,0:T(8,128)(2,1)S(1)}, u32[]{:S(2)}, u32[]{:S(2)}) %collective-permute-start.6) | collective-permute-done | bytes 2097184 | tf_op jit(solution)/shard_map/ppermute | solution.py:87
  147.1 2.4 pad_maximum_fusion
  150.1 11.6 %collective-permute-start.10 = (f32[128,16]{0,1:T(8,128)S(1)}, f32[128,16]{0,1:T(8,128)S(1)}, u32[]{:S(2)}, u32[]{:S(2)}) collective-permute-start(f32[128,16]{0,1:T(8,128)S(1)} %select_reduce_fusion.1), channel_id=1, source_target_pairs={{0,12},{1,13},{2,14},{3,15},{4,0},{5,1},{6,2},{7,3},{8,4},{9,5},{1... | collective-permute-start | bytes 24584 | tf_op jit(solution)/shard_map/ppermute | solution.py:87
  171.7 4.1 %collective-permute-done = bf16[2048,256]{1,0:T(8,128)(2,1)} collective-permute-done((bf16[2048,256]{1,0:T(8,128)(2,1)}, bf16[2048,256]{1,0:T(8,128)(2,1)}, u32[]{:S(2)}, u32[]{:S(2)}) %collective-permute-start) | collective-permute-done | bytes 1048608 | tf_op jit(solution)/shard_map/ppermute | solution.py:52
  177.5 20.8 %collective-permute-done.2 = bf16[256,2048]{1,0:T(8,128)(2,1)} collective-permute-done((bf16[256,2048]{1,0:T(8,128)(2,1)}, bf16[256,2048]{1,0:T(8,128)(2,1)}, u32[]{:S(2)}, u32[]{:S(2)}) %collective-permute-start.2) | collective-permute-done | bytes 1048608 | tf_op jit(solution)/shard_map/ppermute | solution.py:52
  198.2 3.0 broadcast_select_fusion.1
  201.2 19.1 %collective-permute-done.1 = bf16[2048,256]{1,0:T(8,128)(2,1)} collective-permute-done((bf16[2048,256]{1,0:T(8,128)(2,1)}, bf16[2048,256]{1,0:T(8,128)(2,1)}, u32[]{:S(2)}, u32[]{:S(2)}) %collective-permute-start.1) | collective-permute-done | bytes 1048608 | tf_op jit(solution)/shard_map/ppermute | solution.py:52
  220.3 3.0 broadcast_select_fusion.3
  223.4 5.9 %fusion.66 = f32[1024,512]{1,0:T(8,128)} fusion(bf16[1024,2048]{1,0:T(8,128)(2,1)} %bitcast.22, bf16[2048,256]{1,0:T(8,128)(2,1)S(1)} %get-tuple-element.39, bf16[2048,256]{1,0:T(8,128)(2,1)S(1)} %get-tuple-element.38), kind=kOutput, calls=%fused_computation.124 | convolution fusion | flops 2151677952 | bytes 8388608 | tf_op jit(solution)/shard_map/dot_general | solution.py:77
  229.3 10.6 %multiply_convert_fusion = bf16[1024,2048]{1,0:T(8,128)(2,1)} fusion(f32[1024]{0:T(1024)S(1)} %bitcast.168, f32[1024,512]{1,0:T(8,128)} %fusion.66, bf16[256,2048]{1,0:T(8,128)(2,1)} %get-tuple-element.37, bf16[256,2048]{1,0:T(8,128)(2,1)} %get-tuple-element.36, bf16[1024,2048]{1,0:T(8,128)(2,1)} %bitcast.22, bf16[2048,256]{1,0:T(8,128)(2,1)} %get-tuple-element.34, ...), kind=kOutput, calls=%fused_computation.3 | convolution fusion | flops 4314890240 | bytes 14684160 | tf_op jit(solution)/shard_map/dot_general | solution.py:80
  240.0 3.8 fusion.65
  243.8 6.9 %convert_multiply_fusion = f32[512,2048]{1,0:T(8,128)} fusion(f32[512]{0:T(512)S(1)} %bitcast.171, f32[512,512]{1,0:T(8,128)} %fusion.65, bf16[256,2048]{1,0:T(8,128)(2,1)} %get-tuple-element.37, bf16[256,2048]{1,0:T(8,128)(2,1)} %get-tuple-element.36, bf16[512,2048]{1,0:T(8,128)(2,1)S(1)} %bitcast.154, bf16[2048,256]{1,0:T(8,128)(2,1)} %get-tuple-element.34, ...), kind=kOutput, calls=%fused_computation.14 | convolution fusion | flops 2160590848 | bytes 11536384 | tf_op jit(solution)/shard_map/dot_general | solution.py:80
  250.7 3.4 convert_element_type.234
  261.8 6.7 %convert_multiply_fusion.1 = f32[384,2048]{1,0:T(8,128)} fusion(f32[384]{0:T(512)S(1)} %bitcast.172, f32[384,512]{1,0:T(8,128)} %fusion.64, bf16[256,2048]{1,0:T(8,128)(2,1)} %get-tuple-element.37, bf16[256,2048]{1,0:T(8,128)(2,1)} %get-tuple-element.36, bf16[384,2048]{1,0:T(8,128)(2,1)} %bitcast.156, bf16[2048,256]{1,0:T(8,128)(2,1)} %get-tuple-element.34, ...), kind=kOutput, calls=%fused_computation.19 | convolution fusion | flops 1622540288 | bytes 9700864 | tf_op jit(solution)/shard_map/dot_general | solution.py:80
  268.5 37.9 %collective-permute-done.14 = bf16[4,128,2048]{2,1,0:T(8,128)(2,1)S(1)} collective-permute-done((bf16[4,128,2048]{2,1,0:T(8,128)(2,1)}, bf16[4,128,2048]{2,1,0:T(8,128)(2,1)S(1)}, u32[]{:S(2)}, u32[]{:S(2)}) %collective-permute-start.14) | collective-permute-done | bytes 2097184 | tf_op jit(solution)/shard_map/ppermute | solution.py:101
  306.4 2.9 fusion.7
  311.6 11.1 %collective-permute-start.17 = (bf16[128,2048]{1,0:T(8,128)(2,1)S(1)}, bf16[128,2048]{1,0:T(8,128)(2,1)S(1)}, u32[]{:S(2)}, u32[]{:S(2)}) collective-permute-start(bf16[128,2048]{1,0:T(8,128)(2,1)S(1)} %get-tuple-element.22), channel_id=1, source_target_pairs={{12,0},{13,1},{14,2},{15,3},{0,4},{1,5},{2,6},{3,7},{4,8},{5,9},{6... | collective-permute-start | bytes 1572872 | tf_op jit(solution)/shard_map/ppermute | solution.py:101
  325.3 9.9 %collective-permute-done.17 = bf16[128,2048]{1,0:T(8,128)(2,1)S(1)} collective-permute-done((bf16[128,2048]{1,0:T(8,128)(2,1)S(1)}, bf16[128,2048]{1,0:T(8,128)(2,1)S(1)}, u32[]{:S(2)}, u32[]{:S(2)}) %collective-permute-start.17) | collective-permute-done | bytes 524320 | tf_op jit(solution)/shard_map/ppermute | solution.py:101
  335.1 34.8 %collective-permute-done.16 = bf16[128,2048]{1,0:T(8,128)(2,1)S(1)} collective-permute-done((bf16[128,2048]{1,0:T(8,128)(2,1)S(1)}, bf16[128,2048]{1,0:T(8,128)(2,1)S(1)}, u32[]{:S(2)}, u32[]{:S(2)}) %collective-permute-start.16) | collective-permute-done | bytes 524320 | tf_op jit(solution)/shard_map/ppermute | solution.py:101
  370.7 4.3 %fusion.19 = bf16[1,128,2048]{2,1,0:T(8,128)(2,1)} fusion(f32[128,2048]{1,0:T(8,128)S(1)} %get-tuple-element.55, f32[4,128,2048]{2,1,0:T(8,128)} %copy-done.1, bf16[128,2048]{1,0:T(8,128)(2,1)} %copy-done.29, bf16[128,2048]{1,0:T(8,128)(2,1)} %copy-done.30, bf16[128,2048]{1,0:T(8,128)(2,1)} %collective-permute-done.15, f32[128]{0:T(128)S(1)} %select_reduce_fusion.3, ...), kind=kOutput, calls=%fused_computation.31 | convolution fusion | flops 548798464 | bytes 9175552 | tf_op jit(solution)/shard_map/dot_general | solution.py:80
  (132 shorter events, 40.3 us)
Async XLA Ops:
  6.5 50.4 %all-gather.5.cloned.1.call-start = ((), (), s32[]{:S(2)}) async-start(), calls=%async_computation | async-start | bytes 1572864 | tf_op jit(solution)/shard_map/all_gather | solution.py:17
  34.5 13.9 %copy-start.26 = (bf16[2048]{0:T(1024)(128)(2,1)S(1)}, bf16[2048]{0:T(1024)(128)(2,1)}, u32[]{:S(2)}) copy-start(bf16[2048]{0:T(1024)(128)(2,1)} %param.24) | copy-start | bytes 12292
  61.9 38.2 %copy-start.22 = (bf16[128,2048]{1,0:T(8,128)(2,1)}, bf16[128,2048]{1,0:T(8,128)(2,1)S(1)}, u32[]{:S(2)}) copy-start(bf16[128,2048]{1,0:T(8,128)(2,1)S(1)} %multiply_convert_fusion.4) | copy-start | bytes 1572868
  61.9 16.8 %collective-permute-start.5 = (bf16[128,2048]{1,0:T(8,128)(2,1)S(1)}, bf16[128,2048]{1,0:T(8,128)(2,1)S(1)}, u32[]{:S(2)}, u32[]{:S(2)}) collective-permute-start(bf16[128,2048]{1,0:T(8,128)(2,1)S(1)} %multiply_convert_fusion.4), channel_id=1, source_target_pairs={{0,12},{1,13},{2,14},{3,15},{4,0},{5,1},{6,2},{7,3},{8,4},{9,5},{1... | collective-permute-start | bytes 1572872 | tf_op jit(solution)/shard_map/ppermute | solution.py:87
  62.5 37.6 %collective-permute-start.4 = (bf16[128,2048]{1,0:T(8,128)(2,1)S(1)}, bf16[128,2048]{1,0:T(8,128)(2,1)S(1)}, u32[]{:S(2)}, u32[]{:S(2)}) collective-permute-start(bf16[128,2048]{1,0:T(8,128)(2,1)S(1)} %multiply_convert_fusion.4), channel_id=1, source_target_pairs={{0,8},{1,9},{2,10},{3,11},{4,12},{5,13},{6,14},{7,15},{8,0},{9,1},... | collective-permute-start | bytes 1572872 | tf_op jit(solution)/shard_map/ppermute | solution.py:87
  63.0 37.1 %collective-permute-start.3 = (bf16[128,2048]{1,0:T(8,128)(2,1)S(1)}, bf16[128,2048]{1,0:T(8,128)(2,1)S(1)}, u32[]{:S(2)}, u32[]{:S(2)}) collective-permute-start(bf16[128,2048]{1,0:T(8,128)(2,1)S(1)} %multiply_convert_fusion.4), channel_id=1, source_target_pairs={{0,4},{1,5},{2,6},{3,7},{4,8},{5,9},{6,10},{7,11},{8,12},{9,13},{1... | collective-permute-start | bytes 1572872 | tf_op jit(solution)/shard_map/ppermute | solution.py:87
  78.6 21.8 %copy-start.6 = (bf16[128,2048]{1,0:T(8,128)(2,1)}, bf16[128,2048]{1,0:T(8,128)(2,1)S(1)}, u32[]{:S(2)}) copy-start(bf16[128,2048]{1,0:T(8,128)(2,1)S(1)} %collective-permute-done.5) | copy-start | bytes 1572868
  101.1 46.0 %collective-permute-start.6 = (bf16[4,128,2048]{2,1,0:T(8,128)(2,1)S(1)}, bf16[4,128,2048]{2,1,0:T(8,128)(2,1)S(1)}, u32[]{:S(2)}, u32[]{:S(2)}) collective-permute-start(bf16[4,128,2048]{2,1,0:T(8,128)(2,1)S(1)} %get-tuple-element.41), channel_id=1, source_target_pairs={{0,2},{1,3},{2,0},{3,1},{4,6},{5,7},{6,4},{7,5},{8,10},{9,11},{10,... | collective-permute-start | bytes 6291464 | tf_op jit(solution)/shard_map/ppermute | solution.py:87
  149.5 73.9 %collective-permute-start.7 = (bf16[2,4,128,2048]{3,2,1,0:T(8,128)(2,1)}, bf16[2,4,128,2048]{3,2,1,0:T(8,128)(2,1)}, u32[]{:S(2)}, u32[]{:S(2)}) collective-permute-start(bf16[2,4,128,2048]{3,2,1,0:T(8,128)(2,1)} %pad_maximum_fusion), channel_id=1, source_target_pairs={{0,1},{1,0},{2,3},{3,2},{4,5},{5,4},{6,7},{7,6},{8,9},{9,8},{10,11... | collective-permute-start | bytes 12582920 | tf_op jit(solution)/shard_map/ppermute | solution.py:87
  149.5 26.3 %collective-permute-start = (bf16[2048,256]{1,0:T(8,128)(2,1)}, bf16[2048,256]{1,0:T(8,128)(2,1)}, u32[]{:S(2)}, u32[]{:S(2)}) collective-permute-start(bf16[2048,256]{1,0:T(8,128)(2,1)} %bitcast.11), channel_id=1, source_target_pairs={{0,16},{16,0},{1,17},{17,1},{2,18},{18,2},{3,19},{19,3},{4,20},{20... | collective-permute-start | bytes 3145736 | tf_op jit(solution)/shard_map/ppermute | solution.py:52
  150.1 14.1 %collective-permute-start.10 = (f32[128,16]{0,1:T(8,128)S(1)}, f32[128,16]{0,1:T(8,128)S(1)}, u32[]{:S(2)}, u32[]{:S(2)}) collective-permute-start(f32[128,16]{0,1:T(8,128)S(1)} %select_reduce_fusion.1), channel_id=1, source_target_pairs={{0,12},{1,13},{2,14},{3,15},{4,0},{5,1},{6,2},{7,3},{8,4},{9,5},{1... | collective-permute-start | bytes 24584 | tf_op jit(solution)/shard_map/ppermute | solution.py:87
  161.8 4.5 %collective-permute-start.9 = (f32[128,16]{0,1:T(8,128)S(1)}, f32[128,16]{0,1:T(8,128)S(1)}, u32[]{:S(2)}, u32[]{:S(2)}) collective-permute-start(f32[128,16]{0,1:T(8,128)S(1)} %select_reduce_fusion.1), channel_id=1, source_target_pairs={{0,8},{1,9},{2,10},{3,11},{4,12},{5,13},{6,14},{7,15},{8,0},{9,1},... | collective-permute-start | bytes 24584 | tf_op jit(solution)/shard_map/ppermute | solution.py:87
  161.9 4.4 %collective-permute-start.8 = (f32[128,16]{0,1:T(8,128)S(1)}, f32[128,16]{0,1:T(8,128)S(1)}, u32[]{:S(2)}, u32[]{:S(2)}) collective-permute-start(f32[128,16]{0,1:T(8,128)S(1)} %select_reduce_fusion.1), channel_id=1, source_target_pairs={{0,4},{1,5},{2,6},{3,7},{4,8},{5,9},{6,10},{7,11},{8,12},{9,13},{1... | collective-permute-start | bytes 24584 | tf_op jit(solution)/shard_map/ppermute | solution.py:87
  164.2 34.0 %collective-permute-start.2 = (bf16[256,2048]{1,0:T(8,128)(2,1)}, bf16[256,2048]{1,0:T(8,128)(2,1)}, u32[]{:S(2)}, u32[]{:S(2)}) collective-permute-start(bf16[256,2048]{1,0:T(8,128)(2,1)} %bitcast.13), channel_id=1, source_target_pairs={{0,16},{16,0},{1,17},{17,1},{2,18},{18,2},{3,19},{19,3},{4,20},{20... | collective-permute-start | bytes 3145736 | tf_op jit(solution)/shard_map/ppermute | solution.py:52
  166.3 4.0 %collective-permute-start.11 = (f32[4,128,16]{1,2,0:T(8,128)S(1)}, f32[4,128,16]{1,2,0:T(8,128)S(1)}, u32[]{:S(2)}, u32[]{:S(2)}) collective-permute-start(f32[4,128,16]{1,2,0:T(8,128)S(1)} %get-tuple-element.45), channel_id=1, source_target_pairs={{0,2},{1,3},{2,0},{3,1},{4,6},{5,7},{6,4},{7,5},{8,10},{9,11},{10,... | collective-permute-start | bytes 98312 | tf_op jit(solution)/shard_map/ppermute | solution.py:87
  167.9 52.5 %collective-permute-start.1 = (bf16[2048,256]{1,0:T(8,128)(2,1)}, bf16[2048,256]{1,0:T(8,128)(2,1)}, u32[]{:S(2)}, u32[]{:S(2)}) collective-permute-start(bf16[2048,256]{1,0:T(8,128)(2,1)} %bitcast.12), channel_id=1, source_target_pairs={{0,16},{16,0},{1,17},{17,1},{2,18},{18,2},{3,19},{19,3},{4,20},{20... | collective-permute-start | bytes 3145736 | tf_op jit(solution)/shard_map/ppermute | solution.py:52
  170.3 1.3 collective-permute-start.12
  177.5 45.9 %copy-start.15 = (bf16[2048,256]{1,0:T(8,128)(2,1)}, bf16[2048,256]{1,0:T(8,128)(2,1)S(1)}, u32[]{:S(2)}) copy-start(bf16[2048,256]{1,0:T(8,128)(2,1)S(1)} %get-tuple-element.38) | copy-start | bytes 3145732
  177.5 45.9 %copy-start.18 = (bf16[2048,256]{1,0:T(8,128)(2,1)}, bf16[2048,256]{1,0:T(8,128)(2,1)S(1)}, u32[]{:S(2)}) copy-start(bf16[2048,256]{1,0:T(8,128)(2,1)S(1)} %get-tuple-element.39) | copy-start | bytes 3145732
  239.9 10.8 %collective-permute-start.13 = (bf16[2,4,128,2048]{3,2,1,0:T(8,128)(2,1)}, bf16[2,4,128,2048]{3,2,1,0:T(8,128)(2,1)}, u32[]{:S(2)}, u32[]{:S(2)}) collective-permute-start(bf16[2,4,128,2048]{3,2,1,0:T(8,128)(2,1)} %bitcast.173), channel_id=1, source_target_pairs={{1,0},{0,1},{3,2},{2,3},{5,4},{4,5},{7,6},{6,7},{9,8},{8,9},{11,10... | collective-permute-start | bytes 12582920 | tf_op jit(solution)/shard_map/ppermute | solution.py:101
  254.1 5.6 %copy-start.7 = (bf16[128,2048]{1,0:T(8,128)(2,1)S(1)}, bf16[128,2048]{1,0:T(8,128)(2,1)}, u32[]{:S(2)}) copy-start(bf16[128,2048]{1,0:T(8,128)(2,1)} %copy-done.6) | copy-start | bytes 1572868
  254.1 5.6 %copy-start.9 = (bf16[128,2048]{1,0:T(8,128)(2,1)S(1)}, bf16[128,2048]{1,0:T(8,128)(2,1)}, u32[]{:S(2)}) copy-start(bf16[128,2048]{1,0:T(8,128)(2,1)} %copy-done.8) | copy-start | bytes 1572868
  258.1 48.2 %collective-permute-start.14 = (bf16[4,128,2048]{2,1,0:T(8,128)(2,1)}, bf16[4,128,2048]{2,1,0:T(8,128)(2,1)S(1)}, u32[]{:S(2)}, u32[]{:S(2)}) collective-permute-start(bf16[4,128,2048]{2,1,0:T(8,128)(2,1)} %fusion.6), channel_id=1, source_target_pairs={{2,0},{3,1},{0,2},{1,3},{6,4},{7,5},{4,6},{5,7},{10,8},{11,9},{8,1... | collective-permute-start | bytes 6291464 | tf_op jit(solution)/shard_map/ppermute | solution.py:101
  309.5 15.3 %copy-start.17 = (bf16[2048,256]{1,0:T(8,128)(2,1)S(1)}, bf16[2048,256]{1,0:T(8,128)(2,1)}, u32[]{:S(2)}) copy-start(bf16[2048,256]{1,0:T(8,128)(2,1)} %copy-done.15) | copy-start | bytes 3145732
  309.5 15.3 %copy-start.20 = (bf16[2048,256]{1,0:T(8,128)(2,1)S(1)}, bf16[2048,256]{1,0:T(8,128)(2,1)}, u32[]{:S(2)}) copy-start(bf16[2048,256]{1,0:T(8,128)(2,1)} %copy-done.18) | copy-start | bytes 3145732
  309.5 15.3 %copy-start.23 = (bf16[128,2048]{1,0:T(8,128)(2,1)S(1)}, bf16[128,2048]{1,0:T(8,128)(2,1)}, u32[]{:S(2)}) copy-start(bf16[128,2048]{1,0:T(8,128)(2,1)} %copy-done.22) | copy-start | bytes 1572868
  311.6 23.5 %collective-permute-start.17 = (bf16[128,2048]{1,0:T(8,128)(2,1)S(1)}, bf16[128,2048]{1,0:T(8,128)(2,1)S(1)}, u32[]{:S(2)}, u32[]{:S(2)}) collective-permute-start(bf16[128,2048]{1,0:T(8,128)(2,1)S(1)} %get-tuple-element.22), channel_id=1, source_target_pairs={{12,0},{13,1},{14,2},{15,3},{0,4},{1,5},{2,6},{3,7},{4,8},{5,9},{6... | collective-permute-start | bytes 1572872 | tf_op jit(solution)/shard_map/ppermute | solution.py:101
  322.7 47.2 %collective-permute-start.16 = (bf16[128,2048]{1,0:T(8,128)(2,1)S(1)}, bf16[128,2048]{1,0:T(8,128)(2,1)S(1)}, u32[]{:S(2)}, u32[]{:S(2)}) collective-permute-start(bf16[128,2048]{1,0:T(8,128)(2,1)S(1)} %get-tuple-element.23), channel_id=1, source_target_pairs={{8,0},{9,1},{10,2},{11,3},{12,4},{13,5},{14,6},{15,7},{0,8},{1,9},... | collective-permute-start | bytes 1572872 | tf_op jit(solution)/shard_map/ppermute | solution.py:101
  324.7 46.0 %collective-permute-start.15 = (bf16[128,2048]{1,0:T(8,128)(2,1)S(1)}, bf16[128,2048]{1,0:T(8,128)(2,1)}, u32[]{:S(2)}, u32[]{:S(2)}) collective-permute-start(bf16[128,2048]{1,0:T(8,128)(2,1)S(1)} %get-tuple-element.21), channel_id=1, source_target_pairs={{4,0},{5,1},{6,2},{7,3},{8,4},{9,5},{10,6},{11,7},{12,8},{13,9},{1... | collective-permute-start | bytes 1572872 | tf_op jit(solution)/shard_map/ppermute | solution.py:101
  324.8 45.9 %copy-start.13 = (bf16[256,2048]{1,0:T(8,128)(2,1)S(1)}, bf16[256,2048]{1,0:T(8,128)(2,1)}, u32[]{:S(2)}) copy-start(bf16[256,2048]{1,0:T(8,128)(2,1)} %get-tuple-element.36) | copy-start | bytes 3145732
  324.8 45.9 %copy-start.14 = (bf16[256,2048]{1,0:T(8,128)(2,1)S(1)}, bf16[256,2048]{1,0:T(8,128)(2,1)}, u32[]{:S(2)}) copy-start(bf16[256,2048]{1,0:T(8,128)(2,1)} %get-tuple-element.37) | copy-start | bytes 3145732
  335.1 34.8 %copy-start.29 = (bf16[128,2048]{1,0:T(8,128)(2,1)}, bf16[128,2048]{1,0:T(8,128)(2,1)S(1)}, u32[]{:S(2)}) copy-start(bf16[128,2048]{1,0:T(8,128)(2,1)S(1)} %collective-permute-done.17) | copy-start | bytes 1572868
  (19 other events, 52.3 us)
Sparse Core Ops, SparseCore 0:
  34.6 22.3 all-gather.4

commit v3 on v2

--- a/solution.py
+++ b/solution.py
@@ -3,6 +3,7 @@
 
 import jax
 import jax.numpy as jnp
+import numpy as np
 from jax import lax
 from jax.sharding import PartitionSpec as P
 
@@ -60,48 +61,51 @@
 
 
 def dense_moe(plan, normed, route_ids, route_weights, gate_w, up_w, down_w):
+    tok_dev = normed.shape[0]
     expert_count = EXP_DEV * lax.axis_size("ep")
     experts = jnp.arange(expert_count, dtype=jnp.int32)
     own_expert = lax.axis_index("ep")
     chosen = route_ids[:, :, None] == experts[None, None, :]
     weight_table = jnp.sum(jnp.where(chosen, route_weights[:, :, None], 0.0), axis=1)
+    own_weight = jnp.sum(jnp.where(experts == own_expert, weight_table, 0.0), axis=1)
+    every_table = lax.all_gather(weight_table, "ep", axis=0, tiled=True)
     full_gate, full_up, full_down = full_weights(gate_w, up_w, down_w)
-
-    def expert(block):
-        rows, table = block
-        lead = rows.shape[:-1]
-        rows = rows.reshape(-1, D)
-        weights = jnp.sum(
-            jnp.where(experts == own_expert, table.reshape(-1, expert_count), 0.0), axis=1
-        )
+    normed, full_gate, full_up, full_down = lax.optimization_barrier(
+        (normed, full_gate, full_up, full_down)
+    )
+    ep_count = lax.axis_size("ep")
+
+    def expert(rows, origin):
+        if origin is None:
+            weights = own_weight
+        else:
+            source = jnp.asarray(origin, jnp.int32)[own_expert]
+            table = lax.dynamic_slice_in_dim(every_table, source * tok_dev, tok_dev, 0)
+            weights = jnp.sum(jnp.where(experts == own_expert, table, 0.0), axis=1)
         gate_val = jnp.dot(rows, full_gate, preferred_element_type=jnp.float32)
         up_val = jnp.dot(rows, full_up, preferred_element_type=jnp.float32)
         act = (jax.nn.silu(gate_val) * up_val).astype(jnp.bfloat16)
         out_rows = jnp.dot(act, full_down, preferred_element_type=jnp.float32)
         out_rows = out_rows.astype(jnp.bfloat16).astype(jnp.float32)
-        return (out_rows * weights[:, None]).reshape(*lead, D)
-
-    current = (normed, weight_table)
-    arrived = []
+        return out_rows * weights[:, None]
+
+    pieces = [(normed, np.arange(ep_count), None, None)]
     for pairs_list in plan:
-        received = [lax.ppermute(current, "ep", pairs) for pairs in pairs_list]
-        arrived.append(jax.tree.map(lambda *leaves: jnp.stack(leaves), *received))
-        current = jax.tree.map(lambda *leaves: jnp.stack(leaves), current, *received)
-    own_part = expert((normed, weight_table))
-    new_parts = [expert(block) for block in arrived]
-    pending = None
-    for stage in reversed(range(len(plan))):
-        pairs_list = plan[stage]
-        total = None if pending is None else pending[0]
-        for index, pairs in enumerate(pairs_list, 1):
-            outgoing = new_parts[stage][index - 1]
-            if pending is not None:
-                outgoing = outgoing + pending[index]
-            back = [(target, source) for source, target in pairs]
-            sent = lax.ppermute(outgoing.astype(jnp.bfloat16), "ep", back).astype(jnp.float32)
-            total = sent if total is None else total + sent
-        pending = total
-    return own_part + pending
+        grown = []
+        for parent, (rows, origin, _, _) in enumerate(pieces):
+            for pairs in pairs_list:
+                moved = np.zeros_like(origin)
+                for source, target in pairs:
+                    moved[target] = origin[source]
+                grown.append((lax.ppermute(rows, "ep", pairs), moved, parent, pairs))
+        pieces = pieces + grown
+    partial = [expert(rows, None if index == 0 else origin) for index, (rows, origin, _, _) in enumerate(pieces)]
+    for index in reversed(range(1, len(pieces))):
+        _, _, parent, pairs = pieces[index]
+        back = [(target, source) for source, target in pairs]
+        sent = lax.ppermute(partial[index].astype(jnp.bfloat16), "ep", back)
+        partial[parent] = partial[parent] + sent.astype(jnp.float32)
+    return partial[0]
 
 
 def gather_plan(mesh, shapes):

time: 382 us -> 381 us (level); the launches traced: 382 us -> 375 us
  waiting for transfers between devices: 216 us -> 62.1 us
  blocking collectives: 17.5 us -> 103 us
  matrix products: 49.5 us -> 102 us
  between operations: 14.5 us -> 24.3 us
  local copies, waits for them, and re-layouts: 19.4 us -> 24.7 us
    ppermute x15 -> x30, waiting for transfers between devices: 164 us -> 62 us  [the longest x15 40 us: dense_moe(): sent = lax.ppermute(partial[index].astype(jnp.bfloat16), 'ep', back)]
    all_gather x2, blocking collectives: 8.74 us -> 77 us  [combined_all(): lax.all_gather(a.astype(kind), axis)]
    ppermute x3, waiting for transfers between devices: 44 us -> 0.01 us  [full_weights(): other = lax.ppermute(mine, 'kv', [(0, 1), (1, 0)])]
    dot_general x4 -> x16, matrix products: 28.6 us -> 65 us  [expert(): out_rows = jnp.dot(act, full_down, preferred_element_type=jnp.float32)]
    all_gather x0 -> x1, blocking collectives: none -> 17.1 us  [dense_moe(): every_table = lax.all_gather(weight_table, 'ep', axis=0, tiled=True)]
    dot_general x4 -> x16, matrix products: 12 us -> 27.5 us  [expert(): gate_val = jnp.dot(rows, full_gate, preferred_element_type=jnp.float32)]
    dynamic_slice x0 -> x15, local copies, waits for them, and re-layouts: none -> 9.31 us  [expert(): source = jnp.asarray(origin, jnp.int32)[own_expert]]
    all_gather x1, waiting for transfers between devices: 7.46 us -> 0.02 us  [combined_all(): lax.all_gather(a.astype(kind), axis)]
  transfers between devices with their start and end apart: 19 -> 34, of which waited for: 13 -> 7; matrix products, arithmetic and copies ran while one was open for 9% -> 33% of each run, Pallas kernels for 0% -> 0%
where the time goes in v3:
time: 381 us; the launch traced here: 375 us
  blocking collectives  103 us (27%)
  matrix products  102 us (27%)
  waiting for transfers between devices  62.1 us (16%)
  starting transfers between devices  36.7 us (10%)
  local copies, waits for them, and re-layouts  24.7 us (6%)
  between operations  24.3 us (6%)
  other arithmetic  23.2 us (6%)
    all_gather x2, blocking collectives, combined_all(): lax.all_gather(a.astype(kind), axis)  77 us
    dot_general x16, matrix products, expert(): out_rows = jnp.dot(act, full_down, preferred_element_type=jnp.float32)  65 us
    ppermute x15, waiting for transfers between devices, dense_moe(): sent = lax.ppermute(partial[index].astype(jnp.bfloat16), 'ep', back)  40 us
    dot_general x16, matrix products, expert(): gate_val = jnp.dot(rows, full_gate, preferred_element_type=jnp.float32)  27.5 us
    ppermute x15, starting transfers between devices, dense_moe(): sent = lax.ppermute(partial[index].astype(jnp.bfloat16), 'ep', back)  22.8 us
    ppermute x15, waiting for transfers between devices, dense_moe(): grown.append((lax.ppermute(rows, 'ep', pairs), moved, parent, pairs))  22.1 us
    all_gather x1, blocking collectives, dense_moe(): every_table = lax.all_gather(weight_table, 'ep', axis=0, tiled=True)  17.1 us
    ppermute x15, starting transfers between devices, dense_moe(): grown.append((lax.ppermute(rows, 'ep', pairs), moved, parent, pairs))  10.3 us
  transfers between devices with their start and end apart: 34, of which 7 were waited for; matrix products, arithmetic and copies ran while one was open for 33% of the time, Pallas kernels for 0%

profile of v3, /device:TPU:24, one launch (start us, length us, event | category | flops | bytes accessed | tf_op | source)
XLA Modules:
  0.0 375.3 jit_solution(12314369613575826111)
XLA Ops:
  8.3 8.7 %all-gather = bf16[1,256,1024]{1,2,0:T(8,128)(2,1)S(1)} all-gather(bf16[1,128,1024]{1,2,0:T(8,128)(2,1)S(1)} %copy.65), channel_id=2, replica_groups=mesh['kv'=2,'ep'=16] {'kv'}, dimensions={1}, use_global_device_ids=true | all-gather | bytes 786432 | tf_op jit(solution)/shard_map/all_gather | solution.py:177
  17.1 3.6 copy.84
  20.8 4.0 %copy.82 = bf16[1,1024,1024]{1,2,0:T(8,128)(2,1)} copy(bf16[1,1024,1024]{2,1,0:T(8,128)(2,1)} %param.35) | data formatting | bytes 4194304 | tf_op jit(solution)/shard_map/reshape;squeeze | solution.py:181
  38.0 4.5 %fusion.1 = f32[256,8]{0,1:T(8,128)S(1)} fusion(f32[8,1024,256]{2,1,0:T(8,128)} %copy-done, f32[256,8]{0,1:T(8,128)S(1)} %get-tuple-element.54, pred[1024]{0:T(1024)(128)(4,1)S(1)} %add_compare_fusion), kind=kLoop, calls=%fused_computation.4 | loop fusion | flops 8386560 | bytes 8406016 | tf_op jit(solution)/shard_map/reduce_sum | solution.py:197
  42.5 72.6 %all-gather.1 = bf16[512,8]{0,1:T(8,128)(2,1)S(1)} all-gather(bf16[256,8]{0,1:T(8,128)(2,1)S(1)} %get-tuple-element.53), channel_id=3, replica_groups=mesh['kv'=2,'ep'=16] {'kv'}, dimensions={0}, use_global_device_ids=true | all-gather | bytes 12288 | tf_op jit(solution)/shard_map/all_gather | solution.py:18
  115.6 4.3 %all-gather.2 = bf16[512,8]{0,1:T(8,128)(2,1)S(1)} all-gather(bf16[256,8]{0,1:T(8,128)(2,1)S(1)} %add_convert_fusion.8), channel_id=4, replica_groups=mesh['kv'=2,'ep'=16] {'kv'}, dimensions={0}, use_global_device_ids=true | all-gather | bytes 12288 | tf_op jit(solution)/shard_map/all_gather | solution.py:18
  123.8 3.3 multiply_reduce_fusion
  154.7 17.1 %all_gather.22 = f32[2048,16]{0,1:T(8,128)S(1)} all-gather(f32[128,16]{0,1:T(8,128)S(1)} %select_reduce_fusion), channel_id=1, replica_groups=mesh['kv'=2,'ep'=16] {'ep'}, dimensions={0}, use_global_device_ids=true | all-gather | bytes 139264 | tf_op jit(solution)/shard_map/all_gather | solution.py:71
  173.2 4.5 %collective-permute-start.17 = (bf16[128,2048]{1,0:T(8,128)(2,1)}, bf16[128,2048]{1,0:T(8,128)(2,1)}, u32[]{:S(2)}, u32[]{:S(2)}) collective-permute-start(bf16[128,2048]{1,0:T(8,128)(2,1)} %multiply_convert_fusion), channel_id=1, source_target_pairs={{0,8},{1,9},{2,10},{3,11},{4,12},{5,13},{6,14},{7,15},{8,0},{9,1},... | collective-permute-start | bytes 1572872 | tf_op jit(solution)/shard_map/ppermute | solution.py:100
  179.2 4.1 %fusion.48 = bf16[128,2048]{1,0:T(8,128)(2,1)} fusion(bf16[512,2048]{1,0:T(8,128)(2,1)} %pad_maximum_fusion.2, f32[128]{0:T(128)S(1)} %get-tuple-element.37, f32[128,512]{1,0:T(8,128)S(1)} %fusion.147, bf16[128,2048]{1,0:T(8,128)(2,1)} %collective-permute-done.3, bf16[2048,512]{1,0:T(8,128)(2,1)} %pad_maximum_fusion.1), kind=kOutput, calls=%fused_computation.66 | convolution fusion | flops 538312704 | bytes 5505536 | tf_op jit(solution)/shard_map/dot_general | solution.py:88
  183.2 3.2 collective-permute-done.5
  191.7 4.2 %fusion.40 = f32[128,2048]{1,0:T(8,128)} fusion(bf16[512,2048]{1,0:T(8,128)(2,1)} %pad_maximum_fusion.2, f32[128]{0:T(128)S(1)} %get-tuple-element.49, f32[128,512]{1,0:T(8,128)S(1)} %fusion.150, bf16[128,2048]{1,0:T(8,128)(2,1)} %collective-permute-done.9, bf16[2048,512]{1,0:T(8,128)(2,1)} %pad_maximum_fusion.1), kind=kOutput, calls=%fused_computation.55 | convolution fusion | flops 538050560 | bytes 6029824 | tf_op jit(solution)/shard_map/dot_general | solution.py:88
  196.0 16.4 %collective-permute-done.17 = bf16[128,2048]{1,0:T(8,128)(2,1)} collective-permute-done((bf16[128,2048]{1,0:T(8,128)(2,1)}, bf16[128,2048]{1,0:T(8,128)(2,1)}, u32[]{:S(2)}, u32[]{:S(2)}) %collective-permute-start.17) | collective-permute-done | bytes 524320 | tf_op jit(solution)/shard_map/ppermute | solution.py:100
  215.6 4.2 %fusion.30 = f32[128,2048]{1,0:T(8,128)} fusion(bf16[512,2048]{1,0:T(8,128)(2,1)} %pad_maximum_fusion.2, f32[128]{0:T(128)S(1)} %get-tuple-element.45, f32[128,512]{1,0:T(8,128)S(1)} %fusion.154, bf16[128,2048]{1,0:T(8,128)(2,1)} %collective-permute-done.17, bf16[2048,512]{1,0:T(8,128)(2,1)} %pad_maximum_fusion.1), kind=kOutput, calls=%fused_computation.41 | convolution fusion | flops 538050560 | bytes 6029824 | tf_op jit(solution)/shard_map/dot_general | solution.py:88
  221.4 4.2 %fusion.20 = f32[128,2048]{1,0:T(8,128)} fusion(bf16[512,2048]{1,0:T(8,128)(2,1)} %pad_maximum_fusion.2, f32[128]{0:T(128)S(1)} %get-tuple-element.41, f32[128,512]{1,0:T(8,128)S(1)} %fusion.158, bf16[128,2048]{1,0:T(8,128)(2,1)} %collective-permute-done.25, bf16[2048,512]{1,0:T(8,128)(2,1)} %pad_maximum_fusion.1), kind=kOutput, calls=%fused_computation.27 | convolution fusion | flops 538050560 | bytes 6029824 | tf_op jit(solution)/shard_map/dot_general | solution.py:88
  227.4 4.0 %fusion.43 = bf16[128,2048]{1,0:T(8,128)(2,1)} fusion(bf16[512,2048]{1,0:T(8,128)(2,1)} %pad_maximum_fusion.2, f32[128]{0:T(128)S(1)} %get-tuple-element.50, f32[128,512]{1,0:T(8,128)S(1)} %fusion.149, bf16[128,2048]{1,0:T(8,128)(2,1)} %collective-permute-done.6, bf16[2048,512]{1,0:T(8,128)(2,1)} %pad_maximum_fusion.1), kind=kOutput, calls=%fused_computation.59 | convolution fusion | flops 538312704 | bytes 5505536 | tf_op jit(solution)/shard_map/dot_general | solution.py:88
  233.1 4.0 %fusion.38 = bf16[128,2048]{1,0:T(8,128)(2,1)} fusion(bf16[512,2048]{1,0:T(8,128)(2,1)} %pad_maximum_fusion.2, f32[128]{0:T(128)S(1)} %get-tuple-element.48, f32[128,512]{1,0:T(8,128)S(1)} %fusion.151, bf16[128,2048]{1,0:T(8,128)(2,1)} %collective-permute-done.10, bf16[2048,512]{1,0:T(8,128)(2,1)} %pad_maximum_fusion.1), kind=kOutput, calls=%fused_computation.52 | convolution fusion | flops 538312704 | bytes 5505536 | tf_op jit(solution)/shard_map/dot_general | solution.py:88
  240.4 4.1 %fusion.28 = bf16[128,2048]{1,0:T(8,128)(2,1)} fusion(bf16[512,2048]{1,0:T(8,128)(2,1)} %pad_maximum_fusion.2, f32[128]{0:T(128)S(1)} %get-tuple-element.44, f32[128,512]{1,0:T(8,128)S(1)} %fusion.155, bf16[128,2048]{1,0:T(8,128)(2,1)} %collective-permute-done.18, bf16[2048,512]{1,0:T(8,128)(2,1)} %pad_maximum_fusion.1), kind=kOutput, calls=%fused_computation.38 | convolution fusion | flops 538312704 | bytes 5505536 | tf_op jit(solution)/shard_map/dot_general | solution.py:88
  253.8 4.0 %fusion.18 = bf16[128,2048]{1,0:T(8,128)(2,1)} fusion(bf16[512,2048]{1,0:T(8,128)(2,1)} %pad_maximum_fusion.2, f32[128]{0:T(128)S(1)} %get-tuple-element.40, f32[128,512]{1,0:T(8,128)S(1)} %fusion.159, bf16[128,2048]{1,0:T(8,128)(2,1)} %collective-permute-done.26, bf16[2048,512]{1,0:T(8,128)(2,1)} %pad_maximum_fusion.1), kind=kOutput, calls=%fused_computation.24 | convolution fusion | flops 538312704 | bytes 5505536 | tf_op jit(solution)/shard_map/dot_general | solution.py:88
  259.8 4.0 %fusion.33 = bf16[128,2048]{1,0:T(8,128)(2,1)} fusion(bf16[512,2048]{1,0:T(8,128)(2,1)} %pad_maximum_fusion.2, f32[128]{0:T(128)S(1)} %get-tuple-element.46, f32[128,512]{1,0:T(8,128)S(1)} %fusion.153, bf16[128,2048]{1,0:T(8,128)(2,1)} %collective-permute-done.13, bf16[2048,512]{1,0:T(8,128)(2,1)} %pad_maximum_fusion.1), kind=kOutput, calls=%fused_computation.45 | convolution fusion | flops 538312704 | bytes 5505536 | tf_op jit(solution)/shard_map/dot_general | solution.py:88
  266.3 4.1 %fusion.23 = bf16[128,2048]{1,0:T(8,128)(2,1)} fusion(bf16[512,2048]{1,0:T(8,128)(2,1)} %pad_maximum_fusion.2, f32[128]{0:T(128)S(1)} %get-tuple-element.42, f32[128,512]{1,0:T(8,128)} %fusion.157, bf16[128,2048]{1,0:T(8,128)(2,1)} %collective-permute-done.21, bf16[2048,512]{1,0:T(8,128)(2,1)} %pad_maximum_fusion.1), kind=kOutput, calls=%fused_computation.31 | convolution fusion | flops 538312704 | bytes 5505536 | tf_op jit(solution)/shard_map/dot_general | solution.py:88
  270.9 4.1 %add_convert_fusion.7 = bf16[128,2048]{1,0:T(8,128)(2,1)} fusion(bf16[128,2048]{1,0:T(8,128)(2,1)} %collective-permute-done.7, f32[128]{0:T(128)S(1)} %get-tuple-element.51, bf16[512,2048]{1,0:T(8,128)(2,1)} %pad_maximum_fusion.2, f32[128,512]{1,0:T(8,128)S(1)} %copy-done.7, bf16[128,2048]{1,0:T(8,128)(2,1)} %collective-permute-done.5, ...), kind=kOutput, calls=%fused_computation.90 | convolution fusion | flops 538836992 | bytes 6029824 | tf_op jit(solution)/shard_map/dot_general | solution.py:88
  276.6 4.0 %fusion.13 = bf16[128,2048]{1,0:T(8,128)(2,1)} fusion(bf16[512,2048]{1,0:T(8,128)(2,1)} %pad_maximum_fusion.2, f32[128]{0:T(128)S(1)} %get-tuple-element.38, f32[128,512]{1,0:T(8,128)S(1)} %fusion.161, bf16[128,2048]{1,0:T(8,128)(2,1)} %collective-permute-done.29, bf16[2048,512]{1,0:T(8,128)(2,1)} %pad_maximum_fusion.1), kind=kOutput, calls=%fused_computation.17 | convolution fusion | flops 538312704 | bytes 5505536 | tf_op jit(solution)/shard_map/dot_general | solution.py:88
  281.1 4.2 %add_convert_fusion.6 = bf16[128,2048]{1,0:T(8,128)(2,1)} fusion(bf16[128,2048]{1,0:T(8,128)(2,1)} %collective-permute-done.14, f32[128]{0:T(128)S(1)} %get-tuple-element.47, bf16[512,2048]{1,0:T(8,128)(2,1)} %pad_maximum_fusion.2, f32[128,512]{1,0:T(8,128)} %fusion.152, bf16[128,2048]{1,0:T(8,128)(2,1)} %collective-permute-done.12, ...), kind=kOutput, calls=%fused_computation.89 | convolution fusion | flops 538836992 | bytes 6029824 | tf_op jit(solution)/shard_map/dot_general | solution.py:88
  287.1 4.1 %add_convert_fusion.4 = bf16[128,2048]{1,0:T(8,128)(2,1)} fusion(bf16[128,2048]{1,0:T(8,128)(2,1)} %collective-permute-done.22, f32[128]{0:T(128)S(1)} %get-tuple-element.43, bf16[512,2048]{1,0:T(8,128)(2,1)} %pad_maximum_fusion.2, f32[128,512]{1,0:T(8,128)S(1)} %copy-done.8, bf16[128,2048]{1,0:T(8,128)(2,1)} %collective-permute-done.20, ...), kind=kOutput, calls=%fused_computation.87 | convolution fusion | flops 538836992 | bytes 6029824 | tf_op jit(solution)/shard_map/dot_general | solution.py:88
  291.5 4.2 %add_convert_fusion.2 = bf16[128,2048]{1,0:T(8,128)(2,1)} fusion(bf16[128,2048]{1,0:T(8,128)(2,1)} %collective-permute-done.30, f32[128]{0:T(128)S(1)} %get-tuple-element.39, bf16[512,2048]{1,0:T(8,128)(2,1)} %pad_maximum_fusion.2, f32[128,512]{1,0:T(8,128)} %fusion.160, bf16[128,2048]{1,0:T(8,128)(2,1)} %collective-permute-done.28, ...), kind=kOutput, calls=%fused_computation.85 | convolution fusion | flops 538836992 | bytes 6029824 | tf_op jit(solution)/shard_map/dot_general | solution.py:88
  295.8 4.6 %collective-permute-done.15 = bf16[128,2048]{1,0:T(8,128)(2,1)} collective-permute-done((bf16[128,2048]{1,0:T(8,128)(2,1)}, bf16[128,2048]{1,0:T(8,128)(2,1)}, u32[]{:S(2)}, u32[]{:S(2)}) %collective-permute-start.15) | collective-permute-done | bytes 524320 | tf_op jit(solution)/shard_map/ppermute | solution.py:106
  305.0 6.7 %collective-permute-done.23 = bf16[128,2048]{1,0:T(8,128)(2,1)} collective-permute-done((bf16[128,2048]{1,0:T(8,128)(2,1)}, bf16[128,2048]{1,0:T(8,128)(2,1)}, u32[]{:S(2)}, u32[]{:S(2)}) %collective-permute-start.23) | collective-permute-done | bytes 524320 | tf_op jit(solution)/shard_map/ppermute | solution.py:106
  311.7 11.1 %collective-permute-start.16 = (bf16[128,2048]{1,0:T(8,128)(2,1)}, bf16[128,2048]{1,0:T(8,128)(2,1)}, u32[]{:S(2)}, u32[]{:S(2)}) collective-permute-start(bf16[128,2048]{1,0:T(8,128)(2,1)} %add_convert_fusion.5), channel_id=1, source_target_pairs={{12,0},{13,1},{14,2},{15,3},{0,4},{1,5},{2,6},{3,7},{4,8},{5,9},{6... | collective-permute-start | bytes 1572872 | tf_op jit(solution)/shard_map/ppermute | solution.py:106
  326.0 6.1 %collective-permute-start.32 = (bf16[128,2048]{1,0:T(8,128)(2,1)}, bf16[128,2048]{1,0:T(8,128)(2,1)}, u32[]{:S(2)}, u32[]{:S(2)}) collective-permute-start(bf16[128,2048]{1,0:T(8,128)(2,1)} %add_convert_fusion.1), channel_id=1, source_target_pairs={{4,0},{5,1},{6,2},{7,3},{8,4},{9,5},{10,6},{11,7},{12,8},{13,9},{1... | collective-permute-start | bytes 1572872 | tf_op jit(solution)/shard_map/ppermute | solution.py:106
  333.6 3.2 fusion.50
  336.9 28.6 %collective-permute-done.24 = bf16[128,2048]{1,0:T(8,128)(2,1)} collective-permute-done((bf16[128,2048]{1,0:T(8,128)(2,1)}, bf16[128,2048]{1,0:T(8,128)(2,1)}, u32[]{:S(2)}, u32[]{:S(2)}) %collective-permute-start.24) | collective-permute-done | bytes 524320 | tf_op jit(solution)/shard_map/ppermute | solution.py:106
  (187 shorter events, 86.5 us)
Async XLA Ops:
  6.5 115.7 %all-gather.5.cloned.1.call-start = ((), (), s32[]{:S(2)}) async-start(), calls=%async_computation | async-start | bytes 1572864 | tf_op jit(solution)/shard_map/all_gather | solution.py:18
  34.4 92.7 %collective-permute-start = (bf16[2048,256]{1,0:T(8,128)(2,1)}, bf16[2048,256]{1,0:T(8,128)(2,1)}, u32[]{:S(2)}, u32[]{:S(2)}) collective-permute-start(bf16[2048,256]{1,0:T(8,128)(2,1)} %bitcast.11), channel_id=1, source_target_pairs={{0,16},{16,0},{1,17},{17,1},{2,18},{18,2},{3,19},{19,3},{4,20},{20... | collective-permute-start | bytes 3145736 | tf_op jit(solution)/shard_map/ppermute | solution.py:53
  35.9 91.1 %collective-permute-start.1 = (bf16[2048,256]{1,0:T(8,128)(2,1)}, bf16[2048,256]{1,0:T(8,128)(2,1)}, u32[]{:S(2)}, u32[]{:S(2)}) collective-permute-start(bf16[2048,256]{1,0:T(8,128)(2,1)} %bitcast.12), channel_id=1, source_target_pairs={{0,16},{16,0},{1,17},{17,1},{2,18},{18,2},{3,19},{19,3},{4,20},{20... | collective-permute-start | bytes 3145736 | tf_op jit(solution)/shard_map/ppermute | solution.py:53
  36.5 94.7 %collective-permute-start.2 = (bf16[256,2048]{1,0:T(8,128)(2,1)}, bf16[256,2048]{1,0:T(8,128)(2,1)}, u32[]{:S(2)}, u32[]{:S(2)}) collective-permute-start(bf16[256,2048]{1,0:T(8,128)(2,1)} %bitcast.13), channel_id=1, source_target_pairs={{0,16},{16,0},{1,17},{17,1},{2,18},{18,2},{3,19},{19,3},{4,20},{20... | collective-permute-start | bytes 3145736 | tf_op jit(solution)/shard_map/ppermute | solution.py:53
  135.6 42.0 %collective-permute-start.3 = (bf16[128,2048]{1,0:T(8,128)(2,1)}, bf16[128,2048]{1,0:T(8,128)(2,1)}, u32[]{:S(2)}, u32[]{:S(2)}) collective-permute-start(bf16[128,2048]{1,0:T(8,128)(2,1)} %multiply_convert_fusion), channel_id=1, source_target_pairs={{0,1},{1,0},{2,3},{3,2},{4,5},{5,4},{6,7},{7,6},{8,9},{9,8},{10,11... | collective-permute-start | bytes 1572872 | tf_op jit(solution)/shard_map/ppermute | solution.py:100
  171.9 14.6 %collective-permute-start.5 = (bf16[128,2048]{1,0:T(8,128)(2,1)}, bf16[128,2048]{1,0:T(8,128)(2,1)}, u32[]{:S(2)}, u32[]{:S(2)}) collective-permute-start(bf16[128,2048]{1,0:T(8,128)(2,1)} %multiply_convert_fusion), channel_id=1, source_target_pairs={{0,2},{1,3},{2,0},{3,1},{4,6},{5,7},{6,4},{7,5},{8,10},{9,11},{10,... | collective-permute-start | bytes 1572872 | tf_op jit(solution)/shard_map/ppermute | solution.py:100
  173.2 17.1 %collective-permute-start.9 = (bf16[128,2048]{1,0:T(8,128)(2,1)}, bf16[128,2048]{1,0:T(8,128)(2,1)}, u32[]{:S(2)}, u32[]{:S(2)}) collective-permute-start(bf16[128,2048]{1,0:T(8,128)(2,1)} %multiply_convert_fusion), channel_id=1, source_target_pairs={{0,12},{1,13},{2,14},{3,15},{4,0},{5,1},{6,2},{7,3},{8,4},{9,5},{1... | collective-permute-start | bytes 1572872 | tf_op jit(solution)/shard_map/ppermute | solution.py:100
  173.2 39.3 %collective-permute-start.17 = (bf16[128,2048]{1,0:T(8,128)(2,1)}, bf16[128,2048]{1,0:T(8,128)(2,1)}, u32[]{:S(2)}, u32[]{:S(2)}) collective-permute-start(bf16[128,2048]{1,0:T(8,128)(2,1)} %multiply_convert_fusion), channel_id=1, source_target_pairs={{0,8},{1,9},{2,10},{3,11},{4,12},{5,13},{6,14},{7,15},{8,0},{9,1},... | collective-permute-start | bytes 1572872 | tf_op jit(solution)/shard_map/ppermute | solution.py:100
  177.7 42.2 %collective-permute-start.25 = (bf16[128,2048]{1,0:T(8,128)(2,1)}, bf16[128,2048]{1,0:T(8,128)(2,1)}, u32[]{:S(2)}, u32[]{:S(2)}) collective-permute-start(bf16[128,2048]{1,0:T(8,128)(2,1)} %multiply_convert_fusion), channel_id=1, source_target_pairs={{0,4},{1,5},{2,6},{3,7},{4,8},{5,9},{6,10},{7,11},{8,12},{9,13},{1... | collective-permute-start | bytes 1572872 | tf_op jit(solution)/shard_map/ppermute | solution.py:100
  183.2 153.6 %collective-permute-start.4 = (bf16[128,2048]{1,0:T(8,128)(2,1)}, bf16[128,2048]{1,0:T(8,128)(2,1)}, u32[]{:S(2)}, u32[]{:S(2)}) collective-permute-start(bf16[128,2048]{1,0:T(8,128)(2,1)} %fusion.48), channel_id=1, source_target_pairs={{1,0},{0,1},{3,2},{2,3},{5,4},{4,5},{7,6},{6,7},{9,8},{8,9},{11,10... | collective-permute-start | bytes 1572872 | tf_op jit(solution)/shard_map/ppermute | solution.py:106
  186.5 39.1 %collective-permute-start.6 = (bf16[128,2048]{1,0:T(8,128)(2,1)}, bf16[128,2048]{1,0:T(8,128)(2,1)}, u32[]{:S(2)}, u32[]{:S(2)}) collective-permute-start(bf16[128,2048]{1,0:T(8,128)(2,1)} %collective-permute-done.5), channel_id=1, source_target_pairs={{0,1},{1,0},{2,3},{3,2},{4,5},{5,4},{6,7},{7,6},{8,9},{9,8},{10,11... | collective-permute-start | bytes 1572872 | tf_op jit(solution)/shard_map/ppermute | solution.py:100
  190.3 41.2 %collective-permute-start.10 = (bf16[128,2048]{1,0:T(8,128)(2,1)}, bf16[128,2048]{1,0:T(8,128)(2,1)}, u32[]{:S(2)}, u32[]{:S(2)}) collective-permute-start(bf16[128,2048]{1,0:T(8,128)(2,1)} %collective-permute-done.9), channel_id=1, source_target_pairs={{0,1},{1,0},{2,3},{3,2},{4,5},{5,4},{6,7},{7,6},{8,9},{9,8},{10,11... | collective-permute-start | bytes 1572872 | tf_op jit(solution)/shard_map/ppermute | solution.py:100
  212.4 32.0 %collective-permute-start.12 = (bf16[128,2048]{1,0:T(8,128)(2,1)}, bf16[128,2048]{1,0:T(8,128)(2,1)}, u32[]{:S(2)}, u32[]{:S(2)}) collective-permute-start(bf16[128,2048]{1,0:T(8,128)(2,1)} %collective-permute-done.9), channel_id=1, source_target_pairs={{0,2},{1,3},{2,0},{3,1},{4,6},{5,7},{6,4},{7,5},{8,10},{9,11},{10,... | collective-permute-start | bytes 1572872 | tf_op jit(solution)/shard_map/ppermute | solution.py:100
  219.9 17.3 %collective-permute-start.18 = (bf16[128,2048]{1,0:T(8,128)(2,1)}, bf16[128,2048]{1,0:T(8,128)(2,1)}, u32[]{:S(2)}, u32[]{:S(2)}) collective-permute-start(bf16[128,2048]{1,0:T(8,128)(2,1)} %collective-permute-done.17), channel_id=1, source_target_pairs={{0,1},{1,0},{2,3},{3,2},{4,5},{5,4},{6,7},{7,6},{8,9},{9,8},{10,11... | collective-permute-start | bytes 1572872 | tf_op jit(solution)/shard_map/ppermute | solution.py:100
  225.6 21.1 %collective-permute-start.20 = (bf16[128,2048]{1,0:T(8,128)(2,1)}, bf16[128,2048]{1,0:T(8,128)(2,1)}, u32[]{:S(2)}, u32[]{:S(2)}) collective-permute-start(bf16[128,2048]{1,0:T(8,128)(2,1)} %collective-permute-done.17), channel_id=1, source_target_pairs={{0,2},{1,3},{2,0},{3,1},{4,6},{5,7},{6,4},{7,5},{8,10},{9,11},{10,... | collective-permute-start | bytes 1572872 | tf_op jit(solution)/shard_map/ppermute | solution.py:100
  231.4 17.9 %collective-permute-start.26 = (bf16[128,2048]{1,0:T(8,128)(2,1)}, bf16[128,2048]{1,0:T(8,128)(2,1)}, u32[]{:S(2)}, u32[]{:S(2)}) collective-permute-start(bf16[128,2048]{1,0:T(8,128)(2,1)} %collective-permute-done.25), channel_id=1, source_target_pairs={{0,1},{1,0},{2,3},{3,2},{4,5},{5,4},{6,7},{7,6},{8,9},{9,8},{10,11... | collective-permute-start | bytes 1572872 | tf_op jit(solution)/shard_map/ppermute | solution.py:100
  237.2 14.4 %collective-permute-start.28 = (bf16[128,2048]{1,0:T(8,128)(2,1)}, bf16[128,2048]{1,0:T(8,128)(2,1)}, u32[]{:S(2)}, u32[]{:S(2)}) collective-permute-start(bf16[128,2048]{1,0:T(8,128)(2,1)} %collective-permute-done.25), channel_id=1, source_target_pairs={{0,2},{1,3},{2,0},{3,1},{4,6},{5,7},{6,4},{7,5},{8,10},{9,11},{10,... | collective-permute-start | bytes 1572872 | tf_op jit(solution)/shard_map/ppermute | solution.py:100
  244.4 26.0 %collective-permute-start.7 = (bf16[128,2048]{1,0:T(8,128)(2,1)}, bf16[128,2048]{1,0:T(8,128)(2,1)}, u32[]{:S(2)}, u32[]{:S(2)}) collective-permute-start(bf16[128,2048]{1,0:T(8,128)(2,1)} %fusion.43), channel_id=1, source_target_pairs={{1,0},{0,1},{3,2},{2,3},{5,4},{4,5},{7,6},{6,7},{9,8},{8,9},{11,10... | collective-permute-start | bytes 1572872 | tf_op jit(solution)/shard_map/ppermute | solution.py:106
  246.6 49.1 %collective-permute-start.11 = (bf16[128,2048]{1,0:T(8,128)(2,1)}, bf16[128,2048]{1,0:T(8,128)(2,1)}, u32[]{:S(2)}, u32[]{:S(2)}) collective-permute-start(bf16[128,2048]{1,0:T(8,128)(2,1)} %fusion.38), channel_id=1, source_target_pairs={{1,0},{0,1},{3,2},{2,3},{5,4},{4,5},{7,6},{6,7},{9,8},{8,9},{11,10... | collective-permute-start | bytes 1572872 | tf_op jit(solution)/shard_map/ppermute | solution.py:106
  249.3 55.3 %collective-permute-start.19 = (bf16[128,2048]{1,0:T(8,128)(2,1)}, bf16[128,2048]{1,0:T(8,128)(2,1)}, u32[]{:S(2)}, u32[]{:S(2)}) collective-permute-start(bf16[128,2048]{1,0:T(8,128)(2,1)} %fusion.28), channel_id=1, source_target_pairs={{1,0},{0,1},{3,2},{2,3},{5,4},{4,5},{7,6},{6,7},{9,8},{8,9},{11,10... | collective-permute-start | bytes 1572872 | tf_op jit(solution)/shard_map/ppermute | solution.py:106
  263.8 11.2 %collective-permute-start.29 = (bf16[128,2048]{1,0:T(8,128)(2,1)}, bf16[128,2048]{1,0:T(8,128)(2,1)}, u32[]{:S(2)}, u32[]{:S(2)}) collective-permute-start(bf16[128,2048]{1,0:T(8,128)(2,1)} %collective-permute-done.28), channel_id=1, source_target_pairs={{0,1},{1,0},{2,3},{3,2},{4,5},{5,4},{6,7},{7,6},{8,9},{9,8},{10,11... | collective-permute-start | bytes 1572872 | tf_op jit(solution)/shard_map/ppermute | solution.py:100
  270.4 10.2 %collective-permute-start.14 = (bf16[128,2048]{1,0:T(8,128)(2,1)}, bf16[128,2048]{1,0:T(8,128)(2,1)}, u32[]{:S(2)}, u32[]{:S(2)}) collective-permute-start(bf16[128,2048]{1,0:T(8,128)(2,1)} %fusion.33), channel_id=1, source_target_pairs={{1,0},{0,1},{3,2},{2,3},{5,4},{4,5},{7,6},{6,7},{9,8},{8,9},{11,10... | collective-permute-start | bytes 1572872 | tf_op jit(solution)/shard_map/ppermute | solution.py:106
  275.1 10.3 %collective-permute-start.22 = (bf16[128,2048]{1,0:T(8,128)(2,1)}, bf16[128,2048]{1,0:T(8,128)(2,1)}, u32[]{:S(2)}, u32[]{:S(2)}) collective-permute-start(bf16[128,2048]{1,0:T(8,128)(2,1)} %fusion.23), channel_id=1, source_target_pairs={{1,0},{0,1},{3,2},{2,3},{5,4},{4,5},{7,6},{6,7},{9,8},{8,9},{11,10... | collective-permute-start | bytes 1572872 | tf_op jit(solution)/shard_map/ppermute | solution.py:106
  280.6 10.6 %collective-permute-start.30 = (bf16[128,2048]{1,0:T(8,128)(2,1)}, bf16[128,2048]{1,0:T(8,128)(2,1)}, u32[]{:S(2)}, u32[]{:S(2)}) collective-permute-start(bf16[128,2048]{1,0:T(8,128)(2,1)} %fusion.13), channel_id=1, source_target_pairs={{1,0},{0,1},{3,2},{2,3},{5,4},{4,5},{7,6},{6,7},{9,8},{8,9},{11,10... | collective-permute-start | bytes 1572872 | tf_op jit(solution)/shard_map/ppermute | solution.py:106
  285.3 15.1 %collective-permute-start.15 = (bf16[128,2048]{1,0:T(8,128)(2,1)}, bf16[128,2048]{1,0:T(8,128)(2,1)}, u32[]{:S(2)}, u32[]{:S(2)}) collective-permute-start(bf16[128,2048]{1,0:T(8,128)(2,1)} %add_convert_fusion.6), channel_id=1, source_target_pairs={{2,0},{3,1},{0,2},{1,3},{6,4},{7,5},{4,6},{5,7},{10,8},{11,9},{8,1... | collective-permute-start | bytes 1572872 | tf_op jit(solution)/shard_map/ppermute | solution.py:106
  291.2 20.5 %collective-permute-start.23 = (bf16[128,2048]{1,0:T(8,128)(2,1)}, bf16[128,2048]{1,0:T(8,128)(2,1)}, u32[]{:S(2)}, u32[]{:S(2)}) collective-permute-start(bf16[128,2048]{1,0:T(8,128)(2,1)} %add_convert_fusion.4), channel_id=1, source_target_pairs={{2,0},{3,1},{0,2},{1,3},{6,4},{7,5},{4,6},{5,7},{10,8},{11,9},{8,1... | collective-permute-start | bytes 1572872 | tf_op jit(solution)/shard_map/ppermute | solution.py:106
  295.8 29.2 %collective-permute-start.27 = (bf16[128,2048]{1,0:T(8,128)(2,1)}, bf16[128,2048]{1,0:T(8,128)(2,1)S(1)}, u32[]{:S(2)}, u32[]{:S(2)}) collective-permute-start(bf16[128,2048]{1,0:T(8,128)(2,1)} %fusion.18), channel_id=1, source_target_pairs={{1,0},{0,1},{3,2},{2,3},{5,4},{4,5},{7,6},{6,7},{9,8},{8,9},{11,10... | collective-permute-start | bytes 1572872 | tf_op jit(solution)/shard_map/ppermute | solution.py:106
  300.5 24.5 %collective-permute-start.31 = (bf16[128,2048]{1,0:T(8,128)(2,1)}, bf16[128,2048]{1,0:T(8,128)(2,1)S(1)}, u32[]{:S(2)}, u32[]{:S(2)}) collective-permute-start(bf16[128,2048]{1,0:T(8,128)(2,1)} %add_convert_fusion.2), channel_id=1, source_target_pairs={{2,0},{3,1},{0,2},{1,3},{6,4},{7,5},{4,6},{5,7},{10,8},{11,9},{8,1... | collective-permute-start | bytes 1572872 | tf_op jit(solution)/shard_map/ppermute | solution.py:106
  304.7 32.2 %collective-permute-start.8 = (bf16[128,2048]{1,0:T(8,128)(2,1)}, bf16[128,2048]{1,0:T(8,128)(2,1)}, u32[]{:S(2)}, u32[]{:S(2)}) collective-permute-start(bf16[128,2048]{1,0:T(8,128)(2,1)} %add_convert_fusion.7), channel_id=1, source_target_pairs={{2,0},{3,1},{0,2},{1,3},{6,4},{7,5},{4,6},{5,7},{10,8},{11,9},{8,1... | collective-permute-start | bytes 1572872 | tf_op jit(solution)/shard_map/ppermute | solution.py:106
  311.7 25.2 %collective-permute-start.16 = (bf16[128,2048]{1,0:T(8,128)(2,1)}, bf16[128,2048]{1,0:T(8,128)(2,1)}, u32[]{:S(2)}, u32[]{:S(2)}) collective-permute-start(bf16[128,2048]{1,0:T(8,128)(2,1)} %add_convert_fusion.5), channel_id=1, source_target_pairs={{12,0},{13,1},{14,2},{15,3},{0,4},{1,5},{2,6},{3,7},{4,8},{5,9},{6... | collective-permute-start | bytes 1572872 | tf_op jit(solution)/shard_map/ppermute | solution.py:106
  325.0 40.5 %collective-permute-start.24 = (bf16[128,2048]{1,0:T(8,128)(2,1)}, bf16[128,2048]{1,0:T(8,128)(2,1)}, u32[]{:S(2)}, u32[]{:S(2)}) collective-permute-start(bf16[128,2048]{1,0:T(8,128)(2,1)} %add_convert_fusion.3), channel_id=1, source_target_pairs={{8,0},{9,1},{10,2},{11,3},{12,4},{13,5},{14,6},{15,7},{0,8},{1,9},... | collective-permute-start | bytes 1572872 | tf_op jit(solution)/shard_map/ppermute | solution.py:106
  326.0 39.5 %collective-permute-start.32 = (bf16[128,2048]{1,0:T(8,128)(2,1)}, bf16[128,2048]{1,0:T(8,128)(2,1)}, u32[]{:S(2)}, u32[]{:S(2)}) collective-permute-start(bf16[128,2048]{1,0:T(8,128)(2,1)} %add_convert_fusion.1), channel_id=1, source_target_pairs={{4,0},{5,1},{6,2},{7,3},{8,4},{9,5},{10,6},{11,7},{12,8},{13,9},{1... | collective-permute-start | bytes 1572872 | tf_op jit(solution)/shard_map/ppermute | solution.py:106
  (30 other events, 314.1 us)
Sparse Core Ops, SparseCore 0:
  34.5 33.6 all-gather.4

commit v4 on v3

--- a/solution.py
+++ b/solution.py
@@ -60,52 +60,42 @@
     return tuple(joined)
 
 
-def dense_moe(plan, normed, route_ids, route_weights, gate_w, up_w, down_w):
-    tok_dev = normed.shape[0]
+def dense_moe(plan, normed, route_ids, route_weights, weight_parts, anchor):
     expert_count = EXP_DEV * lax.axis_size("ep")
     experts = jnp.arange(expert_count, dtype=jnp.int32)
     own_expert = lax.axis_index("ep")
     chosen = route_ids[:, :, None] == experts[None, None, :]
     weight_table = jnp.sum(jnp.where(chosen, route_weights[:, :, None], 0.0), axis=1)
-    own_weight = jnp.sum(jnp.where(experts == own_expert, weight_table, 0.0), axis=1)
-    every_table = lax.all_gather(weight_table, "ep", axis=0, tiled=True)
-    full_gate, full_up, full_down = full_weights(gate_w, up_w, down_w)
-    normed, full_gate, full_up, full_down = lax.optimization_barrier(
-        (normed, full_gate, full_up, full_down)
-    )
-    ep_count = lax.axis_size("ep")
-
-    def expert(rows, origin):
-        if origin is None:
-            weights = own_weight
-        else:
-            source = jnp.asarray(origin, jnp.int32)[own_expert]
-            table = lax.dynamic_slice_in_dim(every_table, source * tok_dev, tok_dev, 0)
-            weights = jnp.sum(jnp.where(experts == own_expert, table, 0.0), axis=1)
-        gate_val = jnp.dot(rows, full_gate, preferred_element_type=jnp.float32)
-        up_val = jnp.dot(rows, full_up, preferred_element_type=jnp.float32)
+    weight_parts, anchor = lax.optimization_barrier((weight_parts, anchor))
+    full = list(full_weights(*weight_parts))
+
+    def expert(rows, table):
+        weights = jnp.sum(jnp.where(experts == own_expert, table, 0.0), axis=1)
+        gate_val = jnp.dot(rows, full[0], preferred_element_type=jnp.float32)
+        up_val = jnp.dot(rows, full[1], preferred_element_type=jnp.float32)
         act = (jax.nn.silu(gate_val) * up_val).astype(jnp.bfloat16)
-        out_rows = jnp.dot(act, full_down, preferred_element_type=jnp.float32)
+        out_rows = jnp.dot(act, full[2], preferred_element_type=jnp.float32)
         out_rows = out_rows.astype(jnp.bfloat16).astype(jnp.float32)
         return out_rows * weights[:, None]
 
-    pieces = [(normed, np.arange(ep_count), None, None)]
-    for pairs_list in plan:
+    pieces = [((normed, weight_table), None, None)]
+    for number, pairs_list in enumerate(plan):
         grown = []
-        for parent, (rows, origin, _, _) in enumerate(pieces):
+        for parent, (block, _, _) in enumerate(pieces):
             for pairs in pairs_list:
-                moved = np.zeros_like(origin)
-                for source, target in pairs:
-                    moved[target] = origin[source]
-                grown.append((lax.ppermute(rows, "ep", pairs), moved, parent, pairs))
+                grown.append((lax.ppermute(block, "ep", pairs), parent, pairs))
+        if number == 1:
+            tied = lax.optimization_barrier((tuple(full), [piece[0] for piece in grown]))
+            full = list(tied[0])
+            grown = [(block, parent, pairs) for block, (_, parent, pairs) in zip(tied[1], grown)]
         pieces = pieces + grown
-    partial = [expert(rows, None if index == 0 else origin) for index, (rows, origin, _, _) in enumerate(pieces)]
+    partial = [expert(*block) for block, _, _ in pieces]
     for index in reversed(range(1, len(pieces))):
-        _, _, parent, pairs = pieces[index]
+        _, parent, pairs = pieces[index]
         back = [(target, source) for source, target in pairs]
         sent = lax.ppermute(partial[index].astype(jnp.bfloat16), "ep", back)
         partial[parent] = partial[parent] + sent.astype(jnp.float32)
-    return partial[0]
+    return partial[0], anchor
 
 
 def gather_plan(mesh, shapes):
@@ -241,7 +231,9 @@
         * norm_gain.astype(jnp.float32)
     ).astype(jnp.bfloat16)
     if plan is not None:
-        moe_sum = dense_moe(plan, normed, route_ids[0], route_weights[0], gate_w, up_w, down_w)
+        moe_sum, _ = dense_moe(
+            plan, normed, route_ids[0], route_weights[0], (gate_w, up_w, down_w), joint_denom
+        )
         return (hidden_f + moe_sum).astype(jnp.bfloat16)[None]
     expert_count = EXP_DEV * ep_count
     capacity = min(tok_dev, max(2, tok_dev * TOP * 3 // (2 * expert_count)))

time: 381 us -> 341 us (0.90)
  blocking collectives: 103 us -> 16.7 us
  waiting for transfers between devices: 62.1 us -> 146 us
  local copies, waits for them, and re-layouts: 24.7 us -> 14.3 us
  between operations: 24.3 us -> 14.4 us
  other arithmetic: 23.2 us -> 13.7 us
  starting transfers between devices: 36.7 us -> 27.5 us
    all_gather x2, blocking collectives: 77 us -> 8.75 us  [combined_all(): lax.all_gather(a.astype(kind), axis)]
    ppermute x3, waiting for transfers between devices: 0.01 us -> 45.5 us  [full_weights(): other = lax.ppermute(mine, 'kv', [(0, 1), (1, 0)])]
    ppermute x15 -> x30, waiting for transfers between devices: 22.1 us -> 43 us  [dense_moe(): grown.append((lax.ppermute(block, 'ep', pairs), parent, pairs))]
    ppermute x15, starting transfers between devices: 22.8 us -> 5.65 us  [dense_moe(): sent = lax.ppermute(partial[index].astype(jnp.bfloat16), 'ep', back)]
    all_gather x1 -> x0, blocking collectives: 17.1 us -> none  [dense_moe(): every_table = lax.all_gather(weight_table, 'ep', axis=0, tiled=True)]
    all_gather x1, waiting for transfers between devices: 0.02 us -> 14.1 us  [combined_all(): lax.all_gather(a.astype(kind), axis)]
    dynamic_slice x16 -> x0, local copies, waits for them, and re-layouts: 9.31 us -> none  [the longest x15 9.31 us: expert(): source = jnp.asarray(origin, jnp.int32)[own_expert]]
    ppermute x15 -> x30, starting transfers between devices: 10.3 us -> 19.3 us  [dense_moe(): grown.append((lax.ppermute(block, 'ep', pairs), parent, pairs))]
  transfers between devices with their start and end apart: 34 -> 49, of which waited for: 7 -> 12; matrix products, arithmetic and copies ran while one was open for 33% -> 37% of each run, Pallas kernels for 0% -> 0%
where the time goes in v4:
time: 341 us; the launch traced here: 337 us
  waiting for transfers between devices  146 us (43%)
  matrix products  104 us (30%)
  starting transfers between devices  27.5 us (8%)
  blocking collectives  16.7 us (5%)
  between operations  14.4 us (4%)
  local copies, waits for them, and re-layouts  14.3 us (4%)
  other arithmetic  13.7 us (4%)
    dot_general x16, matrix products, expert(): out_rows = jnp.dot(act, full[2], preferred_element_type=jnp.float32)  68.4 us
    ppermute x3, waiting for transfers between devices, full_weights(): other = lax.ppermute(mine, 'kv', [(0, 1), (1, 0)])  45.5 us
    ppermute x15, waiting for transfers between devices, dense_moe(): sent = lax.ppermute(partial[index].astype(jnp.bfloat16), 'ep', back)  43.8 us
    ppermute x30, waiting for transfers between devices, dense_moe(): grown.append((lax.ppermute(block, 'ep', pairs), parent, pairs))  43 us
    dot_general x16, matrix products, expert(): gate_val = jnp.dot(rows, full[0], preferred_element_type=jnp.float32)  26.5 us
    ppermute x30, starting transfers between devices, dense_moe(): grown.append((lax.ppermute(block, 'ep', pairs), parent, pairs))  19.3 us
    all_gather x1, waiting for transfers between devices, combined_all(): lax.all_gather(a.astype(kind), axis)  14.1 us
    all_gather x2, blocking collectives, combined_all(): lax.all_gather(a.astype(kind), axis)  8.75 us
  transfers between devices with their start and end apart: 49, of which 12 were waited for; matrix products, arithmetic and copies ran while one was open for 37% of the time, Pallas kernels for 0%

profile of v4, /device:TPU:24, one launch (start us, length us, event | category | flops | bytes accessed | tf_op | source)
XLA Modules:
  0.0 336.8 jit_solution(1626395800164649413)
XLA Ops:
  13.3 7.9 %all-gather = bf16[1,256,1024]{1,2,0:T(8,128)(2,1)S(1)} all-gather(bf16[1,128,1024]{1,2,0:T(8,128)(2,1)S(1)} %copy.50), channel_id=2, replica_groups=mesh['kv'=2,'ep'=16] {'kv'}, dimensions={1}, use_global_device_ids=true | all-gather | bytes 786432 | tf_op jit(solution)/shard_map/all_gather | solution.py:167
  38.5 4.5 %fusion.1 = f32[256,8]{0,1:T(8,128)S(1)} fusion(f32[8,1024,256]{2,1,0:T(8,128)} %copy-done, f32[256,8]{0,1:T(8,128)S(1)} %get-tuple-element.74, pred[1024]{0:T(1024)(128)(4,1)S(1)} %add_compare_fusion), kind=kLoop, calls=%fused_computation.4 | loop fusion | flops 8386560 | bytes 8406016 | tf_op jit(solution)/shard_map/reduce_sum | solution.py:187
  43.2 4.3 %all-gather.2 = bf16[512,8]{0,1:T(8,128)(2,1)S(1)} all-gather(bf16[256,8]{0,1:T(8,128)(2,1)S(1)} %add_convert_fusion), channel_id=4, replica_groups=mesh['kv'=2,'ep'=16] {'kv'}, dimensions={0}, use_global_device_ids=true | all-gather | bytes 12288 | tf_op jit(solution)/shard_map/all_gather | solution.py:18
  47.6 4.4 %all-gather.1 = bf16[512,8]{0,1:T(8,128)(2,1)S(1)} all-gather(bf16[256,8]{0,1:T(8,128)(2,1)S(1)} %get-tuple-element.73), channel_id=3, replica_groups=mesh['kv'=2,'ep'=16] {'kv'}, dimensions={0}, use_global_device_ids=true | all-gather | bytes 12288 | tf_op jit(solution)/shard_map/all_gather | solution.py:18
  55.6 14.1 %all-gather.5.cloned.1.call-done = bf16[2,256,1024]{2,1,0:T(8,128)(2,1)} async-done(((bf16[1,256,1024]{2,1,0:T(8,128)(2,1)}), bf16[2,256,1024]{2,1,0:T(8,128)(2,1)}) %all-gather.5.cloned.1.call-update) | async-done | bytes 1048592 | tf_op jit(solution)/shard_map/all_gather | solution.py:18
  74.5 10.6 %collective-permute-done.1 = bf16[2048,256]{1,0:T(8,128)(2,1)} collective-permute-done((bf16[2048,256]{1,0:T(8,128)(2,1)}, bf16[2048,256]{1,0:T(8,128)(2,1)}, u32[]{:S(2)}, u32[]{:S(2)}) %collective-permute-start.1) | collective-permute-done | bytes 1048608 | tf_op jit(solution)/shard_map/ppermute | solution.py:53
  88.8 18.7 %collective-permute-done = bf16[2048,256]{1,0:T(8,128)(2,1)} collective-permute-done((bf16[2048,256]{1,0:T(8,128)(2,1)}, bf16[2048,256]{1,0:T(8,128)(2,1)}, u32[]{:S(2)}, u32[]{:S(2)}) %collective-permute-start) | collective-permute-done | bytes 1048608 | tf_op jit(solution)/shard_map/ppermute | solution.py:53
  112.0 16.1 %collective-permute-done.2 = bf16[256,2048]{1,0:T(8,128)(2,1)S(1)} collective-permute-done((bf16[256,2048]{1,0:T(8,128)(2,1)S(1)}, bf16[256,2048]{1,0:T(8,128)(2,1)S(1)}, u32[]{:S(2)}, u32[]{:S(2)}) %collective-permute-start.2) | collective-permute-done | bytes 1048608 | tf_op jit(solution)/shard_map/ppermute | solution.py:53
  130.9 13.7 %collective-permute-done.9 = bf16[128,2048]{1,0:T(8,128)(2,1)S(1)} collective-permute-done((bf16[128,2048]{1,0:T(8,128)(2,1)S(1)}, bf16[128,2048]{1,0:T(8,128)(2,1)S(1)}, u32[]{:S(2)}, u32[]{:S(2)}) %collective-permute-start.9) | collective-permute-done | bytes 524320 | tf_op jit(solution)/shard_map/ppermute | solution.py:86
  146.7 9.0 %collective-permute-done.5 = bf16[128,2048]{1,0:T(8,128)(2,1)S(1)} collective-permute-done((bf16[128,2048]{1,0:T(8,128)(2,1)S(1)}, bf16[128,2048]{1,0:T(8,128)(2,1)S(1)}, u32[]{:S(2)}, u32[]{:S(2)}) %collective-permute-start.5) | collective-permute-done | bytes 524320 | tf_op jit(solution)/shard_map/ppermute | solution.py:86
  160.9 20.1 %collective-permute-done.8 = f32[128,16]{0,1:T(8,128)S(1)} collective-permute-done((f32[128,16]{0,1:T(8,128)S(1)}, f32[128,16]{0,1:T(8,128)S(1)}, u32[]{:S(2)}, u32[]{:S(2)}) %collective-permute-start.8) | collective-permute-done | bytes 8224 | tf_op jit(solution)/shard_map/ppermute | solution.py:86
  201.8 4.1 %fusion.65 = bf16[128,2048]{1,0:T(8,128)(2,1)} fusion(bf16[512,2048]{1,0:T(8,128)(2,1)} %pad_maximum_fusion.2, f32[128]{0:T(128)S(1)} %get-tuple-element.58, f32[128,512]{1,0:T(8,128)} %fusion.164, bf16[128,2048]{1,0:T(8,128)(2,1)} %copy-done.9, bf16[2048,512]{1,0:T(8,128)(2,1)} %get-tuple-element.47), kind=kOutput, calls=%fused_computation.83 | convolution fusion | flops 538312704 | bytes 5505536 | tf_op jit(solution)/shard_map/dot_general | solution.py:77
  206.0 4.1 %fusion.50 = bf16[128,2048]{1,0:T(8,128)(2,1)} fusion(bf16[512,2048]{1,0:T(8,128)(2,1)} %pad_maximum_fusion.2, f32[128]{0:T(128)S(1)} %get-tuple-element.62, f32[128,512]{1,0:T(8,128)} %fusion.168, bf16[128,2048]{1,0:T(8,128)(2,1)} %copy-done.8, bf16[2048,512]{1,0:T(8,128)(2,1)} %get-tuple-element.47), kind=kOutput, calls=%fused_computation.64 | convolution fusion | flops 538312704 | bytes 5505536 | tf_op jit(solution)/shard_map/dot_general | solution.py:77
  210.1 4.1 %fusion.35 = bf16[128,2048]{1,0:T(8,128)(2,1)} fusion(bf16[512,2048]{1,0:T(8,128)(2,1)} %pad_maximum_fusion.2, f32[128]{0:T(128)S(1)} %get-tuple-element.66, f32[128,512]{1,0:T(8,128)} %fusion.172, bf16[128,2048]{1,0:T(8,128)(2,1)} %copy-done.10, bf16[2048,512]{1,0:T(8,128)(2,1)} %get-tuple-element.47), kind=kOutput, calls=%fused_computation.45 | convolution fusion | flops 538312704 | bytes 5505536 | tf_op jit(solution)/shard_map/dot_general | solution.py:77
  214.2 4.2 %fusion.20 = bf16[128,2048]{1,0:T(8,128)(2,1)} fusion(bf16[512,2048]{1,0:T(8,128)(2,1)} %pad_maximum_fusion.2, f32[128]{0:T(128)S(1)} %get-tuple-element.70, f32[128,512]{1,0:T(8,128)} %fusion.176, bf16[128,2048]{1,0:T(8,128)(2,1)} %copy-done.11, bf16[2048,512]{1,0:T(8,128)(2,1)} %get-tuple-element.47), kind=kOutput, calls=%fused_computation.26 | convolution fusion | flops 538312704 | bytes 5505536 | tf_op jit(solution)/shard_map/dot_general | solution.py:77
  221.0 4.1 %fusion.58 = bf16[128,2048]{1,0:T(8,128)(2,1)} fusion(bf16[512,2048]{1,0:T(8,128)(2,1)} %pad_maximum_fusion.2, f32[128]{0:T(128)S(1)} %get-tuple-element.60, f32[128,512]{1,0:T(8,128)} %fusion.166, bf16[128,2048]{1,0:T(8,128)(2,1)} %collective-permute-done.20, bf16[2048,512]{1,0:T(8,128)(2,1)} %get-tuple-element.47), kind=kOutput, calls=%fused_computation.74 | convolution fusion | flops 538312704 | bytes 5505536 | tf_op jit(solution)/shard_map/dot_general | solution.py:77
  227.4 4.1 %fusion.43 = bf16[128,2048]{1,0:T(8,128)(2,1)} fusion(bf16[512,2048]{1,0:T(8,128)(2,1)} %pad_maximum_fusion.2, f32[128]{0:T(128)S(1)} %get-tuple-element.64, f32[128,512]{1,0:T(8,128)} %fusion.170, bf16[128,2048]{1,0:T(8,128)(2,1)} %collective-permute-done.27, bf16[2048,512]{1,0:T(8,128)(2,1)} %get-tuple-element.47), kind=kOutput, calls=%fused_computation.55 | convolution fusion | flops 538312704 | bytes 5505536 | tf_op jit(solution)/shard_map/dot_general | solution.py:77
  234.2 4.4 %fusion.28 = bf16[128,2048]{1,0:T(8,128)(2,1)} fusion(bf16[512,2048]{1,0:T(8,128)(2,1)} %pad_maximum_fusion.2, f32[128]{0:T(128)S(1)} %get-tuple-element.68, f32[128,512]{1,0:T(8,128)} %fusion.174, bf16[128,2048]{1,0:T(8,128)(2,1)} %collective-permute-done.35, bf16[2048,512]{1,0:T(8,128)(2,1)} %get-tuple-element.47), kind=kOutput, calls=%fused_computation.36 | convolution fusion | flops 538312704 | bytes 5505536 | tf_op jit(solution)/shard_map/dot_general | solution.py:77
  240.8 4.1 %fusion.13 = bf16[128,2048]{1,0:T(8,128)(2,1)} fusion(bf16[512,2048]{1,0:T(8,128)(2,1)} %pad_maximum_fusion.2, f32[128]{0:T(128)S(1)} %get-tuple-element.72, f32[128,512]{1,0:T(8,128)} %fusion.178, bf16[128,2048]{1,0:T(8,128)(2,1)} %collective-permute-done.43, bf16[2048,512]{1,0:T(8,128)(2,1)} %get-tuple-element.47), kind=kOutput, calls=%fused_computation.17 | convolution fusion | flops 538312704 | bytes 5505536 | tf_op jit(solution)/shard_map/dot_general | solution.py:77
  245.3 4.2 %fusion.62 = bf16[128,2048]{1,0:T(8,128)(2,1)} fusion(bf16[512,2048]{1,0:T(8,128)(2,1)} %pad_maximum_fusion.2, bf16[128,2048]{1,0:T(8,128)(2,1)} %collective-permute-done.22, f32[128]{0:T(128)S(1)} %get-tuple-element.59, f32[128,512]{1,0:T(8,128)} %fusion.165, bf16[128,2048]{1,0:T(8,128)(2,1)} %collective-permute-done.3, ...), kind=kOutput, calls=%fused_computation.79 | convolution fusion | flops 538836992 | bytes 6029824 | tf_op jit(solution)/shard_map/dot_general | solution.py:77
  249.6 4.2 %fusion.47 = bf16[128,2048]{1,0:T(8,128)(2,1)} fusion(bf16[512,2048]{1,0:T(8,128)(2,1)} %pad_maximum_fusion.2, bf16[128,2048]{1,0:T(8,128)(2,1)} %collective-permute-done.29, f32[128]{0:T(128)S(1)} %get-tuple-element.63, f32[128,512]{1,0:T(8,128)} %fusion.169, bf16[128,2048]{1,0:T(8,128)(2,1)} %collective-permute-done.14, ...), kind=kOutput, calls=%fused_computation.60 | convolution fusion | flops 538836992 | bytes 6029824 | tf_op jit(solution)/shard_map/dot_general | solution.py:77
  254.4 4.2 %fusion.32 = bf16[128,2048]{1,0:T(8,128)(2,1)} fusion(bf16[512,2048]{1,0:T(8,128)(2,1)} %pad_maximum_fusion.2, bf16[128,2048]{1,0:T(8,128)(2,1)} %collective-permute-done.37, f32[128]{0:T(128)S(1)} %get-tuple-element.67, f32[128,512]{1,0:T(8,128)} %fusion.173, bf16[128,2048]{1,0:T(8,128)(2,1)} %collective-permute-done.10, ...), kind=kOutput, calls=%fused_computation.41 | convolution fusion | flops 538836992 | bytes 6029824 | tf_op jit(solution)/shard_map/dot_general | solution.py:77
  260.1 4.2 %fusion.17 = bf16[128,2048]{1,0:T(8,128)(2,1)} fusion(bf16[512,2048]{1,0:T(8,128)(2,1)} %pad_maximum_fusion.2, bf16[128,2048]{1,0:T(8,128)(2,1)} %collective-permute-done.45, f32[128]{0:T(128)S(1)} %get-tuple-element.71, f32[128,512]{1,0:T(8,128)} %fusion.177, bf16[128,2048]{1,0:T(8,128)(2,1)} %collective-permute-done.6, ...), kind=kOutput, calls=%fused_computation.22 | convolution fusion | flops 538836992 | bytes 6029824 | tf_op jit(solution)/shard_map/dot_general | solution.py:77
  264.3 4.6 %collective-permute-done.30 = bf16[128,2048]{1,0:T(8,128)(2,1)} collective-permute-done((bf16[128,2048]{1,0:T(8,128)(2,1)}, bf16[128,2048]{1,0:T(8,128)(2,1)}, u32[]{:S(2)}, u32[]{:S(2)}) %collective-permute-start.30) | collective-permute-done | bytes 524320 | tf_op jit(solution)/shard_map/ppermute | solution.py:96
  269.4 4.5 %fusion.55 = bf16[128,2048]{1,0:T(8,128)(2,1)} fusion(bf16[512,2048]{1,0:T(8,128)(2,1)} %pad_maximum_fusion.2, bf16[128,2048]{1,0:T(8,128)(2,1)} %collective-permute-done.30, bf16[128,2048]{1,0:T(8,128)(2,1)} %collective-permute-done.26, f32[128]{0:T(128)S(1)} %get-tuple-element.61, f32[128,512]{1,0:T(8,128)} %fusion.167, bf16[128,2048]{1,0:T(8,128)(2,1)} %copy-done.7, ...), kind=kOutput, calls=%fused_computation.70 | convolution fusion | flops 539361280 | bytes 6554112 | tf_op jit(solution)/shard_map/dot_general | solution.py:77
  275.4 4.7 %collective-permute-done.38 = bf16[128,2048]{1,0:T(8,128)(2,1)} collective-permute-done((bf16[128,2048]{1,0:T(8,128)(2,1)}, bf16[128,2048]{1,0:T(8,128)(2,1)}, u32[]{:S(2)}, u32[]{:S(2)}) %collective-permute-start.38) | collective-permute-done | bytes 524320 | tf_op jit(solution)/shard_map/ppermute | solution.py:96
  280.1 4.5 %fusion.40 = bf16[128,2048]{1,0:T(8,128)(2,1)} fusion(bf16[512,2048]{1,0:T(8,128)(2,1)} %pad_maximum_fusion.2, bf16[128,2048]{1,0:T(8,128)(2,1)} %collective-permute-done.38, bf16[128,2048]{1,0:T(8,128)(2,1)} %collective-permute-done.34, f32[128]{0:T(128)S(1)} %get-tuple-element.65, f32[128,512]{1,0:T(8,128)} %fusion.171, bf16[128,2048]{1,0:T(8,128)(2,1)} %copy-done.6, ...), kind=kOutput, calls=%fused_computation.51 | convolution fusion | flops 539361280 | bytes 6554112 | tf_op jit(solution)/shard_map/dot_general | solution.py:77
  284.6 6.8 %collective-permute-done.46 = bf16[128,2048]{1,0:T(8,128)(2,1)} collective-permute-done((bf16[128,2048]{1,0:T(8,128)(2,1)}, bf16[128,2048]{1,0:T(8,128)(2,1)}, u32[]{:S(2)}, u32[]{:S(2)}) %collective-permute-start.46) | collective-permute-done | bytes 524320 | tf_op jit(solution)/shard_map/ppermute | solution.py:96
  291.4 4.4 %fusion.25 = bf16[128,2048]{1,0:T(8,128)(2,1)} fusion(bf16[512,2048]{1,0:T(8,128)(2,1)} %pad_maximum_fusion.2, bf16[128,2048]{1,0:T(8,128)(2,1)} %collective-permute-done.46, bf16[128,2048]{1,0:T(8,128)(2,1)} %collective-permute-done.42, f32[128]{0:T(128)S(1)} %get-tuple-element.69, f32[128,512]{1,0:T(8,128)S(1)} %fusion.175, ...), kind=kOutput, calls=%fused_computation.32 | convolution fusion | flops 539361280 | bytes 6554112 | tf_op jit(solution)/shard_map/dot_general | solution.py:77
  297.2 4.9 %collective-permute-done.23 = bf16[128,2048]{1,0:T(8,128)(2,1)} collective-permute-done((bf16[128,2048]{1,0:T(8,128)(2,1)}, bf16[128,2048]{1,0:T(8,128)(2,1)}, u32[]{:S(2)}, u32[]{:S(2)}) %collective-permute-start.23) | collective-permute-done | bytes 524320 | tf_op jit(solution)/shard_map/ppermute | solution.py:96
  302.1 22.8 %collective-permute-done.39 = bf16[128,2048]{1,0:T(8,128)(2,1)} collective-permute-done((bf16[128,2048]{1,0:T(8,128)(2,1)}, bf16[128,2048]{1,0:T(8,128)(2,1)}, u32[]{:S(2)}, u32[]{:S(2)}) %collective-permute-start.39) | collective-permute-done | bytes 524320 | tf_op jit(solution)/shard_map/ppermute | solution.py:96
  324.9 5.0 %fusion.75 = bf16[1,128,2048]{2,1,0:T(8,128)(2,1)} fusion(f32[128,2048]{1,0:T(8,128)S(1)} %get-tuple-element.91, bf16[512,2048]{1,0:T(8,128)(2,1)} %pad_maximum_fusion.2, bf16[128,2048]{1,0:T(8,128)(2,1)} %collective-permute-done.47, bf16[128,2048]{1,0:T(8,128)(2,1)} %collective-permute-done.39, bf16[128,2048]{1,0:T(8,128)(2,1)} %collective-permute-done.31, ...), kind=kOutput, calls=%fused_computation.94 | convolution fusion | flops 541196288 | bytes 9175552 | tf_op jit(solution)/shard_map/dot_general | solution.py:77
  (172 shorter events, 86.6 us)
Async XLA Ops:
  6.5 63.2 %all-gather.5.cloned.1.call-start = ((), (), s32[]{:S(2)}) async-start(), calls=%async_computation | async-start | bytes 1572864 | tf_op jit(solution)/shard_map/all_gather | solution.py:18
  7.3 80.0 %collective-permute-start.11 = (f32[128,16]{0,1:T(8,128)S(1)}, f32[128,16]{0,1:T(8,128)S(1)}, u32[]{:S(2)}, u32[]{:S(2)}) collective-permute-start(f32[128,16]{0,1:T(8,128)S(1)} %select_reduce_fusion), channel_id=1, source_target_pairs={{0,8},{1,9},{2,10},{3,11},{4,12},{5,13},{6,14},{7,15},{8,0},{9,1},... | collective-permute-start | bytes 24584 | tf_op jit(solution)/shard_map/ppermute | solution.py:86
  7.7 103.2 %collective-permute-start.15 = (f32[128,16]{0,1:T(8,128)S(1)}, f32[128,16]{0,1:T(8,128)S(1)}, u32[]{:S(2)}, u32[]{:S(2)}) collective-permute-start(f32[128,16]{0,1:T(8,128)S(1)} %select_reduce_fusion), channel_id=1, source_target_pairs={{0,12},{1,13},{2,14},{3,15},{4,0},{5,1},{6,2},{7,3},{8,4},{9,5},{1... | collective-permute-start | bytes 24584 | tf_op jit(solution)/shard_map/ppermute | solution.py:86
  7.8 103.6 %collective-permute-start.7 = (f32[128,16]{0,1:T(8,128)S(1)}, f32[128,16]{0,1:T(8,128)S(1)}, u32[]{:S(2)}, u32[]{:S(2)}) collective-permute-start(f32[128,16]{0,1:T(8,128)S(1)} %select_reduce_fusion), channel_id=1, source_target_pairs={{0,4},{1,5},{2,6},{3,7},{4,8},{5,9},{6,10},{7,11},{8,12},{9,13},{1... | collective-permute-start | bytes 24584 | tf_op jit(solution)/shard_map/ppermute | solution.py:86
  52.0 33.1 %collective-permute-start.1 = (bf16[2048,256]{1,0:T(8,128)(2,1)}, bf16[2048,256]{1,0:T(8,128)(2,1)}, u32[]{:S(2)}, u32[]{:S(2)}) collective-permute-start(bf16[2048,256]{1,0:T(8,128)(2,1)} %bitcast.12), channel_id=1, source_target_pairs={{0,16},{16,0},{1,17},{17,1},{2,18},{18,2},{3,19},{19,3},{4,20},{20... | collective-permute-start | bytes 3145736 | tf_op jit(solution)/shard_map/ppermute | solution.py:53
  53.6 54.0 %collective-permute-start = (bf16[2048,256]{1,0:T(8,128)(2,1)}, bf16[2048,256]{1,0:T(8,128)(2,1)}, u32[]{:S(2)}, u32[]{:S(2)}) collective-permute-start(bf16[2048,256]{1,0:T(8,128)(2,1)} %bitcast.11), channel_id=1, source_target_pairs={{0,16},{16,0},{1,17},{17,1},{2,18},{18,2},{3,19},{19,3},{4,20},{20... | collective-permute-start | bytes 3145736 | tf_op jit(solution)/shard_map/ppermute | solution.py:53
  85.1 43.1 %collective-permute-start.2 = (bf16[256,2048]{1,0:T(8,128)(2,1)S(1)}, bf16[256,2048]{1,0:T(8,128)(2,1)S(1)}, u32[]{:S(2)}, u32[]{:S(2)}) collective-permute-start(bf16[256,2048]{1,0:T(8,128)(2,1)S(1)} %bitcast.156), channel_id=1, source_target_pairs={{0,16},{16,0},{1,17},{17,1},{2,18},{18,2},{3,19},{19,3},{4,20},{20... | collective-permute-start | bytes 3145736 | tf_op jit(solution)/shard_map/ppermute | solution.py:53
  87.3 41.5 %collective-permute-start.4 = (f32[128,16]{0,1:T(8,128)S(1)}, f32[128,16]{0,1:T(8,128)S(1)}, u32[]{:S(2)}, u32[]{:S(2)}) collective-permute-start(f32[128,16]{0,1:T(8,128)S(1)} %select_reduce_fusion), channel_id=1, source_target_pairs={{0,2},{1,3},{2,0},{3,1},{4,6},{5,7},{6,4},{7,5},{8,10},{9,11},{10,... | collective-permute-start | bytes 24584 | tf_op jit(solution)/shard_map/ppermute | solution.py:86
  107.6 22.8 %collective-permute-start.12 = (f32[128,16]{0,1:T(8,128)S(1)}, f32[128,16]{0,1:T(8,128)S(1)}, u32[]{:S(2)}, u32[]{:S(2)}) collective-permute-start(f32[128,16]{0,1:T(8,128)S(1)} %collective-permute-done.11), channel_id=1, source_target_pairs={{0,2},{1,3},{2,0},{3,1},{4,6},{5,7},{6,4},{7,5},{8,10},{9,11},{10,... | collective-permute-start | bytes 24584 | tf_op jit(solution)/shard_map/ppermute | solution.py:86
  110.9 33.8 %collective-permute-start.9 = (bf16[128,2048]{1,0:T(8,128)(2,1)S(1)}, bf16[128,2048]{1,0:T(8,128)(2,1)S(1)}, u32[]{:S(2)}, u32[]{:S(2)}) collective-permute-start(bf16[128,2048]{1,0:T(8,128)(2,1)S(1)} %multiply_convert_fusion), channel_id=1, source_target_pairs={{0,8},{1,9},{2,10},{3,11},{4,12},{5,13},{6,14},{7,15},{8,0},{9,1},... | collective-permute-start | bytes 1572872 | tf_op jit(solution)/shard_map/ppermute | solution.py:86
  111.5 33.8 %collective-permute-start.13 = (bf16[128,2048]{1,0:T(8,128)(2,1)S(1)}, bf16[128,2048]{1,0:T(8,128)(2,1)S(1)}, u32[]{:S(2)}, u32[]{:S(2)}) collective-permute-start(bf16[128,2048]{1,0:T(8,128)(2,1)S(1)} %multiply_convert_fusion), channel_id=1, source_target_pairs={{0,12},{1,13},{2,14},{3,15},{4,0},{5,1},{6,2},{7,3},{8,4},{9,5},{1... | collective-permute-start | bytes 1572872 | tf_op jit(solution)/shard_map/ppermute | solution.py:86
  128.2 27.5 %collective-permute-start.5 = (bf16[128,2048]{1,0:T(8,128)(2,1)S(1)}, bf16[128,2048]{1,0:T(8,128)(2,1)S(1)}, u32[]{:S(2)}, u32[]{:S(2)}) collective-permute-start(bf16[128,2048]{1,0:T(8,128)(2,1)S(1)} %multiply_convert_fusion), channel_id=1, source_target_pairs={{0,4},{1,5},{2,6},{3,7},{4,8},{5,9},{6,10},{7,11},{8,12},{9,13},{1... | collective-permute-start | bytes 1572872 | tf_op jit(solution)/shard_map/ppermute | solution.py:86
  128.8 29.1 %collective-permute-start.16 = (f32[128,16]{0,1:T(8,128)S(1)}, f32[128,16]{0,1:T(8,128)S(1)}, u32[]{:S(2)}, u32[]{:S(2)}) collective-permute-start(f32[128,16]{0,1:T(8,128)S(1)} %collective-permute-done.15), channel_id=1, source_target_pairs={{0,2},{1,3},{2,0},{3,1},{4,6},{5,7},{6,4},{7,5},{8,10},{9,11},{10,... | collective-permute-start | bytes 24584 | tf_op jit(solution)/shard_map/ppermute | solution.py:86
  130.4 50.6 %collective-permute-start.3 = (bf16[128,2048]{1,0:T(8,128)(2,1)S(1)}, bf16[128,2048]{1,0:T(8,128)(2,1)}, u32[]{:S(2)}, u32[]{:S(2)}) collective-permute-start(bf16[128,2048]{1,0:T(8,128)(2,1)S(1)} %multiply_convert_fusion), channel_id=1, source_target_pairs={{0,2},{1,3},{2,0},{3,1},{4,6},{5,7},{6,4},{7,5},{8,10},{9,11},{10,... | collective-permute-start | bytes 1572872 | tf_op jit(solution)/shard_map/ppermute | solution.py:86
  144.7 36.9 %collective-permute-start.10 = (bf16[128,2048]{1,0:T(8,128)(2,1)S(1)}, bf16[128,2048]{1,0:T(8,128)(2,1)}, u32[]{:S(2)}, u32[]{:S(2)}) collective-permute-start(bf16[128,2048]{1,0:T(8,128)(2,1)S(1)} %collective-permute-done.9), channel_id=1, source_target_pairs={{0,2},{1,3},{2,0},{3,1},{4,6},{5,7},{6,4},{7,5},{8,10},{9,11},{10,... | collective-permute-start | bytes 1572872 | tf_op jit(solution)/shard_map/ppermute | solution.py:86
  145.2 36.4 %collective-permute-start.14 = (bf16[128,2048]{1,0:T(8,128)(2,1)S(1)}, bf16[128,2048]{1,0:T(8,128)(2,1)}, u32[]{:S(2)}, u32[]{:S(2)}) collective-permute-start(bf16[128,2048]{1,0:T(8,128)(2,1)S(1)} %collective-permute-done.13), channel_id=1, source_target_pairs={{0,2},{1,3},{2,0},{3,1},{4,6},{5,7},{6,4},{7,5},{8,10},{9,11},{10,... | collective-permute-start | bytes 1572872 | tf_op jit(solution)/shard_map/ppermute | solution.py:86
  155.7 26.3 %collective-permute-start.6 = (bf16[128,2048]{1,0:T(8,128)(2,1)S(1)}, bf16[128,2048]{1,0:T(8,128)(2,1)}, u32[]{:S(2)}, u32[]{:S(2)}) collective-permute-start(bf16[128,2048]{1,0:T(8,128)(2,1)S(1)} %collective-permute-done.5), channel_id=1, source_target_pairs={{0,2},{1,3},{2,0},{3,1},{4,6},{5,7},{6,4},{7,5},{8,10},{9,11},{10,... | collective-permute-start | bytes 1572872 | tf_op jit(solution)/shard_map/ppermute | solution.py:86
  157.9 23.1 %collective-permute-start.8 = (f32[128,16]{0,1:T(8,128)S(1)}, f32[128,16]{0,1:T(8,128)S(1)}, u32[]{:S(2)}, u32[]{:S(2)}) collective-permute-start(f32[128,16]{0,1:T(8,128)S(1)} %collective-permute-done.7), channel_id=1, source_target_pairs={{0,2},{1,3},{2,0},{3,1},{4,6},{5,7},{6,4},{7,5},{8,10},{9,11},{10,... | collective-permute-start | bytes 24584 | tf_op jit(solution)/shard_map/ppermute | solution.py:86
  200.6 17.8 %collective-permute-start.20 = (bf16[128,2048]{1,0:T(8,128)(2,1)}, bf16[128,2048]{1,0:T(8,128)(2,1)}, u32[]{:S(2)}, u32[]{:S(2)}) collective-permute-start(bf16[128,2048]{1,0:T(8,128)(2,1)} %collective-permute-done.3), channel_id=1, source_target_pairs={{0,1},{1,0},{2,3},{3,2},{4,5},{5,4},{6,7},{7,6},{8,9},{9,8},{10,11... | collective-permute-start | bytes 1572872 | tf_op jit(solution)/shard_map/ppermute | solution.py:86
  200.7 24.4 %collective-permute-start.27 = (bf16[128,2048]{1,0:T(8,128)(2,1)}, bf16[128,2048]{1,0:T(8,128)(2,1)}, u32[]{:S(2)}, u32[]{:S(2)}) collective-permute-start(bf16[128,2048]{1,0:T(8,128)(2,1)} %collective-permute-done.14), channel_id=1, source_target_pairs={{0,1},{1,0},{2,3},{3,2},{4,5},{5,4},{6,7},{7,6},{8,9},{9,8},{10,11... | collective-permute-start | bytes 1572872 | tf_op jit(solution)/shard_map/ppermute | solution.py:86
  201.2 30.4 %collective-permute-start.35 = (bf16[128,2048]{1,0:T(8,128)(2,1)}, bf16[128,2048]{1,0:T(8,128)(2,1)}, u32[]{:S(2)}, u32[]{:S(2)}) collective-permute-start(bf16[128,2048]{1,0:T(8,128)(2,1)} %collective-permute-done.10), channel_id=1, source_target_pairs={{0,1},{1,0},{2,3},{3,2},{4,5},{5,4},{6,7},{7,6},{8,9},{9,8},{10,11... | collective-permute-start | bytes 1572872 | tf_op jit(solution)/shard_map/ppermute | solution.py:86
  201.2 37.3 %collective-permute-start.43 = (bf16[128,2048]{1,0:T(8,128)(2,1)}, bf16[128,2048]{1,0:T(8,128)(2,1)}, u32[]{:S(2)}, u32[]{:S(2)}) collective-permute-start(bf16[128,2048]{1,0:T(8,128)(2,1)} %collective-permute-done.6), channel_id=1, source_target_pairs={{0,1},{1,0},{2,3},{3,2},{4,5},{5,4},{6,7},{7,6},{8,9},{9,8},{10,11... | collective-permute-start | bytes 1572872 | tf_op jit(solution)/shard_map/ppermute | solution.py:86
  205.9 91.3 %collective-permute-start.19 = (bf16[128,2048]{1,0:T(8,128)(2,1)}, bf16[128,2048]{1,0:T(8,128)(2,1)}, u32[]{:S(2)}, u32[]{:S(2)}) collective-permute-start(bf16[128,2048]{1,0:T(8,128)(2,1)} %fusion.65), channel_id=1, source_target_pairs={{1,0},{0,1},{3,2},{2,3},{5,4},{4,5},{7,6},{6,7},{9,8},{8,9},{11,10... | collective-permute-start | bytes 1572872 | tf_op jit(solution)/shard_map/ppermute | solution.py:96
  218.4 45.9 %collective-permute-start.26 = (bf16[128,2048]{1,0:T(8,128)(2,1)}, bf16[128,2048]{1,0:T(8,128)(2,1)}, u32[]{:S(2)}, u32[]{:S(2)}) collective-permute-start(bf16[128,2048]{1,0:T(8,128)(2,1)} %fusion.50), channel_id=1, source_target_pairs={{1,0},{0,1},{3,2},{2,3},{5,4},{4,5},{7,6},{6,7},{9,8},{8,9},{11,10... | collective-permute-start | bytes 1572872 | tf_op jit(solution)/shard_map/ppermute | solution.py:96
  225.1 48.7 %collective-permute-start.34 = (bf16[128,2048]{1,0:T(8,128)(2,1)}, bf16[128,2048]{1,0:T(8,128)(2,1)}, u32[]{:S(2)}, u32[]{:S(2)}) collective-permute-start(bf16[128,2048]{1,0:T(8,128)(2,1)} %fusion.35), channel_id=1, source_target_pairs={{1,0},{0,1},{3,2},{2,3},{5,4},{4,5},{7,6},{6,7},{9,8},{8,9},{11,10... | collective-permute-start | bytes 1572872 | tf_op jit(solution)/shard_map/ppermute | solution.py:96
  258.6 21.5 %collective-permute-start.38 = (bf16[128,2048]{1,0:T(8,128)(2,1)}, bf16[128,2048]{1,0:T(8,128)(2,1)}, u32[]{:S(2)}, u32[]{:S(2)}) collective-permute-start(bf16[128,2048]{1,0:T(8,128)(2,1)} %fusion.32), channel_id=1, source_target_pairs={{2,0},{3,1},{0,2},{1,3},{6,4},{7,5},{4,6},{5,7},{10,8},{11,9},{8,1... | collective-permute-start | bytes 1572872 | tf_op jit(solution)/shard_map/ppermute | solution.py:96
  264.3 20.3 %collective-permute-start.42 = (bf16[128,2048]{1,0:T(8,128)(2,1)}, bf16[128,2048]{1,0:T(8,128)(2,1)}, u32[]{:S(2)}, u32[]{:S(2)}) collective-permute-start(bf16[128,2048]{1,0:T(8,128)(2,1)} %fusion.20), channel_id=1, source_target_pairs={{1,0},{0,1},{3,2},{2,3},{5,4},{4,5},{7,6},{6,7},{9,8},{8,9},{11,10... | collective-permute-start | bytes 1572872 | tf_op jit(solution)/shard_map/ppermute | solution.py:96
  268.9 22.5 %collective-permute-start.46 = (bf16[128,2048]{1,0:T(8,128)(2,1)}, bf16[128,2048]{1,0:T(8,128)(2,1)}, u32[]{:S(2)}, u32[]{:S(2)}) collective-permute-start(bf16[128,2048]{1,0:T(8,128)(2,1)} %fusion.17), channel_id=1, source_target_pairs={{2,0},{3,1},{0,2},{1,3},{6,4},{7,5},{4,6},{5,7},{10,8},{11,9},{8,1... | collective-permute-start | bytes 1572872 | tf_op jit(solution)/shard_map/ppermute | solution.py:96
  273.9 28.3 %collective-permute-start.23 = (bf16[128,2048]{1,0:T(8,128)(2,1)}, bf16[128,2048]{1,0:T(8,128)(2,1)}, u32[]{:S(2)}, u32[]{:S(2)}) collective-permute-start(bf16[128,2048]{1,0:T(8,128)(2,1)} %fusion.62), channel_id=1, source_target_pairs={{2,0},{3,1},{0,2},{1,3},{6,4},{7,5},{4,6},{5,7},{10,8},{11,9},{8,1... | collective-permute-start | bytes 1572872 | tf_op jit(solution)/shard_map/ppermute | solution.py:96
  280.1 22.0 %collective-permute-start.31 = (bf16[128,2048]{1,0:T(8,128)(2,1)}, bf16[128,2048]{1,0:T(8,128)(2,1)}, u32[]{:S(2)}, u32[]{:S(2)}) collective-permute-start(bf16[128,2048]{1,0:T(8,128)(2,1)} %fusion.55), channel_id=1, source_target_pairs={{12,0},{13,1},{14,2},{15,3},{0,4},{1,5},{2,6},{3,7},{4,8},{5,9},{6... | collective-permute-start | bytes 1572872 | tf_op jit(solution)/shard_map/ppermute | solution.py:96
  284.6 40.4 %collective-permute-start.39 = (bf16[128,2048]{1,0:T(8,128)(2,1)}, bf16[128,2048]{1,0:T(8,128)(2,1)}, u32[]{:S(2)}, u32[]{:S(2)}) collective-permute-start(bf16[128,2048]{1,0:T(8,128)(2,1)} %fusion.40), channel_id=1, source_target_pairs={{8,0},{9,1},{10,2},{11,3},{12,4},{13,5},{14,6},{15,7},{0,8},{1,9},... | collective-permute-start | bytes 1572872 | tf_op jit(solution)/shard_map/ppermute | solution.py:96
  295.7 29.2 %collective-permute-start.47 = (bf16[128,2048]{1,0:T(8,128)(2,1)}, bf16[128,2048]{1,0:T(8,128)(2,1)}, u32[]{:S(2)}, u32[]{:S(2)}) collective-permute-start(bf16[128,2048]{1,0:T(8,128)(2,1)} %fusion.25), channel_id=1, source_target_pairs={{4,0},{5,1},{6,2},{7,3},{8,4},{9,5},{10,6},{11,7},{12,8},{13,9},{1... | collective-permute-start | bytes 1572872 | tf_op jit(solution)/shard_map/ppermute | solution.py:96
  (33 other events, 421.8 us)
Sparse Core Ops, SparseCore 0:
  38.6 31.0 all-gather.4

commit v5 on v4

--- a/solution.py
+++ b/solution.py
@@ -89,7 +89,17 @@
             full = list(tied[0])
             grown = [(block, parent, pairs) for block, (_, parent, pairs) in zip(tied[1], grown)]
         pieces = pieces + grown
-    partial = [expert(*block) for block, _, _ in pieces]
+    partial = [None] * len(pieces)
+    counts = [1]
+    for pairs_list in plan:
+        counts.append(counts[-1] * (len(pairs_list) + 1))
+    for low, high in zip([0] + counts[1:-1], counts[1:]):
+        rows = jnp.concatenate([pieces[i][0][0] for i in range(low, high)], axis=0)
+        table = jnp.concatenate([pieces[i][0][1] for i in range(low, high)], axis=0)
+        out = expert(rows, table)
+        size = pieces[0][0][0].shape[0]
+        for offset, i in enumerate(range(low, high)):
+            partial[i] = out[offset * size:(offset + 1) * size]
     for index in reversed(range(1, len(pieces))):
         _, parent, pairs = pieces[index]
         back = [(target, source) for source, target in pairs]

time: 341 us -> 331 us (0.971)
  matrix products: 104 us -> 41.2 us
  waiting for transfers between devices: 146 us -> 180 us
  other arithmetic: 13.7 us -> 23.3 us
  local copies, waits for them, and re-layouts: 14.3 us -> 22 us
    dot_general x16 -> x3, matrix products: 68.4 us -> 23.9 us  [expert(): out_rows = jnp.dot(act, full[2], preferred_element_type=jnp.float32)]
    ppermute x15, waiting for transfers between devices: 43.8 us -> 67.8 us  [dense_moe(): sent = lax.ppermute(partial[index].astype(jnp.bfloat16), 'ep', back)]
    dot_general x16 -> x2, matrix products: 26.5 us -> 5.9 us  [expert(): gate_val = jnp.dot(rows, full[0], preferred_element_type=jnp.float32)]
    ppermute x30, waiting for transfers between devices: 43 us -> 53.9 us  [dense_moe(): grown.append((lax.ppermute(block, 'ep', pairs), parent, pairs))]
    convert_element_type x0 -> x2, other arithmetic: none -> 7.07 us  [dense_moe(): sent = lax.ppermute(partial[index].astype(jnp.bfloat16), 'ep', back)]
    all_gather x1, waiting for transfers between devices: 14.1 us -> 8.25 us  [combined_all(): lax.all_gather(a.astype(kind), axis)]
    dot_general x0 -> x1, matrix products: none -> 4.61 us  [expert(): up_val = jnp.dot(rows, full[1], preferred_element_type=jnp.float32)]
    ppermute x3, waiting for transfers between devices: 45.5 us -> 50.1 us  [full_weights(): other = lax.ppermute(mine, 'kv', [(0, 1), (1, 0)])]
  transfers between devices with their start and end apart: 49 -> 49, of which waited for: 12 -> 21; matrix products, arithmetic and copies ran while one was open for 37% -> 19% of each run, Pallas kernels for 0% -> 0%
where the time goes in v5:
time: 331 us; the launch traced here: 327 us
  waiting for transfers between devices  180 us (54%)
  matrix products  41.2 us (12%)
  starting transfers between devices  28.2 us (9%)
  other arithmetic  23.3 us (7%)
  local copies, waits for them, and re-layouts  22 us (7%)
  blocking collectives  18.1 us (5%)
  between operations  14.6 us (4%)
    ppermute x15, waiting for transfers between devices, dense_moe(): sent = lax.ppermute(partial[index].astype(jnp.bfloat16), 'ep', back)  67.8 us
    ppermute x30, waiting for transfers between devices, dense_moe(): grown.append((lax.ppermute(block, 'ep', pairs), parent, pairs))  53.9 us
    ppermute x3, waiting for transfers between devices, full_weights(): other = lax.ppermute(mine, 'kv', [(0, 1), (1, 0)])  50.1 us
    dot_general x3, matrix products, expert(): out_rows = jnp.dot(act, full[2], preferred_element_type=jnp.float32)  23.9 us
    ppermute x30, starting transfers between devices, dense_moe(): grown.append((lax.ppermute(block, 'ep', pairs), parent, pairs))  17.2 us
    unnamed x57, local copies, waits for them, and re-layouts  10.8 us
    all_gather x1, blocking collectives, shards(): every_query = lax.all_gather(queries[0], 'kv', axis=0, tiled=True)  9.4 us
    all_gather x2, blocking collectives, combined_all(): lax.all_gather(a.astype(kind), axis)  8.72 us
  transfers between devices with their start and end apart: 49, of which 21 were waited for; matrix products, arithmetic and copies ran while one was open for 19% of the time, Pallas kernels for 0%

profile of v5, /device:TPU:24, one launch (start us, length us, event | category | flops | bytes accessed | tf_op | source)
XLA Modules:
  0.0 327.5 jit_solution(5259213199645319318)
XLA Ops:
  11.5 9.4 %all-gather = bf16[1,256,1024]{1,2,0:T(8,128)(2,1)S(1)} all-gather(bf16[1,128,1024]{1,2,0:T(8,128)(2,1)S(1)} %copy.50), channel_id=2, replica_groups=mesh['kv'=2,'ep'=16] {'kv'}, dimensions={1}, use_global_device_ids=true | all-gather | bytes 786432 | tf_op jit(solution)/shard_map/all_gather | solution.py:177
  20.9 3.6 %copy.69 = bf16[128,8,8,128]{3,2,1,0:T(8,128)(2,1)} copy(bf16[128,8,8,128]{3,1,2,0:T(8,128)(2,1)} %bitcast.85) | data formatting | bytes 4194304
  24.6 4.0 %copy.67 = bf16[1,1024,1024]{1,2,0:T(8,128)(2,1)} copy(bf16[1,1024,1024]{2,1,0:T(8,128)(2,1)} %param.20) | data formatting | bytes 4194304 | tf_op jit(solution)/shard_map/reshape;squeeze | solution.py:181
  30.3 3.2 bitcast_reduce_fusion
  33.5 1.9 fusion.3
  38.1 4.5 %fusion.1 = f32[256,8]{0,1:T(8,128)S(1)} fusion(f32[8,1024,256]{2,1,0:T(8,128)} %copy-done, f32[256,8]{0,1:T(8,128)S(1)} %get-tuple-element.60, pred[1024]{0:T(1024)(128)(4,1)S(1)} %add_compare_fusion), kind=kLoop, calls=%fused_computation.5 | loop fusion | flops 8386560 | bytes 8406016 | tf_op jit(solution)/shard_map/reduce_sum | solution.py:197
  42.9 4.3 %all-gather.2 = bf16[512,8]{0,1:T(8,128)(2,1)S(1)} all-gather(bf16[256,8]{0,1:T(8,128)(2,1)S(1)} %add_convert_fusion), channel_id=4, replica_groups=mesh['kv'=2,'ep'=16] {'kv'}, dimensions={0}, use_global_device_ids=true | all-gather | bytes 12288 | tf_op jit(solution)/shard_map/all_gather | solution.py:18
  47.2 4.4 %all-gather.1 = bf16[512,8]{0,1:T(8,128)(2,1)S(1)} all-gather(bf16[256,8]{0,1:T(8,128)(2,1)S(1)} %get-tuple-element.59), channel_id=3, replica_groups=mesh['kv'=2,'ep'=16] {'kv'}, dimensions={0}, use_global_device_ids=true | all-gather | bytes 12288 | tf_op jit(solution)/shard_map/all_gather | solution.py:18
  60.4 8.2 %all-gather.5.cloned.1.call-done = bf16[2,256,1024]{2,1,0:T(8,128)(2,1)} async-done(((bf16[1,256,1024]{2,1,0:T(8,128)(2,1)}), bf16[2,256,1024]{2,1,0:T(8,128)(2,1)}) %all-gather.5.cloned.1.call-update) | async-done | bytes 1048592 | tf_op jit(solution)/shard_map/all_gather | solution.py:18
  70.0 14.2 %collective-permute-done.4 = bf16[2048,256]{1,0:T(8,128)(2,1)S(1)} collective-permute-done((bf16[2048,256]{1,0:T(8,128)(2,1)}, bf16[2048,256]{1,0:T(8,128)(2,1)S(1)}, u32[]{:S(2)}, u32[]{:S(2)}) %collective-permute-start.4) | collective-permute-done | bytes 1048608 | tf_op jit(solution)/shard_map/ppermute | solution.py:53
  88.5 18.3 %collective-permute-done.3 = bf16[2048,256]{1,0:T(8,128)(2,1)} collective-permute-done((bf16[2048,256]{1,0:T(8,128)(2,1)}, bf16[2048,256]{1,0:T(8,128)(2,1)}, u32[]{:S(2)}, u32[]{:S(2)}) %collective-permute-start.3) | collective-permute-done | bytes 1048608 | tf_op jit(solution)/shard_map/ppermute | solution.py:53
  110.6 17.5 %collective-permute-done.5 = bf16[256,2048]{1,0:T(8,128)(2,1)} collective-permute-done((bf16[256,2048]{1,0:T(8,128)(2,1)}, bf16[256,2048]{1,0:T(8,128)(2,1)}, u32[]{:S(2)}, u32[]{:S(2)}) %collective-permute-start.5) | collective-permute-done | bytes 1048608 | tf_op jit(solution)/shard_map/ppermute | solution.py:53
  132.0 20.2 %collective-permute-done.1 = bf16[128,2048]{1,0:T(8,128)(2,1)S(1)} collective-permute-done((bf16[128,2048]{1,0:T(8,128)(2,1)S(1)}, bf16[128,2048]{1,0:T(8,128)(2,1)S(1)}, u32[]{:S(2)}, u32[]{:S(2)}) %collective-permute-start.1) | collective-permute-done | bytes 524320 | tf_op jit(solution)/shard_map/ppermute | solution.py:86
  158.3 27.3 %collective-permute-done.16 = f32[128,16]{0,1:T(8,128)S(1)} collective-permute-done((f32[128,16]{0,1:T(8,128)S(1)}, f32[128,16]{0,1:T(8,128)S(1)}, u32[]{:S(2)}, u32[]{:S(2)}) %collective-permute-start.16) | collective-permute-done | bytes 8224 | tf_op jit(solution)/shard_map/ppermute | solution.py:86
  188.5 2.2 fusion.70
  195.9 2.0 copy-done.12
  197.9 3.6 %fusion.69 = f32[1024,512]{1,0:T(8,128)} fusion(bf16[1024,2048]{1,0:T(8,128)(2,1)S(1)} %constant_dynamic-update-slice_fusion, bf16[2048,512]{1,0:T(8,128)(2,1)S(1)} %get-tuple-element.46), kind=kOutput, calls=%fused_computation.140 | convolution fusion | flops 2147483648 | bytes 8388608 | tf_op jit(solution)/shard_map/dot_general | solution.py:74
  201.6 10.0 %multiply_convert_fusion = bf16[1024,2048]{1,0:T(8,128)(2,1)} fusion(f32[1024]{0:T(1024)S(1)} %select_reduce_fusion, bf16[512,2048]{1,0:T(8,128)(2,1)S(1)} %pad_maximum_fusion.3, f32[1024,512]{1,0:T(8,128)} %fusion.69, bf16[1024,2048]{1,0:T(8,128)(2,1)} %copy-done.12, bf16[2048,512]{1,0:T(8,128)(2,1)} %get-tuple-element.47), kind=kOutput, calls=%fused_computation.3 | convolution fusion | flops 4306501632 | bytes 14684160 | tf_op jit(solution)/shard_map/dot_general | solution.py:77
  211.6 4.3 %fusion.63 = (bf16[128,2048]{1,0:T(8,128)(2,1)}, bf16[128,2048]{1,0:T(8,128)(2,1)}, bf16[128,2048]{1,0:T(8,128)(2,1)}, bf16[128,2048]{1,0:T(8,128)(2,1)}, bf16[1...) fusion(bf16[1024,2048]{1,0:T(8,128)(2,1)} %multiply_convert_fusion), kind=kLoop, calls=%fused_computation.136 | loop fusion | bytes 8388608 | tf_op jit(solution)/shard_map/slice | solution.py:102
  216.9 6.9 %convert_multiply_fusion = f32[512,2048]{1,0:T(8,128)} fusion(bf16[512,2048]{1,0:T(8,128)(2,1)S(1)} %pad_maximum_fusion.3, f32[512]{0:T(512)S(1)} %get-tuple-element.57, f32[512,512]{1,0:T(8,128)} %fusion.70, bf16[512,2048]{1,0:T(8,128)(2,1)} %copy-done.11, bf16[2048,512]{1,0:T(8,128)(2,1)} %get-tuple-element.47), kind=kOutput, calls=%fused_computation.8 | convolution fusion | flops 2152202240 | bytes 11536384 | tf_op jit(solution)/shard_map/dot_general | solution.py:77
  223.8 4.6 %fusion.41 = f32[512,512]{1,0:T(8,128)} fusion(bf16[2048,512]{1,0:T(8,128)(2,1)} %get-tuple-element.47, bf16[128,2048]{1,0:T(8,128)(2,1)} %copy-done.16, bf16[128,2048]{1,0:T(8,128)(2,1)} %copy-done.15, bf16[128,2048]{1,0:T(8,128)(2,1)} %copy-done.14, bf16[128,2048]{1,0:T(8,128)(2,1)} %copy-done.7), kind=kOutput, calls=%fused_computation.81 | convolution fusion | flops 1082130432 | bytes 5242880 | tf_op jit(solution)/shard_map/dot_general | solution.py:75
  229.2 3.6 %fusion.24 = (bf16[128,2048]{1,0:T(8,128)(2,1)}, bf16[128,2048]{1,0:T(8,128)(2,1)}, bf16[128,2048]{1,0:T(8,128)(2,1)}, bf16[128,2048]{1,0:T(8,128)(2,1)}) fusion(f32[512,2048]{1,0:T(8,128)S(1)} %copy-done.2, bf16[128,2048]{1,0:T(8,128)(2,1)} %collective-permute-done.34, bf16[128,2048]{1,0:T(8,128)(2,1)} %collective-permute-done.45, ...), kind=kLoop, calls=%fused_computation.48 | loop fusion | flops 3145728 | bytes 8388608 | tf_op jit(solution)/shard_map/convert_element_type | solution.py:106
  237.2 7.0 %convert_multiply_fusion.1 = f32[512,2048]{1,0:T(8,128)} fusion(bf16[512,2048]{1,0:T(8,128)(2,1)S(1)} %pad_maximum_fusion.3, f32[512]{0:T(512)S(1)} %get-tuple-element.58, f32[512,512]{1,0:T(8,128)} %fusion.41, bf16[2048,512]{1,0:T(8,128)(2,1)} %copy-done.4, bf16[128,2048]{1,0:T(8,128)(2,1)} %copy-done.16, bf16[128,2048]{1,0:T(8,128)(2,1)} %copy-done.15, ...), kind=kOutput, calls=%fused_computation.9 | convolution fusion | flops 2160590848 | bytes 11536384 | tf_op jit(solution)/shard_map/dot_general | solution.py:77
  244.7 3.1 collective-permute-done.38
  247.8 11.2 %collective-permute-done.42 = bf16[128,2048]{1,0:T(8,128)(2,1)} collective-permute-done((bf16[128,2048]{1,0:T(8,128)(2,1)}, bf16[128,2048]{1,0:T(8,128)(2,1)}, u32[]{:S(2)}, u32[]{:S(2)}) %collective-permute-start.42) | collective-permute-done | bytes 524320 | tf_op jit(solution)/shard_map/ppermute | solution.py:106
  259.1 11.2 %collective-permute-done.46 = bf16[128,2048]{1,0:T(8,128)(2,1)} collective-permute-done((bf16[128,2048]{1,0:T(8,128)(2,1)}, bf16[128,2048]{1,0:T(8,128)(2,1)}, u32[]{:S(2)}, u32[]{:S(2)}) %collective-permute-start.46) | collective-permute-done | bytes 524320 | tf_op jit(solution)/shard_map/ppermute | solution.py:106
  270.3 3.5 %fusion.23 = (bf16[128,2048]{1,0:T(8,128)(2,1)S(1)}, bf16[128,2048]{1,0:T(8,128)(2,1)S(1)}, bf16[128,2048]{1,0:T(8,128)(2,1)S(1)}) fusion(f32[512,2048]{1,0:T(8,128)} %convert_multiply_fusion.1, bf16[128,2048]{1,0:T(8,128)(2,1)} %collective-permute-done.38, bf16[128,2048]{1,0:T(8,128)(2,1)} %copy-done.8, bf16[128,2048]{1,0:T(8,128)(2,1)} %collective-permute-done.46, ...), kind=kLoop, calls=%fused_computation.46 | loop fusion | flops 3932160 | bytes 7864320 | tf_op jit(solution)/shard_map/convert_element_type | solution.py:106
  273.9 1.9 collective-permute-start.47
  275.9 5.0 %collective-permute-done.35 = bf16[128,2048]{1,0:T(8,128)(2,1)S(1)} collective-permute-done((bf16[128,2048]{1,0:T(8,128)(2,1)}, bf16[128,2048]{1,0:T(8,128)(2,1)S(1)}, u32[]{:S(2)}, u32[]{:S(2)}) %collective-permute-start.35) | collective-permute-done | bytes 524320 | tf_op jit(solution)/shard_map/ppermute | solution.py:106
  280.8 7.3 %collective-permute-done.39 = bf16[128,2048]{1,0:T(8,128)(2,1)S(1)} collective-permute-done((bf16[128,2048]{1,0:T(8,128)(2,1)S(1)}, bf16[128,2048]{1,0:T(8,128)(2,1)S(1)}, u32[]{:S(2)}, u32[]{:S(2)}) %collective-permute-start.39) | collective-permute-done | bytes 524320 | tf_op jit(solution)/shard_map/ppermute | solution.py:106
  288.2 29.9 %collective-permute-done.43 = bf16[128,2048]{1,0:T(8,128)(2,1)S(1)} collective-permute-done((bf16[128,2048]{1,0:T(8,128)(2,1)S(1)}, bf16[128,2048]{1,0:T(8,128)(2,1)S(1)}, u32[]{:S(2)}, u32[]{:S(2)}) %collective-permute-start.43) | collective-permute-done | bytes 524320 | tf_op jit(solution)/shard_map/ppermute | solution.py:106
  318.0 2.6 fusion.35
  (175 shorter events, 51.6 us)
Async XLA Ops:
  6.5 62.1 %all-gather.5.cloned.1.call-start = ((), (), s32[]{:S(2)}) async-start(), calls=%async_computation | async-start | bytes 1572864 | tf_op jit(solution)/shard_map/all_gather | solution.py:18
  7.3 47.4 %collective-permute-start.9 = (f32[128,16]{0,1:T(8,128)S(1)}, f32[128,16]{0,1:T(8,128)S(1)}, u32[]{:S(2)}, u32[]{:S(2)}) collective-permute-start(f32[128,16]{0,1:T(8,128)S(1)} %select_reduce_fusion.1), channel_id=1, source_target_pairs={{0,4},{1,5},{2,6},{3,7},{4,8},{5,9},{6,10},{7,11},{8,12},{9,13},{1... | collective-permute-start | bytes 24584 | tf_op jit(solution)/shard_map/ppermute | solution.py:86
  7.4 49.0 %collective-permute-start.12 = (f32[128,16]{0,1:T(8,128)S(1)}, f32[128,16]{0,1:T(8,128)S(1)}, u32[]{:S(2)}, u32[]{:S(2)}) collective-permute-start(f32[128,16]{0,1:T(8,128)S(1)} %select_reduce_fusion.1), channel_id=1, source_target_pairs={{0,8},{1,9},{2,10},{3,11},{4,12},{5,13},{6,14},{7,15},{8,0},{9,1},... | collective-permute-start | bytes 24584 | tf_op jit(solution)/shard_map/ppermute | solution.py:86
  9.3 48.4 %collective-permute-start.15 = (f32[128,16]{0,1:T(8,128)S(1)}, f32[128,16]{0,1:T(8,128)S(1)}, u32[]{:S(2)}, u32[]{:S(2)}) collective-permute-start(f32[128,16]{0,1:T(8,128)S(1)} %select_reduce_fusion.1), channel_id=1, source_target_pairs={{0,12},{1,13},{2,14},{3,15},{4,0},{5,1},{6,2},{7,3},{8,4},{9,5},{1... | collective-permute-start | bytes 24584 | tf_op jit(solution)/shard_map/ppermute | solution.py:86
  9.7 46.6 %collective-permute-start.25 = (f32[128,16]{0,1:T(8,128)S(1)}, f32[128,16]{0,1:T(8,128)S(1)}, u32[]{:S(2)}, u32[]{:S(2)}) collective-permute-start(f32[128,16]{0,1:T(8,128)S(1)} %select_reduce_fusion.1), channel_id=1, source_target_pairs={{0,1},{1,0},{2,3},{3,2},{4,5},{5,4},{6,7},{7,6},{8,9},{9,8},{10,11... | collective-permute-start | bytes 24584 | tf_op jit(solution)/shard_map/ppermute | solution.py:86
  51.6 32.6 %collective-permute-start.4 = (bf16[2048,256]{1,0:T(8,128)(2,1)}, bf16[2048,256]{1,0:T(8,128)(2,1)S(1)}, u32[]{:S(2)}, u32[]{:S(2)}) collective-permute-start(bf16[2048,256]{1,0:T(8,128)(2,1)} %bitcast.12), channel_id=1, source_target_pairs={{0,16},{16,0},{1,17},{17,1},{2,18},{18,2},{3,19},{19,3},{4,20},{20... | collective-permute-start | bytes 3145736 | tf_op jit(solution)/shard_map/ppermute | solution.py:53
  54.7 54.2 %collective-permute-start.7 = (f32[128,16]{0,1:T(8,128)S(1)}, f32[128,16]{0,1:T(8,128)S(1)}, u32[]{:S(2)}, u32[]{:S(2)}) collective-permute-start(f32[128,16]{0,1:T(8,128)S(1)} %select_reduce_fusion.1), channel_id=1, source_target_pairs={{0,2},{1,3},{2,0},{3,1},{4,6},{5,7},{6,4},{7,5},{8,10},{9,11},{10,... | collective-permute-start | bytes 24584 | tf_op jit(solution)/shard_map/ppermute | solution.py:86
  56.3 50.5 %collective-permute-start.3 = (bf16[2048,256]{1,0:T(8,128)(2,1)}, bf16[2048,256]{1,0:T(8,128)(2,1)}, u32[]{:S(2)}, u32[]{:S(2)}) collective-permute-start(bf16[2048,256]{1,0:T(8,128)(2,1)} %bitcast.11), channel_id=1, source_target_pairs={{0,16},{16,0},{1,17},{17,1},{2,18},{18,2},{3,19},{19,3},{4,20},{20... | collective-permute-start | bytes 3145736 | tf_op jit(solution)/shard_map/ppermute | solution.py:53
  57.7 70.4 %collective-permute-start.5 = (bf16[256,2048]{1,0:T(8,128)(2,1)}, bf16[256,2048]{1,0:T(8,128)(2,1)}, u32[]{:S(2)}, u32[]{:S(2)}) collective-permute-start(bf16[256,2048]{1,0:T(8,128)(2,1)} %bitcast.13), channel_id=1, source_target_pairs={{0,16},{16,0},{1,17},{17,1},{2,18},{18,2},{3,19},{19,3},{4,20},{20... | collective-permute-start | bytes 3145736 | tf_op jit(solution)/shard_map/ppermute | solution.py:53
  59.8 70.5 %collective-permute-start.10 = (f32[128,16]{0,1:T(8,128)S(1)}, f32[128,16]{0,1:T(8,128)S(1)}, u32[]{:S(2)}, u32[]{:S(2)}) collective-permute-start(f32[128,16]{0,1:T(8,128)S(1)} %collective-permute-done.9), channel_id=1, source_target_pairs={{0,2},{1,3},{2,0},{3,1},{4,6},{5,7},{6,4},{7,5},{8,10},{9,11},{10,... | collective-permute-start | bytes 24584 | tf_op jit(solution)/shard_map/ppermute | solution.py:86
  84.2 46.2 %collective-permute-start.13 = (f32[128,16]{0,1:T(8,128)S(1)}, f32[128,16]{0,1:T(8,128)S(1)}, u32[]{:S(2)}, u32[]{:S(2)}) collective-permute-start(f32[128,16]{0,1:T(8,128)S(1)} %collective-permute-done.12), channel_id=1, source_target_pairs={{0,2},{1,3},{2,0},{3,1},{4,6},{5,7},{6,4},{7,5},{8,10},{9,11},{10,... | collective-permute-start | bytes 24584 | tf_op jit(solution)/shard_map/ppermute | solution.py:86
  106.8 47.4 %collective-permute-start = (bf16[128,2048]{1,0:T(8,128)(2,1)S(1)}, bf16[128,2048]{1,0:T(8,128)(2,1)S(1)}, u32[]{:S(2)}, u32[]{:S(2)}) collective-permute-start(bf16[128,2048]{1,0:T(8,128)(2,1)S(1)} %multiply_convert_fusion.5), channel_id=1, source_target_pairs={{0,4},{1,5},{2,6},{3,7},{4,8},{5,9},{6,10},{7,11},{8,12},{9,13},{1... | collective-permute-start | bytes 1572872 | tf_op jit(solution)/shard_map/ppermute | solution.py:86
  109.0 43.2 %collective-permute-start.1 = (bf16[128,2048]{1,0:T(8,128)(2,1)S(1)}, bf16[128,2048]{1,0:T(8,128)(2,1)S(1)}, u32[]{:S(2)}, u32[]{:S(2)}) collective-permute-start(bf16[128,2048]{1,0:T(8,128)(2,1)S(1)} %multiply_convert_fusion.5), channel_id=1, source_target_pairs={{0,8},{1,9},{2,10},{3,11},{4,12},{5,13},{6,14},{7,15},{8,0},{9,1},... | collective-permute-start | bytes 1572872 | tf_op jit(solution)/shard_map/ppermute | solution.py:86
  128.1 25.6 %collective-permute-start.2 = (bf16[128,2048]{1,0:T(8,128)(2,1)S(1)}, bf16[128,2048]{1,0:T(8,128)(2,1)S(1)}, u32[]{:S(2)}, u32[]{:S(2)}) collective-permute-start(bf16[128,2048]{1,0:T(8,128)(2,1)S(1)} %multiply_convert_fusion.5), channel_id=1, source_target_pairs={{0,12},{1,13},{2,14},{3,15},{4,0},{5,1},{6,2},{7,3},{8,4},{9,5},{1... | collective-permute-start | bytes 1572872 | tf_op jit(solution)/shard_map/ppermute | solution.py:86
  130.4 27.2 %collective-permute-start.17 = (bf16[128,2048]{1,0:T(8,128)(2,1)S(1)}, bf16[128,2048]{1,0:T(8,128)(2,1)S(1)}, u32[]{:S(2)}, u32[]{:S(2)}) collective-permute-start(bf16[128,2048]{1,0:T(8,128)(2,1)S(1)} %multiply_convert_fusion.5), channel_id=1, source_target_pairs={{0,1},{1,0},{2,3},{3,2},{4,5},{5,4},{6,7},{7,6},{8,9},{9,8},{10,11... | collective-permute-start | bytes 1572872 | tf_op jit(solution)/shard_map/ppermute | solution.py:86
  130.5 55.1 %collective-permute-start.6 = (bf16[128,2048]{1,0:T(8,128)(2,1)S(1)}, bf16[128,2048]{1,0:T(8,128)(2,1)S(1)}, u32[]{:S(2)}, u32[]{:S(2)}) collective-permute-start(bf16[128,2048]{1,0:T(8,128)(2,1)S(1)} %multiply_convert_fusion.5), channel_id=1, source_target_pairs={{0,2},{1,3},{2,0},{3,1},{4,6},{5,7},{6,4},{7,5},{8,10},{9,11},{10,... | collective-permute-start | bytes 1572872 | tf_op jit(solution)/shard_map/ppermute | solution.py:86
  152.2 33.9 %collective-permute-start.11 = (bf16[128,2048]{1,0:T(8,128)(2,1)S(1)}, bf16[128,2048]{1,0:T(8,128)(2,1)S(1)}, u32[]{:S(2)}, u32[]{:S(2)}) collective-permute-start(bf16[128,2048]{1,0:T(8,128)(2,1)S(1)} %collective-permute-done.1), channel_id=1, source_target_pairs={{0,2},{1,3},{2,0},{3,1},{4,6},{5,7},{6,4},{7,5},{8,10},{9,11},{10,... | collective-permute-start | bytes 1572872 | tf_op jit(solution)/shard_map/ppermute | solution.py:86
  153.7 32.5 %collective-permute-start.14 = (bf16[128,2048]{1,0:T(8,128)(2,1)S(1)}, bf16[128,2048]{1,0:T(8,128)(2,1)S(1)}, u32[]{:S(2)}, u32[]{:S(2)}) collective-permute-start(bf16[128,2048]{1,0:T(8,128)(2,1)S(1)} %collective-permute-done.2), channel_id=1, source_target_pairs={{0,2},{1,3},{2,0},{3,1},{4,6},{5,7},{6,4},{7,5},{8,10},{9,11},{10,... | collective-permute-start | bytes 1572872 | tf_op jit(solution)/shard_map/ppermute | solution.py:86
  154.2 32.0 %collective-permute-start.8 = (bf16[128,2048]{1,0:T(8,128)(2,1)S(1)}, bf16[128,2048]{1,0:T(8,128)(2,1)S(1)}, u32[]{:S(2)}, u32[]{:S(2)}) collective-permute-start(bf16[128,2048]{1,0:T(8,128)(2,1)S(1)} %collective-permute-done), channel_id=1, source_target_pairs={{0,2},{1,3},{2,0},{3,1},{4,6},{5,7},{6,4},{7,5},{8,10},{9,11},{10,... | collective-permute-start | bytes 1572872 | tf_op jit(solution)/shard_map/ppermute | solution.py:86
  157.6 28.0 %collective-permute-start.16 = (f32[128,16]{0,1:T(8,128)S(1)}, f32[128,16]{0,1:T(8,128)S(1)}, u32[]{:S(2)}, u32[]{:S(2)}) collective-permute-start(f32[128,16]{0,1:T(8,128)S(1)} %collective-permute-done.15), channel_id=1, source_target_pairs={{0,2},{1,3},{2,0},{3,1},{4,6},{5,7},{6,4},{7,5},{8,10},{9,11},{10,... | collective-permute-start | bytes 24584 | tf_op jit(solution)/shard_map/ppermute | solution.py:86
  216.1 12.9 %collective-permute-start.37 = (bf16[128,2048]{1,0:T(8,128)(2,1)}, bf16[128,2048]{1,0:T(8,128)(2,1)}, u32[]{:S(2)}, u32[]{:S(2)}) collective-permute-start(bf16[128,2048]{1,0:T(8,128)(2,1)} %get-tuple-element.66), channel_id=1, source_target_pairs={{1,0},{0,1},{3,2},{2,3},{5,4},{4,5},{7,6},{6,7},{9,8},{8,9},{11,10... | collective-permute-start | bytes 1572872 | tf_op jit(solution)/shard_map/ppermute | solution.py:106
  216.4 12.8 %collective-permute-start.41 = (bf16[128,2048]{1,0:T(8,128)(2,1)}, bf16[128,2048]{1,0:T(8,128)(2,1)}, u32[]{:S(2)}, u32[]{:S(2)}) collective-permute-start(bf16[128,2048]{1,0:T(8,128)(2,1)} %get-tuple-element.64), channel_id=1, source_target_pairs={{1,0},{0,1},{3,2},{2,3},{5,4},{4,5},{7,6},{6,7},{9,8},{8,9},{11,10... | collective-permute-start | bytes 1572872 | tf_op jit(solution)/shard_map/ppermute | solution.py:106
  228.7 15.5 %collective-permute-start.40 = (bf16[128,2048]{1,0:T(8,128)(2,1)}, bf16[128,2048]{1,0:T(8,128)(2,1)}, u32[]{:S(2)}, u32[]{:S(2)}) collective-permute-start(bf16[128,2048]{1,0:T(8,128)(2,1)} %get-tuple-element.65), channel_id=1, source_target_pairs={{1,0},{0,1},{3,2},{2,3},{5,4},{4,5},{7,6},{6,7},{9,8},{8,9},{11,10... | collective-permute-start | bytes 1572872 | tf_op jit(solution)/shard_map/ppermute | solution.py:106
  229.0 15.2 %collective-permute-start.44 = (bf16[128,2048]{1,0:T(8,128)(2,1)}, bf16[128,2048]{1,0:T(8,128)(2,1)}, u32[]{:S(2)}, u32[]{:S(2)}) collective-permute-start(bf16[128,2048]{1,0:T(8,128)(2,1)} %get-tuple-element.63), channel_id=1, source_target_pairs={{1,0},{0,1},{3,2},{2,3},{5,4},{4,5},{7,6},{6,7},{9,8},{8,9},{11,10... | collective-permute-start | bytes 1572872 | tf_op jit(solution)/shard_map/ppermute | solution.py:106
  232.8 15.1 %collective-permute-start.38 = (bf16[128,2048]{1,0:T(8,128)(2,1)}, bf16[128,2048]{1,0:T(8,128)(2,1)}, u32[]{:S(2)}, u32[]{:S(2)}) collective-permute-start(bf16[128,2048]{1,0:T(8,128)(2,1)} %get-tuple-element.72), channel_id=1, source_target_pairs={{2,0},{3,1},{0,2},{1,3},{6,4},{7,5},{4,6},{5,7},{10,8},{11,9},{8,1... | collective-permute-start | bytes 1572872 | tf_op jit(solution)/shard_map/ppermute | solution.py:106
  234.4 24.7 %collective-permute-start.42 = (bf16[128,2048]{1,0:T(8,128)(2,1)}, bf16[128,2048]{1,0:T(8,128)(2,1)}, u32[]{:S(2)}, u32[]{:S(2)}) collective-permute-start(bf16[128,2048]{1,0:T(8,128)(2,1)} %get-tuple-element.71), channel_id=1, source_target_pairs={{2,0},{3,1},{0,2},{1,3},{6,4},{7,5},{4,6},{5,7},{10,8},{11,9},{8,1... | collective-permute-start | bytes 1572872 | tf_op jit(solution)/shard_map/ppermute | solution.py:106
  235.6 34.7 %collective-permute-start.46 = (bf16[128,2048]{1,0:T(8,128)(2,1)}, bf16[128,2048]{1,0:T(8,128)(2,1)}, u32[]{:S(2)}, u32[]{:S(2)}) collective-permute-start(bf16[128,2048]{1,0:T(8,128)(2,1)} %get-tuple-element.70), channel_id=1, source_target_pairs={{2,0},{3,1},{0,2},{1,3},{6,4},{7,5},{4,6},{5,7},{10,8},{11,9},{8,1... | collective-permute-start | bytes 1572872 | tf_op jit(solution)/shard_map/ppermute | solution.py:106
  244.2 31.7 %collective-permute-start.33 = (bf16[128,2048]{1,0:T(8,128)(2,1)}, bf16[128,2048]{1,0:T(8,128)(2,1)S(1)}, u32[]{:S(2)}, u32[]{:S(2)}) collective-permute-start(bf16[128,2048]{1,0:T(8,128)(2,1)} %get-tuple-element.61), channel_id=1, source_target_pairs={{1,0},{0,1},{3,2},{2,3},{5,4},{4,5},{7,6},{6,7},{9,8},{8,9},{11,10... | collective-permute-start | bytes 1572872 | tf_op jit(solution)/shard_map/ppermute | solution.py:106
  244.2 36.6 %collective-permute-start.35 = (bf16[128,2048]{1,0:T(8,128)(2,1)}, bf16[128,2048]{1,0:T(8,128)(2,1)S(1)}, u32[]{:S(2)}, u32[]{:S(2)}) collective-permute-start(bf16[128,2048]{1,0:T(8,128)(2,1)} %get-tuple-element.69), channel_id=1, source_target_pairs={{2,0},{3,1},{0,2},{1,3},{6,4},{7,5},{4,6},{5,7},{10,8},{11,9},{8,1... | collective-permute-start | bytes 1572872 | tf_op jit(solution)/shard_map/ppermute | solution.py:106
  273.8 14.4 %collective-permute-start.39 = (bf16[128,2048]{1,0:T(8,128)(2,1)S(1)}, bf16[128,2048]{1,0:T(8,128)(2,1)S(1)}, u32[]{:S(2)}, u32[]{:S(2)}) collective-permute-start(bf16[128,2048]{1,0:T(8,128)(2,1)S(1)} %get-tuple-element.73), channel_id=1, source_target_pairs={{12,0},{13,1},{14,2},{15,3},{0,4},{1,5},{2,6},{3,7},{4,8},{5,9},{6... | collective-permute-start | bytes 1572872 | tf_op jit(solution)/shard_map/ppermute | solution.py:106
  273.9 44.2 %collective-permute-start.43 = (bf16[128,2048]{1,0:T(8,128)(2,1)S(1)}, bf16[128,2048]{1,0:T(8,128)(2,1)S(1)}, u32[]{:S(2)}, u32[]{:S(2)}) collective-permute-start(bf16[128,2048]{1,0:T(8,128)(2,1)S(1)} %get-tuple-element.75), channel_id=1, source_target_pairs={{8,0},{9,1},{10,2},{11,3},{12,4},{13,5},{14,6},{15,7},{0,8},{1,9},... | collective-permute-start | bytes 1572872 | tf_op jit(solution)/shard_map/ppermute | solution.py:106
  273.9 44.1 %collective-permute-start.47 = (bf16[128,2048]{1,0:T(8,128)(2,1)S(1)}, bf16[128,2048]{1,0:T(8,128)(2,1)S(1)}, u32[]{:S(2)}, u32[]{:S(2)}) collective-permute-start(bf16[128,2048]{1,0:T(8,128)(2,1)S(1)} %get-tuple-element.74), channel_id=1, source_target_pairs={{4,0},{5,1},{6,2},{7,3},{8,4},{9,5},{10,6},{11,7},{12,8},{13,9},{1... | collective-permute-start | bytes 1572872 | tf_op jit(solution)/shard_map/ppermute | solution.py:106
  (35 other events, 366.8 us)
Sparse Core Ops, SparseCore 0:
  38.3 30.2 all-gather.4

commit v6 on v5

--- a/solution.py
+++ b/solution.py
@@ -49,11 +49,15 @@
             lax.all_gather(up_w[0], "kv", axis=1, tiled=True),
             lax.all_gather(down_w[0], "kv", axis=0, tiled=True),
         )
-    mine = (gate_w[0], up_w[0], down_w[0])
-    other = lax.ppermute(mine, "kv", [(0, 1), (1, 0)])
+    hidden = gate_w.shape[2]
+    packed = jnp.stack([gate_w[0], up_w[0], down_w[0].reshape(-1, hidden)])
+    other = lax.ppermute(packed, "kv", [(0, 1), (1, 0)])
     first = lax.axis_index("kv") == 0
     joined = []
-    for own, far, axis in zip(mine, other, (1, 1, 0)):
+    for slot, axis in zip(range(3), (1, 1, 0)):
+        own, far = packed[slot], other[slot]
+        if axis == 0:
+            own, far = own.reshape(hidden, -1), far.reshape(hidden, -1)
         low = jnp.where(first, own, far)
         high = jnp.where(first, far, own)
         joined.append(jnp.concatenate([low, high], axis=axis))
@@ -79,25 +83,30 @@
         return out_rows * weights[:, None]
 
     pieces = [((normed, weight_table), None, None)]
-    for number, pairs_list in enumerate(plan):
+    groups = []
+    low = 0
+    tie_at = next((n + 1 for n, (_, ends) in enumerate(plan) if ends), 0)
+    for number, (pairs_list, ends) in enumerate(plan):
         grown = []
         for parent, (block, _, _) in enumerate(pieces):
             for pairs in pairs_list:
                 grown.append((lax.ppermute(block, "ep", pairs), parent, pairs))
-        if number == 1:
+        if number == tie_at:
             tied = lax.optimization_barrier((tuple(full), [piece[0] for piece in grown]))
             full = list(tied[0])
             grown = [(block, parent, pairs) for block, (_, parent, pairs) in zip(tied[1], grown)]
         pieces = pieces + grown
+        if ends:
+            groups.append((low, len(pieces)))
+            low = len(pieces)
+    if low < len(pieces) or not groups:
+        groups.append((low, len(pieces)))
     partial = [None] * len(pieces)
-    counts = [1]
-    for pairs_list in plan:
-        counts.append(counts[-1] * (len(pairs_list) + 1))
-    for low, high in zip([0] + counts[1:-1], counts[1:]):
+    size = normed.shape[0]
+    for low, high in groups:
         rows = jnp.concatenate([pieces[i][0][0] for i in range(low, high)], axis=0)
         table = jnp.concatenate([pieces[i][0][1] for i in range(low, high)], axis=0)
         out = expert(rows, table)
-        size = pieces[0][0][0].shape[0]
         for offset, i in enumerate(range(low, high)):
             partial[i] = out[offset * size:(offset + 1) * size]
     for index in reversed(range(1, len(pieces))):
@@ -135,15 +144,27 @@
     plan = []
     for a in order:
         size = len(values[a])
-        stage = []
-        for shift in range(1, size):
-            pairs = []
-            for r, p in enumerate(places):
-                moved = list(p)
-                moved[a] = values[a][(values[a].index(p[a]) + shift) % size]
-                pairs.append((r, rank_of[tuple(moved)]))
-            stage.append(pairs)
-        plan.append(stage)
+        if size & (size - 1) == 0:
+            steps = []
+            span = size // 2
+            while span:
+                steps.append(("xor", span))
+                span //= 2
+        else:
+            steps = [("shift", shift) for shift in range(1, size)]
+            steps = [steps]
+        for number, step in enumerate(steps):
+            group = step if isinstance(step, list) else [step]
+            stage = []
+            for kind, amount in group:
+                pairs = []
+                for r, p in enumerate(places):
+                    index = values[a].index(p[a])
+                    moved = list(p)
+                    moved[a] = values[a][index ^ amount if kind == "xor" else (index + amount) % size]
+                    pairs.append((r, rank_of[tuple(moved)]))
+                stage.append(pairs)
+            plan.append((stage, number == len(steps) - 1))
     return plan
 
 

time: 331 us -> 290 us (0.88)
  waiting for transfers between devices: 180 us -> 126 us
  local copies, waits for them, and re-layouts: 22 us -> 29.8 us
    ppermute x3 -> x1, waiting for transfers between devices: 50.1 us -> 6.19 us  [full_weights(): other = lax.ppermute(packed, 'kv', [(0, 1), (1, 0)])]
    ppermute x15, waiting for transfers between devices: 67.8 us -> 52.1 us  [dense_moe(): sent = lax.ppermute(partial[index].astype(jnp.bfloat16), 'ep', back)]
    ppermute x30, waiting for transfers between devices: 53.9 us -> 63.7 us  [dense_moe(): grown.append((lax.ppermute(block, 'ep', pairs), parent, pairs))]
    unnamed x57 -> x69, local copies, waits for them, and re-layouts: 10.8 us -> 15.1 us
    all_gather x1, waiting for transfers between devices: 8.25 us -> 4.28 us  [combined_all(): lax.all_gather(a.astype(kind), axis)]
    convert_element_type x2 -> x3, other arithmetic: 7.07 us -> 6.22 us  [dense_moe(): sent = lax.ppermute(partial[index].astype(jnp.bfloat16), 'ep', back)]
  transfers between devices with their start and end apart: 49 -> 47, of which waited for: 21 -> 17; matrix products, arithmetic and copies ran while one was open for 19% -> 20% of each run, Pallas kernels for 0% -> 0%
where the time goes in v6:
time: 290 us; the launch traced here: 287 us
  waiting for transfers between devices  126 us (43%)
  matrix products  44.2 us (15%)
  local copies, waits for them, and re-layouts  29.8 us (10%)
  starting transfers between devices  29.3 us (10%)
  other arithmetic  24.4 us (8%)
  blocking collectives  17.8 us (6%)
  between operations  14.7 us (5%)
    ppermute x30, waiting for transfers between devices, dense_moe(): grown.append((lax.ppermute(block, 'ep', pairs), parent, pairs))  63.7 us
    ppermute x15, waiting for transfers between devices, dense_moe(): sent = lax.ppermute(partial[index].astype(jnp.bfloat16), 'ep', back)  52.1 us
    dot_general x3, matrix products, expert(): out_rows = jnp.dot(act, full[2], preferred_element_type=jnp.float32)  24.2 us
    ppermute x30, starting transfers between devices, dense_moe(): grown.append((lax.ppermute(block, 'ep', pairs), parent, pairs))  19.2 us
    unnamed x69, local copies, waits for them, and re-layouts  15.1 us
    all_gather x2, blocking collectives, combined_all(): lax.all_gather(a.astype(kind), axis)  9.04 us
    all_gather x1, blocking collectives, shards(): every_query = lax.all_gather(queries[0], 'kv', axis=0, tiled=True)  8.74 us
    ppermute x15, starting transfers between devices, dense_moe(): sent = lax.ppermute(partial[index].astype(jnp.bfloat16), 'ep', back)  8.61 us
  transfers between devices with their start and end apart: 47, of which 17 were waited for; matrix products, arithmetic and copies ran while one was open for 20% of the time, Pallas kernels for 0%

profile of v6, /device:TPU:24, one launch (start us, length us, event | category | flops | bytes accessed | tf_op | source)
XLA Modules:
  0.0 286.5 jit_solution(1884044811251811185)
XLA Ops:
  8.4 8.7 %all-gather = bf16[1,256,1024]{1,2,0:T(8,128)(2,1)S(1)} all-gather(bf16[1,128,1024]{1,2,0:T(8,128)(2,1)S(1)} %copy.50), channel_id=2, replica_groups=mesh['kv'=2,'ep'=16] {'kv'}, dimensions={1}, use_global_device_ids=true | all-gather | bytes 786432 | tf_op jit(solution)/shard_map/all_gather | solution.py:198
  17.1 3.6 %copy.69 = bf16[128,8,8,128]{3,2,1,0:T(8,128)(2,1)} copy(bf16[128,8,8,128]{3,1,2,0:T(8,128)(2,1)} %bitcast.87) | data formatting | bytes 4194304
  20.7 4.0 %copy.67 = bf16[1,1024,1024]{1,2,0:T(8,128)(2,1)} copy(bf16[1,1024,1024]{2,1,0:T(8,128)(2,1)} %param.20) | data formatting | bytes 4194304 | tf_op jit(solution)/shard_map/reshape;squeeze | solution.py:202
  26.6 3.2 %bitcast_reduce_fusion = (f32[256,8]{0,1:T(8,128)S(1)}, f32[8,1024,256]{2,1,0:T(8,128)S(1)}) fusion(pred[1024]{0:T(1024)(128)(4,1)S(1)} %add_compare_fusion, bf16[256,8,128]{0,2,1:T(8,128)(2,1)S(1)} %bitcast.85, bf16[1024,8,128]{2,1,0:T(8,128)(2,1)} %bitcast.89), kind=kOutput, calls=%fused_computation.1 | convolution fusion | flops 543160320 | bytes 11019264 | tf_op jit(solution)/shard_map/qhd,khd->qhk/dot_general | solution.py:206
  34.6 4.6 %fusion.1 = f32[256,8]{0,1:T(8,128)S(1)} fusion(f32[8,1024,256]{2,1,0:T(8,128)} %copy-done, f32[256,8]{0,1:T(8,128)S(1)} %get-tuple-element.60, pred[1024]{0:T(1024)(128)(4,1)S(1)} %add_compare_fusion), kind=kLoop, calls=%fused_computation.5 | loop fusion | flops 8386560 | bytes 8406016 | tf_op jit(solution)/shard_map/reduce_sum | solution.py:218
  39.4 4.5 %all-gather.2 = bf16[512,8]{0,1:T(8,128)(2,1)S(1)} all-gather(bf16[256,8]{0,1:T(8,128)(2,1)S(1)} %add_convert_fusion), channel_id=4, replica_groups=mesh['kv'=2,'ep'=16] {'kv'}, dimensions={0}, use_global_device_ids=true | all-gather | bytes 12288 | tf_op jit(solution)/shard_map/all_gather | solution.py:18
  43.8 4.6 %all-gather.1 = bf16[512,8]{0,1:T(8,128)(2,1)S(1)} all-gather(bf16[256,8]{0,1:T(8,128)(2,1)S(1)} %get-tuple-element.59), channel_id=3, replica_groups=mesh['kv'=2,'ep'=16] {'kv'}, dimensions={0}, use_global_device_ids=true | all-gather | bytes 12288 | tf_op jit(solution)/shard_map/all_gather | solution.py:18
  49.0 3.3 %pad_maximum_fusion = bf16[3,2048,256]{2,1,0:T(8,128)(2,1)} fusion(bf16[1,2048,256]{2,1,0:T(8,128)(2,1)S(1)} %stack_reshape_squeeze.3, bf16[1,2048,256]{2,1,0:T(8,128)(2,1)S(1)} %copy-done.4, bf16[1,2048,256]{2,1,0:T(8,128)(2,1)} %param.27), kind=kLoop, calls=%fused_computation.14 | loop fusion | flops 3145728 | bytes 6291456 | tf_op jit(solution)/shard_map/stack | solution.py:53
  56.6 4.3 %all-gather.5.cloned.1.call-done = bf16[2,256,1024]{2,1,0:T(8,128)(2,1)} async-done(((bf16[1,256,1024]{2,1,0:T(8,128)(2,1)}), bf16[2,256,1024]{2,1,0:T(8,128)(2,1)}) %all-gather.5.cloned.1.call-update) | async-done | bytes 1048592 | tf_op jit(solution)/shard_map/all_gather | solution.py:18
  62.4 3.6 %multiply_reduce_fusion = (f32[128]{0:T(128)S(1)}, f32[128,2048]{1,0:T(8,128)S(1)}) fusion(bf16[1024,2048]{1,0:T(8,128)(2,1)} %param.23, f32[16,8,8,128]{3,2,1,0:T(8,128)S(1)} %bitcast.86, f32[256,1024]{1,0:T(8,128)} %get-tuple-element.97, s32[]{:T(128)S(6)} %select_n.86, f32[256,1024]{1,0:T(8,128)} %get-tuple-element.98, ...), kind=kOutput, calls=%fused_computation.67 | convolution fusion | flops 539361152 | bytes 7864836 | tf_op jit(solution)/shard_map/dot_general | solution.py:256
  68.4 2.2 collective-permute-start.7
  72.0 20.8 %collective-permute-done.7 = f32[128,16]{0,1:T(8,128)S(1)} collective-permute-done((f32[128,16]{0,1:T(8,128)S(1)}, f32[128,16]{0,1:T(8,128)S(1)}, u32[]{:S(2)}, u32[]{:S(2)}) %collective-permute-start.7) | collective-permute-done | bytes 8224 | tf_op jit(solution)/shard_map/ppermute | solution.py:93
  94.1 2.4 collective-permute-done.13
  100.8 10.4 %collective-permute-done.2 = bf16[128,2048]{1,0:T(8,128)(2,1)} collective-permute-done((bf16[128,2048]{1,0:T(8,128)(2,1)}, bf16[128,2048]{1,0:T(8,128)(2,1)}, u32[]{:S(2)}, u32[]{:S(2)}) %collective-permute-start.2) | collective-permute-done | bytes 524320 | tf_op jit(solution)/shard_map/ppermute | solution.py:93
  118.1 6.2 %collective-permute-done.3 = bf16[3,2048,256]{2,1,0:T(8,128)(2,1)} collective-permute-done((bf16[3,2048,256]{2,1,0:T(8,128)(2,1)}, bf16[3,2048,256]{2,1,0:T(8,128)(2,1)}, u32[]{:S(2)}, u32[]{:S(2)}) %collective-permute-start.3) | collective-permute-done | bytes 3145760 | tf_op jit(solution)/shard_map/ppermute | solution.py:54
  125.8 4.3 %select_bitcast_fusion.1 = (bf16[2048,256]{1,0:T(8,128)(2,1)}, bf16[2048,256]{1,0:T(8,128)(2,1)}, bf16[1,2048,256]{2,1,0:T(8,128)(2,1)}, bf16[2048,256]{1,0:T(8,128)(2,1)}, bf16[2048,256]{1,0:T(8,128)(2,1)}) fusion(bf16[1,2048,256]{2,1,0:T(8,128)(2,1)S(1)} %copy-done.4, pred[]{:T(512)S(6)} %eq.36, bf16[3,2048,256]{2,1,0:T(8,128)(2,1)} %collective-permute-done.3, ...), kind=kLoop, calls=%fused_computation.63 | loop fusion | flops 2097152 | bytes 10485761 | tf_op jit(solution)/shard_map/jit(_where)/select_n | solution.py:61
  136.6 26.0 %collective-permute-done.14 = f32[128,16]{0,1:T(8,128)S(1)} collective-permute-done((f32[128,16]{0,1:T(8,128)S(1)}, f32[128,16]{0,1:T(8,128)S(1)}, u32[]{:S(2)}, u32[]{:S(2)}) %collective-permute-start.14) | collective-permute-done | bytes 8224 | tf_op jit(solution)/shard_map/ppermute | solution.py:93
  166.1 2.2 fusion.70
  174.5 3.7 %fusion.69 = f32[1024,512]{1,0:T(8,128)} fusion(bf16[1024,2048]{1,0:T(8,128)(2,1)S(1)} %constant_dynamic-update-slice_fusion, bf16[2048,512]{1,0:T(8,128)(2,1)S(1)} %get-tuple-element.46), kind=kOutput, calls=%fused_computation.141 | convolution fusion | flops 2147483648 | bytes 8388608 | tf_op jit(solution)/shard_map/dot_general | solution.py:78
  178.2 10.0 %multiply_convert_fusion = bf16[1024,2048]{1,0:T(8,128)(2,1)} fusion(f32[1024]{0:T(1024)S(1)} %select_reduce_fusion, bf16[512,2048]{1,0:T(8,128)(2,1)S(1)} %pad_maximum_fusion.4, f32[1024,512]{1,0:T(8,128)} %fusion.69, bf16[1024,2048]{1,0:T(8,128)(2,1)} %copy-done.19, bf16[2048,512]{1,0:T(8,128)(2,1)} %get-tuple-element.47), kind=kOutput, calls=%fused_computation.3 | convolution fusion | flops 4306501632 | bytes 14684160 | tf_op jit(solution)/shard_map/dot_general | solution.py:81
  188.2 4.2 %fusion.63 = (bf16[128,2048]{1,0:T(8,128)(2,1)}, bf16[128,2048]{1,0:T(8,128)(2,1)}, bf16[128,2048]{1,0:T(8,128)(2,1)}, bf16[128,2048]{1,0:T(8,128)(2,1)}, bf16[1...) fusion(bf16[1024,2048]{1,0:T(8,128)(2,1)} %multiply_convert_fusion), kind=kLoop, calls=%fused_computation.137 | loop fusion | bytes 8388608 | tf_op jit(solution)/shard_map/slice | solution.py:111
  193.4 6.9 %convert_multiply_fusion = f32[512,2048]{1,0:T(8,128)} fusion(bf16[512,2048]{1,0:T(8,128)(2,1)S(1)} %pad_maximum_fusion.4, f32[512]{0:T(512)S(1)} %get-tuple-element.57, f32[512,512]{1,0:T(8,128)} %fusion.70, bf16[512,2048]{1,0:T(8,128)(2,1)} %copy-done.16, bf16[2048,512]{1,0:T(8,128)(2,1)} %get-tuple-element.47), kind=kOutput, calls=%fused_computation.8 | convolution fusion | flops 2152202240 | bytes 11536384 | tf_op jit(solution)/shard_map/dot_general | solution.py:81
  200.3 4.7 %fusion.41 = f32[512,512]{1,0:T(8,128)} fusion(bf16[2048,512]{1,0:T(8,128)(2,1)} %get-tuple-element.47, bf16[128,2048]{1,0:T(8,128)(2,1)} %collective-permute-done.2, bf16[128,2048]{1,0:T(8,128)(2,1)} %collective-permute-done.1, bf16[128,2048]{1,0:T(8,128)(2,1)} %collective-permute-done, bf16[128,2048]{1,0:T(8,128)(2,1)} %multiply_convert_fusion.5), kind=kOutput, calls=%fused_computation.82 | convolution fusion | flops 1082130432 | bytes 5242880 | tf_op jit(solution)/shard_map/dot_general | solution.py:79
  205.5 3.3 %fusion.25 = (bf16[128,2048]{1,0:T(8,128)(2,1)}, bf16[128,2048]{1,0:T(8,128)(2,1)}, bf16[128,2048]{1,0:T(8,128)(2,1)}, bf16[128,2048]{1,0:T(8,128)(2,1)}) fusion(f32[512,2048]{1,0:T(8,128)S(1)} %copy-done.3, bf16[128,2048]{1,0:T(8,128)(2,1)} %collective-permute-done.32, bf16[128,2048]{1,0:T(8,128)(2,1)} %collective-permute-done.42, ...), kind=kLoop, calls=%fused_computation.50 | loop fusion | flops 3145728 | bytes 8388608 | tf_op jit(solution)/shard_map/convert_element_type | solution.py:115
  210.9 7.4 %convert_multiply_fusion.1 = f32[512,2048]{1,0:T(8,128)} fusion(bf16[512,2048]{1,0:T(8,128)(2,1)S(1)} %pad_maximum_fusion.4, f32[512]{0:T(512)S(1)} %get-tuple-element.58, f32[512,512]{1,0:T(8,128)} %fusion.41, bf16[2048,512]{1,0:T(8,128)(2,1)} %copy-done.11, bf16[128,2048]{1,0:T(8,128)(2,1)} %collective-permute-done.2, ...), kind=kOutput, calls=%fused_computation.9 | convolution fusion | flops 2160590848 | bytes 11536384 | tf_op jit(solution)/shard_map/dot_general | solution.py:81
  219.8 4.2 %collective-permute-done.36 = bf16[128,2048]{1,0:T(8,128)(2,1)} collective-permute-done((bf16[128,2048]{1,0:T(8,128)(2,1)}, bf16[128,2048]{1,0:T(8,128)(2,1)}, u32[]{:S(2)}, u32[]{:S(2)}) %collective-permute-start.36) | collective-permute-done | bytes 524320 | tf_op jit(solution)/shard_map/ppermute | solution.py:115
  223.9 11.2 %collective-permute-done.43 = bf16[128,2048]{1,0:T(8,128)(2,1)} collective-permute-done((bf16[128,2048]{1,0:T(8,128)(2,1)}, bf16[128,2048]{1,0:T(8,128)(2,1)}, u32[]{:S(2)}, u32[]{:S(2)}) %collective-permute-start.43) | collective-permute-done | bytes 524320 | tf_op jit(solution)/shard_map/ppermute | solution.py:115
  235.2 2.6 fusion.24
  241.3 5.0 %collective-permute-done.40 = bf16[128,2048]{1,0:T(8,128)(2,1)S(1)} collective-permute-done((bf16[128,2048]{1,0:T(8,128)(2,1)}, bf16[128,2048]{1,0:T(8,128)(2,1)S(1)}, u32[]{:S(2)}, u32[]{:S(2)}) %collective-permute-start.40) | collective-permute-done | bytes 524320 | tf_op jit(solution)/shard_map/ppermute | solution.py:115
  246.3 12.0 %collective-permute-done.44 = bf16[128,2048]{1,0:T(8,128)(2,1)S(1)} collective-permute-done((bf16[128,2048]{1,0:T(8,128)(2,1)S(1)}, bf16[128,2048]{1,0:T(8,128)(2,1)S(1)}, u32[]{:S(2)}, u32[]{:S(2)}) %collective-permute-start.44) | collective-permute-done | bytes 524320 | tf_op jit(solution)/shard_map/ppermute | solution.py:115
  258.7 9.3 %collective-permute-done.37 = bf16[128,2048]{1,0:T(8,128)(2,1)S(1)} collective-permute-done((bf16[128,2048]{1,0:T(8,128)(2,1)S(1)}, bf16[128,2048]{1,0:T(8,128)(2,1)S(1)}, u32[]{:S(2)}, u32[]{:S(2)}) %collective-permute-start.37) | collective-permute-done | bytes 524320 | tf_op jit(solution)/shard_map/ppermute | solution.py:115
  268.0 10.4 %collective-permute-done.45 = bf16[128,2048]{1,0:T(8,128)(2,1)S(1)} collective-permute-done((bf16[128,2048]{1,0:T(8,128)(2,1)S(1)}, bf16[128,2048]{1,0:T(8,128)(2,1)S(1)}, u32[]{:S(2)}, u32[]{:S(2)}) %collective-permute-start.45) | collective-permute-done | bytes 524320 | tf_op jit(solution)/shard_map/ppermute | solution.py:115
  (186 shorter events, 58.1 us)
Async XLA Ops:
  6.5 54.3 %all-gather.5.cloned.1.call-start = ((), (), s32[]{:S(2)}) async-start(), calls=%async_computation | async-start | bytes 1572864 | tf_op jit(solution)/shard_map/all_gather | solution.py:18
  52.2 72.1 %collective-permute-start.3 = (bf16[3,2048,256]{2,1,0:T(8,128)(2,1)}, bf16[3,2048,256]{2,1,0:T(8,128)(2,1)}, u32[]{:S(2)}, u32[]{:S(2)}) collective-permute-start(bf16[3,2048,256]{2,1,0:T(8,128)(2,1)} %pad_maximum_fusion), channel_id=1, source_target_pairs={{0,16},{16,0},{1,17},{17,1},{2,18},{18,2},{3,19},{19,3},{4,20},{20... | collective-permute-start | bytes 9437192 | tf_op jit(solution)/shard_map/ppermute | solution.py:54
  66.9 30.1 %collective-permute-start = (bf16[128,2048]{1,0:T(8,128)(2,1)}, bf16[128,2048]{1,0:T(8,128)(2,1)}, u32[]{:S(2)}, u32[]{:S(2)}) collective-permute-start(bf16[128,2048]{1,0:T(8,128)(2,1)} %multiply_convert_fusion.5), channel_id=1, source_target_pairs={{0,8},{1,9},{2,10},{3,11},{4,12},{5,13},{6,14},{7,15},{8,0},{9,1},... | collective-permute-start | bytes 1572872 | tf_op jit(solution)/shard_map/ppermute | solution.py:93
  67.6 31.4 %collective-permute-start.1 = (bf16[128,2048]{1,0:T(8,128)(2,1)}, bf16[128,2048]{1,0:T(8,128)(2,1)}, u32[]{:S(2)}, u32[]{:S(2)}) collective-permute-start(bf16[128,2048]{1,0:T(8,128)(2,1)} %multiply_convert_fusion.5), channel_id=1, source_target_pairs={{0,4},{1,5},{2,6},{3,7},{4,0},{5,1},{6,2},{7,3},{8,12},{9,13},{10,... | collective-permute-start | bytes 1572872 | tf_op jit(solution)/shard_map/ppermute | solution.py:93
  68.4 24.4 %collective-permute-start.7 = (f32[128,16]{0,1:T(8,128)S(1)}, f32[128,16]{0,1:T(8,128)S(1)}, u32[]{:S(2)}, u32[]{:S(2)}) collective-permute-start(f32[128,16]{0,1:T(8,128)S(1)} %select_reduce_fusion.1), channel_id=1, source_target_pairs={{0,8},{1,9},{2,10},{3,11},{4,12},{5,13},{6,14},{7,15},{8,0},{9,1},... | collective-permute-start | bytes 24584 | tf_op jit(solution)/shard_map/ppermute | solution.py:93
  70.6 22.3 %collective-permute-start.10 = (f32[128,16]{0,1:T(8,128)S(1)}, f32[128,16]{0,1:T(8,128)S(1)}, u32[]{:S(2)}, u32[]{:S(2)}) collective-permute-start(f32[128,16]{0,1:T(8,128)S(1)} %select_reduce_fusion.1), channel_id=1, source_target_pairs={{0,4},{1,5},{2,6},{3,7},{4,0},{5,1},{6,2},{7,3},{8,12},{9,13},{10,... | collective-permute-start | bytes 24584 | tf_op jit(solution)/shard_map/ppermute | solution.py:93
  97.0 14.2 %collective-permute-start.2 = (bf16[128,2048]{1,0:T(8,128)(2,1)}, bf16[128,2048]{1,0:T(8,128)(2,1)}, u32[]{:S(2)}, u32[]{:S(2)}) collective-permute-start(bf16[128,2048]{1,0:T(8,128)(2,1)} %collective-permute-done), channel_id=1, source_target_pairs={{0,4},{1,5},{2,6},{3,7},{4,0},{5,1},{6,2},{7,3},{8,12},{9,13},{10,... | collective-permute-start | bytes 1572872 | tf_op jit(solution)/shard_map/ppermute | solution.py:93
  98.9 13.5 %collective-permute-start.16 = (bf16[128,2048]{1,0:T(8,128)(2,1)}, bf16[128,2048]{1,0:T(8,128)(2,1)S(1)}, u32[]{:S(2)}, u32[]{:S(2)}) collective-permute-start(bf16[128,2048]{1,0:T(8,128)(2,1)} %collective-permute-done), channel_id=1, source_target_pairs={{0,1},{1,0},{2,3},{3,2},{4,5},{5,4},{6,7},{7,6},{8,9},{9,8},{10,11... | collective-permute-start | bytes 1572872 | tf_op jit(solution)/shard_map/ppermute | solution.py:93
  99.0 14.8 %collective-permute-start.17 = (bf16[128,2048]{1,0:T(8,128)(2,1)}, bf16[128,2048]{1,0:T(8,128)(2,1)S(1)}, u32[]{:S(2)}, u32[]{:S(2)}) collective-permute-start(bf16[128,2048]{1,0:T(8,128)(2,1)} %collective-permute-done.1), channel_id=1, source_target_pairs={{0,1},{1,0},{2,3},{3,2},{4,5},{5,4},{6,7},{7,6},{8,9},{9,8},{10,11... | collective-permute-start | bytes 1572872 | tf_op jit(solution)/shard_map/ppermute | solution.py:93
  99.4 32.7 %collective-permute-start.5 = (f32[128,16]{0,1:T(8,128)S(1)}, f32[128,16]{0,1:T(8,128)S(1)}, u32[]{:S(2)}, u32[]{:S(2)}) collective-permute-start(f32[128,16]{0,1:T(8,128)S(1)} %select_reduce_fusion.1), channel_id=1, source_target_pairs={{0,2},{1,3},{2,0},{3,1},{4,6},{5,7},{6,4},{7,5},{8,10},{9,11},{10,... | collective-permute-start | bytes 24584 | tf_op jit(solution)/shard_map/ppermute | solution.py:93
  112.3 20.4 %collective-permute-start.8 = (f32[128,16]{0,1:T(8,128)S(1)}, f32[128,16]{0,1:T(8,128)S(1)}, u32[]{:S(2)}, u32[]{:S(2)}) collective-permute-start(f32[128,16]{0,1:T(8,128)S(1)} %collective-permute-done.7), channel_id=1, source_target_pairs={{0,2},{1,3},{2,0},{3,1},{4,6},{5,7},{6,4},{7,5},{8,10},{9,11},{10,... | collective-permute-start | bytes 24584 | tf_op jit(solution)/shard_map/ppermute | solution.py:93
  113.9 22.0 %collective-permute-start.11 = (f32[128,16]{0,1:T(8,128)S(1)}, f32[128,16]{0,1:T(8,128)S(1)}, u32[]{:S(2)}, u32[]{:S(2)}) collective-permute-start(f32[128,16]{0,1:T(8,128)S(1)} %collective-permute-done.10), channel_id=1, source_target_pairs={{0,2},{1,3},{2,0},{3,1},{4,6},{5,7},{6,4},{7,5},{8,10},{9,11},{10,... | collective-permute-start | bytes 24584 | tf_op jit(solution)/shard_map/ppermute | solution.py:93
  114.6 48.0 %collective-permute-start.4 = (bf16[128,2048]{1,0:T(8,128)(2,1)}, bf16[128,2048]{1,0:T(8,128)(2,1)}, u32[]{:S(2)}, u32[]{:S(2)}) collective-permute-start(bf16[128,2048]{1,0:T(8,128)(2,1)} %multiply_convert_fusion.5), channel_id=1, source_target_pairs={{0,2},{1,3},{2,0},{3,1},{4,6},{5,7},{6,4},{7,5},{8,10},{9,11},{10,... | collective-permute-start | bytes 1572872 | tf_op jit(solution)/shard_map/ppermute | solution.py:93
  124.3 38.3 %collective-permute-start.6 = (bf16[128,2048]{1,0:T(8,128)(2,1)}, bf16[128,2048]{1,0:T(8,128)(2,1)}, u32[]{:S(2)}, u32[]{:S(2)}) collective-permute-start(bf16[128,2048]{1,0:T(8,128)(2,1)} %collective-permute-done), channel_id=1, source_target_pairs={{0,2},{1,3},{2,0},{3,1},{4,6},{5,7},{6,4},{7,5},{8,10},{9,11},{10,... | collective-permute-start | bytes 1572872 | tf_op jit(solution)/shard_map/ppermute | solution.py:93
  132.1 30.6 %collective-permute-start.9 = (bf16[128,2048]{1,0:T(8,128)(2,1)}, bf16[128,2048]{1,0:T(8,128)(2,1)S(1)}, u32[]{:S(2)}, u32[]{:S(2)}) collective-permute-start(bf16[128,2048]{1,0:T(8,128)(2,1)} %collective-permute-done.1), channel_id=1, source_target_pairs={{0,2},{1,3},{2,0},{3,1},{4,6},{5,7},{6,4},{7,5},{8,10},{9,11},{10,... | collective-permute-start | bytes 1572872 | tf_op jit(solution)/shard_map/ppermute | solution.py:93
  132.7 29.9 %collective-permute-start.12 = (bf16[128,2048]{1,0:T(8,128)(2,1)}, bf16[128,2048]{1,0:T(8,128)(2,1)S(1)}, u32[]{:S(2)}, u32[]{:S(2)}) collective-permute-start(bf16[128,2048]{1,0:T(8,128)(2,1)} %collective-permute-done.2), channel_id=1, source_target_pairs={{0,2},{1,3},{2,0},{3,1},{4,6},{5,7},{6,4},{7,5},{8,10},{9,11},{10,... | collective-permute-start | bytes 1572872 | tf_op jit(solution)/shard_map/ppermute | solution.py:93
  135.9 26.7 %collective-permute-start.14 = (f32[128,16]{0,1:T(8,128)S(1)}, f32[128,16]{0,1:T(8,128)S(1)}, u32[]{:S(2)}, u32[]{:S(2)}) collective-permute-start(f32[128,16]{0,1:T(8,128)S(1)} %collective-permute-done.13), channel_id=1, source_target_pairs={{0,2},{1,3},{2,0},{3,1},{4,6},{5,7},{6,4},{7,5},{8,10},{9,11},{10,... | collective-permute-start | bytes 24584 | tf_op jit(solution)/shard_map/ppermute | solution.py:93
  192.4 12.9 %collective-permute-start.32 = (bf16[128,2048]{1,0:T(8,128)(2,1)}, bf16[128,2048]{1,0:T(8,128)(2,1)}, u32[]{:S(2)}, u32[]{:S(2)}) collective-permute-start(bf16[128,2048]{1,0:T(8,128)(2,1)} %get-tuple-element.68), channel_id=1, source_target_pairs={{1,0},{0,1},{3,2},{2,3},{5,4},{4,5},{7,6},{6,7},{9,8},{8,9},{11,10... | collective-permute-start | bytes 1572872 | tf_op jit(solution)/shard_map/ppermute | solution.py:115
  192.7 12.8 %collective-permute-start.35 = (bf16[128,2048]{1,0:T(8,128)(2,1)}, bf16[128,2048]{1,0:T(8,128)(2,1)}, u32[]{:S(2)}, u32[]{:S(2)}) collective-permute-start(bf16[128,2048]{1,0:T(8,128)(2,1)} %get-tuple-element.66), channel_id=1, source_target_pairs={{1,0},{0,1},{3,2},{2,3},{5,4},{4,5},{7,6},{6,7},{9,8},{8,9},{11,10... | collective-permute-start | bytes 1572872 | tf_op jit(solution)/shard_map/ppermute | solution.py:115
  192.9 12.6 %collective-permute-start.39 = (bf16[128,2048]{1,0:T(8,128)(2,1)}, bf16[128,2048]{1,0:T(8,128)(2,1)}, u32[]{:S(2)}, u32[]{:S(2)}) collective-permute-start(bf16[128,2048]{1,0:T(8,128)(2,1)} %get-tuple-element.64), channel_id=1, source_target_pairs={{1,0},{0,1},{3,2},{2,3},{5,4},{4,5},{7,6},{6,7},{9,8},{8,9},{11,10... | collective-permute-start | bytes 1572872 | tf_op jit(solution)/shard_map/ppermute | solution.py:115
  193.3 12.3 %collective-permute-start.42 = (bf16[128,2048]{1,0:T(8,128)(2,1)}, bf16[128,2048]{1,0:T(8,128)(2,1)}, u32[]{:S(2)}, u32[]{:S(2)}) collective-permute-start(bf16[128,2048]{1,0:T(8,128)(2,1)} %get-tuple-element.62), channel_id=1, source_target_pairs={{1,0},{0,1},{3,2},{2,3},{5,4},{4,5},{7,6},{6,7},{9,8},{8,9},{11,10... | collective-permute-start | bytes 1572872 | tf_op jit(solution)/shard_map/ppermute | solution.py:115
  205.0 13.4 %collective-permute-start.34 = (bf16[128,2048]{1,0:T(8,128)(2,1)}, bf16[128,2048]{1,0:T(8,128)(2,1)}, u32[]{:S(2)}, u32[]{:S(2)}) collective-permute-start(bf16[128,2048]{1,0:T(8,128)(2,1)} %get-tuple-element.67), channel_id=1, source_target_pairs={{1,0},{0,1},{3,2},{2,3},{5,4},{4,5},{7,6},{6,7},{9,8},{8,9},{11,10... | collective-permute-start | bytes 1572872 | tf_op jit(solution)/shard_map/ppermute | solution.py:115
  205.3 14.4 %collective-permute-start.41 = (bf16[128,2048]{1,0:T(8,128)(2,1)}, bf16[128,2048]{1,0:T(8,128)(2,1)}, u32[]{:S(2)}, u32[]{:S(2)}) collective-permute-start(bf16[128,2048]{1,0:T(8,128)(2,1)} %get-tuple-element.63), channel_id=1, source_target_pairs={{1,0},{0,1},{3,2},{2,3},{5,4},{4,5},{7,6},{6,7},{9,8},{8,9},{11,10... | collective-permute-start | bytes 1572872 | tf_op jit(solution)/shard_map/ppermute | solution.py:115
  208.9 15.1 %collective-permute-start.36 = (bf16[128,2048]{1,0:T(8,128)(2,1)}, bf16[128,2048]{1,0:T(8,128)(2,1)}, u32[]{:S(2)}, u32[]{:S(2)}) collective-permute-start(bf16[128,2048]{1,0:T(8,128)(2,1)} %get-tuple-element.72), channel_id=1, source_target_pairs={{2,0},{3,1},{0,2},{1,3},{6,4},{7,5},{4,6},{5,7},{10,8},{11,9},{8,1... | collective-permute-start | bytes 1572872 | tf_op jit(solution)/shard_map/ppermute | solution.py:115
  210.2 24.9 %collective-permute-start.43 = (bf16[128,2048]{1,0:T(8,128)(2,1)}, bf16[128,2048]{1,0:T(8,128)(2,1)}, u32[]{:S(2)}, u32[]{:S(2)}) collective-permute-start(bf16[128,2048]{1,0:T(8,128)(2,1)} %get-tuple-element.70), channel_id=1, source_target_pairs={{2,0},{3,1},{0,2},{1,3},{6,4},{7,5},{4,6},{5,7},{10,8},{11,9},{8,1... | collective-permute-start | bytes 1572872 | tf_op jit(solution)/shard_map/ppermute | solution.py:115
  218.3 21.6 %collective-permute-start.38 = (bf16[128,2048]{1,0:T(8,128)(2,1)}, bf16[128,2048]{1,0:T(8,128)(2,1)S(1)}, u32[]{:S(2)}, u32[]{:S(2)}) collective-permute-start(bf16[128,2048]{1,0:T(8,128)(2,1)} %get-tuple-element.65), channel_id=1, source_target_pairs={{1,0},{0,1},{3,2},{2,3},{5,4},{4,5},{7,6},{6,7},{9,8},{8,9},{11,10... | collective-permute-start | bytes 1572872 | tf_op jit(solution)/shard_map/ppermute | solution.py:115
  218.4 27.9 %collective-permute-start.40 = (bf16[128,2048]{1,0:T(8,128)(2,1)}, bf16[128,2048]{1,0:T(8,128)(2,1)S(1)}, u32[]{:S(2)}, u32[]{:S(2)}) collective-permute-start(bf16[128,2048]{1,0:T(8,128)(2,1)} %get-tuple-element.71), channel_id=1, source_target_pairs={{2,0},{3,1},{0,2},{1,3},{6,4},{7,5},{4,6},{5,7},{10,8},{11,9},{8,1... | collective-permute-start | bytes 1572872 | tf_op jit(solution)/shard_map/ppermute | solution.py:115
  237.8 20.5 %collective-permute-start.44 = (bf16[128,2048]{1,0:T(8,128)(2,1)S(1)}, bf16[128,2048]{1,0:T(8,128)(2,1)S(1)}, u32[]{:S(2)}, u32[]{:S(2)}) collective-permute-start(bf16[128,2048]{1,0:T(8,128)(2,1)S(1)} %get-tuple-element.74), channel_id=1, source_target_pairs={{4,0},{5,1},{6,2},{7,3},{0,4},{1,5},{2,6},{3,7},{12,8},{13,9},{14,... | collective-permute-start | bytes 1572872 | tf_op jit(solution)/shard_map/ppermute | solution.py:115
  238.4 20.3 %collective-permute-start.31 = (bf16[128,2048]{1,0:T(8,128)(2,1)S(1)}, bf16[128,2048]{1,0:T(8,128)(2,1)S(1)}, u32[]{:S(2)}, u32[]{:S(2)}) collective-permute-start(bf16[128,2048]{1,0:T(8,128)(2,1)S(1)} %copy-done.12), channel_id=1, source_target_pairs={{1,0},{0,1},{3,2},{2,3},{5,4},{4,5},{7,6},{6,7},{9,8},{8,9},{11,10... | collective-permute-start | bytes 1572872 | tf_op jit(solution)/shard_map/ppermute | solution.py:115
  238.4 20.3 %collective-permute-start.33 = (bf16[128,2048]{1,0:T(8,128)(2,1)S(1)}, bf16[128,2048]{1,0:T(8,128)(2,1)S(1)}, u32[]{:S(2)}, u32[]{:S(2)}) collective-permute-start(bf16[128,2048]{1,0:T(8,128)(2,1)S(1)} %copy-done.13), channel_id=1, source_target_pairs={{2,0},{3,1},{0,2},{1,3},{6,4},{7,5},{4,6},{5,7},{10,8},{11,9},{8,1... | collective-permute-start | bytes 1572872 | tf_op jit(solution)/shard_map/ppermute | solution.py:115
  239.8 28.2 %collective-permute-start.37 = (bf16[128,2048]{1,0:T(8,128)(2,1)S(1)}, bf16[128,2048]{1,0:T(8,128)(2,1)S(1)}, u32[]{:S(2)}, u32[]{:S(2)}) collective-permute-start(bf16[128,2048]{1,0:T(8,128)(2,1)S(1)} %get-tuple-element.73), channel_id=1, source_target_pairs={{4,0},{5,1},{6,2},{7,3},{0,4},{1,5},{2,6},{3,7},{12,8},{13,9},{14,... | collective-permute-start | bytes 1572872 | tf_op jit(solution)/shard_map/ppermute | solution.py:115
  258.6 19.8 %collective-permute-start.45 = (bf16[128,2048]{1,0:T(8,128)(2,1)S(1)}, bf16[128,2048]{1,0:T(8,128)(2,1)S(1)}, u32[]{:S(2)}, u32[]{:S(2)}) collective-permute-start(bf16[128,2048]{1,0:T(8,128)(2,1)S(1)} %fusion.21), channel_id=1, source_target_pairs={{8,0},{9,1},{10,2},{11,3},{12,4},{13,5},{14,6},{15,7},{0,8},{1,9},... | collective-permute-start | bytes 1572872 | tf_op jit(solution)/shard_map/ppermute | solution.py:115
  (39 other events, 299.2 us)
Sparse Core Ops, SparseCore 0:
  34.7 26.1 all-gather.4

commit v7 on v6

--- a/solution.py
+++ b/solution.py
@@ -168,6 +168,129 @@
     return plan
 
 
+def joined_attention(queries, new_keys, new_values, cache_keys, cache_values, length):
+    kv_rank = lax.axis_index("kv")
+    tok_dev = queries.shape[1]
+    cl_dev = cache_keys.shape[1]
+    feat = queries.shape[2]
+    head_count = feat // HEAD_DIM
+    score_scale = 1.0 / math.sqrt(HEAD_DIM)
+    every_query = lax.all_gather(queries[0], "kv", axis=0, tiled=True)
+    new_total = every_query.shape[0]
+    query_heads = every_query.reshape(new_total, head_count, HEAD_DIM)
+    key_cache = cache_keys[0].reshape(cl_dev, head_count, HEAD_DIM)
+    value_cache = cache_values[0].reshape(cl_dev, head_count, HEAD_DIM)
+    key_new = new_keys[0].reshape(tok_dev, head_count, HEAD_DIM)
+    value_new = new_values[0].reshape(tok_dev, head_count, HEAD_DIM)
+    score_cache = (
+        jnp.einsum("qhd,khd->qhk", query_heads, key_cache, preferred_element_type=jnp.float32)
+        * score_scale
+    )
+    position = kv_rank * cl_dev + jnp.arange(cl_dev, dtype=jnp.int32)
+    score_cache = jnp.where((position < length)[None, None, :], score_cache, -jnp.inf)
+    score_new = (
+        jnp.einsum("qhd,khd->qhk", query_heads, key_new, preferred_element_type=jnp.float32)
+        * score_scale
+    )
+    local_top = jnp.maximum(jnp.max(score_cache, axis=-1), jnp.max(score_new, axis=-1))
+    expo_cache = jnp.exp(score_cache - local_top[..., None])
+    expo_new = jnp.exp(score_new - local_top[..., None])
+    denom = jnp.sum(expo_cache, axis=-1) + jnp.sum(expo_new, axis=-1)
+    summed = jnp.einsum(
+        "qhk,khd->qhd",
+        expo_cache.astype(jnp.bfloat16),
+        value_cache,
+        preferred_element_type=jnp.float32,
+    )
+    summed = summed + jnp.einsum(
+        "qhk,khd->qhd", expo_new.astype(jnp.bfloat16), value_new, preferred_element_type=jnp.float32
+    )
+    summed, denom = (summed.reshape(new_total, feat), denom)
+
+    def join(first, second):
+        first_top, first_denom, first_sum = first
+        second_top, second_denom, second_sum = second
+        joint_top = jnp.maximum(first_top, second_top)
+        first_factor = jnp.exp(first_top - joint_top)
+        second_factor = jnp.exp(second_top - joint_top)
+        rows_here = first_sum.shape[0]
+        joint_sum = (
+            first_sum.reshape(rows_here, head_count, HEAD_DIM) * first_factor[..., None]
+            + second_sum.reshape(rows_here, head_count, HEAD_DIM) * second_factor[..., None]
+        )
+        return (
+            joint_top,
+            first_denom * first_factor + second_denom * second_factor,
+            joint_sum.reshape(rows_here, feat),
+        )
+
+    joint_top, joint_denom, joint_sum = combined_all((local_top, denom, summed), "kv", join)
+    row_start = kv_rank * tok_dev
+    own_sum = lax.dynamic_slice_in_dim(joint_sum, row_start, tok_dev, 0)
+    own_denom = lax.dynamic_slice_in_dim(joint_denom, row_start, tok_dev, 0)
+    attended = (
+        (own_sum.reshape(tok_dev, head_count, HEAD_DIM) / own_denom[..., None])
+        .reshape(tok_dev, feat)
+        .astype(jnp.bfloat16)
+    )
+    return attended
+
+
+def partial_softmax(query_rows, key_cache, value_cache, key_new, value_new, usable):
+    rows, feat = query_rows.shape
+    head_count = feat // HEAD_DIM
+    score_scale = 1.0 / math.sqrt(HEAD_DIM)
+    query_heads = query_rows.reshape(rows, head_count, HEAD_DIM)
+    score_cache = (
+        jnp.einsum("qhd,khd->qhk", query_heads, key_cache, preferred_element_type=jnp.float32)
+        * score_scale
+    )
+    score_cache = jnp.where(usable[None, None, :], score_cache, -jnp.inf)
+    score_new = (
+        jnp.einsum("qhd,khd->qhk", query_heads, key_new, preferred_element_type=jnp.float32)
+        * score_scale
+    )
+    top = jnp.maximum(jnp.max(score_cache, axis=-1), jnp.max(score_new, axis=-1))
+    expo_cache = jnp.exp(score_cache - top[..., None])
+    expo_new = jnp.exp(score_new - top[..., None])
+    denom = jnp.sum(expo_cache, axis=-1) + jnp.sum(expo_new, axis=-1)
+    summed = jnp.einsum(
+        "qhk,khd->qhd", expo_cache.astype(jnp.bfloat16), value_cache,
+        preferred_element_type=jnp.float32,
+    )
+    summed = summed + jnp.einsum(
+        "qhk,khd->qhd", expo_new.astype(jnp.bfloat16), value_new, preferred_element_type=jnp.float32
+    )
+    return top, denom, summed
+
+
+def paired_attention(own_queries, key_new, value_new, key_cache, value_cache, length):
+    kv_rank = lax.axis_index("kv")
+    swap = [(0, 1), (1, 0)]
+    tok_dev, feat = own_queries.shape
+    cl_dev = key_cache.shape[0]
+    head_count = feat // HEAD_DIM
+    far_queries = lax.ppermute(own_queries, "kv", swap)
+    key_cache = key_cache.reshape(cl_dev, head_count, HEAD_DIM)
+    value_cache = value_cache.reshape(cl_dev, head_count, HEAD_DIM)
+    key_new = key_new.reshape(tok_dev, head_count, HEAD_DIM)
+    value_new = value_new.reshape(tok_dev, head_count, HEAD_DIM)
+    position = kv_rank * cl_dev + jnp.arange(cl_dev, dtype=jnp.int32)
+    usable = position < length
+    operands = (key_cache, value_cache, key_new, value_new, usable)
+    own_top, own_denom, own_sum = partial_softmax(own_queries, *operands)
+    far_top, far_denom, far_sum = partial_softmax(far_queries, *operands)
+    back_top, back_denom, back_sum = lax.ppermute(
+        (far_top, far_denom, far_sum.astype(jnp.bfloat16)), "kv", swap
+    )
+    joint_top = jnp.maximum(own_top, back_top)
+    own_factor = jnp.exp(own_top - joint_top)
+    back_factor = jnp.exp(back_top - joint_top)
+    joint_sum = own_sum * own_factor[..., None] + back_sum.astype(jnp.float32) * back_factor[..., None]
+    joint_denom = own_denom * own_factor + back_denom * back_factor
+    return (joint_sum / joint_denom[..., None]).reshape(tok_dev, feat).astype(jnp.bfloat16)
+
+
 def shards(
     plan,
     resid,
@@ -195,64 +318,14 @@
     score_scale = 1.0 / math.sqrt(HEAD_DIM)
     request_index = jnp.arange(cached_len.shape[0], dtype=jnp.int32)
     length = jnp.sum(jnp.where(request_index == group_request[0], cached_len, 0))
-    every_query = lax.all_gather(queries[0], "kv", axis=0, tiled=True)
-    new_total = every_query.shape[0]
-    query_heads = every_query.reshape(new_total, head_count, HEAD_DIM)
-    key_cache = cache_keys[0].reshape(cl_dev, head_count, HEAD_DIM)
-    value_cache = cache_values[0].reshape(cl_dev, head_count, HEAD_DIM)
-    key_new = new_keys[0].reshape(tok_dev, head_count, HEAD_DIM)
-    value_new = new_values[0].reshape(tok_dev, head_count, HEAD_DIM)
-    score_cache = (
-        jnp.einsum("qhd,khd->qhk", query_heads, key_cache, preferred_element_type=jnp.float32)
-        * score_scale
-    )
-    position = kv_rank * cl_dev + jnp.arange(cl_dev, dtype=jnp.int32)
-    score_cache = jnp.where((position < length)[None, None, :], score_cache, -jnp.inf)
-    score_new = (
-        jnp.einsum("qhd,khd->qhk", query_heads, key_new, preferred_element_type=jnp.float32)
-        * score_scale
-    )
-    local_top = jnp.maximum(jnp.max(score_cache, axis=-1), jnp.max(score_new, axis=-1))
-    expo_cache = jnp.exp(score_cache - local_top[..., None])
-    expo_new = jnp.exp(score_new - local_top[..., None])
-    denom = jnp.sum(expo_cache, axis=-1) + jnp.sum(expo_new, axis=-1)
-    summed = jnp.einsum(
-        "qhk,khd->qhd",
-        expo_cache.astype(jnp.bfloat16),
-        value_cache,
-        preferred_element_type=jnp.float32,
-    )
-    summed = summed + jnp.einsum(
-        "qhk,khd->qhd", expo_new.astype(jnp.bfloat16), value_new, preferred_element_type=jnp.float32
-    )
-    summed, denom = (summed.reshape(new_total, feat), denom)
-
-    def join(first, second):
-        first_top, first_denom, first_sum = first
-        second_top, second_denom, second_sum = second
-        joint_top = jnp.maximum(first_top, second_top)
-        first_factor = jnp.exp(first_top - joint_top)
-        second_factor = jnp.exp(second_top - joint_top)
-        rows_here = first_sum.shape[0]
-        joint_sum = (
-            first_sum.reshape(rows_here, head_count, HEAD_DIM) * first_factor[..., None]
-            + second_sum.reshape(rows_here, head_count, HEAD_DIM) * second_factor[..., None]
-        )
-        return (
-            joint_top,
-            first_denom * first_factor + second_denom * second_factor,
-            joint_sum.reshape(rows_here, feat),
-        )
-
-    joint_top, joint_denom, joint_sum = combined_all((local_top, denom, summed), "kv", join)
-    row_start = kv_rank * tok_dev
-    own_sum = lax.dynamic_slice_in_dim(joint_sum, row_start, tok_dev, 0)
-    own_denom = lax.dynamic_slice_in_dim(joint_denom, row_start, tok_dev, 0)
-    attended = (
-        (own_sum.reshape(tok_dev, head_count, HEAD_DIM) / own_denom[..., None])
-        .reshape(tok_dev, feat)
-        .astype(jnp.bfloat16)
-    )
+    if lax.axis_size("kv") == 2 and plan is not None:
+        attended = paired_attention(
+            queries[0], new_keys[0], new_values[0], cache_keys[0], cache_values[0], length
+        )
+    else:
+        attended = joined_attention(
+            queries, new_keys, new_values, cache_keys, cache_values, length
+        )
     proj = jnp.dot(attended, w_out, preferred_element_type=jnp.float32)
     hidden = (resid[0].astype(jnp.float32) + proj).astype(jnp.bfloat16)
     hidden_f = hidden.astype(jnp.float32)
@@ -263,7 +336,7 @@
     ).astype(jnp.bfloat16)
     if plan is not None:
         moe_sum, _ = dense_moe(
-            plan, normed, route_ids[0], route_weights[0], (gate_w, up_w, down_w), joint_denom
+            plan, normed, route_ids[0], route_weights[0], (gate_w, up_w, down_w), attended
         )
         return (hidden_f + moe_sum).astype(jnp.bfloat16)[None]
     expert_count = EXP_DEV * ep_count

time: 290 us -> 259 us (0.89)
  blocking collectives: 17.8 us -> 0 us
  between operations: 14.7 us -> 1.36 us
  local copies, waits for them, and re-layouts: 29.8 us -> 21.3 us
  waiting for transfers between devices: 126 us -> 132 us
  starting transfers between devices: 29.3 us -> 33.1 us
  other arithmetic: 24.4 us -> 21 us
    all_gather x3 -> x0, blocking collectives: 17.8 us -> none  [the longest x2 9.04 us: combined_all(): lax.all_gather(a.astype(kind), axis)]
    ppermute x1, waiting for transfers between devices: 6.19 us -> 16.4 us  [full_weights(): other = lax.ppermute(packed, 'kv', [(0, 1), (1, 0)])]
    ppermute x0 -> x4, waiting for transfers between devices: none -> 6.61 us  [the longest x3 6.6 us: paired_attention(): lax.ppermute((far_top, far_denom, far_sum.astype(jnp.bfloat16)), 'kv', swap)]
    ppermute x30, waiting for transfers between devices: 63.7 us -> 57.8 us  [dense_moe(): grown.append((lax.ppermute(block, 'ep', pairs), parent, pairs))]
    dot_general x4 -> x8, matrix products: 5.73 us -> 10.8 us  [the longest x2 5.24 us: partial_softmax(): jnp.einsum('qhd,khd->qhk', query_heads, key_cache, preferred_element_type...]
    ppermute x0 -> x4, starting transfers between devices: none -> 4.3 us  [the longest x3 2.74 us: paired_attention(): lax.ppermute((far_top, far_denom, far_sum.astype(jnp.bfloat16)), 'kv', swap)]
    all_gather x1 -> x0, waiting for transfers between devices: 4.28 us -> none  [combined_all(): lax.all_gather(a.astype(kind), axis)]
    another operation x2 -> x0, local copies, waits for them, and re-layouts: 4.14 us -> none  [the longest x1 3.97 us: shards(): value_cache = cache_values[0].reshape(cl_dev, head_count, HEAD_DIM)]
  transfers between devices with their start and end apart: 47 -> 50, of which waited for: 17 -> 19; matrix products, arithmetic and copies ran while one was open for 20% -> 22% of each run, Pallas kernels for 0% -> 0%
where the time goes in v7:
time: 259 us; the launch traced here: 256 us
  waiting for transfers between devices  132 us (51%)
  matrix products  46.4 us (18%)
  starting transfers between devices  33.1 us (13%)
  local copies, waits for them, and re-layouts  21.3 us (8%)
  other arithmetic  21 us (8%)
    ppermute x30, waiting for transfers between devices, dense_moe(): grown.append((lax.ppermute(block, 'ep', pairs), parent, pairs))  57.8 us
    ppermute x15, waiting for transfers between devices, dense_moe(): sent = lax.ppermute(partial[index].astype(jnp.bfloat16), 'ep', back)  51.6 us
    dot_general x3, matrix products, expert(): out_rows = jnp.dot(act, full[2], preferred_element_type=jnp.float32)  24.2 us
    ppermute x30, starting transfers between devices, dense_moe(): grown.append((lax.ppermute(block, 'ep', pairs), parent, pairs))  19.3 us
    ppermute x1, waiting for transfers between devices, full_weights(): other = lax.ppermute(packed, 'kv', [(0, 1), (1, 0)])  16.4 us
    unnamed x79, local copies, waits for them, and re-layouts  14.7 us
    ppermute x15, starting transfers between devices, dense_moe(): sent = lax.ppermute(partial[index].astype(jnp.bfloat16), 'ep', back)  9.01 us
    ppermute x3, waiting for transfers between devices, paired_attention(): lax.ppermute((far_top, far_denom, far_sum.astype(jnp.bfloat16)), 'kv', swap)  6.6 us
  transfers between devices with their start and end apart: 50, of which 19 were waited for; matrix products, arithmetic and copies ran while one was open for 22% of the time, Pallas kernels for 0%

profile of v7, /device:TPU:24, one launch (start us, length us, event | category | flops | bytes accessed | tf_op | source)
XLA Modules:
  0.0 255.6 jit_solution(3018384726103477749)
XLA Ops:
  3.5 3.6 %copy.104 = bf16[128,8,8,128]{3,2,1,0:T(8,128)(2,1)} copy(bf16[128,8,8,128]{3,1,2,0:T(8,128)(2,1)} %bitcast.87) | data formatting | bytes 4194304
  7.2 2.0 copy.103
  11.0 2.6 %bitcast_reduce_fusion.1 = (f32[128,8]{0,1:T(8,128)S(1)}, f32[8,1024,128]{2,1,0:T(8,128)S(1)}) fusion(pred[1024]{0:T(1024)(128)(4,1)S(1)} %add_compare_fusion, bf16[128,8,128]{2,1,0:T(8,128)(2,1)S(1)} %bitcast.97, bf16[1024,8,128]{2,1,0:T(8,128)(2,1)} %bitcast.91), kind=kOutput, calls=%fused_computation.5 | convolution fusion | flops 271580160 | bytes 6558720 | tf_op jit(solution)/shard_map/qhd,khd->qhk/dot_general | solution.py:245
  13.7 1.7 fusion.10
  15.5 2.6 %fusion.2 = (f32[128,8]{0,1:T(8,128)S(1)}, f32[128,8]{0,1:T(8,128)S(1)}, f32[8,1024,128]{2,1,0:T(8,128)S(1)}) fusion(f32[8,1024,128]{2,1,0:T(8,128)S(1)} %get-tuple-element.64, f32[128,8]{0,1:T(8,128)S(1)} %max.17, pred[1024]{0:T(1024)(128)(4,1)S(1)} %add_compare_fusion, bf16[128,8,128]{0,2,1:T(8,128)(2,1)} %bitcast.6, bf16[1024,8,128]{2,1,0:T(8,128)(2,1)S(1)} %bitcast.92), kind=kOutput, calls=%fused_computation.11 | convolution fusion | flops 275773440 | bytes 10761216 | tf_op jit(solution)/shard_map/qhd,khd->qhk/dot_general | solution.py:245
  20.8 1.7 fusion.8
  26.4 5.4 %collective-permute-done.2 = bf16[128,8,128]{0,2,1:T(8,128)(2,1)S(1)} collective-permute-done((bf16[128,8,128]{0,2,1:T(8,128)(2,1)S(1)}, bf16[128,8,128]{0,2,1:T(8,128)(2,1)S(1)}, u32[]{:S(2)}, u32[]{:S(2)}) %collective-permute-start.2) | collective-permute-done | bytes 262176 | tf_op jit(solution)/shard_map/ppermute | solution.py:283
  32.9 3.4 %pad_maximum_fusion = bf16[3,2048,256]{2,1,0:T(8,128)(2,1)} fusion(bf16[1,2048,256]{2,1,0:T(8,128)(2,1)S(1)} %stack_reshape_squeeze.3, bf16[1,2048,256]{2,1,0:T(8,128)(2,1)S(1)} %copy-done.4, bf16[1,2048,256]{2,1,0:T(8,128)(2,1)} %param.27), kind=kLoop, calls=%fused_computation.15 | loop fusion | flops 3145728 | bytes 6291456 | tf_op jit(solution)/shard_map/stack | solution.py:53
  39.3 2.9 %collective-permute-start.11 = (f32[128,16]{0,1:T(8,128)S(1)}, f32[128,16]{0,1:T(8,128)S(1)}, u32[]{:S(2)}, u32[]{:S(2)}) collective-permute-start(f32[128,16]{0,1:T(8,128)S(1)} %select_reduce_fusion.1), channel_id=1, source_target_pairs={{0,8},{1,9},{2,10},{3,11},{4,12},{5,13},{6,14},{7,15},{8,0},{9,1},... | collective-permute-start | bytes 24584 | tf_op jit(solution)/shard_map/ppermute | solution.py:93
  43.7 19.1 %collective-permute-done.11 = f32[128,16]{0,1:T(8,128)S(1)} collective-permute-done((f32[128,16]{0,1:T(8,128)S(1)}, f32[128,16]{0,1:T(8,128)S(1)}, u32[]{:S(2)}, u32[]{:S(2)}) %collective-permute-start.11) | collective-permute-done | bytes 8224 | tf_op jit(solution)/shard_map/ppermute | solution.py:93
  64.2 2.4 collective-permute-done.17
  71.0 10.4 %collective-permute-done.6 = bf16[128,2048]{1,0:T(8,128)(2,1)} collective-permute-done((bf16[128,2048]{1,0:T(8,128)(2,1)}, bf16[128,2048]{1,0:T(8,128)(2,1)}, u32[]{:S(2)}, u32[]{:S(2)}) %collective-permute-start.6) | collective-permute-done | bytes 524320 | tf_op jit(solution)/shard_map/ppermute | solution.py:93
  86.4 2.0 copy-done.21
  88.4 16.4 %collective-permute-done.7 = bf16[3,2048,256]{2,1,0:T(8,128)(2,1)} collective-permute-done((bf16[3,2048,256]{2,1,0:T(8,128)(2,1)}, bf16[3,2048,256]{2,1,0:T(8,128)(2,1)}, u32[]{:S(2)}, u32[]{:S(2)}) %collective-permute-start.7) | collective-permute-done | bytes 3145760 | tf_op jit(solution)/shard_map/ppermute | solution.py:54
  106.3 4.4 %select_bitcast_fusion.1 = (bf16[2048,256]{1,0:T(8,128)(2,1)}, bf16[2048,256]{1,0:T(8,128)(2,1)}, bf16[1,2048,256]{2,1,0:T(8,128)(2,1)}, bf16[2048,256]{1,0:T(8,128)(2,1)}, bf16[2048,256]{1,0:T(8,128)(2,1)}) fusion(bf16[1,2048,256]{2,1,0:T(8,128)(2,1)S(1)} %copy-done.4, pred[]{:T(512)S(6)} %eq.36, bf16[3,2048,256]{2,1,0:T(8,128)(2,1)} %collective-permute-done.7, ...), kind=kLoop, calls=%fused_computation.81 | loop fusion | flops 2097152 | bytes 10485761 | tf_op jit(solution)/shard_map/jit(_where)/select_n | solution.py:61
  116.9 21.7 %collective-permute-done.18 = f32[128,16]{0,1:T(8,128)S(1)} collective-permute-done((f32[128,16]{0,1:T(8,128)S(1)}, f32[128,16]{0,1:T(8,128)S(1)}, u32[]{:S(2)}, u32[]{:S(2)}) %collective-permute-start.18) | collective-permute-done | bytes 8224 | tf_op jit(solution)/shard_map/ppermute | solution.py:93
  142.2 2.2 fusion.94
  148.5 2.0 copy-done.23
  150.6 3.7 %fusion.93 = f32[1024,512]{1,0:T(8,128)} fusion(bf16[1024,2048]{1,0:T(8,128)(2,1)S(1)} %constant_dynamic-update-slice_fusion, bf16[2048,512]{1,0:T(8,128)(2,1)S(1)} %get-tuple-element.22), kind=kOutput, calls=%fused_computation.157 | convolution fusion | flops 2147483648 | bytes 8388608 | tf_op jit(solution)/shard_map/dot_general | solution.py:78
  154.2 10.0 %multiply_convert_fusion = bf16[1024,2048]{1,0:T(8,128)(2,1)} fusion(f32[1024]{0:T(1024)S(1)} %select_reduce_fusion, bf16[512,2048]{1,0:T(8,128)(2,1)S(1)} %pad_maximum_fusion.4, f32[1024,512]{1,0:T(8,128)} %fusion.93, bf16[1024,2048]{1,0:T(8,128)(2,1)} %copy-done.23, bf16[2048,512]{1,0:T(8,128)(2,1)} %get-tuple-element.23), kind=kOutput, calls=%fused_computation | convolution fusion | flops 4306501632 | bytes 14684160 | tf_op jit(solution)/shard_map/dot_general | solution.py:81
  164.3 4.2 %fusion.86 = (bf16[128,2048]{1,0:T(8,128)(2,1)}, bf16[128,2048]{1,0:T(8,128)(2,1)}, bf16[128,2048]{1,0:T(8,128)(2,1)}, bf16[128,2048]{1,0:T(8,128)(2,1)}, bf16[1...) fusion(bf16[1024,2048]{1,0:T(8,128)(2,1)} %multiply_convert_fusion), kind=kLoop, calls=%fused_computation.152 | loop fusion | bytes 8388608 | tf_op jit(solution)/shard_map/slice | solution.py:111
  169.5 6.9 %convert_multiply_fusion = f32[512,2048]{1,0:T(8,128)} fusion(bf16[512,2048]{1,0:T(8,128)(2,1)S(1)} %pad_maximum_fusion.4, f32[512]{0:T(512)S(1)} %get-tuple-element.35, f32[512,512]{1,0:T(8,128)} %fusion.94, bf16[512,2048]{1,0:T(8,128)(2,1)} %copy-done.20, bf16[2048,512]{1,0:T(8,128)(2,1)} %get-tuple-element.23), kind=kOutput, calls=%fused_computation.7 | convolution fusion | flops 2152202240 | bytes 11536384 | tf_op jit(solution)/shard_map/dot_general | solution.py:81
  176.4 4.7 %fusion.55 = f32[512,512]{1,0:T(8,128)} fusion(bf16[2048,512]{1,0:T(8,128)(2,1)} %get-tuple-element.23, bf16[128,2048]{1,0:T(8,128)(2,1)} %collective-permute-done.6, bf16[128,2048]{1,0:T(8,128)(2,1)} %collective-permute-done.5, bf16[128,2048]{1,0:T(8,128)(2,1)} %collective-permute-done.4, bf16[128,2048]{1,0:T(8,128)(2,1)} %multiply_convert_fusion.5), kind=kOutput, calls=%fused_computation.96 | convolution fusion | flops 1082130432 | bytes 5242880 | tf_op jit(solution)/shard_map/dot_general | solution.py:79
  181.6 3.3 %fusion.41 = (bf16[128,2048]{1,0:T(8,128)(2,1)}, bf16[128,2048]{1,0:T(8,128)(2,1)}, bf16[128,2048]{1,0:T(8,128)(2,1)}, bf16[128,2048]{1,0:T(8,128)(2,1)}) fusion(f32[512,2048]{1,0:T(8,128)S(1)} %copy-done.3, bf16[128,2048]{1,0:T(8,128)(2,1)} %collective-permute-done.36, bf16[128,2048]{1,0:T(8,128)(2,1)} %collective-permute-done.46, ...), kind=kLoop, calls=%fused_computation.68 | loop fusion | flops 3145728 | bytes 8388608 | tf_op jit(solution)/shard_map/convert_element_type | solution.py:115
  187.0 7.3 %convert_multiply_fusion.1 = f32[512,2048]{1,0:T(8,128)} fusion(bf16[512,2048]{1,0:T(8,128)(2,1)S(1)} %pad_maximum_fusion.4, f32[512]{0:T(512)S(1)} %get-tuple-element.36, f32[512,512]{1,0:T(8,128)} %fusion.55, bf16[2048,512]{1,0:T(8,128)(2,1)} %copy-done.13, bf16[128,2048]{1,0:T(8,128)(2,1)} %collective-permute-done.6, ...), kind=kOutput, calls=%fused_computation.8 | convolution fusion | flops 2160590848 | bytes 11536384 | tf_op jit(solution)/shard_map/dot_general | solution.py:81
  196.0 4.0 %collective-permute-done.40 = bf16[128,2048]{1,0:T(8,128)(2,1)} collective-permute-done((bf16[128,2048]{1,0:T(8,128)(2,1)}, bf16[128,2048]{1,0:T(8,128)(2,1)}, u32[]{:S(2)}, u32[]{:S(2)}) %collective-permute-start.40) | collective-permute-done | bytes 524320 | tf_op jit(solution)/shard_map/ppermute | solution.py:115
  200.0 11.2 %collective-permute-done.47 = bf16[128,2048]{1,0:T(8,128)(2,1)} collective-permute-done((bf16[128,2048]{1,0:T(8,128)(2,1)}, bf16[128,2048]{1,0:T(8,128)(2,1)}, u32[]{:S(2)}, u32[]{:S(2)}) %collective-permute-start.47) | collective-permute-done | bytes 524320 | tf_op jit(solution)/shard_map/ppermute | solution.py:115
  211.3 2.6 %fusion.40 = (bf16[128,2048]{1,0:T(8,128)(2,1)S(1)}, bf16[128,2048]{1,0:T(8,128)(2,1)S(1)}) fusion(f32[512,2048]{1,0:T(8,128)} %convert_multiply_fusion.1, bf16[128,2048]{1,0:T(8,128)(2,1)} %collective-permute-done.40, bf16[128,2048]{1,0:T(8,128)(2,1)} %collective-permute-done.38, bf16[128,2048]{1,0:T(8,128)(2,1)} %collective-permute-done.47, ...), kind=kLoop, calls=%fused_computation.66 | loop fusion | flops 2621440 | bytes 5242880 | tf_op jit(solution)/shard_map/convert_element_type | solution.py:115
  217.6 4.8 %collective-permute-done.44 = bf16[128,2048]{1,0:T(8,128)(2,1)S(1)} collective-permute-done((bf16[128,2048]{1,0:T(8,128)(2,1)}, bf16[128,2048]{1,0:T(8,128)(2,1)S(1)}, u32[]{:S(2)}, u32[]{:S(2)}) %collective-permute-start.44) | collective-permute-done | bytes 524320 | tf_op jit(solution)/shard_map/ppermute | solution.py:115
  222.4 12.0 %collective-permute-done.48 = bf16[128,2048]{1,0:T(8,128)(2,1)S(1)} collective-permute-done((bf16[128,2048]{1,0:T(8,128)(2,1)S(1)}, bf16[128,2048]{1,0:T(8,128)(2,1)S(1)}, u32[]{:S(2)}, u32[]{:S(2)}) %collective-permute-start.48) | collective-permute-done | bytes 524320 | tf_op jit(solution)/shard_map/ppermute | solution.py:115
  234.8 9.2 %collective-permute-done.41 = bf16[128,2048]{1,0:T(8,128)(2,1)S(1)} collective-permute-done((bf16[128,2048]{1,0:T(8,128)(2,1)S(1)}, bf16[128,2048]{1,0:T(8,128)(2,1)S(1)}, u32[]{:S(2)}, u32[]{:S(2)}) %collective-permute-start.41) | collective-permute-done | bytes 524320 | tf_op jit(solution)/shard_map/ppermute | solution.py:115
  244.0 10.3 %collective-permute-done.49 = bf16[128,2048]{1,0:T(8,128)(2,1)S(1)} collective-permute-done((bf16[128,2048]{1,0:T(8,128)(2,1)S(1)}, bf16[128,2048]{1,0:T(8,128)(2,1)S(1)}, u32[]{:S(2)}, u32[]{:S(2)}) %collective-permute-start.49) | collective-permute-done | bytes 524320 | tf_op jit(solution)/shard_map/ppermute | solution.py:115
  (193 shorter events, 53.1 us)
Async XLA Ops:
  1.3 14.2 %collective-permute-start = (bf16[128,1024]{0,1:T(8,128)(2,1)S(1)}, bf16[128,1024]{0,1:T(8,128)(2,1)}, u32[]{:S(2)}, u32[]{:S(2)}) collective-permute-start(bf16[128,1024]{0,1:T(8,128)(2,1)S(1)} %bitcast.101), channel_id=1, source_target_pairs={{0,16},{16,0},{1,17},{17,1},{2,18},{18,2},{3,19},{19,3},{4,20},{20... | collective-permute-start | bytes 786440 | tf_op jit(solution)/shard_map/ppermute | solution.py:273
  36.3 68.4 %collective-permute-start.7 = (bf16[3,2048,256]{2,1,0:T(8,128)(2,1)}, bf16[3,2048,256]{2,1,0:T(8,128)(2,1)}, u32[]{:S(2)}, u32[]{:S(2)}) collective-permute-start(bf16[3,2048,256]{2,1,0:T(8,128)(2,1)} %pad_maximum_fusion), channel_id=1, source_target_pairs={{0,16},{16,0},{1,17},{17,1},{2,18},{18,2},{3,19},{19,3},{4,20},{20... | collective-permute-start | bytes 9437192 | tf_op jit(solution)/shard_map/ppermute | solution.py:54
  38.7 28.5 %collective-permute-start.4 = (bf16[128,2048]{1,0:T(8,128)(2,1)}, bf16[128,2048]{1,0:T(8,128)(2,1)}, u32[]{:S(2)}, u32[]{:S(2)}) collective-permute-start(bf16[128,2048]{1,0:T(8,128)(2,1)} %multiply_convert_fusion.5), channel_id=1, source_target_pairs={{0,8},{1,9},{2,10},{3,11},{4,12},{5,13},{6,14},{7,15},{8,0},{9,1},... | collective-permute-start | bytes 1572872 | tf_op jit(solution)/shard_map/ppermute | solution.py:93
  39.0 30.1 %collective-permute-start.5 = (bf16[128,2048]{1,0:T(8,128)(2,1)}, bf16[128,2048]{1,0:T(8,128)(2,1)}, u32[]{:S(2)}, u32[]{:S(2)}) collective-permute-start(bf16[128,2048]{1,0:T(8,128)(2,1)} %multiply_convert_fusion.5), channel_id=1, source_target_pairs={{0,4},{1,5},{2,6},{3,7},{4,0},{5,1},{6,2},{7,3},{8,12},{9,13},{10,... | collective-permute-start | bytes 1572872 | tf_op jit(solution)/shard_map/ppermute | solution.py:93
  39.3 23.6 %collective-permute-start.11 = (f32[128,16]{0,1:T(8,128)S(1)}, f32[128,16]{0,1:T(8,128)S(1)}, u32[]{:S(2)}, u32[]{:S(2)}) collective-permute-start(f32[128,16]{0,1:T(8,128)S(1)} %select_reduce_fusion.1), channel_id=1, source_target_pairs={{0,8},{1,9},{2,10},{3,11},{4,12},{5,13},{6,14},{7,15},{8,0},{9,1},... | collective-permute-start | bytes 24584 | tf_op jit(solution)/shard_map/ppermute | solution.py:93
  42.2 20.8 %collective-permute-start.14 = (f32[128,16]{0,1:T(8,128)S(1)}, f32[128,16]{0,1:T(8,128)S(1)}, u32[]{:S(2)}, u32[]{:S(2)}) collective-permute-start(f32[128,16]{0,1:T(8,128)S(1)} %select_reduce_fusion.1), channel_id=1, source_target_pairs={{0,4},{1,5},{2,6},{3,7},{4,0},{5,1},{6,2},{7,3},{8,12},{9,13},{10,... | collective-permute-start | bytes 24584 | tf_op jit(solution)/shard_map/ppermute | solution.py:93
  67.2 14.2 %collective-permute-start.6 = (bf16[128,2048]{1,0:T(8,128)(2,1)}, bf16[128,2048]{1,0:T(8,128)(2,1)}, u32[]{:S(2)}, u32[]{:S(2)}) collective-permute-start(bf16[128,2048]{1,0:T(8,128)(2,1)} %collective-permute-done.4), channel_id=1, source_target_pairs={{0,4},{1,5},{2,6},{3,7},{4,0},{5,1},{6,2},{7,3},{8,12},{9,13},{10,... | collective-permute-start | bytes 1572872 | tf_op jit(solution)/shard_map/ppermute | solution.py:93
  69.0 13.5 %collective-permute-start.20 = (bf16[128,2048]{1,0:T(8,128)(2,1)}, bf16[128,2048]{1,0:T(8,128)(2,1)S(1)}, u32[]{:S(2)}, u32[]{:S(2)}) collective-permute-start(bf16[128,2048]{1,0:T(8,128)(2,1)} %collective-permute-done.4), channel_id=1, source_target_pairs={{0,1},{1,0},{2,3},{3,2},{4,5},{5,4},{6,7},{7,6},{8,9},{9,8},{10,11... | collective-permute-start | bytes 1572872 | tf_op jit(solution)/shard_map/ppermute | solution.py:93
  69.2 14.9 %collective-permute-start.21 = (bf16[128,2048]{1,0:T(8,128)(2,1)}, bf16[128,2048]{1,0:T(8,128)(2,1)S(1)}, u32[]{:S(2)}, u32[]{:S(2)}) collective-permute-start(bf16[128,2048]{1,0:T(8,128)(2,1)} %collective-permute-done.5), channel_id=1, source_target_pairs={{0,1},{1,0},{2,3},{3,2},{4,5},{5,4},{6,7},{7,6},{8,9},{9,8},{10,11... | collective-permute-start | bytes 1572872 | tf_op jit(solution)/shard_map/ppermute | solution.py:93
  69.5 43.0 %collective-permute-start.9 = (f32[128,16]{0,1:T(8,128)S(1)}, f32[128,16]{0,1:T(8,128)S(1)}, u32[]{:S(2)}, u32[]{:S(2)}) collective-permute-start(f32[128,16]{0,1:T(8,128)S(1)} %select_reduce_fusion.1), channel_id=1, source_target_pairs={{0,2},{1,3},{2,0},{3,1},{4,6},{5,7},{6,4},{7,5},{8,10},{9,11},{10,... | collective-permute-start | bytes 24584 | tf_op jit(solution)/shard_map/ppermute | solution.py:93
  82.5 30.6 %collective-permute-start.12 = (f32[128,16]{0,1:T(8,128)S(1)}, f32[128,16]{0,1:T(8,128)S(1)}, u32[]{:S(2)}, u32[]{:S(2)}) collective-permute-start(f32[128,16]{0,1:T(8,128)S(1)} %collective-permute-done.11), channel_id=1, source_target_pairs={{0,2},{1,3},{2,0},{3,1},{4,6},{5,7},{6,4},{7,5},{8,10},{9,11},{10,... | collective-permute-start | bytes 24584 | tf_op jit(solution)/shard_map/ppermute | solution.py:93
  84.1 32.2 %collective-permute-start.15 = (f32[128,16]{0,1:T(8,128)S(1)}, f32[128,16]{0,1:T(8,128)S(1)}, u32[]{:S(2)}, u32[]{:S(2)}) collective-permute-start(f32[128,16]{0,1:T(8,128)S(1)} %collective-permute-done.14), channel_id=1, source_target_pairs={{0,2},{1,3},{2,0},{3,1},{4,6},{5,7},{6,4},{7,5},{8,10},{9,11},{10,... | collective-permute-start | bytes 24584 | tf_op jit(solution)/shard_map/ppermute | solution.py:93
  84.7 53.9 %collective-permute-start.8 = (bf16[128,2048]{1,0:T(8,128)(2,1)}, bf16[128,2048]{1,0:T(8,128)(2,1)}, u32[]{:S(2)}, u32[]{:S(2)}) collective-permute-start(bf16[128,2048]{1,0:T(8,128)(2,1)} %multiply_convert_fusion.5), channel_id=1, source_target_pairs={{0,2},{1,3},{2,0},{3,1},{4,6},{5,7},{6,4},{7,5},{8,10},{9,11},{10,... | collective-permute-start | bytes 1572872 | tf_op jit(solution)/shard_map/ppermute | solution.py:93
  104.8 33.9 %collective-permute-start.10 = (bf16[128,2048]{1,0:T(8,128)(2,1)}, bf16[128,2048]{1,0:T(8,128)(2,1)}, u32[]{:S(2)}, u32[]{:S(2)}) collective-permute-start(bf16[128,2048]{1,0:T(8,128)(2,1)} %collective-permute-done.4), channel_id=1, source_target_pairs={{0,2},{1,3},{2,0},{3,1},{4,6},{5,7},{6,4},{7,5},{8,10},{9,11},{10,... | collective-permute-start | bytes 1572872 | tf_op jit(solution)/shard_map/ppermute | solution.py:93
  112.5 26.2 %collective-permute-start.13 = (bf16[128,2048]{1,0:T(8,128)(2,1)}, bf16[128,2048]{1,0:T(8,128)(2,1)S(1)}, u32[]{:S(2)}, u32[]{:S(2)}) collective-permute-start(bf16[128,2048]{1,0:T(8,128)(2,1)} %collective-permute-done.5), channel_id=1, source_target_pairs={{0,2},{1,3},{2,0},{3,1},{4,6},{5,7},{6,4},{7,5},{8,10},{9,11},{10,... | collective-permute-start | bytes 1572872 | tf_op jit(solution)/shard_map/ppermute | solution.py:93
  113.1 25.6 %collective-permute-start.16 = (bf16[128,2048]{1,0:T(8,128)(2,1)}, bf16[128,2048]{1,0:T(8,128)(2,1)S(1)}, u32[]{:S(2)}, u32[]{:S(2)}) collective-permute-start(bf16[128,2048]{1,0:T(8,128)(2,1)} %collective-permute-done.6), channel_id=1, source_target_pairs={{0,2},{1,3},{2,0},{3,1},{4,6},{5,7},{6,4},{7,5},{8,10},{9,11},{10,... | collective-permute-start | bytes 1572872 | tf_op jit(solution)/shard_map/ppermute | solution.py:93
  116.3 22.3 %collective-permute-start.18 = (f32[128,16]{0,1:T(8,128)S(1)}, f32[128,16]{0,1:T(8,128)S(1)}, u32[]{:S(2)}, u32[]{:S(2)}) collective-permute-start(f32[128,16]{0,1:T(8,128)S(1)} %collective-permute-done.17), channel_id=1, source_target_pairs={{0,2},{1,3},{2,0},{3,1},{4,6},{5,7},{6,4},{7,5},{8,10},{9,11},{10,... | collective-permute-start | bytes 24584 | tf_op jit(solution)/shard_map/ppermute | solution.py:93
  168.5 13.0 %collective-permute-start.36 = (bf16[128,2048]{1,0:T(8,128)(2,1)}, bf16[128,2048]{1,0:T(8,128)(2,1)}, u32[]{:S(2)}, u32[]{:S(2)}) collective-permute-start(bf16[128,2048]{1,0:T(8,128)(2,1)} %get-tuple-element.47), channel_id=1, source_target_pairs={{1,0},{0,1},{3,2},{2,3},{5,4},{4,5},{7,6},{6,7},{9,8},{8,9},{11,10... | collective-permute-start | bytes 1572872 | tf_op jit(solution)/shard_map/ppermute | solution.py:115
  168.9 12.7 %collective-permute-start.39 = (bf16[128,2048]{1,0:T(8,128)(2,1)}, bf16[128,2048]{1,0:T(8,128)(2,1)}, u32[]{:S(2)}, u32[]{:S(2)}) collective-permute-start(bf16[128,2048]{1,0:T(8,128)(2,1)} %get-tuple-element.45), channel_id=1, source_target_pairs={{1,0},{0,1},{3,2},{2,3},{5,4},{4,5},{7,6},{6,7},{9,8},{8,9},{11,10... | collective-permute-start | bytes 1572872 | tf_op jit(solution)/shard_map/ppermute | solution.py:115
  169.0 12.6 %collective-permute-start.43 = (bf16[128,2048]{1,0:T(8,128)(2,1)}, bf16[128,2048]{1,0:T(8,128)(2,1)}, u32[]{:S(2)}, u32[]{:S(2)}) collective-permute-start(bf16[128,2048]{1,0:T(8,128)(2,1)} %get-tuple-element.43), channel_id=1, source_target_pairs={{1,0},{0,1},{3,2},{2,3},{5,4},{4,5},{7,6},{6,7},{9,8},{8,9},{11,10... | collective-permute-start | bytes 1572872 | tf_op jit(solution)/shard_map/ppermute | solution.py:115
  169.4 12.2 %collective-permute-start.46 = (bf16[128,2048]{1,0:T(8,128)(2,1)}, bf16[128,2048]{1,0:T(8,128)(2,1)}, u32[]{:S(2)}, u32[]{:S(2)}) collective-permute-start(bf16[128,2048]{1,0:T(8,128)(2,1)} %get-tuple-element.41), channel_id=1, source_target_pairs={{1,0},{0,1},{3,2},{2,3},{5,4},{4,5},{7,6},{6,7},{9,8},{8,9},{11,10... | collective-permute-start | bytes 1572872 | tf_op jit(solution)/shard_map/ppermute | solution.py:115
  181.1 13.3 %collective-permute-start.38 = (bf16[128,2048]{1,0:T(8,128)(2,1)}, bf16[128,2048]{1,0:T(8,128)(2,1)}, u32[]{:S(2)}, u32[]{:S(2)}) collective-permute-start(bf16[128,2048]{1,0:T(8,128)(2,1)} %get-tuple-element.46), channel_id=1, source_target_pairs={{1,0},{0,1},{3,2},{2,3},{5,4},{4,5},{7,6},{6,7},{9,8},{8,9},{11,10... | collective-permute-start | bytes 1572872 | tf_op jit(solution)/shard_map/ppermute | solution.py:115
  181.5 14.5 %collective-permute-start.45 = (bf16[128,2048]{1,0:T(8,128)(2,1)}, bf16[128,2048]{1,0:T(8,128)(2,1)}, u32[]{:S(2)}, u32[]{:S(2)}) collective-permute-start(bf16[128,2048]{1,0:T(8,128)(2,1)} %get-tuple-element.42), channel_id=1, source_target_pairs={{1,0},{0,1},{3,2},{2,3},{5,4},{4,5},{7,6},{6,7},{9,8},{8,9},{11,10... | collective-permute-start | bytes 1572872 | tf_op jit(solution)/shard_map/ppermute | solution.py:115
  185.0 15.1 %collective-permute-start.40 = (bf16[128,2048]{1,0:T(8,128)(2,1)}, bf16[128,2048]{1,0:T(8,128)(2,1)}, u32[]{:S(2)}, u32[]{:S(2)}) collective-permute-start(bf16[128,2048]{1,0:T(8,128)(2,1)} %get-tuple-element.51), channel_id=1, source_target_pairs={{2,0},{3,1},{0,2},{1,3},{6,4},{7,5},{4,6},{5,7},{10,8},{11,9},{8,1... | collective-permute-start | bytes 1572872 | tf_op jit(solution)/shard_map/ppermute | solution.py:115
  186.5 24.8 %collective-permute-start.47 = (bf16[128,2048]{1,0:T(8,128)(2,1)}, bf16[128,2048]{1,0:T(8,128)(2,1)}, u32[]{:S(2)}, u32[]{:S(2)}) collective-permute-start(bf16[128,2048]{1,0:T(8,128)(2,1)} %get-tuple-element.49), channel_id=1, source_target_pairs={{2,0},{3,1},{0,2},{1,3},{6,4},{7,5},{4,6},{5,7},{10,8},{11,9},{8,1... | collective-permute-start | bytes 1572872 | tf_op jit(solution)/shard_map/ppermute | solution.py:115
  194.3 21.7 %collective-permute-start.42 = (bf16[128,2048]{1,0:T(8,128)(2,1)}, bf16[128,2048]{1,0:T(8,128)(2,1)S(1)}, u32[]{:S(2)}, u32[]{:S(2)}) collective-permute-start(bf16[128,2048]{1,0:T(8,128)(2,1)} %get-tuple-element.44), channel_id=1, source_target_pairs={{1,0},{0,1},{3,2},{2,3},{5,4},{4,5},{7,6},{6,7},{9,8},{8,9},{11,10... | collective-permute-start | bytes 1572872 | tf_op jit(solution)/shard_map/ppermute | solution.py:115
  194.4 28.0 %collective-permute-start.44 = (bf16[128,2048]{1,0:T(8,128)(2,1)}, bf16[128,2048]{1,0:T(8,128)(2,1)S(1)}, u32[]{:S(2)}, u32[]{:S(2)}) collective-permute-start(bf16[128,2048]{1,0:T(8,128)(2,1)} %get-tuple-element.50), channel_id=1, source_target_pairs={{2,0},{3,1},{0,2},{1,3},{6,4},{7,5},{4,6},{5,7},{10,8},{11,9},{8,1... | collective-permute-start | bytes 1572872 | tf_op jit(solution)/shard_map/ppermute | solution.py:115
  213.9 20.5 %collective-permute-start.48 = (bf16[128,2048]{1,0:T(8,128)(2,1)S(1)}, bf16[128,2048]{1,0:T(8,128)(2,1)S(1)}, u32[]{:S(2)}, u32[]{:S(2)}) collective-permute-start(bf16[128,2048]{1,0:T(8,128)(2,1)S(1)} %get-tuple-element.53), channel_id=1, source_target_pairs={{4,0},{5,1},{6,2},{7,3},{0,4},{1,5},{2,6},{3,7},{12,8},{13,9},{14,... | collective-permute-start | bytes 1572872 | tf_op jit(solution)/shard_map/ppermute | solution.py:115
  214.4 20.4 %collective-permute-start.35 = (bf16[128,2048]{1,0:T(8,128)(2,1)S(1)}, bf16[128,2048]{1,0:T(8,128)(2,1)S(1)}, u32[]{:S(2)}, u32[]{:S(2)}) collective-permute-start(bf16[128,2048]{1,0:T(8,128)(2,1)S(1)} %copy-done.16), channel_id=1, source_target_pairs={{1,0},{0,1},{3,2},{2,3},{5,4},{4,5},{7,6},{6,7},{9,8},{8,9},{11,10... | collective-permute-start | bytes 1572872 | tf_op jit(solution)/shard_map/ppermute | solution.py:115
  214.4 20.4 %collective-permute-start.37 = (bf16[128,2048]{1,0:T(8,128)(2,1)S(1)}, bf16[128,2048]{1,0:T(8,128)(2,1)S(1)}, u32[]{:S(2)}, u32[]{:S(2)}) collective-permute-start(bf16[128,2048]{1,0:T(8,128)(2,1)S(1)} %copy-done.17), channel_id=1, source_target_pairs={{2,0},{3,1},{0,2},{1,3},{6,4},{7,5},{4,6},{5,7},{10,8},{11,9},{8,1... | collective-permute-start | bytes 1572872 | tf_op jit(solution)/shard_map/ppermute | solution.py:115
  216.0 28.0 %collective-permute-start.41 = (bf16[128,2048]{1,0:T(8,128)(2,1)S(1)}, bf16[128,2048]{1,0:T(8,128)(2,1)S(1)}, u32[]{:S(2)}, u32[]{:S(2)}) collective-permute-start(bf16[128,2048]{1,0:T(8,128)(2,1)S(1)} %get-tuple-element.52), channel_id=1, source_target_pairs={{4,0},{5,1},{6,2},{7,3},{0,4},{1,5},{2,6},{3,7},{12,8},{13,9},{14,... | collective-permute-start | bytes 1572872 | tf_op jit(solution)/shard_map/ppermute | solution.py:115
  234.7 19.6 %collective-permute-start.49 = (bf16[128,2048]{1,0:T(8,128)(2,1)S(1)}, bf16[128,2048]{1,0:T(8,128)(2,1)S(1)}, u32[]{:S(2)}, u32[]{:S(2)}) collective-permute-start(bf16[128,2048]{1,0:T(8,128)(2,1)S(1)} %fusion.37), channel_id=1, source_target_pairs={{8,0},{9,1},{10,2},{11,3},{12,4},{13,5},{14,6},{15,7},{0,8},{1,9},... | collective-permute-start | bytes 1572872 | tf_op jit(solution)/shard_map/ppermute | solution.py:115
  (46 other events, 333.8 us)

commit v8 on v7

--- a/solution.py
+++ b/solution.py
@@ -82,38 +82,45 @@
         out_rows = out_rows.astype(jnp.bfloat16).astype(jnp.float32)
         return out_rows * weights[:, None]
 
-    pieces = [((normed, weight_table), None, None)]
-    groups = []
-    low = 0
-    tie_at = next((n + 1 for n, (_, ends) in enumerate(plan) if ends), 0)
-    for number, (pairs_list, ends) in enumerate(plan):
-        grown = []
-        for parent, (block, _, _) in enumerate(pieces):
-            for pairs in pairs_list:
-                grown.append((lax.ppermute(block, "ep", pairs), parent, pairs))
-        if number == tie_at:
-            tied = lax.optimization_barrier((tuple(full), [piece[0] for piece in grown]))
-            full = list(tied[0])
-            grown = [(block, parent, pairs) for block, (_, parent, pairs) in zip(tied[1], grown)]
-        pieces = pieces + grown
-        if ends:
-            groups.append((low, len(pieces)))
-            low = len(pieces)
-    if low < len(pieces) or not groups:
-        groups.append((low, len(pieces)))
+    pieces = [((normed, weight_table), None, None, -1)]
+    waves = [[0]]
+    tie_at = min(2, len(plan) - 1)
+    while True:
+        fresh = []
+        for parent in waves[-1]:
+            block, _, _, last = pieces[parent]
+            for stage in range(last + 1, len(plan)):
+                for pairs in plan[stage][0]:
+                    fresh.append((lax.ppermute(block, "ep", pairs), parent, pairs, stage))
+        if not fresh:
+            break
+        blocks = [piece[0] for piece in fresh]
+        if len(waves) == tie_at + 1:
+            full, blocks = lax.optimization_barrier((tuple(full), blocks))
+            full = list(full)
+        else:
+            blocks = lax.optimization_barrier(blocks)
+        waves.append(list(range(len(pieces), len(pieces) + len(fresh))))
+        pieces += [(b,) + piece[1:] for b, piece in zip(blocks, fresh)]
     partial = [None] * len(pieces)
     size = normed.shape[0]
-    for low, high in groups:
-        rows = jnp.concatenate([pieces[i][0][0] for i in range(low, high)], axis=0)
-        table = jnp.concatenate([pieces[i][0][1] for i in range(low, high)], axis=0)
+    groups = [[0] + waves[1]] + waves[2:] if len(waves) > 1 else [[0]]
+    for group in groups:
+        rows = jnp.concatenate([pieces[i][0][0] for i in group], axis=0)
+        table = jnp.concatenate([pieces[i][0][1] for i in group], axis=0)
         out = expert(rows, table)
-        for offset, i in enumerate(range(low, high)):
+        for offset, i in enumerate(group):
             partial[i] = out[offset * size:(offset + 1) * size]
-    for index in reversed(range(1, len(pieces))):
-        _, parent, pairs = pieces[index]
-        back = [(target, source) for source, target in pairs]
-        sent = lax.ppermute(partial[index].astype(jnp.bfloat16), "ep", back)
-        partial[parent] = partial[parent] + sent.astype(jnp.float32)
+    for wave in reversed(waves[1:]):
+        sent = []
+        for index in wave:
+            _, parent, pairs, _ = pieces[index]
+            back = [(target, source) for source, target in pairs]
+            sent.append(lax.ppermute(partial[index].astype(jnp.bfloat16), "ep", back))
+        sent = lax.optimization_barrier(sent)
+        for index, value in zip(wave, sent):
+            parent = pieces[index][1]
+            partial[parent] = partial[parent] + value.astype(jnp.float32)
     return partial[0], anchor
 
 

time: 259 us -> 269 us (1.039)
  matrix products: 46.4 us -> 52.2 us
  waiting for transfers between devices: 132 us -> 127 us
  starting transfers between devices: 33.1 us -> 37.5 us
  local copies, waits for them, and re-layouts: 21.3 us -> 25 us
    ppermute x45, waiting for transfers between devices: 109 us -> 90.9 us  [the longest x30 51.7 us: dense_moe(): fresh.append((lax.ppermute(block, 'ep', pairs), parent, pairs, stage))]
    ppermute x1, waiting for transfers between devices: 16.4 us -> 28.9 us  [full_weights(): other = lax.ppermute(packed, 'kv', [(0, 1), (1, 0)])]
    dot_general x3 -> x4, matrix products: 24.2 us -> 31.3 us  [expert(): out_rows = jnp.dot(act, full[2], preferred_element_type=jnp.float32)]
    dot_general x2 -> x4, matrix products: 5.9 us -> 11.4 us  [expert(): gate_val = jnp.dot(rows, full[0], preferred_element_type=jnp.float32)]
    dot_general x1 -> x0, matrix products: 4.67 us -> none  [expert(): up_val = jnp.dot(rows, full[1], preferred_element_type=jnp.float32)]
    ppermute x45, starting transfers between devices: 28.3 us -> 32.6 us  [the longest x30 21 us: dense_moe(): fresh.append((lax.ppermute(block, 'ep', pairs), parent, pairs, stage))]
    convert_element_type x4 -> x3, other arithmetic: 7.19 us -> 8.18 us  [dense_moe(): sent.append(lax.ppermute(partial[index].astype(jnp.bfloat16), 'ep', back))]
    unnamed x79 -> x76, local copies, waits for them, and re-layouts: 14.7 us -> 15.6 us
  transfers between devices with their start and end apart: 50 -> 50, of which waited for: 19 -> 17; matrix products, arithmetic and copies ran while one was open for 22% -> 36% of each run, Pallas kernels for 0% -> 0%
where the time goes in v8:
time: 269 us; the launch traced here: 266 us
  waiting for transfers between devices  127 us (47%)
  matrix products  52.2 us (19%)
  starting transfers between devices  37.5 us (14%)
  local copies, waits for them, and re-layouts  25 us (9%)
  other arithmetic  23 us (9%)
    ppermute x30, waiting for transfers between devices, dense_moe(): fresh.append((lax.ppermute(block, 'ep', pairs), parent, pairs, stage))  51.7 us
    ppermute x15, waiting for transfers between devices, dense_moe(): sent.append(lax.ppermute(partial[index].astype(jnp.bfloat16), 'ep', back))  39.2 us
    dot_general x4, matrix products, expert(): out_rows = jnp.dot(act, full[2], preferred_element_type=jnp.float32)  31.3 us
    ppermute x1, waiting for transfers between devices, full_weights(): other = lax.ppermute(packed, 'kv', [(0, 1), (1, 0)])  28.9 us
    ppermute x30, starting transfers between devices, dense_moe(): fresh.append((lax.ppermute(block, 'ep', pairs), parent, pairs, stage))  21 us
    unnamed x76, local copies, waits for them, and re-layouts  15.6 us
    ppermute x15, starting transfers between devices, dense_moe(): sent.append(lax.ppermute(partial[index].astype(jnp.bfloat16), 'ep', back))  11.6 us
    dot_general x4, matrix products, expert(): gate_val = jnp.dot(rows, full[0], preferred_element_type=jnp.float32)  11.4 us
  transfers between devices with their start and end apart: 50, of which 17 were waited for; matrix products, arithmetic and copies ran while one was open for 36% of the time, Pallas kernels for 0%

profile of v8, /device:TPU:24, one launch (start us, length us, event | category | flops | bytes accessed | tf_op | source)
XLA Modules:
  0.0 265.9 jit_solution(6310981881172328802)
XLA Ops:
  9.0 2.0 copy.104
  13.2 2.4 bitcast_reduce_fusion.1
  15.6 1.7 fusion.13
  19.3 1.7 fusion.11
  26.4 5.8 %collective-permute-done.2 = bf16[128,8,128]{0,2,1:T(8,128)(2,1)S(1)} collective-permute-done((bf16[128,8,128]{0,2,1:T(8,128)(2,1)S(1)}, bf16[128,8,128]{0,2,1:T(8,128)(2,1)S(1)}, u32[]{:S(2)}, u32[]{:S(2)}) %collective-permute-start.2) | collective-permute-done | bytes 262176 | tf_op jit(solution)/shard_map/ppermute | solution.py:290
  37.9 21.5 %collective-permute-done.7 = f32[128,16]{0,1:T(8,128)S(1)} collective-permute-done((f32[128,16]{0,1:T(8,128)S(1)}, f32[128,16]{0,1:T(8,128)S(1)}, u32[]{:S(2)}, u32[]{:S(2)}) %collective-permute-start.7) | collective-permute-done | bytes 8224 | tf_op jit(solution)/shard_map/ppermute | solution.py:94
  61.1 1.9 pad_maximum_fusion
  70.1 2.1 collective-permute-done.20
  78.0 1.7 collective-permute-start.13
  82.0 9.1 %collective-permute-done.19 = bf16[128,2048]{1,0:T(8,128)(2,1)} collective-permute-done((bf16[128,2048]{1,0:T(8,128)(2,1)}, bf16[128,2048]{1,0:T(8,128)(2,1)}, u32[]{:S(2)}, u32[]{:S(2)}) %collective-permute-start.19) | collective-permute-done | bytes 524320 | tf_op jit(solution)/shard_map/ppermute | solution.py:94
  91.1 8.7 %collective-permute-done.15 = bf16[128,2048]{1,0:T(8,128)(2,1)} collective-permute-done((bf16[128,2048]{1,0:T(8,128)(2,1)}, bf16[128,2048]{1,0:T(8,128)(2,1)}, u32[]{:S(2)}, u32[]{:S(2)}) %collective-permute-start.15) | collective-permute-done | bytes 524320 | tf_op jit(solution)/shard_map/ppermute | solution.py:94
  103.4 28.9 %collective-permute-done.12 = bf16[3,2048,256]{2,1,0:T(8,128)(2,1)S(1)} collective-permute-done((bf16[3,2048,256]{2,1,0:T(8,128)(2,1)S(1)}, bf16[3,2048,256]{2,1,0:T(8,128)(2,1)S(1)}, u32[]{:S(2)}, u32[]{:S(2)}) %collective-permute-start.12) | collective-permute-done | bytes 3145760 | tf_op jit(solution)/shard_map/ppermute | solution.py:54
  132.4 2.4 select_bitcast_fusion.1
  143.3 8.2 %collective-permute-done.26 = f32[128,16]{0,1:T(8,128)S(1)} collective-permute-done((f32[128,16]{0,1:T(8,128)S(1)}, f32[128,16]{0,1:T(8,128)S(1)}, u32[]{:S(2)}, u32[]{:S(2)}) %collective-permute-start.26) | collective-permute-done | bytes 8224 | tf_op jit(solution)/shard_map/ppermute | solution.py:94
  155.4 2.2 fusion.101
  157.7 8.3 %fusion.89 = (bf16[512,2048]{1,0:T(8,128)(2,1)}, f32[512,2048]{1,0:T(8,128)}) fusion(f32[512]{0:T(512)S(1)} %fusion.71, bf16[512,2048]{1,0:T(8,128)(2,1)} %pad_maximum_fusion.3, f32[512,512]{1,0:T(8,128)} %fusion.101, bf16[512,2048]{1,0:T(8,128)(2,1)} %copy-done.16, bf16[2048,512]{1,0:T(8,128)(2,1)} %get-tuple-element.72), kind=kOutput, calls=%fused_computation.166 | convolution fusion | flops 2153250816 | bytes 13633536 | tf_op jit(solution)/shard_map/dot_general | solution.py:81
  166.0 5.1 %fusion.100 = f32[768,512]{1,0:T(8,128)} fusion(bf16[768,2048]{1,0:T(8,128)(2,1)} %copy-done.20, bf16[2048,512]{1,0:T(8,128)(2,1)S(1)} %get-tuple-element.71), kind=kOutput, calls=%fused_computation.173 | convolution fusion | flops 1610612736 | bytes 6815744 | tf_op jit(solution)/shard_map/dot_general | solution.py:78
  174.4 4.0 %fusion.10 = bf16[128,2048]{1,0:T(8,128)(2,1)} fusion(bf16[512,2048]{1,0:T(8,128)(2,1)} %pad_maximum_fusion.3, f32[128]{0:T(128)S(1)} %select_reduce_fusion.3, f32[128,512]{1,0:T(8,128)S(1)} %fusion.102, bf16[128,2048]{1,0:T(8,128)(2,1)} %collective-permute-done.33, bf16[2048,512]{1,0:T(8,128)(2,1)} %get-tuple-element.72), kind=kOutput, calls=%fused_computation.25 | convolution fusion | flops 538312704 | bytes 5505536 | tf_op jit(solution)/shard_map/dot_general | solution.py:81
  178.9 10.7 %fusion.90 = (bf16[768,2048]{1,0:T(8,128)(2,1)}, f32[768,2048]{1,0:T(8,128)}) fusion(f32[768]{0:T(1024)S(1)} %select_reduce_fusion.1, bf16[512,2048]{1,0:T(8,128)(2,1)} %pad_maximum_fusion.3, f32[768,512]{1,0:T(8,128)} %fusion.100, bf16[768,2048]{1,0:T(8,128)(2,1)} %copy-done.20, bf16[2048,512]{1,0:T(8,128)(2,1)} %get-tuple-element.72), kind=kOutput, calls=%fused_computation.167 | convolution fusion | flops 3229876224 | bytes 18353152 | tf_op jit(solution)/shard_map/dot_general | solution.py:81
  192.8 2.7 %fusion.85 = (bf16[128,2048]{1,0:T(8,128)(2,1)S(1)}, bf16[128,2048]{1,0:T(8,128)(2,1)}, bf16[128,2048]{1,0:T(8,128)(2,1)}) fusion(bf16[768,2048]{1,0:T(8,128)(2,1)} %get-tuple-element.144), kind=kLoop, calls=%fused_computation.162 | loop fusion | bytes 3145728 | tf_op jit(solution)/shard_map/slice | solution.py:113
  195.6 2.6 fusion.99
  198.8 6.4 %collective-permute-done.36 = bf16[128,2048]{1,0:T(8,128)(2,1)S(1)} collective-permute-done((bf16[128,2048]{1,0:T(8,128)(2,1)S(1)}, bf16[128,2048]{1,0:T(8,128)(2,1)S(1)}, u32[]{:S(2)}, u32[]{:S(2)}) %collective-permute-start.36) | collective-permute-done | bytes 524320 | tf_op jit(solution)/shard_map/ppermute | solution.py:119
  205.2 3.1 %fusion.37 = (bf16[128,2048]{1,0:T(8,128)(2,1)}, bf16[128,2048]{1,0:T(8,128)(2,1)}, bf16[128,2048]{1,0:T(8,128)(2,1)}) fusion(f32[768,2048]{1,0:T(8,128)S(1)} %bitcast.101, bf16[128,2048]{1,0:T(8,128)(2,1)} %collective-permute-done.39, bf16[128,2048]{1,0:T(8,128)(2,1)} %collective-permute-done.38, bf16[128,2048]{1,0:T(8,128)(2,1)} %collective-permute-done.37, ...), kind=kLoop, calls=%fused_computation.63 | loop fusion | flops 2883584 | bytes 6815744 | tf_op jit(solution)/shard_map/convert_element_type | solution.py:119
  211.1 1.8 collective-permute-start.40
  212.8 8.3 %convert_multiply_fusion.1 = f32[640,2048]{1,0:T(8,128)} fusion(bf16[512,2048]{1,0:T(8,128)(2,1)S(1)} %copy-done.10, f32[640]{0:T(1024)S(1)} %select_reduce_fusion.2, f32[640,512]{1,0:T(8,128)} %fusion.99, bf16[640,2048]{1,0:T(8,128)(2,1)} %copy-done.18, bf16[2048,512]{1,0:T(8,128)(2,1)} %get-tuple-element.72), kind=kOutput, calls=%fused_computation.1 | convolution fusion | flops 2690252800 | bytes 13371904 | tf_op jit(solution)/shard_map/dot_general | solution.py:81
  223.4 9.4 %collective-permute-done.41 = bf16[128,2048]{1,0:T(8,128)(2,1)} collective-permute-done((bf16[128,2048]{1,0:T(8,128)(2,1)}, bf16[128,2048]{1,0:T(8,128)(2,1)}, u32[]{:S(2)}, u32[]{:S(2)}) %collective-permute-start.41) | collective-permute-done | bytes 524320 | tf_op jit(solution)/shard_map/ppermute | solution.py:119
  232.8 3.5 %fusion.34 = (bf16[128,2048]{1,0:T(8,128)(2,1)S(1)}, bf16[128,2048]{1,0:T(8,128)(2,1)S(1)}, bf16[128,2048]{1,0:T(8,128)(2,1)S(1)}) fusion(f32[640,2048]{1,0:T(8,128)} %convert_multiply_fusion.1, bf16[128,2048]{1,0:T(8,128)(2,1)} %copy-done.15, bf16[128,2048]{1,0:T(8,128)(2,1)} %collective-permute-done.44, bf16[128,2048]{1,0:T(8,128)(2,1)} %collective-permute-done.43, ...), kind=kLoop, calls=%fused_computation.58 | loop fusion | flops 3932160 | bytes 7864320 | tf_op jit(solution)/shard_map/convert_element_type | solution.py:119
  237.9 1.7 collective-permute-start.47
  240.9 7.6 %collective-permute-done.48 = bf16[128,2048]{1,0:T(8,128)(2,1)S(1)} collective-permute-done((bf16[128,2048]{1,0:T(8,128)(2,1)S(1)}, bf16[128,2048]{1,0:T(8,128)(2,1)S(1)}, u32[]{:S(2)}, u32[]{:S(2)}) %collective-permute-start.48) | collective-permute-done | bytes 524320 | tf_op jit(solution)/shard_map/ppermute | solution.py:119
  248.4 11.2 %collective-permute-done.47 = bf16[128,2048]{1,0:T(8,128)(2,1)S(1)} collective-permute-done((bf16[128,2048]{1,0:T(8,128)(2,1)S(1)}, bf16[128,2048]{1,0:T(8,128)(2,1)S(1)}, u32[]{:S(2)}, u32[]{:S(2)}) %collective-permute-start.47) | collective-permute-done | bytes 524320 | tf_op jit(solution)/shard_map/ppermute | solution.py:119
  259.7 3.7 %collective-permute-done.46 = bf16[128,2048]{1,0:T(8,128)(2,1)S(1)} collective-permute-done((bf16[128,2048]{1,0:T(8,128)(2,1)S(1)}, bf16[128,2048]{1,0:T(8,128)(2,1)S(1)}, u32[]{:S(2)}, u32[]{:S(2)}) %collective-permute-start.46) | collective-permute-done | bytes 524320 | tf_op jit(solution)/shard_map/ppermute | solution.py:119
  263.4 2.5 fusion.52
  (199 shorter events, 71.6 us)
Async XLA Ops:
  0.9 34.6 %collective-permute-start.11 = (f32[128,16]{0,1:T(8,128)S(1)}, f32[128,16]{0,1:T(8,128)S(1)}, u32[]{:S(2)}, u32[]{:S(2)}) collective-permute-start(f32[128,16]{0,1:T(8,128)S(1)} %select_reduce_fusion), channel_id=1, source_target_pairs={{0,1},{1,0},{2,3},{3,2},{4,5},{5,4},{6,7},{7,6},{8,9},{9,8},{10,11... | collective-permute-start | bytes 24584 | tf_op jit(solution)/shard_map/ppermute | solution.py:94
  0.9 34.9 %collective-permute-start.9 = (f32[128,16]{0,1:T(8,128)S(1)}, f32[128,16]{0,1:T(8,128)S(1)}, u32[]{:S(2)}, u32[]{:S(2)}) collective-permute-start(f32[128,16]{0,1:T(8,128)S(1)} %select_reduce_fusion), channel_id=1, source_target_pairs={{0,2},{1,3},{2,0},{3,1},{4,6},{5,7},{6,4},{7,5},{8,10},{9,11},{10,... | collective-permute-start | bytes 24584 | tf_op jit(solution)/shard_map/ppermute | solution.py:94
  34.5 30.1 %collective-permute-start.10 = (bf16[128,2048]{1,0:T(8,128)(2,1)}, bf16[128,2048]{1,0:T(8,128)(2,1)}, u32[]{:S(2)}, u32[]{:S(2)}) collective-permute-start(bf16[128,2048]{1,0:T(8,128)(2,1)} %get-tuple-element.108), channel_id=1, source_target_pairs={{0,1},{1,0},{2,3},{3,2},{4,5},{5,4},{6,7},{7,6},{8,9},{9,8},{10,11... | collective-permute-start | bytes 1572872 | tf_op jit(solution)/shard_map/ppermute | solution.py:94
  34.5 30.1 %collective-permute-start.8 = (bf16[128,2048]{1,0:T(8,128)(2,1)}, bf16[128,2048]{1,0:T(8,128)(2,1)}, u32[]{:S(2)}, u32[]{:S(2)}) collective-permute-start(bf16[128,2048]{1,0:T(8,128)(2,1)} %get-tuple-element.108), channel_id=1, source_target_pairs={{0,2},{1,3},{2,0},{3,1},{4,6},{5,7},{6,4},{7,5},{8,10},{9,11},{10,... | collective-permute-start | bytes 1572872 | tf_op jit(solution)/shard_map/ppermute | solution.py:94
  35.0 29.6 %collective-permute-start.6 = (bf16[128,2048]{1,0:T(8,128)(2,1)}, bf16[128,2048]{1,0:T(8,128)(2,1)}, u32[]{:S(2)}, u32[]{:S(2)}) collective-permute-start(bf16[128,2048]{1,0:T(8,128)(2,1)} %get-tuple-element.108), channel_id=1, source_target_pairs={{0,4},{1,5},{2,6},{3,7},{4,0},{5,1},{6,2},{7,3},{8,12},{9,13},{10,... | collective-permute-start | bytes 1572872 | tf_op jit(solution)/shard_map/ppermute | solution.py:94
  35.5 29.1 %collective-permute-start.4 = (bf16[128,2048]{1,0:T(8,128)(2,1)}, bf16[128,2048]{1,0:T(8,128)(2,1)}, u32[]{:S(2)}, u32[]{:S(2)}) collective-permute-start(bf16[128,2048]{1,0:T(8,128)(2,1)} %get-tuple-element.108), channel_id=1, source_target_pairs={{0,8},{1,9},{2,10},{3,11},{4,12},{5,13},{6,14},{7,15},{8,0},{9,1},... | collective-permute-start | bytes 1572872 | tf_op jit(solution)/shard_map/ppermute | solution.py:94
  35.8 23.6 %collective-permute-start.7 = (f32[128,16]{0,1:T(8,128)S(1)}, f32[128,16]{0,1:T(8,128)S(1)}, u32[]{:S(2)}, u32[]{:S(2)}) collective-permute-start(f32[128,16]{0,1:T(8,128)S(1)} %select_reduce_fusion), channel_id=1, source_target_pairs={{0,4},{1,5},{2,6},{3,7},{4,0},{5,1},{6,2},{7,3},{8,12},{9,13},{10,... | collective-permute-start | bytes 24584 | tf_op jit(solution)/shard_map/ppermute | solution.py:94
  64.0 68.4 %collective-permute-start.12 = (bf16[3,2048,256]{2,1,0:T(8,128)(2,1)S(1)}, bf16[3,2048,256]{2,1,0:T(8,128)(2,1)S(1)}, u32[]{:S(2)}, u32[]{:S(2)}) collective-permute-start(bf16[3,2048,256]{2,1,0:T(8,128)(2,1)S(1)} %pad_maximum_fusion), channel_id=1, source_target_pairs={{0,16},{16,0},{1,17},{17,1},{2,18},{18,2},{3,19},{19,3},{4,20},{20... | collective-permute-start | bytes 9437192 | tf_op jit(solution)/shard_map/ppermute | solution.py:54
  75.9 15.2 %collective-permute-start.19 = (bf16[128,2048]{1,0:T(8,128)(2,1)}, bf16[128,2048]{1,0:T(8,128)(2,1)}, u32[]{:S(2)}, u32[]{:S(2)}) collective-permute-start(bf16[128,2048]{1,0:T(8,128)(2,1)} %collective-permute-done.6), channel_id=1, source_target_pairs={{0,2},{1,3},{2,0},{3,1},{4,6},{5,7},{6,4},{7,5},{8,10},{9,11},{10,... | collective-permute-start | bytes 1572872 | tf_op jit(solution)/shard_map/ppermute | solution.py:94
  77.4 22.3 %collective-permute-start.15 = (bf16[128,2048]{1,0:T(8,128)(2,1)}, bf16[128,2048]{1,0:T(8,128)(2,1)}, u32[]{:S(2)}, u32[]{:S(2)}) collective-permute-start(bf16[128,2048]{1,0:T(8,128)(2,1)} %collective-permute-done.4), channel_id=1, source_target_pairs={{0,2},{1,3},{2,0},{3,1},{4,6},{5,7},{6,4},{7,5},{8,10},{9,11},{10,... | collective-permute-start | bytes 1572872 | tf_op jit(solution)/shard_map/ppermute | solution.py:94
  78.0 21.7 %collective-permute-start.13 = (bf16[128,2048]{1,0:T(8,128)(2,1)}, bf16[128,2048]{1,0:T(8,128)(2,1)S(1)}, u32[]{:S(2)}, u32[]{:S(2)}) collective-permute-start(bf16[128,2048]{1,0:T(8,128)(2,1)} %collective-permute-done.4), channel_id=1, source_target_pairs={{0,4},{1,5},{2,6},{3,7},{4,0},{5,1},{6,2},{7,3},{8,12},{9,13},{10,... | collective-permute-start | bytes 1572872 | tf_op jit(solution)/shard_map/ppermute | solution.py:94
  99.7 36.8 %collective-permute-start.30 = (f32[128,16]{0,1:T(8,128)S(1)}, f32[128,16]{0,1:T(8,128)S(1)}, u32[]{:S(2)}, u32[]{:S(2)}) collective-permute-start(f32[128,16]{0,1:T(8,128)S(1)} %collective-permute-done.16), channel_id=1, source_target_pairs={{0,1},{1,0},{2,3},{3,2},{4,5},{5,4},{6,7},{7,6},{8,9},{9,8},{10,11... | collective-permute-start | bytes 24584 | tf_op jit(solution)/shard_map/ppermute | solution.py:94
  99.7 37.4 %collective-permute-start.32 = (f32[128,16]{0,1:T(8,128)S(1)}, f32[128,16]{0,1:T(8,128)S(1)}, u32[]{:S(2)}, u32[]{:S(2)}) collective-permute-start(f32[128,16]{0,1:T(8,128)S(1)} %collective-permute-done.20), channel_id=1, source_target_pairs={{0,1},{1,0},{2,3},{3,2},{4,5},{5,4},{6,7},{7,6},{8,9},{9,8},{10,11... | collective-permute-start | bytes 24584 | tf_op jit(solution)/shard_map/ppermute | solution.py:94
  100.2 40.1 %collective-permute-start.28 = (f32[128,16]{0,1:T(8,128)S(1)}, f32[128,16]{0,1:T(8,128)S(1)}, u32[]{:S(2)}, u32[]{:S(2)}) collective-permute-start(f32[128,16]{0,1:T(8,128)S(1)} %collective-permute-done.14), channel_id=1, source_target_pairs={{0,1},{1,0},{2,3},{3,2},{4,5},{5,4},{6,7},{7,6},{8,9},{9,8},{10,11... | collective-permute-start | bytes 24584 | tf_op jit(solution)/shard_map/ppermute | solution.py:94
  100.3 51.1 %collective-permute-start.29 = (bf16[128,2048]{1,0:T(8,128)(2,1)}, bf16[128,2048]{1,0:T(8,128)(2,1)}, u32[]{:S(2)}, u32[]{:S(2)}) collective-permute-start(bf16[128,2048]{1,0:T(8,128)(2,1)} %collective-permute-done.15), channel_id=1, source_target_pairs={{0,1},{1,0},{2,3},{3,2},{4,5},{5,4},{6,7},{7,6},{8,9},{9,8},{10,11... | collective-permute-start | bytes 1572872 | tf_op jit(solution)/shard_map/ppermute | solution.py:94
  132.4 19.1 %collective-permute-start.31 = (bf16[128,2048]{1,0:T(8,128)(2,1)}, bf16[128,2048]{1,0:T(8,128)(2,1)}, u32[]{:S(2)}, u32[]{:S(2)}) collective-permute-start(bf16[128,2048]{1,0:T(8,128)(2,1)} %collective-permute-done.19), channel_id=1, source_target_pairs={{0,1},{1,0},{2,3},{3,2},{4,5},{5,4},{6,7},{7,6},{8,9},{9,8},{10,11... | collective-permute-start | bytes 1572872 | tf_op jit(solution)/shard_map/ppermute | solution.py:94
  136.6 14.9 %collective-permute-start.27 = (bf16[128,2048]{1,0:T(8,128)(2,1)}, bf16[128,2048]{1,0:T(8,128)(2,1)S(1)}, u32[]{:S(2)}, u32[]{:S(2)}) collective-permute-start(bf16[128,2048]{1,0:T(8,128)(2,1)} %copy-done.14), channel_id=1, source_target_pairs={{0,1},{1,0},{2,3},{3,2},{4,5},{5,4},{6,7},{7,6},{8,9},{9,8},{10,11... | collective-permute-start | bytes 1572872 | tf_op jit(solution)/shard_map/ppermute | solution.py:94
  137.1 14.3 %collective-permute-start.25 = (bf16[128,2048]{1,0:T(8,128)(2,1)}, bf16[128,2048]{1,0:T(8,128)(2,1)}, u32[]{:S(2)}, u32[]{:S(2)}) collective-permute-start(bf16[128,2048]{1,0:T(8,128)(2,1)} %copy-done.14), channel_id=1, source_target_pairs={{0,2},{1,3},{2,0},{3,1},{4,6},{5,7},{6,4},{7,5},{8,10},{9,11},{10,... | collective-permute-start | bytes 1572872 | tf_op jit(solution)/shard_map/ppermute | solution.py:94
  151.5 21.3 %collective-permute-start.33 = (bf16[128,2048]{1,0:T(8,128)(2,1)}, bf16[128,2048]{1,0:T(8,128)(2,1)}, u32[]{:S(2)}, u32[]{:S(2)}) collective-permute-start(bf16[128,2048]{1,0:T(8,128)(2,1)} %collective-permute-done.25), channel_id=1, source_target_pairs={{0,1},{1,0},{2,3},{3,2},{4,5},{5,4},{6,7},{7,6},{8,9},{9,8},{10,11... | collective-permute-start | bytes 1572872 | tf_op jit(solution)/shard_map/ppermute | solution.py:94
  152.6 20.2 %collective-permute-start.34 = (f32[128,16]{0,1:T(8,128)S(1)}, f32[128,16]{0,1:T(8,128)S(1)}, u32[]{:S(2)}, u32[]{:S(2)}) collective-permute-start(f32[128,16]{0,1:T(8,128)S(1)} %collective-permute-done.26), channel_id=1, source_target_pairs={{0,1},{1,0},{2,3},{3,2},{4,5},{5,4},{6,7},{7,6},{8,9},{9,8},{10,11... | collective-permute-start | bytes 24584 | tf_op jit(solution)/shard_map/ppermute | solution.py:94
  172.3 25.9 %collective-permute-start.39 = (bf16[128,2048]{1,0:T(8,128)(2,1)}, bf16[128,2048]{1,0:T(8,128)(2,1)}, u32[]{:S(2)}, u32[]{:S(2)}) collective-permute-start(bf16[128,2048]{1,0:T(8,128)(2,1)} %get-tuple-element.128), channel_id=1, source_target_pairs={{1,0},{0,1},{3,2},{2,3},{5,4},{4,5},{7,6},{6,7},{9,8},{8,9},{11,10... | collective-permute-start | bytes 1572872 | tf_op jit(solution)/shard_map/ppermute | solution.py:119
  172.3 26.4 %collective-permute-start.38 = (bf16[128,2048]{1,0:T(8,128)(2,1)}, bf16[128,2048]{1,0:T(8,128)(2,1)}, u32[]{:S(2)}, u32[]{:S(2)}) collective-permute-start(bf16[128,2048]{1,0:T(8,128)(2,1)} %get-tuple-element.129), channel_id=1, source_target_pairs={{1,0},{0,1},{3,2},{2,3},{5,4},{4,5},{7,6},{6,7},{9,8},{8,9},{11,10... | collective-permute-start | bytes 1572872 | tf_op jit(solution)/shard_map/ppermute | solution.py:119
  172.8 26.0 %collective-permute-start.37 = (bf16[128,2048]{1,0:T(8,128)(2,1)}, bf16[128,2048]{1,0:T(8,128)(2,1)}, u32[]{:S(2)}, u32[]{:S(2)}) collective-permute-start(bf16[128,2048]{1,0:T(8,128)(2,1)} %get-tuple-element.130), channel_id=1, source_target_pairs={{1,0},{0,1},{3,2},{2,3},{5,4},{4,5},{7,6},{6,7},{9,8},{8,9},{11,10... | collective-permute-start | bytes 1572872 | tf_op jit(solution)/shard_map/ppermute | solution.py:119
  195.6 14.7 %collective-permute-start.45 = (bf16[128,2048]{1,0:T(8,128)(2,1)S(1)}, bf16[128,2048]{1,0:T(8,128)(2,1)S(1)}, u32[]{:S(2)}, u32[]{:S(2)}) collective-permute-start(bf16[128,2048]{1,0:T(8,128)(2,1)S(1)} %get-tuple-element.122), channel_id=1, source_target_pairs={{1,0},{0,1},{3,2},{2,3},{5,4},{4,5},{7,6},{6,7},{9,8},{8,9},{11,10... | collective-permute-start | bytes 1572872 | tf_op jit(solution)/shard_map/ppermute | solution.py:119
  198.2 24.3 %collective-permute-start.44 = (bf16[128,2048]{1,0:T(8,128)(2,1)}, bf16[128,2048]{1,0:T(8,128)(2,1)}, u32[]{:S(2)}, u32[]{:S(2)}) collective-permute-start(bf16[128,2048]{1,0:T(8,128)(2,1)} %get-tuple-element.123), channel_id=1, source_target_pairs={{1,0},{0,1},{3,2},{2,3},{5,4},{4,5},{7,6},{6,7},{9,8},{8,9},{11,10... | collective-permute-start | bytes 1572872 | tf_op jit(solution)/shard_map/ppermute | solution.py:119
  198.7 23.8 %collective-permute-start.42 = (bf16[128,2048]{1,0:T(8,128)(2,1)}, bf16[128,2048]{1,0:T(8,128)(2,1)}, u32[]{:S(2)}, u32[]{:S(2)}) collective-permute-start(bf16[128,2048]{1,0:T(8,128)(2,1)} %get-tuple-element.124), channel_id=1, source_target_pairs={{1,0},{0,1},{3,2},{2,3},{5,4},{4,5},{7,6},{6,7},{9,8},{8,9},{11,10... | collective-permute-start | bytes 1572872 | tf_op jit(solution)/shard_map/ppermute | solution.py:119
  208.3 15.2 %collective-permute-start.43 = (bf16[128,2048]{1,0:T(8,128)(2,1)}, bf16[128,2048]{1,0:T(8,128)(2,1)}, u32[]{:S(2)}, u32[]{:S(2)}) collective-permute-start(bf16[128,2048]{1,0:T(8,128)(2,1)} %get-tuple-element.112), channel_id=1, source_target_pairs={{2,0},{3,1},{0,2},{1,3},{6,4},{7,5},{4,6},{5,7},{10,8},{11,9},{8,1... | collective-permute-start | bytes 1572872 | tf_op jit(solution)/shard_map/ppermute | solution.py:119
  209.8 23.0 %collective-permute-start.41 = (bf16[128,2048]{1,0:T(8,128)(2,1)}, bf16[128,2048]{1,0:T(8,128)(2,1)}, u32[]{:S(2)}, u32[]{:S(2)}) collective-permute-start(bf16[128,2048]{1,0:T(8,128)(2,1)} %get-tuple-element.113), channel_id=1, source_target_pairs={{2,0},{3,1},{0,2},{1,3},{6,4},{7,5},{4,6},{5,7},{10,8},{11,9},{8,1... | collective-permute-start | bytes 1572872 | tf_op jit(solution)/shard_map/ppermute | solution.py:119
  211.1 21.7 %collective-permute-start.40 = (bf16[128,2048]{1,0:T(8,128)(2,1)}, bf16[128,2048]{1,0:T(8,128)(2,1)}, u32[]{:S(2)}, u32[]{:S(2)}) collective-permute-start(bf16[128,2048]{1,0:T(8,128)(2,1)} %get-tuple-element.114), channel_id=1, source_target_pairs={{4,0},{5,1},{6,2},{7,3},{0,4},{1,5},{2,6},{3,7},{12,8},{13,9},{14,... | collective-permute-start | bytes 1572872 | tf_op jit(solution)/shard_map/ppermute | solution.py:119
  222.4 18.4 %collective-permute-start.49 = (bf16[128,2048]{1,0:T(8,128)(2,1)S(1)}, bf16[128,2048]{1,0:T(8,128)(2,1)S(1)}, u32[]{:S(2)}, u32[]{:S(2)}) collective-permute-start(bf16[128,2048]{1,0:T(8,128)(2,1)S(1)} %slice.144), channel_id=1, source_target_pairs={{1,0},{0,1},{3,2},{2,3},{5,4},{4,5},{7,6},{6,7},{9,8},{8,9},{11,10... | collective-permute-start | bytes 1572872 | tf_op jit(solution)/shard_map/ppermute | solution.py:119
  237.9 21.8 %collective-permute-start.47 = (bf16[128,2048]{1,0:T(8,128)(2,1)S(1)}, bf16[128,2048]{1,0:T(8,128)(2,1)S(1)}, u32[]{:S(2)}, u32[]{:S(2)}) collective-permute-start(bf16[128,2048]{1,0:T(8,128)(2,1)S(1)} %get-tuple-element.116), channel_id=1, source_target_pairs={{4,0},{5,1},{6,2},{7,3},{0,4},{1,5},{2,6},{3,7},{12,8},{13,9},{14,... | collective-permute-start | bytes 1572872 | tf_op jit(solution)/shard_map/ppermute | solution.py:119
  239.7 23.7 %collective-permute-start.46 = (bf16[128,2048]{1,0:T(8,128)(2,1)S(1)}, bf16[128,2048]{1,0:T(8,128)(2,1)S(1)}, u32[]{:S(2)}, u32[]{:S(2)}) collective-permute-start(bf16[128,2048]{1,0:T(8,128)(2,1)S(1)} %get-tuple-element.117), channel_id=1, source_target_pairs={{8,0},{9,1},{10,2},{11,3},{12,4},{13,5},{14,6},{15,7},{0,8},{1,9},... | collective-permute-start | bytes 1572872 | tf_op jit(solution)/shard_map/ppermute | solution.py:119
  (43 other events, 381.9 us)

commit v9 on v8

--- a/solution.py
+++ b/solution.py
@@ -70,7 +70,6 @@
     own_expert = lax.axis_index("ep")
     chosen = route_ids[:, :, None] == experts[None, None, :]
     weight_table = jnp.sum(jnp.where(chosen, route_weights[:, :, None], 0.0), axis=1)
-    weight_parts, anchor = lax.optimization_barrier((weight_parts, anchor))
     full = list(full_weights(*weight_parts))
 
     def expert(rows, table):
@@ -84,7 +83,7 @@
 
     pieces = [((normed, weight_table), None, None, -1)]
     waves = [[0]]
-    tie_at = min(2, len(plan) - 1)
+    tie_at = min(1, len(plan) - 1)
     while True:
         fresh = []
         for parent in waves[-1]:

time: 269 us -> 266 us (0.989)
  starting transfers between devices: 37.5 us -> 27.8 us
  local copies, waits for them, and re-layouts: 25 us -> 34.2 us
    unnamed x76, local copies, waits for them, and re-layouts: 15.6 us -> 25 us
    ppermute x30, starting transfers between devices: 21 us -> 14.6 us  [dense_moe(): fresh.append((lax.ppermute(block, 'ep', pairs), parent, pairs, stage))]
    ppermute x15, waiting for transfers between devices: 39.2 us -> 43.3 us  [dense_moe(): sent.append(lax.ppermute(partial[index].astype(jnp.bfloat16), 'ep', back))]
    ppermute x30, waiting for transfers between devices: 51.7 us -> 48 us  [dense_moe(): fresh.append((lax.ppermute(block, 'ep', pairs), parent, pairs, stage))]
    ppermute x15, starting transfers between devices: 11.6 us -> 8.38 us  [dense_moe(): sent.append(lax.ppermute(partial[index].astype(jnp.bfloat16), 'ep', back))]
    dot_general x4, matrix products: 11.4 us -> 8.36 us  [expert(): gate_val = jnp.dot(rows, full[0], preferred_element_type=jnp.float32)]
  transfers between devices with their start and end apart: 50 -> 50, of which waited for: 17 -> 17; matrix products, arithmetic and copies ran while one was open for 36% -> 38% of each run, Pallas kernels for 0% -> 0%
where the time goes in v9:
time: 266 us; the launch traced here: 264 us
  waiting for transfers between devices  126 us (47%)
  matrix products  51.1 us (19%)
  local copies, waits for them, and re-layouts  34.2 us (13%)
  starting transfers between devices  27.8 us (10%)
  other arithmetic  23.8 us (9%)
    ppermute x30, waiting for transfers between devices, dense_moe(): fresh.append((lax.ppermute(block, 'ep', pairs), parent, pairs, stage))  48 us
    ppermute x15, waiting for transfers between devices, dense_moe(): sent.append(lax.ppermute(partial[index].astype(jnp.bfloat16), 'ep', back))  43.3 us
    dot_general x4, matrix products, expert(): out_rows = jnp.dot(act, full[2], preferred_element_type=jnp.float32)  31.2 us
    ppermute x1, waiting for transfers between devices, full_weights(): other = lax.ppermute(packed, 'kv', [(0, 1), (1, 0)])  28.8 us
    unnamed x76, local copies, waits for them, and re-layouts  25 us
    ppermute x30, starting transfers between devices, dense_moe(): fresh.append((lax.ppermute(block, 'ep', pairs), parent, pairs, stage))  14.6 us
    ppermute x15, starting transfers between devices, dense_moe(): sent.append(lax.ppermute(partial[index].astype(jnp.bfloat16), 'ep', back))  8.38 us
    dot_general x4, matrix products, expert(): gate_val = jnp.dot(rows, full[0], preferred_element_type=jnp.float32)  8.36 us
  transfers between devices with their start and end apart: 50, of which 17 were waited for; matrix products, arithmetic and copies ran while one was open for 38% of the time, Pallas kernels for 0%

profile of v9, /device:TPU:24, one launch (start us, length us, event | category | flops | bytes accessed | tf_op | source)
XLA Modules:
  0.0 264.4 jit_solution(17126848319722620132)
XLA Ops:
  10.7 3.7 %copy.104 = bf16[128,8,8,128]{3,2,1,0:T(8,128)(2,1)} copy(bf16[128,8,8,128]{3,1,2,0:T(8,128)(2,1)} %bitcast.94) | data formatting | bytes 4194304
  14.4 2.0 copy.103
  17.9 2.6 bitcast_reduce_fusion.1
  22.3 2.0 pad_maximum_fusion
  25.5 2.6 fusion.2
  36.1 5.0 %collective-permute-done.2 = bf16[128,8,128]{0,2,1:T(8,128)(2,1)S(1)} collective-permute-done((bf16[128,8,128]{0,2,1:T(8,128)(2,1)S(1)}, bf16[128,8,128]{0,2,1:T(8,128)(2,1)S(1)}, u32[]{:S(2)}, u32[]{:S(2)}) %collective-permute-start.2) | collective-permute-done | bytes 262176 | tf_op jit(solution)/shard_map/ppermute | solution.py:289
  46.2 12.4 %collective-permute-done.8 = bf16[128,2048]{1,0:T(8,128)(2,1)} collective-permute-done((bf16[128,2048]{1,0:T(8,128)(2,1)}, bf16[128,2048]{1,0:T(8,128)(2,1)}, u32[]{:S(2)}, u32[]{:S(2)}) %collective-permute-start.8) | collective-permute-done | bytes 524320 | tf_op jit(solution)/shard_map/ppermute | solution.py:93
  58.6 10.2 %collective-permute-done.6 = bf16[128,2048]{1,0:T(8,128)(2,1)} collective-permute-done((bf16[128,2048]{1,0:T(8,128)(2,1)}, bf16[128,2048]{1,0:T(8,128)(2,1)}, u32[]{:S(2)}, u32[]{:S(2)}) %collective-permute-start.6) | collective-permute-done | bytes 524320 | tf_op jit(solution)/shard_map/ppermute | solution.py:93
  68.8 2.4 collective-permute-done.4
  73.3 1.9 constant_dynamic-update-slice_fusion.3
  75.2 1.9 constant_dynamic-update-slice_fusion.2
  77.1 1.9 constant_dynamic-update-slice_fusion.1
  79.0 1.9 constant_dynamic-update-slice_fusion
  80.9 28.8 %collective-permute-done.12 = bf16[3,2048,256]{2,1,0:T(8,128)(2,1)} collective-permute-done((bf16[3,2048,256]{2,1,0:T(8,128)(2,1)}, bf16[3,2048,256]{2,1,0:T(8,128)(2,1)}, u32[]{:S(2)}, u32[]{:S(2)}) %collective-permute-start.12) | collective-permute-done | bytes 3145760 | tf_op jit(solution)/shard_map/ppermute | solution.py:54
  110.3 4.4 %select_bitcast_fusion.1 = (bf16[2048,256]{1,0:T(8,128)(2,1)}, bf16[2048,256]{1,0:T(8,128)(2,1)}, bf16[1,2048,256]{2,1,0:T(8,128)(2,1)}, bf16[2048,256]{1,0:T(8,128)(2,1)}, bf16[2048,256]{1,0:T(8,128)(2,1)}) fusion(bf16[1,2048,256]{2,1,0:T(8,128)(2,1)S(1)} %copy-done.2, pred[]{:T(512)S(6)} %eq.42, bf16[3,2048,256]{2,1,0:T(8,128)(2,1)} %collective-permute-done.12, ...), kind=kLoop, calls=%fused_computation.85 | loop fusion | flops 2097152 | bytes 10485761 | tf_op jit(solution)/shard_map/jit(_where)/select_n | solution.py:61
  125.2 7.4 %collective-permute-done.19 = bf16[128,2048]{1,0:T(8,128)(2,1)} collective-permute-done((bf16[128,2048]{1,0:T(8,128)(2,1)}, bf16[128,2048]{1,0:T(8,128)(2,1)}, u32[]{:S(2)}, u32[]{:S(2)}) %collective-permute-start.19) | collective-permute-done | bytes 524320 | tf_op jit(solution)/shard_map/ppermute | solution.py:93
  132.7 10.4 %collective-permute-done.15 = bf16[128,2048]{1,0:T(8,128)(2,1)} collective-permute-done((bf16[128,2048]{1,0:T(8,128)(2,1)}, bf16[128,2048]{1,0:T(8,128)(2,1)}, u32[]{:S(2)}, u32[]{:S(2)}) %collective-permute-start.15) | collective-permute-done | bytes 524320 | tf_op jit(solution)/shard_map/ppermute | solution.py:93
  148.7 3.0 %fusion.100 = f32[768,512]{1,0:T(8,128)} fusion(bf16[768,2048]{1,0:T(8,128)(2,1)S(1)} %constant_dynamic-update-slice_fusion.10, bf16[2048,512]{1,0:T(8,128)(2,1)S(1)} %get-tuple-element.59), kind=kOutput, calls=%fused_computation.173 | convolution fusion | flops 1610612736 | bytes 6815744 | tf_op jit(solution)/shard_map/dot_general | solution.py:77
  152.9 10.8 %fusion.90 = (bf16[768,2048]{1,0:T(8,128)(2,1)}, f32[768,2048]{1,0:T(8,128)}) fusion(f32[768]{0:T(1024)S(1)} %select_reduce_fusion.1, bf16[512,2048]{1,0:T(8,128)(2,1)} %pad_maximum_fusion.3, f32[768,512]{1,0:T(8,128)} %fusion.100, bf16[768,2048]{1,0:T(8,128)(2,1)} %copy-done.20, bf16[2048,512]{1,0:T(8,128)(2,1)} %get-tuple-element.60), kind=kOutput, calls=%fused_computation.167 | convolution fusion | flops 3229876224 | bytes 18353152 | tf_op jit(solution)/shard_map/dot_general | solution.py:80
  163.7 3.1 %collective-permute-done.25 = bf16[128,2048]{1,0:T(8,128)(2,1)} collective-permute-done((bf16[128,2048]{1,0:T(8,128)(2,1)}, bf16[128,2048]{1,0:T(8,128)(2,1)}, u32[]{:S(2)}, u32[]{:S(2)}) %collective-permute-start.25) | collective-permute-done | bytes 524320 | tf_op jit(solution)/shard_map/ppermute | solution.py:93
  171.7 2.3 fusion.101
  175.4 4.0 %fusion.10 = bf16[128,2048]{1,0:T(8,128)(2,1)} fusion(bf16[512,2048]{1,0:T(8,128)(2,1)} %pad_maximum_fusion.3, f32[128]{0:T(128)S(1)} %select_reduce_fusion.3, f32[128,512]{1,0:T(8,128)S(1)} %fusion.102, bf16[128,2048]{1,0:T(8,128)(2,1)} %copy-done.16, bf16[2048,512]{1,0:T(8,128)(2,1)} %get-tuple-element.60), kind=kOutput, calls=%fused_computation.25 | convolution fusion | flops 538312704 | bytes 5505536 | tf_op jit(solution)/shard_map/dot_general | solution.py:80
  179.4 8.3 %fusion.89 = (bf16[512,2048]{1,0:T(8,128)(2,1)}, f32[512,2048]{1,0:T(8,128)}) fusion(f32[512]{0:T(512)S(1)} %fusion.71, bf16[512,2048]{1,0:T(8,128)(2,1)} %pad_maximum_fusion.3, f32[512,512]{1,0:T(8,128)} %fusion.101, bf16[512,2048]{1,0:T(8,128)(2,1)} %copy-done.18, bf16[2048,512]{1,0:T(8,128)(2,1)} %get-tuple-element.60), kind=kOutput, calls=%fused_computation.166 | convolution fusion | flops 2153250816 | bytes 13633536 | tf_op jit(solution)/shard_map/dot_general | solution.py:80
  193.8 2.6 fusion.99
  197.0 9.1 %collective-permute-done.36 = bf16[128,2048]{1,0:T(8,128)(2,1)S(1)} collective-permute-done((bf16[128,2048]{1,0:T(8,128)(2,1)S(1)}, bf16[128,2048]{1,0:T(8,128)(2,1)S(1)}, u32[]{:S(2)}, u32[]{:S(2)}) %collective-permute-start.36) | collective-permute-done | bytes 524320 | tf_op jit(solution)/shard_map/ppermute | solution.py:118
  212.2 8.0 %convert_multiply_fusion.1 = f32[640,2048]{1,0:T(8,128)} fusion(bf16[512,2048]{1,0:T(8,128)(2,1)S(1)} %copy-done.10, f32[640]{0:T(1024)S(1)} %select_reduce_fusion.2, f32[640,512]{1,0:T(8,128)} %fusion.99, bf16[640,2048]{1,0:T(8,128)(2,1)} %constant_dynamic-update-slice_fusion, bf16[2048,512]{1,0:T(8,128)(2,1)} %get-tuple-element.60), kind=kOutput, calls=%fused_computation.1 | convolution fusion | flops 2690252800 | bytes 13371904 | tf_op jit(solution)/shard_map/dot_general | solution.py:80
  223.0 9.4 %collective-permute-done.41 = bf16[128,2048]{1,0:T(8,128)(2,1)} collective-permute-done((bf16[128,2048]{1,0:T(8,128)(2,1)}, bf16[128,2048]{1,0:T(8,128)(2,1)}, u32[]{:S(2)}, u32[]{:S(2)}) %collective-permute-start.41) | collective-permute-done | bytes 524320 | tf_op jit(solution)/shard_map/ppermute | solution.py:118
  232.4 3.5 %fusion.34 = (bf16[128,2048]{1,0:T(8,128)(2,1)S(1)}, bf16[128,2048]{1,0:T(8,128)(2,1)S(1)}, bf16[128,2048]{1,0:T(8,128)(2,1)S(1)}) fusion(f32[640,2048]{1,0:T(8,128)} %convert_multiply_fusion.1, bf16[128,2048]{1,0:T(8,128)(2,1)} %copy-done.17, bf16[128,2048]{1,0:T(8,128)(2,1)} %collective-permute-done.44, bf16[128,2048]{1,0:T(8,128)(2,1)} %collective-permute-done.43, ...), kind=kLoop, calls=%fused_computation.58 | loop fusion | flops 3932160 | bytes 7864320 | tf_op jit(solution)/shard_map/convert_element_type | solution.py:118
  238.4 9.7 %collective-permute-done.48 = bf16[128,2048]{1,0:T(8,128)(2,1)S(1)} collective-permute-done((bf16[128,2048]{1,0:T(8,128)(2,1)S(1)}, bf16[128,2048]{1,0:T(8,128)(2,1)S(1)}, u32[]{:S(2)}, u32[]{:S(2)}) %collective-permute-start.48) | collective-permute-done | bytes 524320 | tf_op jit(solution)/shard_map/ppermute | solution.py:118
  248.1 9.1 %collective-permute-done.47 = bf16[128,2048]{1,0:T(8,128)(2,1)S(1)} collective-permute-done((bf16[128,2048]{1,0:T(8,128)(2,1)S(1)}, bf16[128,2048]{1,0:T(8,128)(2,1)S(1)}, u32[]{:S(2)}, u32[]{:S(2)}) %collective-permute-start.47) | collective-permute-done | bytes 524320 | tf_op jit(solution)/shard_map/ppermute | solution.py:118
  257.2 4.7 %collective-permute-done.46 = bf16[128,2048]{1,0:T(8,128)(2,1)S(1)} collective-permute-done((bf16[128,2048]{1,0:T(8,128)(2,1)S(1)}, bf16[128,2048]{1,0:T(8,128)(2,1)S(1)}, u32[]{:S(2)}, u32[]{:S(2)}) %collective-permute-start.46) | collective-permute-done | bytes 524320 | tf_op jit(solution)/shard_map/ppermute | solution.py:118
  261.9 2.5 fusion.52
  (199 shorter events, 71.4 us)
Async XLA Ops:
  0.8 43.1 %collective-permute-start.11 = (f32[128,16]{0,1:T(8,128)S(1)}, f32[128,16]{0,1:T(8,128)S(1)}, u32[]{:S(2)}, u32[]{:S(2)}) collective-permute-start(f32[128,16]{0,1:T(8,128)S(1)} %select_reduce_fusion), channel_id=1, source_target_pairs={{0,1},{1,0},{2,3},{3,2},{4,5},{5,4},{6,7},{7,6},{8,9},{9,8},{10,11... | collective-permute-start | bytes 24584 | tf_op jit(solution)/shard_map/ppermute | solution.py:93
  0.9 43.0 %collective-permute-start.9 = (f32[128,16]{0,1:T(8,128)S(1)}, f32[128,16]{0,1:T(8,128)S(1)}, u32[]{:S(2)}, u32[]{:S(2)}) collective-permute-start(f32[128,16]{0,1:T(8,128)S(1)} %select_reduce_fusion), channel_id=1, source_target_pairs={{0,2},{1,3},{2,0},{3,1},{4,6},{5,7},{6,4},{7,5},{8,10},{9,11},{10,... | collective-permute-start | bytes 24584 | tf_op jit(solution)/shard_map/ppermute | solution.py:93
  4.3 20.1 %collective-permute-start = (bf16[128,1024]{0,1:T(8,128)(2,1)}, bf16[128,1024]{0,1:T(8,128)(2,1)}, u32[]{:S(2)}, u32[]{:S(2)}) collective-permute-start(bf16[128,1024]{0,1:T(8,128)(2,1)} %bitcast.5), channel_id=1, source_target_pairs={{0,16},{16,0},{1,17},{17,1},{2,18},{18,2},{3,19},{19,3},{4,20},{20... | collective-permute-start | bytes 786440 | tf_op jit(solution)/shard_map/ppermute | solution.py:279
  41.0 68.7 %collective-permute-start.12 = (bf16[3,2048,256]{2,1,0:T(8,128)(2,1)}, bf16[3,2048,256]{2,1,0:T(8,128)(2,1)}, u32[]{:S(2)}, u32[]{:S(2)}) collective-permute-start(bf16[3,2048,256]{2,1,0:T(8,128)(2,1)} %pad_maximum_fusion), channel_id=1, source_target_pairs={{0,16},{16,0},{1,17},{17,1},{2,18},{18,2},{3,19},{19,3},{4,20},{20... | collective-permute-start | bytes 9437192 | tf_op jit(solution)/shard_map/ppermute | solution.py:54
  43.9 14.7 %collective-permute-start.8 = (bf16[128,2048]{1,0:T(8,128)(2,1)}, bf16[128,2048]{1,0:T(8,128)(2,1)}, u32[]{:S(2)}, u32[]{:S(2)}) collective-permute-start(bf16[128,2048]{1,0:T(8,128)(2,1)} %get-tuple-element.102), channel_id=1, source_target_pairs={{0,2},{1,3},{2,0},{3,1},{4,6},{5,7},{6,4},{7,5},{8,10},{9,11},{10,... | collective-permute-start | bytes 1572872 | tf_op jit(solution)/shard_map/ppermute | solution.py:93
  44.5 24.3 %collective-permute-start.6 = (bf16[128,2048]{1,0:T(8,128)(2,1)}, bf16[128,2048]{1,0:T(8,128)(2,1)}, u32[]{:S(2)}, u32[]{:S(2)}) collective-permute-start(bf16[128,2048]{1,0:T(8,128)(2,1)} %get-tuple-element.102), channel_id=1, source_target_pairs={{0,4},{1,5},{2,6},{3,7},{4,0},{5,1},{6,2},{7,3},{8,12},{9,13},{10,... | collective-permute-start | bytes 1572872 | tf_op jit(solution)/shard_map/ppermute | solution.py:93
  45.0 26.2 %collective-permute-start.4 = (bf16[128,2048]{1,0:T(8,128)(2,1)}, bf16[128,2048]{1,0:T(8,128)(2,1)}, u32[]{:S(2)}, u32[]{:S(2)}) collective-permute-start(bf16[128,2048]{1,0:T(8,128)(2,1)} %get-tuple-element.102), channel_id=1, source_target_pairs={{0,8},{1,9},{2,10},{3,11},{4,12},{5,13},{6,14},{7,15},{8,0},{9,1},... | collective-permute-start | bytes 1572872 | tf_op jit(solution)/shard_map/ppermute | solution.py:93
  71.2 45.6 %collective-permute-start.22 = (f32[128,16]{0,1:T(8,128)S(1)}, f32[128,16]{0,1:T(8,128)S(1)}, u32[]{:S(2)}, u32[]{:S(2)}) collective-permute-start(f32[128,16]{0,1:T(8,128)S(1)} %collective-permute-done.7), channel_id=1, source_target_pairs={{0,1},{1,0},{2,3},{3,2},{4,5},{5,4},{6,7},{7,6},{8,9},{9,8},{10,11... | collective-permute-start | bytes 24584 | tf_op jit(solution)/shard_map/ppermute | solution.py:93
  71.2 45.8 %collective-permute-start.20 = (f32[128,16]{0,1:T(8,128)S(1)}, f32[128,16]{0,1:T(8,128)S(1)}, u32[]{:S(2)}, u32[]{:S(2)}) collective-permute-start(f32[128,16]{0,1:T(8,128)S(1)} %collective-permute-done.7), channel_id=1, source_target_pairs={{0,2},{1,3},{2,0},{3,1},{4,6},{5,7},{6,4},{7,5},{8,10},{9,11},{10,... | collective-permute-start | bytes 24584 | tf_op jit(solution)/shard_map/ppermute | solution.py:93
  72.7 43.6 %collective-permute-start.24 = (f32[128,16]{0,1:T(8,128)S(1)}, f32[128,16]{0,1:T(8,128)S(1)}, u32[]{:S(2)}, u32[]{:S(2)}) collective-permute-start(f32[128,16]{0,1:T(8,128)S(1)} %collective-permute-done.9), channel_id=1, source_target_pairs={{0,1},{1,0},{2,3},{3,2},{4,5},{5,4},{6,7},{7,6},{8,9},{9,8},{10,11... | collective-permute-start | bytes 24584 | tf_op jit(solution)/shard_map/ppermute | solution.py:93
  72.9 44.6 %collective-permute-start.18 = (f32[128,16]{0,1:T(8,128)S(1)}, f32[128,16]{0,1:T(8,128)S(1)}, u32[]{:S(2)}, u32[]{:S(2)}) collective-permute-start(f32[128,16]{0,1:T(8,128)S(1)} %collective-permute-done.5), channel_id=1, source_target_pairs={{0,1},{1,0},{2,3},{3,2},{4,5},{5,4},{6,7},{7,6},{8,9},{9,8},{10,11... | collective-permute-start | bytes 24584 | tf_op jit(solution)/shard_map/ppermute | solution.py:93
  117.6 15.1 %collective-permute-start.19 = (bf16[128,2048]{1,0:T(8,128)(2,1)}, bf16[128,2048]{1,0:T(8,128)(2,1)}, u32[]{:S(2)}, u32[]{:S(2)}) collective-permute-start(bf16[128,2048]{1,0:T(8,128)(2,1)} %collective-permute-done.6), channel_id=1, source_target_pairs={{0,2},{1,3},{2,0},{3,1},{4,6},{5,7},{6,4},{7,5},{8,10},{9,11},{10,... | collective-permute-start | bytes 1572872 | tf_op jit(solution)/shard_map/ppermute | solution.py:93
  119.1 13.6 %collective-permute-start.17 = (bf16[128,2048]{1,0:T(8,128)(2,1)}, bf16[128,2048]{1,0:T(8,128)(2,1)S(1)}, u32[]{:S(2)}, u32[]{:S(2)}) collective-permute-start(bf16[128,2048]{1,0:T(8,128)(2,1)} %collective-permute-done.4), channel_id=1, source_target_pairs={{0,1},{1,0},{2,3},{3,2},{4,5},{5,4},{6,7},{7,6},{8,9},{9,8},{10,11... | collective-permute-start | bytes 1572872 | tf_op jit(solution)/shard_map/ppermute | solution.py:93
  120.0 23.0 %collective-permute-start.15 = (bf16[128,2048]{1,0:T(8,128)(2,1)}, bf16[128,2048]{1,0:T(8,128)(2,1)}, u32[]{:S(2)}, u32[]{:S(2)}) collective-permute-start(bf16[128,2048]{1,0:T(8,128)(2,1)} %collective-permute-done.4), channel_id=1, source_target_pairs={{0,2},{1,3},{2,0},{3,1},{4,6},{5,7},{6,4},{7,5},{8,10},{9,11},{10,... | collective-permute-start | bytes 1572872 | tf_op jit(solution)/shard_map/ppermute | solution.py:93
  121.5 21.5 %collective-permute-start.13 = (bf16[128,2048]{1,0:T(8,128)(2,1)}, bf16[128,2048]{1,0:T(8,128)(2,1)}, u32[]{:S(2)}, u32[]{:S(2)}) collective-permute-start(bf16[128,2048]{1,0:T(8,128)(2,1)} %collective-permute-done.4), channel_id=1, source_target_pairs={{0,4},{1,5},{2,6},{3,7},{4,0},{5,1},{6,2},{7,3},{8,12},{9,13},{10,... | collective-permute-start | bytes 1572872 | tf_op jit(solution)/shard_map/ppermute | solution.py:93
  143.0 20.6 %collective-permute-start.26 = (f32[128,16]{0,1:T(8,128)S(1)}, f32[128,16]{0,1:T(8,128)S(1)}, u32[]{:S(2)}, u32[]{:S(2)}) collective-permute-start(f32[128,16]{0,1:T(8,128)S(1)} %collective-permute-done.14), channel_id=1, source_target_pairs={{0,2},{1,3},{2,0},{3,1},{4,6},{5,7},{6,4},{7,5},{8,10},{9,11},{10,... | collective-permute-start | bytes 24584 | tf_op jit(solution)/shard_map/ppermute | solution.py:93
  145.1 18.6 %collective-permute-start.29 = (bf16[128,2048]{1,0:T(8,128)(2,1)}, bf16[128,2048]{1,0:T(8,128)(2,1)}, u32[]{:S(2)}, u32[]{:S(2)}) collective-permute-start(bf16[128,2048]{1,0:T(8,128)(2,1)} %collective-permute-done.15), channel_id=1, source_target_pairs={{0,1},{1,0},{2,3},{3,2},{4,5},{5,4},{6,7},{7,6},{8,9},{9,8},{10,11... | collective-permute-start | bytes 1572872 | tf_op jit(solution)/shard_map/ppermute | solution.py:93
  151.8 11.9 %collective-permute-start.31 = (bf16[128,2048]{1,0:T(8,128)(2,1)}, bf16[128,2048]{1,0:T(8,128)(2,1)}, u32[]{:S(2)}, u32[]{:S(2)}) collective-permute-start(bf16[128,2048]{1,0:T(8,128)(2,1)} %collective-permute-done.19), channel_id=1, source_target_pairs={{0,1},{1,0},{2,3},{3,2},{4,5},{5,4},{6,7},{7,6},{8,9},{9,8},{10,11... | collective-permute-start | bytes 1572872 | tf_op jit(solution)/shard_map/ppermute | solution.py:93
  152.2 11.5 %collective-permute-start.27 = (bf16[128,2048]{1,0:T(8,128)(2,1)}, bf16[128,2048]{1,0:T(8,128)(2,1)}, u32[]{:S(2)}, u32[]{:S(2)}) collective-permute-start(bf16[128,2048]{1,0:T(8,128)(2,1)} %collective-permute-done.13), channel_id=1, source_target_pairs={{0,1},{1,0},{2,3},{3,2},{4,5},{5,4},{6,7},{7,6},{8,9},{9,8},{10,11... | collective-permute-start | bytes 1572872 | tf_op jit(solution)/shard_map/ppermute | solution.py:93
  152.4 14.4 %collective-permute-start.25 = (bf16[128,2048]{1,0:T(8,128)(2,1)}, bf16[128,2048]{1,0:T(8,128)(2,1)}, u32[]{:S(2)}, u32[]{:S(2)}) collective-permute-start(bf16[128,2048]{1,0:T(8,128)(2,1)} %collective-permute-done.13), channel_id=1, source_target_pairs={{0,2},{1,3},{2,0},{3,1},{4,6},{5,7},{6,4},{7,5},{8,10},{9,11},{10,... | collective-permute-start | bytes 1572872 | tf_op jit(solution)/shard_map/ppermute | solution.py:93
  179.4 11.1 %collective-permute-start.35 = (bf16[128,2048]{1,0:T(8,128)(2,1)}, bf16[128,2048]{1,0:T(8,128)(2,1)}, u32[]{:S(2)}, u32[]{:S(2)}) collective-permute-start(bf16[128,2048]{1,0:T(8,128)(2,1)} %fusion.10), channel_id=1, source_target_pairs={{1,0},{0,1},{3,2},{2,3},{5,4},{4,5},{7,6},{6,7},{9,8},{8,9},{11,10... | collective-permute-start | bytes 1572872 | tf_op jit(solution)/shard_map/ppermute | solution.py:118
  192.1 14.0 %collective-permute-start.36 = (bf16[128,2048]{1,0:T(8,128)(2,1)S(1)}, bf16[128,2048]{1,0:T(8,128)(2,1)S(1)}, u32[]{:S(2)}, u32[]{:S(2)}) collective-permute-start(bf16[128,2048]{1,0:T(8,128)(2,1)S(1)} %fusion.39), channel_id=1, source_target_pairs={{2,0},{3,1},{0,2},{1,3},{6,4},{7,5},{4,6},{5,7},{10,8},{11,9},{8,1... | collective-permute-start | bytes 1572872 | tf_op jit(solution)/shard_map/ppermute | solution.py:118
  193.8 16.0 %collective-permute-start.45 = (bf16[128,2048]{1,0:T(8,128)(2,1)S(1)}, bf16[128,2048]{1,0:T(8,128)(2,1)S(1)}, u32[]{:S(2)}, u32[]{:S(2)}) collective-permute-start(bf16[128,2048]{1,0:T(8,128)(2,1)S(1)} %get-tuple-element.116), channel_id=1, source_target_pairs={{1,0},{0,1},{3,2},{2,3},{5,4},{4,5},{7,6},{6,7},{9,8},{8,9},{11,10... | collective-permute-start | bytes 1572872 | tf_op jit(solution)/shard_map/ppermute | solution.py:118
  196.4 25.1 %collective-permute-start.44 = (bf16[128,2048]{1,0:T(8,128)(2,1)}, bf16[128,2048]{1,0:T(8,128)(2,1)}, u32[]{:S(2)}, u32[]{:S(2)}) collective-permute-start(bf16[128,2048]{1,0:T(8,128)(2,1)} %get-tuple-element.117), channel_id=1, source_target_pairs={{1,0},{0,1},{3,2},{2,3},{5,4},{4,5},{7,6},{6,7},{9,8},{8,9},{11,10... | collective-permute-start | bytes 1572872 | tf_op jit(solution)/shard_map/ppermute | solution.py:118
  197.0 24.7 %collective-permute-start.42 = (bf16[128,2048]{1,0:T(8,128)(2,1)}, bf16[128,2048]{1,0:T(8,128)(2,1)}, u32[]{:S(2)}, u32[]{:S(2)}) collective-permute-start(bf16[128,2048]{1,0:T(8,128)(2,1)} %get-tuple-element.118), channel_id=1, source_target_pairs={{1,0},{0,1},{3,2},{2,3},{5,4},{4,5},{7,6},{6,7},{9,8},{8,9},{11,10... | collective-permute-start | bytes 1572872 | tf_op jit(solution)/shard_map/ppermute | solution.py:118
  207.8 15.2 %collective-permute-start.43 = (bf16[128,2048]{1,0:T(8,128)(2,1)}, bf16[128,2048]{1,0:T(8,128)(2,1)}, u32[]{:S(2)}, u32[]{:S(2)}) collective-permute-start(bf16[128,2048]{1,0:T(8,128)(2,1)} %get-tuple-element.106), channel_id=1, source_target_pairs={{2,0},{3,1},{0,2},{1,3},{6,4},{7,5},{4,6},{5,7},{10,8},{11,9},{8,1... | collective-permute-start | bytes 1572872 | tf_op jit(solution)/shard_map/ppermute | solution.py:118
  208.3 24.1 %collective-permute-start.41 = (bf16[128,2048]{1,0:T(8,128)(2,1)}, bf16[128,2048]{1,0:T(8,128)(2,1)}, u32[]{:S(2)}, u32[]{:S(2)}) collective-permute-start(bf16[128,2048]{1,0:T(8,128)(2,1)} %get-tuple-element.107), channel_id=1, source_target_pairs={{2,0},{3,1},{0,2},{1,3},{6,4},{7,5},{4,6},{5,7},{10,8},{11,9},{8,1... | collective-permute-start | bytes 1572872 | tf_op jit(solution)/shard_map/ppermute | solution.py:118
  210.6 21.8 %collective-permute-start.40 = (bf16[128,2048]{1,0:T(8,128)(2,1)}, bf16[128,2048]{1,0:T(8,128)(2,1)}, u32[]{:S(2)}, u32[]{:S(2)}) collective-permute-start(bf16[128,2048]{1,0:T(8,128)(2,1)} %get-tuple-element.108), channel_id=1, source_target_pairs={{4,0},{5,1},{6,2},{7,3},{0,4},{1,5},{2,6},{3,7},{12,8},{13,9},{14,... | collective-permute-start | bytes 1572872 | tf_op jit(solution)/shard_map/ppermute | solution.py:118
  221.6 16.9 %collective-permute-start.49 = (bf16[128,2048]{1,0:T(8,128)(2,1)S(1)}, bf16[128,2048]{1,0:T(8,128)(2,1)S(1)}, u32[]{:S(2)}, u32[]{:S(2)}) collective-permute-start(bf16[128,2048]{1,0:T(8,128)(2,1)S(1)} %slice.144), channel_id=1, source_target_pairs={{1,0},{0,1},{3,2},{2,3},{5,4},{4,5},{7,6},{6,7},{9,8},{8,9},{11,10... | collective-permute-start | bytes 1572872 | tf_op jit(solution)/shard_map/ppermute | solution.py:118
  235.9 12.2 %collective-permute-start.48 = (bf16[128,2048]{1,0:T(8,128)(2,1)S(1)}, bf16[128,2048]{1,0:T(8,128)(2,1)S(1)}, u32[]{:S(2)}, u32[]{:S(2)}) collective-permute-start(bf16[128,2048]{1,0:T(8,128)(2,1)S(1)} %get-tuple-element.109), channel_id=1, source_target_pairs={{2,0},{3,1},{0,2},{1,3},{6,4},{7,5},{4,6},{5,7},{10,8},{11,9},{8,1... | collective-permute-start | bytes 1572872 | tf_op jit(solution)/shard_map/ppermute | solution.py:118
  236.5 20.7 %collective-permute-start.47 = (bf16[128,2048]{1,0:T(8,128)(2,1)S(1)}, bf16[128,2048]{1,0:T(8,128)(2,1)S(1)}, u32[]{:S(2)}, u32[]{:S(2)}) collective-permute-start(bf16[128,2048]{1,0:T(8,128)(2,1)S(1)} %get-tuple-element.110), channel_id=1, source_target_pairs={{4,0},{5,1},{6,2},{7,3},{0,4},{1,5},{2,6},{3,7},{12,8},{13,9},{14,... | collective-permute-start | bytes 1572872 | tf_op jit(solution)/shard_map/ppermute | solution.py:118
  238.1 23.8 %collective-permute-start.46 = (bf16[128,2048]{1,0:T(8,128)(2,1)S(1)}, bf16[128,2048]{1,0:T(8,128)(2,1)S(1)}, u32[]{:S(2)}, u32[]{:S(2)}) collective-permute-start(bf16[128,2048]{1,0:T(8,128)(2,1)S(1)} %get-tuple-element.111), channel_id=1, source_target_pairs={{8,0},{9,1},{10,2},{11,3},{12,4},{13,5},{14,6},{15,7},{0,8},{1,9},... | collective-permute-start | bytes 1572872 | tf_op jit(solution)/shard_map/ppermute | solution.py:118
  (43 other events, 313.4 us)

commit v10 on v7

--- a/solution.py
+++ b/solution.py
@@ -86,11 +86,18 @@
     groups = []
     low = 0
     tie_at = next((n + 1 for n, (_, ends) in enumerate(plan) if ends), 0)
+    first_wave = [
+        [lax.ppermute(pieces[0][0], "ep", pairs) for pairs in pairs_list] for pairs_list, _ in plan
+    ]
+    first_wave = lax.optimization_barrier(first_wave)
     for number, (pairs_list, ends) in enumerate(plan):
         grown = []
         for parent, (block, _, _) in enumerate(pieces):
-            for pairs in pairs_list:
-                grown.append((lax.ppermute(block, "ep", pairs), parent, pairs))
+            for slot, pairs in enumerate(pairs_list):
+                if parent == 0:
+                    grown.append((first_wave[number][slot], parent, pairs))
+                else:
+                    grown.append((lax.ppermute(block, "ep", pairs), parent, pairs))
         if number == tie_at:
             tied = lax.optimization_barrier((tuple(full), [piece[0] for piece in grown]))
             full = list(tied[0])

time: 259 us -> 247 us (0.954)
  waiting for transfers between devices: 132 us -> 118 us
  local copies, waits for them, and re-layouts: 21.3 us -> 25.5 us
    ppermute x30 -> x22, waiting for transfers between devices: 57.8 us -> 22.5 us  [dense_moe(): grown.append((lax.ppermute(block, 'ep', pairs), parent, pairs))]
    ppermute x0 -> x8, waiting for transfers between devices: none -> 22.8 us  [dense_moe(): lax.ppermute(pieces[0][0], 'ep', pairs)]
    ppermute x30 -> x22, starting transfers between devices: 19.3 us -> 11.6 us  [dense_moe(): grown.append((lax.ppermute(block, 'ep', pairs), parent, pairs))]
    ppermute x0 -> x8, starting transfers between devices: none -> 6.76 us  [dense_moe(): lax.ppermute(pieces[0][0], 'ep', pairs)]
    ppermute x1, waiting for transfers between devices: 16.4 us -> 12.5 us  [full_weights(): other = lax.ppermute(packed, 'kv', [(0, 1), (1, 0)])]
    unnamed x79, local copies, waits for them, and re-layouts: 14.7 us -> 17.7 us
  transfers between devices with their start and end apart: 50 -> 50, of which waited for: 19 -> 19; matrix products, arithmetic and copies ran while one was open for 22% -> 24% of each run, Pallas kernels for 0% -> 0%
where the time goes in v10:
time: 247 us; the launch traced here: 243 us
  waiting for transfers between devices  118 us (48%)
  matrix products  46.4 us (19%)
  starting transfers between devices  30.7 us (12%)
  local copies, waits for them, and re-layouts  25.5 us (10%)
  other arithmetic  20.8 us (8%)
    ppermute x15, waiting for transfers between devices, dense_moe(): sent = lax.ppermute(partial[index].astype(jnp.bfloat16), 'ep', back)  53.9 us
    dot_general x3, matrix products, expert(): out_rows = jnp.dot(act, full[2], preferred_element_type=jnp.float32)  24.2 us
    ppermute x8, waiting for transfers between devices, dense_moe(): lax.ppermute(pieces[0][0], 'ep', pairs)  22.8 us
    ppermute x22, waiting for transfers between devices, dense_moe(): grown.append((lax.ppermute(block, 'ep', pairs), parent, pairs))  22.5 us
    unnamed x79, local copies, waits for them, and re-layouts  17.7 us
    ppermute x1, waiting for transfers between devices, full_weights(): other = lax.ppermute(packed, 'kv', [(0, 1), (1, 0)])  12.5 us
    ppermute x22, starting transfers between devices, dense_moe(): grown.append((lax.ppermute(block, 'ep', pairs), parent, pairs))  11.6 us
    ppermute x15, starting transfers between devices, dense_moe(): sent = lax.ppermute(partial[index].astype(jnp.bfloat16), 'ep', back)  7.54 us
  transfers between devices with their start and end apart: 50, of which 19 were waited for; matrix products, arithmetic and copies ran while one was open for 24% of the time, Pallas kernels for 0%

profile of v10, /device:TPU:24, one launch (start us, length us, event | category | flops | bytes accessed | tf_op | source)
XLA Modules:
  0.0 243.1 jit_solution(7974341455021609676)
XLA Ops:
  3.5 3.6 %copy.104 = bf16[128,8,8,128]{3,2,1,0:T(8,128)(2,1)} copy(bf16[128,8,8,128]{3,1,2,0:T(8,128)(2,1)} %bitcast.87) | data formatting | bytes 4194304
  7.2 2.0 copy.103
  11.0 2.6 %bitcast_reduce_fusion.1 = (f32[128,8]{0,1:T(8,128)S(1)}, f32[8,1024,128]{2,1,0:T(8,128)S(1)}) fusion(pred[1024]{0:T(1024)(128)(4,1)S(1)} %add_compare_fusion, bf16[128,8,128]{2,1,0:T(8,128)(2,1)S(1)} %bitcast.97, bf16[1024,8,128]{2,1,0:T(8,128)(2,1)} %bitcast.91), kind=kOutput, calls=%fused_computation.5 | convolution fusion | flops 271580160 | bytes 6558720 | tf_op jit(solution)/shard_map/qhd,khd->qhk/dot_general | solution.py:252
  13.7 1.7 fusion.10
  15.5 2.6 %fusion.2 = (f32[128,8]{0,1:T(8,128)S(1)}, f32[128,8]{0,1:T(8,128)S(1)}, f32[8,1024,128]{2,1,0:T(8,128)S(1)}) fusion(f32[8,1024,128]{2,1,0:T(8,128)S(1)} %get-tuple-element.80, f32[128,8]{0,1:T(8,128)S(1)} %max.17, pred[1024]{0:T(1024)(128)(4,1)S(1)} %add_compare_fusion, bf16[128,8,128]{0,2,1:T(8,128)(2,1)} %bitcast.6, bf16[1024,8,128]{2,1,0:T(8,128)(2,1)S(1)} %bitcast.92), kind=kOutput, calls=%fused_computation.11 | convolution fusion | flops 275773440 | bytes 10761216 | tf_op jit(solution)/shard_map/qhd,khd->qhk/dot_general | solution.py:252
  20.8 1.7 fusion.8
  26.4 5.4 %collective-permute-done.2 = bf16[128,8,128]{0,2,1:T(8,128)(2,1)S(1)} collective-permute-done((bf16[128,8,128]{0,2,1:T(8,128)(2,1)S(1)}, bf16[128,8,128]{0,2,1:T(8,128)(2,1)S(1)}, u32[]{:S(2)}, u32[]{:S(2)}) %collective-permute-start.2) | collective-permute-done | bytes 262176 | tf_op jit(solution)/shard_map/ppermute | solution.py:290
  32.9 3.4 %pad_maximum_fusion = bf16[3,2048,256]{2,1,0:T(8,128)(2,1)} fusion(bf16[1,2048,256]{2,1,0:T(8,128)(2,1)S(1)} %stack_reshape_squeeze.3, bf16[1,2048,256]{2,1,0:T(8,128)(2,1)S(1)} %copy-done.4, bf16[1,2048,256]{2,1,0:T(8,128)(2,1)} %param.27), kind=kLoop, calls=%fused_computation.15 | loop fusion | flops 3145728 | bytes 6291456 | tf_op jit(solution)/shard_map/stack | solution.py:53
  37.6 1.7 collective-permute-start.9
  41.6 2.2 collective-permute-start.4
  45.9 22.1 %collective-permute-done.4 = bf16[128,2048]{1,0:T(8,128)(2,1)} collective-permute-done((bf16[128,2048]{1,0:T(8,128)(2,1)}, bf16[128,2048]{1,0:T(8,128)(2,1)}, u32[]{:S(2)}, u32[]{:S(2)}) %collective-permute-start.4) | collective-permute-done | bytes 524320 | tf_op jit(solution)/shard_map/ppermute | solution.py:90
  71.4 11.6 %collective-permute-done.19 = f32[128,16]{0,1:T(8,128)S(1)} collective-permute-done((f32[128,16]{0,1:T(8,128)S(1)}, f32[128,16]{0,1:T(8,128)S(1)}, u32[]{:S(2)}, u32[]{:S(2)}) %collective-permute-start.19) | collective-permute-done | bytes 8224 | tf_op jit(solution)/shard_map/ppermute | solution.py:100
  90.2 2.0 copy-done.21
  92.2 12.5 %collective-permute-done.13 = bf16[3,2048,256]{2,1,0:T(8,128)(2,1)} collective-permute-done((bf16[3,2048,256]{2,1,0:T(8,128)(2,1)}, bf16[3,2048,256]{2,1,0:T(8,128)(2,1)}, u32[]{:S(2)}, u32[]{:S(2)}) %collective-permute-start.13) | collective-permute-done | bytes 3145760 | tf_op jit(solution)/shard_map/ppermute | solution.py:54
  106.2 4.3 %select_bitcast_fusion.1 = (bf16[2048,256]{1,0:T(8,128)(2,1)}, bf16[2048,256]{1,0:T(8,128)(2,1)}, bf16[1,2048,256]{2,1,0:T(8,128)(2,1)}, bf16[2048,256]{1,0:T(8,128)(2,1)}, bf16[2048,256]{1,0:T(8,128)(2,1)}) fusion(bf16[1,2048,256]{2,1,0:T(8,128)(2,1)S(1)} %copy-done.4, pred[]{:T(512)S(6)} %eq.40, bf16[3,2048,256]{2,1,0:T(8,128)(2,1)} %collective-permute-done.13, ...), kind=kLoop, calls=%fused_computation.81 | loop fusion | flops 2097152 | bytes 10485761 | tf_op jit(solution)/shard_map/jit(_where)/select_n | solution.py:61
  116.6 6.5 %collective-permute-done.20 = f32[128,16]{0,1:T(8,128)S(1)} collective-permute-done((f32[128,16]{0,1:T(8,128)S(1)}, f32[128,16]{0,1:T(8,128)S(1)}, u32[]{:S(2)}, u32[]{:S(2)}) %collective-permute-start.20) | collective-permute-done | bytes 8224 | tf_op jit(solution)/shard_map/ppermute | solution.py:100
  128.9 2.2 fusion.94
  135.2 2.0 copy-done.23
  137.3 3.7 %fusion.93 = f32[1024,512]{1,0:T(8,128)} fusion(bf16[1024,2048]{1,0:T(8,128)(2,1)S(1)} %constant_dynamic-update-slice_fusion, bf16[2048,512]{1,0:T(8,128)(2,1)S(1)} %get-tuple-element.36), kind=kOutput, calls=%fused_computation.157 | convolution fusion | flops 2147483648 | bytes 8388608 | tf_op jit(solution)/shard_map/dot_general | solution.py:78
  140.9 10.0 %multiply_convert_fusion = bf16[1024,2048]{1,0:T(8,128)(2,1)} fusion(f32[1024]{0:T(1024)S(1)} %select_reduce_fusion, bf16[512,2048]{1,0:T(8,128)(2,1)S(1)} %pad_maximum_fusion.4, f32[1024,512]{1,0:T(8,128)} %fusion.93, bf16[1024,2048]{1,0:T(8,128)(2,1)} %copy-done.23, bf16[2048,512]{1,0:T(8,128)(2,1)} %get-tuple-element.37), kind=kOutput, calls=%fused_computation | convolution fusion | flops 4306501632 | bytes 14684160 | tf_op jit(solution)/shard_map/dot_general | solution.py:81
  151.0 4.2 %fusion.86 = (bf16[128,2048]{1,0:T(8,128)(2,1)}, bf16[128,2048]{1,0:T(8,128)(2,1)}, bf16[128,2048]{1,0:T(8,128)(2,1)}, bf16[128,2048]{1,0:T(8,128)(2,1)}, bf16[1...) fusion(bf16[1024,2048]{1,0:T(8,128)(2,1)} %multiply_convert_fusion), kind=kLoop, calls=%fused_computation.152 | loop fusion | bytes 8388608 | tf_op jit(solution)/shard_map/slice | solution.py:118
  156.2 6.9 %convert_multiply_fusion = f32[512,2048]{1,0:T(8,128)} fusion(bf16[512,2048]{1,0:T(8,128)(2,1)S(1)} %pad_maximum_fusion.4, f32[512]{0:T(512)S(1)} %get-tuple-element.51, f32[512,512]{1,0:T(8,128)} %fusion.94, bf16[512,2048]{1,0:T(8,128)(2,1)} %copy-done.20, bf16[2048,512]{1,0:T(8,128)(2,1)} %get-tuple-element.37), kind=kOutput, calls=%fused_computation.7 | convolution fusion | flops 2152202240 | bytes 11536384 | tf_op jit(solution)/shard_map/dot_general | solution.py:81
  163.1 4.7 %fusion.55 = f32[512,512]{1,0:T(8,128)} fusion(bf16[2048,512]{1,0:T(8,128)(2,1)} %get-tuple-element.37, bf16[128,2048]{1,0:T(8,128)(2,1)} %collective-permute-done.12, bf16[128,2048]{1,0:T(8,128)(2,1)} %collective-permute-done.6, bf16[128,2048]{1,0:T(8,128)(2,1)} %collective-permute-done.4, bf16[128,2048]{1,0:T(8,128)(2,1)} %multiply_convert_fusion.5), kind=kOutput, calls=%fused_computation.96 | convolution fusion | flops 1082130432 | bytes 5242880 | tf_op jit(solution)/shard_map/dot_general | solution.py:79
  168.3 3.3 %fusion.41 = (bf16[128,2048]{1,0:T(8,128)(2,1)}, bf16[128,2048]{1,0:T(8,128)(2,1)}, bf16[128,2048]{1,0:T(8,128)(2,1)}, bf16[128,2048]{1,0:T(8,128)(2,1)}) fusion(f32[512,2048]{1,0:T(8,128)S(1)} %copy-done.3, bf16[128,2048]{1,0:T(8,128)(2,1)} %collective-permute-done.36, bf16[128,2048]{1,0:T(8,128)(2,1)} %collective-permute-done.46, ...), kind=kLoop, calls=%fused_computation.68 | loop fusion | flops 3145728 | bytes 8388608 | tf_op jit(solution)/shard_map/convert_element_type | solution.py:122
  173.7 7.3 %convert_multiply_fusion.1 = f32[512,2048]{1,0:T(8,128)} fusion(bf16[512,2048]{1,0:T(8,128)(2,1)S(1)} %pad_maximum_fusion.4, f32[512]{0:T(512)S(1)} %get-tuple-element.52, f32[512,512]{1,0:T(8,128)} %fusion.55, bf16[2048,512]{1,0:T(8,128)(2,1)} %copy-done.13, bf16[128,2048]{1,0:T(8,128)(2,1)} %collective-permute-done.12, ...), kind=kOutput, calls=%fused_computation.8 | convolution fusion | flops 2160590848 | bytes 11536384 | tf_op jit(solution)/shard_map/dot_general | solution.py:81
  182.0 4.7 %collective-permute-done.40 = bf16[128,2048]{1,0:T(8,128)(2,1)} collective-permute-done((bf16[128,2048]{1,0:T(8,128)(2,1)}, bf16[128,2048]{1,0:T(8,128)(2,1)}, u32[]{:S(2)}, u32[]{:S(2)}) %collective-permute-start.40) | collective-permute-done | bytes 524320 | tf_op jit(solution)/shard_map/ppermute | solution.py:122
  186.7 11.2 %collective-permute-done.47 = bf16[128,2048]{1,0:T(8,128)(2,1)} collective-permute-done((bf16[128,2048]{1,0:T(8,128)(2,1)}, bf16[128,2048]{1,0:T(8,128)(2,1)}, u32[]{:S(2)}, u32[]{:S(2)}) %collective-permute-start.47) | collective-permute-done | bytes 524320 | tf_op jit(solution)/shard_map/ppermute | solution.py:122
  198.0 2.6 %fusion.40 = (bf16[128,2048]{1,0:T(8,128)(2,1)S(1)}, bf16[128,2048]{1,0:T(8,128)(2,1)S(1)}) fusion(f32[512,2048]{1,0:T(8,128)} %convert_multiply_fusion.1, bf16[128,2048]{1,0:T(8,128)(2,1)} %collective-permute-done.40, bf16[128,2048]{1,0:T(8,128)(2,1)} %collective-permute-done.38, bf16[128,2048]{1,0:T(8,128)(2,1)} %collective-permute-done.47, ...), kind=kLoop, calls=%fused_computation.66 | loop fusion | flops 2621440 | bytes 5242880 | tf_op jit(solution)/shard_map/convert_element_type | solution.py:122
  203.6 5.5 %collective-permute-done.44 = bf16[128,2048]{1,0:T(8,128)(2,1)S(1)} collective-permute-done((bf16[128,2048]{1,0:T(8,128)(2,1)}, bf16[128,2048]{1,0:T(8,128)(2,1)S(1)}, u32[]{:S(2)}, u32[]{:S(2)}) %collective-permute-start.44) | collective-permute-done | bytes 524320 | tf_op jit(solution)/shard_map/ppermute | solution.py:122
  209.1 12.0 %collective-permute-done.48 = bf16[128,2048]{1,0:T(8,128)(2,1)S(1)} collective-permute-done((bf16[128,2048]{1,0:T(8,128)(2,1)S(1)}, bf16[128,2048]{1,0:T(8,128)(2,1)S(1)}, u32[]{:S(2)}, u32[]{:S(2)}) %collective-permute-start.48) | collective-permute-done | bytes 524320 | tf_op jit(solution)/shard_map/ppermute | solution.py:122
  221.5 10.0 %collective-permute-done.41 = bf16[128,2048]{1,0:T(8,128)(2,1)S(1)} collective-permute-done((bf16[128,2048]{1,0:T(8,128)(2,1)S(1)}, bf16[128,2048]{1,0:T(8,128)(2,1)S(1)}, u32[]{:S(2)}, u32[]{:S(2)}) %collective-permute-start.41) | collective-permute-done | bytes 524320 | tf_op jit(solution)/shard_map/ppermute | solution.py:122
  231.5 10.4 %collective-permute-done.49 = bf16[128,2048]{1,0:T(8,128)(2,1)S(1)} collective-permute-done((bf16[128,2048]{1,0:T(8,128)(2,1)S(1)}, bf16[128,2048]{1,0:T(8,128)(2,1)S(1)}, u32[]{:S(2)}, u32[]{:S(2)}) %collective-permute-start.49) | collective-permute-done | bytes 524320 | tf_op jit(solution)/shard_map/ppermute | solution.py:122
  (193 shorter events, 54.7 us)
Async XLA Ops:
  1.3 14.2 %collective-permute-start = (bf16[128,1024]{0,1:T(8,128)(2,1)S(1)}, bf16[128,1024]{0,1:T(8,128)(2,1)}, u32[]{:S(2)}, u32[]{:S(2)}) collective-permute-start(bf16[128,1024]{0,1:T(8,128)(2,1)S(1)} %bitcast.101), channel_id=1, source_target_pairs={{0,16},{16,0},{1,17},{17,1},{2,18},{18,2},{3,19},{19,3},{4,20},{20... | collective-permute-start | bytes 786440 | tf_op jit(solution)/shard_map/ppermute | solution.py:280
  36.3 68.4 %collective-permute-start.13 = (bf16[3,2048,256]{2,1,0:T(8,128)(2,1)}, bf16[3,2048,256]{2,1,0:T(8,128)(2,1)}, u32[]{:S(2)}, u32[]{:S(2)}) collective-permute-start(bf16[3,2048,256]{2,1,0:T(8,128)(2,1)} %pad_maximum_fusion), channel_id=1, source_target_pairs={{0,16},{16,0},{1,17},{17,1},{2,18},{18,2},{3,19},{19,3},{4,20},{20... | collective-permute-start | bytes 9437192 | tf_op jit(solution)/shard_map/ppermute | solution.py:54
  41.6 26.5 %collective-permute-start.4 = (bf16[128,2048]{1,0:T(8,128)(2,1)}, bf16[128,2048]{1,0:T(8,128)(2,1)}, u32[]{:S(2)}, u32[]{:S(2)}) collective-permute-start(bf16[128,2048]{1,0:T(8,128)(2,1)} %multiply_convert_fusion.5), channel_id=1, source_target_pairs={{0,8},{1,9},{2,10},{3,11},{4,12},{5,13},{6,14},{7,15},{8,0},{9,1},... | collective-permute-start | bytes 1572872 | tf_op jit(solution)/shard_map/ppermute | solution.py:90
  43.8 24.4 %collective-permute-start.6 = (bf16[128,2048]{1,0:T(8,128)(2,1)}, bf16[128,2048]{1,0:T(8,128)(2,1)}, u32[]{:S(2)}, u32[]{:S(2)}) collective-permute-start(bf16[128,2048]{1,0:T(8,128)(2,1)} %multiply_convert_fusion.5), channel_id=1, source_target_pairs={{0,4},{1,5},{2,6},{3,7},{4,0},{5,1},{6,2},{7,3},{8,12},{9,13},{10,... | collective-permute-start | bytes 1572872 | tf_op jit(solution)/shard_map/ppermute | solution.py:90
  45.4 22.8 %collective-permute-start.8 = (bf16[128,2048]{1,0:T(8,128)(2,1)}, bf16[128,2048]{1,0:T(8,128)(2,1)}, u32[]{:S(2)}, u32[]{:S(2)}) collective-permute-start(bf16[128,2048]{1,0:T(8,128)(2,1)} %multiply_convert_fusion.5), channel_id=1, source_target_pairs={{0,2},{1,3},{2,0},{3,1},{4,6},{5,7},{6,4},{7,5},{8,10},{9,11},{10,... | collective-permute-start | bytes 1572872 | tf_op jit(solution)/shard_map/ppermute | solution.py:90
  68.2 18.4 %collective-permute-start.21 = (bf16[128,2048]{1,0:T(8,128)(2,1)}, bf16[128,2048]{1,0:T(8,128)(2,1)S(1)}, u32[]{:S(2)}, u32[]{:S(2)}) collective-permute-start(bf16[128,2048]{1,0:T(8,128)(2,1)} %collective-permute-done.4), channel_id=1, source_target_pairs={{0,1},{1,0},{2,3},{3,2},{4,5},{5,4},{6,7},{7,6},{8,9},{9,8},{10,11... | collective-permute-start | bytes 1572872 | tf_op jit(solution)/shard_map/ppermute | solution.py:100
  68.2 18.3 %collective-permute-start.12 = (bf16[128,2048]{1,0:T(8,128)(2,1)}, bf16[128,2048]{1,0:T(8,128)(2,1)}, u32[]{:S(2)}, u32[]{:S(2)}) collective-permute-start(bf16[128,2048]{1,0:T(8,128)(2,1)} %collective-permute-done.4), channel_id=1, source_target_pairs={{0,4},{1,5},{2,6},{3,7},{4,0},{5,1},{6,2},{7,3},{8,12},{9,13},{10,... | collective-permute-start | bytes 1572872 | tf_op jit(solution)/shard_map/ppermute | solution.py:100
  69.7 13.3 %collective-permute-start.19 = (f32[128,16]{0,1:T(8,128)S(1)}, f32[128,16]{0,1:T(8,128)S(1)}, u32[]{:S(2)}, u32[]{:S(2)}) collective-permute-start(f32[128,16]{0,1:T(8,128)S(1)} %collective-permute-done.5), channel_id=1, source_target_pairs={{0,4},{1,5},{2,6},{3,7},{4,0},{5,1},{6,2},{7,3},{8,12},{9,13},{10,... | collective-permute-start | bytes 24584 | tf_op jit(solution)/shard_map/ppermute | solution.py:100
  70.3 12.7 %collective-permute-start.28 = (f32[128,16]{0,1:T(8,128)S(1)}, f32[128,16]{0,1:T(8,128)S(1)}, u32[]{:S(2)}, u32[]{:S(2)}) collective-permute-start(f32[128,16]{0,1:T(8,128)S(1)} %collective-permute-done.5), channel_id=1, source_target_pairs={{0,1},{1,0},{2,3},{3,2},{4,5},{5,4},{6,7},{7,6},{8,9},{9,8},{10,11... | collective-permute-start | bytes 24584 | tf_op jit(solution)/shard_map/ppermute | solution.py:100
  85.7 37.4 %collective-permute-start.14 = (bf16[128,2048]{1,0:T(8,128)(2,1)}, bf16[128,2048]{1,0:T(8,128)(2,1)}, u32[]{:S(2)}, u32[]{:S(2)}) collective-permute-start(bf16[128,2048]{1,0:T(8,128)(2,1)} %collective-permute-done.4), channel_id=1, source_target_pairs={{0,2},{1,3},{2,0},{3,1},{4,6},{5,7},{6,4},{7,5},{8,10},{9,11},{10,... | collective-permute-start | bytes 1572872 | tf_op jit(solution)/shard_map/ppermute | solution.py:100
  86.6 36.5 %collective-permute-start.16 = (bf16[128,2048]{1,0:T(8,128)(2,1)}, bf16[128,2048]{1,0:T(8,128)(2,1)}, u32[]{:S(2)}, u32[]{:S(2)}) collective-permute-start(bf16[128,2048]{1,0:T(8,128)(2,1)} %collective-permute-done.6), channel_id=1, source_target_pairs={{0,2},{1,3},{2,0},{3,1},{4,6},{5,7},{6,4},{7,5},{8,10},{9,11},{10,... | collective-permute-start | bytes 1572872 | tf_op jit(solution)/shard_map/ppermute | solution.py:100
  87.9 28.1 %collective-permute-start.15 = (f32[128,16]{0,1:T(8,128)S(1)}, f32[128,16]{0,1:T(8,128)S(1)}, u32[]{:S(2)}, u32[]{:S(2)}) collective-permute-start(f32[128,16]{0,1:T(8,128)S(1)} %collective-permute-done.5), channel_id=1, source_target_pairs={{0,2},{1,3},{2,0},{3,1},{4,6},{5,7},{6,4},{7,5},{8,10},{9,11},{10,... | collective-permute-start | bytes 24584 | tf_op jit(solution)/shard_map/ppermute | solution.py:100
  88.8 27.8 %collective-permute-start.17 = (f32[128,16]{0,1:T(8,128)S(1)}, f32[128,16]{0,1:T(8,128)S(1)}, u32[]{:S(2)}, u32[]{:S(2)}) collective-permute-start(f32[128,16]{0,1:T(8,128)S(1)} %collective-permute-done.7), channel_id=1, source_target_pairs={{0,2},{1,3},{2,0},{3,1},{4,6},{5,7},{6,4},{7,5},{8,10},{9,11},{10,... | collective-permute-start | bytes 24584 | tf_op jit(solution)/shard_map/ppermute | solution.py:100
  104.7 18.4 %collective-permute-start.18 = (bf16[128,2048]{1,0:T(8,128)(2,1)}, bf16[128,2048]{1,0:T(8,128)(2,1)}, u32[]{:S(2)}, u32[]{:S(2)}) collective-permute-start(bf16[128,2048]{1,0:T(8,128)(2,1)} %collective-permute-done.12), channel_id=1, source_target_pairs={{0,2},{1,3},{2,0},{3,1},{4,6},{5,7},{6,4},{7,5},{8,10},{9,11},{10,... | collective-permute-start | bytes 1572872 | tf_op jit(solution)/shard_map/ppermute | solution.py:100
  123.1 11.8 %collective-permute-start.24 = (bf16[128,2048]{1,0:T(8,128)(2,1)}, bf16[128,2048]{1,0:T(8,128)(2,1)S(1)}, u32[]{:S(2)}, u32[]{:S(2)}) collective-permute-start(bf16[128,2048]{1,0:T(8,128)(2,1)} %collective-permute-done.8), channel_id=1, source_target_pairs={{0,1},{1,0},{2,3},{3,2},{4,5},{5,4},{6,7},{7,6},{8,9},{9,8},{10,11... | collective-permute-start | bytes 1572872 | tf_op jit(solution)/shard_map/ppermute | solution.py:100
  124.3 10.7 %collective-permute-start.25 = (bf16[128,2048]{1,0:T(8,128)(2,1)}, bf16[128,2048]{1,0:T(8,128)(2,1)S(1)}, u32[]{:S(2)}, u32[]{:S(2)}) collective-permute-start(bf16[128,2048]{1,0:T(8,128)(2,1)} %collective-permute-done.14), channel_id=1, source_target_pairs={{0,1},{1,0},{2,3},{3,2},{4,5},{5,4},{6,7},{7,6},{8,9},{9,8},{10,11... | collective-permute-start | bytes 1572872 | tf_op jit(solution)/shard_map/ppermute | solution.py:100
  124.9 10.2 %collective-permute-start.26 = (bf16[128,2048]{1,0:T(8,128)(2,1)}, bf16[128,2048]{1,0:T(8,128)(2,1)S(1)}, u32[]{:S(2)}, u32[]{:S(2)}) collective-permute-start(bf16[128,2048]{1,0:T(8,128)(2,1)} %collective-permute-done.16), channel_id=1, source_target_pairs={{0,1},{1,0},{2,3},{3,2},{4,5},{5,4},{6,7},{7,6},{8,9},{9,8},{10,11... | collective-permute-start | bytes 1572872 | tf_op jit(solution)/shard_map/ppermute | solution.py:100
  155.2 12.9 %collective-permute-start.36 = (bf16[128,2048]{1,0:T(8,128)(2,1)}, bf16[128,2048]{1,0:T(8,128)(2,1)}, u32[]{:S(2)}, u32[]{:S(2)}) collective-permute-start(bf16[128,2048]{1,0:T(8,128)(2,1)} %get-tuple-element.63), channel_id=1, source_target_pairs={{1,0},{0,1},{3,2},{2,3},{5,4},{4,5},{7,6},{6,7},{9,8},{8,9},{11,10... | collective-permute-start | bytes 1572872 | tf_op jit(solution)/shard_map/ppermute | solution.py:122
  155.5 12.8 %collective-permute-start.39 = (bf16[128,2048]{1,0:T(8,128)(2,1)}, bf16[128,2048]{1,0:T(8,128)(2,1)}, u32[]{:S(2)}, u32[]{:S(2)}) collective-permute-start(bf16[128,2048]{1,0:T(8,128)(2,1)} %get-tuple-element.61), channel_id=1, source_target_pairs={{1,0},{0,1},{3,2},{2,3},{5,4},{4,5},{7,6},{6,7},{9,8},{8,9},{11,10... | collective-permute-start | bytes 1572872 | tf_op jit(solution)/shard_map/ppermute | solution.py:122
  155.7 12.6 %collective-permute-start.43 = (bf16[128,2048]{1,0:T(8,128)(2,1)}, bf16[128,2048]{1,0:T(8,128)(2,1)}, u32[]{:S(2)}, u32[]{:S(2)}) collective-permute-start(bf16[128,2048]{1,0:T(8,128)(2,1)} %get-tuple-element.59), channel_id=1, source_target_pairs={{1,0},{0,1},{3,2},{2,3},{5,4},{4,5},{7,6},{6,7},{9,8},{8,9},{11,10... | collective-permute-start | bytes 1572872 | tf_op jit(solution)/shard_map/ppermute | solution.py:122
  156.1 12.3 %collective-permute-start.46 = (bf16[128,2048]{1,0:T(8,128)(2,1)}, bf16[128,2048]{1,0:T(8,128)(2,1)}, u32[]{:S(2)}, u32[]{:S(2)}) collective-permute-start(bf16[128,2048]{1,0:T(8,128)(2,1)} %get-tuple-element.57), channel_id=1, source_target_pairs={{1,0},{0,1},{3,2},{2,3},{5,4},{4,5},{7,6},{6,7},{9,8},{8,9},{11,10... | collective-permute-start | bytes 1572872 | tf_op jit(solution)/shard_map/ppermute | solution.py:122
  167.8 13.3 %collective-permute-start.38 = (bf16[128,2048]{1,0:T(8,128)(2,1)}, bf16[128,2048]{1,0:T(8,128)(2,1)}, u32[]{:S(2)}, u32[]{:S(2)}) collective-permute-start(bf16[128,2048]{1,0:T(8,128)(2,1)} %get-tuple-element.62), channel_id=1, source_target_pairs={{1,0},{0,1},{3,2},{2,3},{5,4},{4,5},{7,6},{6,7},{9,8},{8,9},{11,10... | collective-permute-start | bytes 1572872 | tf_op jit(solution)/shard_map/ppermute | solution.py:122
  168.1 13.8 %collective-permute-start.45 = (bf16[128,2048]{1,0:T(8,128)(2,1)}, bf16[128,2048]{1,0:T(8,128)(2,1)}, u32[]{:S(2)}, u32[]{:S(2)}) collective-permute-start(bf16[128,2048]{1,0:T(8,128)(2,1)} %get-tuple-element.58), channel_id=1, source_target_pairs={{1,0},{0,1},{3,2},{2,3},{5,4},{4,5},{7,6},{6,7},{9,8},{8,9},{11,10... | collective-permute-start | bytes 1572872 | tf_op jit(solution)/shard_map/ppermute | solution.py:122
  171.7 15.1 %collective-permute-start.40 = (bf16[128,2048]{1,0:T(8,128)(2,1)}, bf16[128,2048]{1,0:T(8,128)(2,1)}, u32[]{:S(2)}, u32[]{:S(2)}) collective-permute-start(bf16[128,2048]{1,0:T(8,128)(2,1)} %get-tuple-element.67), channel_id=1, source_target_pairs={{2,0},{3,1},{0,2},{1,3},{6,4},{7,5},{4,6},{5,7},{10,8},{11,9},{8,1... | collective-permute-start | bytes 1572872 | tf_op jit(solution)/shard_map/ppermute | solution.py:122
  172.5 25.5 %collective-permute-start.47 = (bf16[128,2048]{1,0:T(8,128)(2,1)}, bf16[128,2048]{1,0:T(8,128)(2,1)}, u32[]{:S(2)}, u32[]{:S(2)}) collective-permute-start(bf16[128,2048]{1,0:T(8,128)(2,1)} %get-tuple-element.65), channel_id=1, source_target_pairs={{2,0},{3,1},{0,2},{1,3},{6,4},{7,5},{4,6},{5,7},{10,8},{11,9},{8,1... | collective-permute-start | bytes 1572872 | tf_op jit(solution)/shard_map/ppermute | solution.py:122
  181.0 21.7 %collective-permute-start.42 = (bf16[128,2048]{1,0:T(8,128)(2,1)}, bf16[128,2048]{1,0:T(8,128)(2,1)S(1)}, u32[]{:S(2)}, u32[]{:S(2)}) collective-permute-start(bf16[128,2048]{1,0:T(8,128)(2,1)} %get-tuple-element.60), channel_id=1, source_target_pairs={{1,0},{0,1},{3,2},{2,3},{5,4},{4,5},{7,6},{6,7},{9,8},{8,9},{11,10... | collective-permute-start | bytes 1572872 | tf_op jit(solution)/shard_map/ppermute | solution.py:122
  181.1 28.0 %collective-permute-start.44 = (bf16[128,2048]{1,0:T(8,128)(2,1)}, bf16[128,2048]{1,0:T(8,128)(2,1)S(1)}, u32[]{:S(2)}, u32[]{:S(2)}) collective-permute-start(bf16[128,2048]{1,0:T(8,128)(2,1)} %get-tuple-element.66), channel_id=1, source_target_pairs={{2,0},{3,1},{0,2},{1,3},{6,4},{7,5},{4,6},{5,7},{10,8},{11,9},{8,1... | collective-permute-start | bytes 1572872 | tf_op jit(solution)/shard_map/ppermute | solution.py:122
  200.6 20.5 %collective-permute-start.48 = (bf16[128,2048]{1,0:T(8,128)(2,1)S(1)}, bf16[128,2048]{1,0:T(8,128)(2,1)S(1)}, u32[]{:S(2)}, u32[]{:S(2)}) collective-permute-start(bf16[128,2048]{1,0:T(8,128)(2,1)S(1)} %get-tuple-element.69), channel_id=1, source_target_pairs={{4,0},{5,1},{6,2},{7,3},{0,4},{1,5},{2,6},{3,7},{12,8},{13,9},{14,... | collective-permute-start | bytes 1572872 | tf_op jit(solution)/shard_map/ppermute | solution.py:122
  202.1 19.4 %collective-permute-start.35 = (bf16[128,2048]{1,0:T(8,128)(2,1)S(1)}, bf16[128,2048]{1,0:T(8,128)(2,1)S(1)}, u32[]{:S(2)}, u32[]{:S(2)}) collective-permute-start(bf16[128,2048]{1,0:T(8,128)(2,1)S(1)} %copy-done.16), channel_id=1, source_target_pairs={{1,0},{0,1},{3,2},{2,3},{5,4},{4,5},{7,6},{6,7},{9,8},{8,9},{11,10... | collective-permute-start | bytes 1572872 | tf_op jit(solution)/shard_map/ppermute | solution.py:122
  202.1 19.4 %collective-permute-start.37 = (bf16[128,2048]{1,0:T(8,128)(2,1)S(1)}, bf16[128,2048]{1,0:T(8,128)(2,1)S(1)}, u32[]{:S(2)}, u32[]{:S(2)}) collective-permute-start(bf16[128,2048]{1,0:T(8,128)(2,1)S(1)} %copy-done.17), channel_id=1, source_target_pairs={{2,0},{3,1},{0,2},{1,3},{6,4},{7,5},{4,6},{5,7},{10,8},{11,9},{8,1... | collective-permute-start | bytes 1572872 | tf_op jit(solution)/shard_map/ppermute | solution.py:122
  202.7 28.8 %collective-permute-start.41 = (bf16[128,2048]{1,0:T(8,128)(2,1)S(1)}, bf16[128,2048]{1,0:T(8,128)(2,1)S(1)}, u32[]{:S(2)}, u32[]{:S(2)}) collective-permute-start(bf16[128,2048]{1,0:T(8,128)(2,1)S(1)} %get-tuple-element.68), channel_id=1, source_target_pairs={{4,0},{5,1},{6,2},{7,3},{0,4},{1,5},{2,6},{3,7},{12,8},{13,9},{14,... | collective-permute-start | bytes 1572872 | tf_op jit(solution)/shard_map/ppermute | solution.py:122
  221.4 20.4 %collective-permute-start.49 = (bf16[128,2048]{1,0:T(8,128)(2,1)S(1)}, bf16[128,2048]{1,0:T(8,128)(2,1)S(1)}, u32[]{:S(2)}, u32[]{:S(2)}) collective-permute-start(bf16[128,2048]{1,0:T(8,128)(2,1)S(1)} %fusion.37), channel_id=1, source_target_pairs={{8,0},{9,1},{10,2},{11,3},{12,4},{13,5},{14,6},{15,7},{0,8},{1,9},... | collective-permute-start | bytes 1572872 | tf_op jit(solution)/shard_map/ppermute | solution.py:122
  (46 other events, 361.4 us)

commit v11 on v10

--- a/solution.py
+++ b/solution.py
@@ -110,11 +110,19 @@
         groups.append((low, len(pieces)))
     partial = [None] * len(pieces)
     size = normed.shape[0]
-    for low, high in groups:
-        rows = jnp.concatenate([pieces[i][0][0] for i in range(low, high)], axis=0)
-        table = jnp.concatenate([pieces[i][0][1] for i in range(low, high)], axis=0)
+    ordered = []
+    for low, high in reversed(groups):
+        members = list(range(low, high))
+        if len(members) >= 8:
+            half = len(members) // 2
+            ordered += [members[:half], members[half:]]
+        else:
+            ordered.append(members)
+    for members in ordered:
+        rows = jnp.concatenate([pieces[i][0][0] for i in members], axis=0)
+        table = jnp.concatenate([pieces[i][0][1] for i in members], axis=0)
         out = expert(rows, table)
-        for offset, i in enumerate(range(low, high)):
+        for offset, i in enumerate(members):
             partial[i] = out[offset * size:(offset + 1) * size]
     for index in reversed(range(1, len(pieces))):
         _, parent, pairs = pieces[index]

time: 247 us -> 242 us (0.980)
  waiting for transfers between devices: 118 us -> 107 us
  local copies, waits for them, and re-layouts: 25.5 us -> 29.9 us
  starting transfers between devices: 30.7 us -> 33.4 us
    ppermute x22, waiting for transfers between devices: 22.5 us -> 12.9 us  [dense_moe(): grown.append((lax.ppermute(block, 'ep', pairs), parent, pairs))]
    ppermute x15, waiting for transfers between devices: 53.9 us -> 48.8 us  [dense_moe(): sent = lax.ppermute(partial[index].astype(jnp.bfloat16), 'ep', back)]
    ppermute x1, waiting for transfers between devices: 12.5 us -> 15.2 us  [full_weights(): other = lax.ppermute(packed, 'kv', [(0, 1), (1, 0)])]
    dot_general x3 -> x4, matrix products: 24.2 us -> 26.6 us  [expert(): out_rows = jnp.dot(act, full[2], preferred_element_type=jnp.float32)]
    unnamed x79 -> x81, local copies, waits for them, and re-layouts: 17.7 us -> 19.5 us
    slice x1 -> x2, local copies, waits for them, and re-layouts: 4.25 us -> 5.92 us  [dense_moe(): partial[i] = out[offset * size:(offset + 1) * size]]
    dot_general x2 -> x3, matrix products: 5.91 us -> 6.65 us  [expert(): gate_val = jnp.dot(rows, full[0], preferred_element_type=jnp.float32)]
  transfers between devices with their start and end apart: 50 -> 50, of which waited for: 19 -> 16; matrix products, arithmetic and copies ran while one was open for 24% -> 35% of each run, Pallas kernels for 0% -> 0%
where the time goes in v11:
time: 242 us; the launch traced here: 240 us
  waiting for transfers between devices  107 us (44%)
  matrix products  48.1 us (20%)
  starting transfers between devices  33.4 us (14%)
  local copies, waits for them, and re-layouts  29.9 us (12%)
  other arithmetic  20.9 us (9%)
    ppermute x15, waiting for transfers between devices, dense_moe(): sent = lax.ppermute(partial[index].astype(jnp.bfloat16), 'ep', back)  48.8 us
    dot_general x4, matrix products, expert(): out_rows = jnp.dot(act, full[2], preferred_element_type=jnp.float32)  26.6 us
    ppermute x8, waiting for transfers between devices, dense_moe(): lax.ppermute(pieces[0][0], 'ep', pairs)  23.1 us
    unnamed x81, local copies, waits for them, and re-layouts  19.5 us
    ppermute x1, waiting for transfers between devices, full_weights(): other = lax.ppermute(packed, 'kv', [(0, 1), (1, 0)])  15.2 us
    ppermute x22, starting transfers between devices, dense_moe(): grown.append((lax.ppermute(block, 'ep', pairs), parent, pairs))  13 us
    ppermute x22, waiting for transfers between devices, dense_moe(): grown.append((lax.ppermute(block, 'ep', pairs), parent, pairs))  12.9 us
    ppermute x15, starting transfers between devices, dense_moe(): sent = lax.ppermute(partial[index].astype(jnp.bfloat16), 'ep', back)  9.38 us
  transfers between devices with their start and end apart: 50, of which 16 were waited for; matrix products, arithmetic and copies ran while one was open for 35% of the time, Pallas kernels for 0%

profile of v11, /device:TPU:24, one launch (start us, length us, event | category | flops | bytes accessed | tf_op | source)
XLA Modules:
  0.0 240.2 jit_solution(10903021086686550227)
XLA Ops:
  3.4 3.7 %copy.104 = bf16[128,8,8,128]{3,2,1,0:T(8,128)(2,1)} copy(bf16[128,8,8,128]{3,1,2,0:T(8,128)(2,1)} %bitcast.92) | data formatting | bytes 4194304
  9.9 2.4 %bitcast_reduce_fusion.1 = (f32[128,8]{0,1:T(8,128)S(1)}, f32[8,1024,128]{2,1,0:T(8,128)S(1)}) fusion(pred[1024]{0:T(1024)(128)(4,1)S(1)} %add_compare_fusion, bf16[128,8,128]{2,1,0:T(8,128)(2,1)S(1)} %bitcast.102, bf16[1024,8,128]{2,1,0:T(8,128)(2,1)} %bitcast.96), kind=kOutput, calls=%fused_computation.4 | convolution fusion | flops 271580160 | bytes 6558720 | tf_op jit(solution)/shard_map/qhd,khd->qhk/dot_general | solution.py:260
  12.4 1.7 fusion.10
  14.1 2.6 %fusion.2 = (f32[128,8]{0,1:T(8,128)S(1)}, f32[128,8]{0,1:T(8,128)S(1)}, f32[8,1024,128]{2,1,0:T(8,128)S(1)}) fusion(f32[8,1024,128]{2,1,0:T(8,128)S(1)} %get-tuple-element.82, f32[128,8]{0,1:T(8,128)S(1)} %max.17, pred[1024]{0:T(1024)(128)(4,1)S(1)} %add_compare_fusion, bf16[128,8,128]{0,2,1:T(8,128)(2,1)} %bitcast.6, bf16[1024,8,128]{2,1,0:T(8,128)(2,1)S(1)} %bitcast.97), kind=kOutput, calls=%fused_computation.12 | convolution fusion | flops 275773440 | bytes 10761216 | tf_op jit(solution)/shard_map/qhd,khd->qhk/dot_general | solution.py:260
  19.5 1.7 fusion.8
  25.1 5.4 %collective-permute-done.2 = bf16[128,8,128]{0,2,1:T(8,128)(2,1)S(1)} collective-permute-done((bf16[128,8,128]{0,2,1:T(8,128)(2,1)S(1)}, bf16[128,8,128]{0,2,1:T(8,128)(2,1)S(1)}, u32[]{:S(2)}, u32[]{:S(2)}) %collective-permute-start.2) | collective-permute-done | bytes 262176 | tf_op jit(solution)/shard_map/ppermute | solution.py:298
  31.8 3.4 %pad_maximum_fusion = bf16[3,2048,256]{2,1,0:T(8,128)(2,1)} fusion(bf16[1,2048,256]{2,1,0:T(8,128)(2,1)S(1)} %stack_reshape_squeeze.3, bf16[1,2048,256]{2,1,0:T(8,128)(2,1)S(1)} %copy-done.3, bf16[1,2048,256]{2,1,0:T(8,128)(2,1)} %param.27), kind=kLoop, calls=%fused_computation.16 | loop fusion | flops 3145728 | bytes 6291456 | tf_op jit(solution)/shard_map/stack | solution.py:53
  36.4 1.8 collective-permute-start.9
  44.1 21.9 %collective-permute-done.4 = bf16[128,2048]{1,0:T(8,128)(2,1)} collective-permute-done((bf16[128,2048]{1,0:T(8,128)(2,1)S(1)}, bf16[128,2048]{1,0:T(8,128)(2,1)}, u32[]{:S(2)}, u32[]{:S(2)}) %collective-permute-start.4) | collective-permute-done | bytes 524320 | tf_op jit(solution)/shard_map/ppermute | solution.py:90
  68.9 10.9 %collective-permute-done.12 = bf16[128,2048]{1,0:T(8,128)(2,1)} collective-permute-done((bf16[128,2048]{1,0:T(8,128)(2,1)}, bf16[128,2048]{1,0:T(8,128)(2,1)}, u32[]{:S(2)}, u32[]{:S(2)}) %collective-permute-start.12) | collective-permute-done | bytes 524320 | tf_op jit(solution)/shard_map/ppermute | solution.py:100
  80.8 2.0 collective-permute-start.16
  88.4 15.2 %collective-permute-done.13 = bf16[3,2048,256]{2,1,0:T(8,128)(2,1)} collective-permute-done((bf16[3,2048,256]{2,1,0:T(8,128)(2,1)}, bf16[3,2048,256]{2,1,0:T(8,128)(2,1)}, u32[]{:S(2)}, u32[]{:S(2)}) %collective-permute-start.13) | collective-permute-done | bytes 3145760 | tf_op jit(solution)/shard_map/ppermute | solution.py:54
  105.1 4.3 %select_bitcast_fusion.1 = (bf16[2048,256]{1,0:T(8,128)(2,1)}, bf16[2048,256]{1,0:T(8,128)(2,1)}, bf16[1,2048,256]{2,1,0:T(8,128)(2,1)}, bf16[2048,256]{1,0:T(8,128)(2,1)}, bf16[2048,256]{1,0:T(8,128)(2,1)}) fusion(bf16[1,2048,256]{2,1,0:T(8,128)(2,1)S(1)} %copy-done.3, pred[]{:T(512)S(6)} %eq.42, bf16[3,2048,256]{2,1,0:T(8,128)(2,1)} %collective-permute-done.13, ...), kind=kLoop, calls=%fused_computation.84 | loop fusion | flops 2097152 | bytes 10485761 | tf_op jit(solution)/shard_map/jit(_where)/select_n | solution.py:61
  119.9 2.2 fusion.100
  124.4 3.4 %fusion.56 = f32[512,512]{1,0:T(8,128)} fusion(bf16[2048,512]{1,0:T(8,128)(2,1)S(1)} %get-tuple-element.37, bf16[128,2048]{1,0:T(8,128)(2,1)} %collective-permute-done.12, bf16[128,2048]{1,0:T(8,128)(2,1)S(1)} %copy-done.31, bf16[128,2048]{1,0:T(8,128)(2,1)} %collective-permute-done.4, bf16[128,2048]{1,0:T(8,128)(2,1)S(1)} %copy-done.18), kind=kOutput, calls=%fused_computation.101 | convolution fusion | flops 1082130432 | bytes 5242880 | tf_op jit(solution)/shard_map/dot_general | solution.py:79
  129.5 2.2 fusion.101
  132.9 6.3 %multiply_convert_fusion.1 = bf16[512,2048]{1,0:T(8,128)(2,1)} fusion(f32[512]{0:T(512)S(1)} %get-tuple-element.51, bf16[512,2048]{1,0:T(8,128)(2,1)S(1)} %pad_maximum_fusion.4, f32[512,512]{1,0:T(8,128)} %fusion.100, bf16[512,2048]{1,0:T(8,128)(2,1)} %copy-done.23, bf16[2048,512]{1,0:T(8,128)(2,1)} %copy-done.13), kind=kOutput, calls=%fused_computation.8 | convolution fusion | flops 2153250816 | bytes 9439232 | tf_op jit(solution)/shard_map/dot_general | solution.py:81
  139.2 3.0 %fusion.90 = (bf16[128,2048]{1,0:T(8,128)(2,1)}, bf16[128,2048]{1,0:T(8,128)(2,1)}, bf16[128,2048]{1,0:T(8,128)(2,1)}, bf16[128,2048]{1,0:T(8,128)(2,1)}) fusion(bf16[512,2048]{1,0:T(8,128)(2,1)} %multiply_convert_fusion.1), kind=kLoop, calls=%fused_computation.153 | loop fusion | bytes 4194304 | tf_op jit(solution)/shard_map/slice | solution.py:126
  146.8 2.2 fusion.102
  149.0 6.3 %multiply_convert_fusion = bf16[512,2048]{1,0:T(8,128)(2,1)} fusion(bf16[512,2048]{1,0:T(8,128)(2,1)S(1)} %pad_maximum_fusion.4, f32[512]{0:T(512)S(1)} %get-tuple-element.53, f32[512,512]{1,0:T(8,128)} %fusion.102, bf16[512,2048]{1,0:T(8,128)(2,1)} %copy-done.25, bf16[2048,512]{1,0:T(8,128)(2,1)} %copy-done.13), kind=kOutput, calls=%fused_computation.6 | convolution fusion | flops 2153250816 | bytes 9439232 | tf_op jit(solution)/shard_map/dot_general | solution.py:81
  155.2 2.9 %fusion.91 = (bf16[128,2048]{1,0:T(8,128)(2,1)}, bf16[128,2048]{1,0:T(8,128)(2,1)}, bf16[128,2048]{1,0:T(8,128)(2,1)}, bf16[128,2048]{1,0:T(8,128)(2,1)}) fusion(bf16[512,2048]{1,0:T(8,128)(2,1)} %multiply_convert_fusion), kind=kLoop, calls=%fused_computation.154 | loop fusion | bytes 4194304 | tf_op jit(solution)/shard_map/slice | solution.py:126
  159.2 6.9 %convert_multiply_fusion = f32[512,2048]{1,0:T(8,128)} fusion(bf16[512,2048]{1,0:T(8,128)(2,1)S(1)} %pad_maximum_fusion.4, f32[512]{0:T(512)S(1)} %get-tuple-element.52, f32[512,512]{1,0:T(8,128)} %fusion.101, bf16[512,2048]{1,0:T(8,128)(2,1)} %copy-done.26, bf16[2048,512]{1,0:T(8,128)(2,1)} %copy-done.13), kind=kOutput, calls=%fused_computation.7 | convolution fusion | flops 2152202240 | bytes 11536384 | tf_op jit(solution)/shard_map/dot_general | solution.py:81
  166.7 4.6 %fusion.41 = (bf16[128,2048]{1,0:T(8,128)(2,1)}, bf16[128,2048]{1,0:T(8,128)(2,1)}, bf16[128,2048]{1,0:T(8,128)(2,1)}, bf16[128,2048]{1,0:T(8,128)(2,1)}) fusion(f32[512,2048]{1,0:T(8,128)} %convert_multiply_fusion, bf16[128,2048]{1,0:T(8,128)(2,1)} %collective-permute-done.36, bf16[128,2048]{1,0:T(8,128)(2,1)} %collective-permute-done.46, ...), kind=kLoop, calls=%fused_computation.70 | loop fusion | flops 3145728 | bytes 8388608 | tf_op jit(solution)/shard_map/convert_element_type | solution.py:130
  173.3 7.2 %convert_multiply_fusion.1 = f32[512,2048]{1,0:T(8,128)} fusion(bf16[512,2048]{1,0:T(8,128)(2,1)S(1)} %pad_maximum_fusion.4, f32[512]{0:T(512)S(1)} %get-tuple-element.54, f32[512,512]{1,0:T(8,128)} %fusion.56, bf16[2048,512]{1,0:T(8,128)(2,1)} %copy-done.11, bf16[128,2048]{1,0:T(8,128)(2,1)} %collective-permute-done.12, bf16[128,2048]{1,0:T(8,128)(2,1)} %copy-done.30, ...), kind=kOutput, calls=%fused_computation.9 | convolution fusion | flops 2160590848 | bytes 11536384 | tf_op jit(solution)/shard_map/dot_general | solution.py:81
  182.1 4.2 %collective-permute-done.40 = bf16[128,2048]{1,0:T(8,128)(2,1)} collective-permute-done((bf16[128,2048]{1,0:T(8,128)(2,1)}, bf16[128,2048]{1,0:T(8,128)(2,1)}, u32[]{:S(2)}, u32[]{:S(2)}) %collective-permute-start.40) | collective-permute-done | bytes 524320 | tf_op jit(solution)/shard_map/ppermute | solution.py:130
  186.3 11.2 %collective-permute-done.47 = bf16[128,2048]{1,0:T(8,128)(2,1)} collective-permute-done((bf16[128,2048]{1,0:T(8,128)(2,1)}, bf16[128,2048]{1,0:T(8,128)(2,1)}, u32[]{:S(2)}, u32[]{:S(2)}) %collective-permute-start.47) | collective-permute-done | bytes 524320 | tf_op jit(solution)/shard_map/ppermute | solution.py:130
  197.5 2.6 %fusion.40 = (bf16[128,2048]{1,0:T(8,128)(2,1)S(1)}, bf16[128,2048]{1,0:T(8,128)(2,1)S(1)}) fusion(f32[512,2048]{1,0:T(8,128)} %convert_multiply_fusion.1, bf16[128,2048]{1,0:T(8,128)(2,1)} %collective-permute-done.40, bf16[128,2048]{1,0:T(8,128)(2,1)} %collective-permute-done.38, bf16[128,2048]{1,0:T(8,128)(2,1)} %collective-permute-done.47, ...), kind=kLoop, calls=%fused_computation.68 | loop fusion | flops 2621440 | bytes 5242880 | tf_op jit(solution)/shard_map/convert_element_type | solution.py:130
  203.8 4.8 %collective-permute-done.44 = bf16[128,2048]{1,0:T(8,128)(2,1)S(1)} collective-permute-done((bf16[128,2048]{1,0:T(8,128)(2,1)}, bf16[128,2048]{1,0:T(8,128)(2,1)S(1)}, u32[]{:S(2)}, u32[]{:S(2)}) %collective-permute-start.44) | collective-permute-done | bytes 524320 | tf_op jit(solution)/shard_map/ppermute | solution.py:130
  208.7 6.4 %collective-permute-done.48 = bf16[128,2048]{1,0:T(8,128)(2,1)S(1)} collective-permute-done((bf16[128,2048]{1,0:T(8,128)(2,1)S(1)}, bf16[128,2048]{1,0:T(8,128)(2,1)S(1)}, u32[]{:S(2)}, u32[]{:S(2)}) %collective-permute-start.48) | collective-permute-done | bytes 524320 | tf_op jit(solution)/shard_map/ppermute | solution.py:130
  216.8 2.6 %collective-permute-done.37 = bf16[128,2048]{1,0:T(8,128)(2,1)S(1)} collective-permute-done((bf16[128,2048]{1,0:T(8,128)(2,1)S(1)}, bf16[128,2048]{1,0:T(8,128)(2,1)S(1)}, u32[]{:S(2)}, u32[]{:S(2)}) %collective-permute-start.37) | collective-permute-done | bytes 524320 | tf_op jit(solution)/shard_map/ppermute | solution.py:130
  219.4 12.9 %collective-permute-done.41 = bf16[128,2048]{1,0:T(8,128)(2,1)S(1)} collective-permute-done((bf16[128,2048]{1,0:T(8,128)(2,1)S(1)}, bf16[128,2048]{1,0:T(8,128)(2,1)S(1)}, u32[]{:S(2)}, u32[]{:S(2)}) %collective-permute-start.41) | collective-permute-done | bytes 524320 | tf_op jit(solution)/shard_map/ppermute | solution.py:130
  232.4 6.5 %collective-permute-done.49 = bf16[128,2048]{1,0:T(8,128)(2,1)S(1)} collective-permute-done((bf16[128,2048]{1,0:T(8,128)(2,1)S(1)}, bf16[128,2048]{1,0:T(8,128)(2,1)S(1)}, u32[]{:S(2)}, u32[]{:S(2)}) %collective-permute-start.49) | collective-permute-done | bytes 524320 | tf_op jit(solution)/shard_map/ppermute | solution.py:130
  (197 shorter events, 63.2 us)
Async XLA Ops:
  1.1 13.0 %collective-permute-start = (bf16[128,1024]{0,1:T(8,128)(2,1)S(1)}, bf16[128,1024]{0,1:T(8,128)(2,1)}, u32[]{:S(2)}, u32[]{:S(2)}) collective-permute-start(bf16[128,1024]{0,1:T(8,128)(2,1)S(1)} %bitcast.106), channel_id=1, source_target_pairs={{0,16},{16,0},{1,17},{17,1},{2,18},{18,2},{3,19},{19,3},{4,20},{20... | collective-permute-start | bytes 786440 | tf_op jit(solution)/shard_map/ppermute | solution.py:288
  35.2 68.4 %collective-permute-start.13 = (bf16[3,2048,256]{2,1,0:T(8,128)(2,1)}, bf16[3,2048,256]{2,1,0:T(8,128)(2,1)}, u32[]{:S(2)}, u32[]{:S(2)}) collective-permute-start(bf16[3,2048,256]{2,1,0:T(8,128)(2,1)} %pad_maximum_fusion), channel_id=1, source_target_pairs={{0,16},{16,0},{1,17},{17,1},{2,18},{18,2},{3,19},{19,3},{4,20},{20... | collective-permute-start | bytes 9437192 | tf_op jit(solution)/shard_map/ppermute | solution.py:54
  40.4 25.6 %collective-permute-start.4 = (bf16[128,2048]{1,0:T(8,128)(2,1)S(1)}, bf16[128,2048]{1,0:T(8,128)(2,1)}, u32[]{:S(2)}, u32[]{:S(2)}) collective-permute-start(bf16[128,2048]{1,0:T(8,128)(2,1)S(1)} %multiply_convert_fusion.6), channel_id=1, source_target_pairs={{0,8},{1,9},{2,10},{3,11},{4,12},{5,13},{6,14},{7,15},{8,0},{9,1},... | collective-permute-start | bytes 1572872 | tf_op jit(solution)/shard_map/ppermute | solution.py:90
  41.9 24.1 %collective-permute-start.6 = (bf16[128,2048]{1,0:T(8,128)(2,1)S(1)}, bf16[128,2048]{1,0:T(8,128)(2,1)S(1)}, u32[]{:S(2)}, u32[]{:S(2)}) collective-permute-start(bf16[128,2048]{1,0:T(8,128)(2,1)S(1)} %multiply_convert_fusion.6), channel_id=1, source_target_pairs={{0,4},{1,5},{2,6},{3,7},{4,0},{5,1},{6,2},{7,3},{8,12},{9,13},{10,... | collective-permute-start | bytes 1572872 | tf_op jit(solution)/shard_map/ppermute | solution.py:90
  43.5 22.5 %collective-permute-start.8 = (bf16[128,2048]{1,0:T(8,128)(2,1)S(1)}, bf16[128,2048]{1,0:T(8,128)(2,1)}, u32[]{:S(2)}, u32[]{:S(2)}) collective-permute-start(bf16[128,2048]{1,0:T(8,128)(2,1)S(1)} %multiply_convert_fusion.6), channel_id=1, source_target_pairs={{0,2},{1,3},{2,0},{3,1},{4,6},{5,7},{6,4},{7,5},{8,10},{9,11},{10,... | collective-permute-start | bytes 1572872 | tf_op jit(solution)/shard_map/ppermute | solution.py:90
  66.0 13.7 %collective-permute-start.12 = (bf16[128,2048]{1,0:T(8,128)(2,1)}, bf16[128,2048]{1,0:T(8,128)(2,1)}, u32[]{:S(2)}, u32[]{:S(2)}) collective-permute-start(bf16[128,2048]{1,0:T(8,128)(2,1)} %collective-permute-done.4), channel_id=1, source_target_pairs={{0,4},{1,5},{2,6},{3,7},{4,0},{5,1},{6,2},{7,3},{8,12},{9,13},{10,... | collective-permute-start | bytes 1572872 | tf_op jit(solution)/shard_map/ppermute | solution.py:100
  67.6 13.2 %collective-permute-start.21 = (bf16[128,2048]{1,0:T(8,128)(2,1)}, bf16[128,2048]{1,0:T(8,128)(2,1)}, u32[]{:S(2)}, u32[]{:S(2)}) collective-permute-start(bf16[128,2048]{1,0:T(8,128)(2,1)} %collective-permute-done.4), channel_id=1, source_target_pairs={{0,1},{1,0},{2,3},{3,2},{4,5},{5,4},{6,7},{7,6},{8,9},{9,8},{10,11... | collective-permute-start | bytes 1572872 | tf_op jit(solution)/shard_map/ppermute | solution.py:100
  67.6 16.3 %collective-permute-start.22 = (bf16[128,2048]{1,0:T(8,128)(2,1)}, bf16[128,2048]{1,0:T(8,128)(2,1)}, u32[]{:S(2)}, u32[]{:S(2)}) collective-permute-start(bf16[128,2048]{1,0:T(8,128)(2,1)} %copy-done.30), channel_id=1, source_target_pairs={{0,1},{1,0},{2,3},{3,2},{4,5},{5,4},{6,7},{7,6},{8,9},{9,8},{10,11... | collective-permute-start | bytes 1572872 | tf_op jit(solution)/shard_map/ppermute | solution.py:100
  68.1 49.7 %collective-permute-start.14 = (bf16[128,2048]{1,0:T(8,128)(2,1)}, bf16[128,2048]{1,0:T(8,128)(2,1)}, u32[]{:S(2)}, u32[]{:S(2)}) collective-permute-start(bf16[128,2048]{1,0:T(8,128)(2,1)} %collective-permute-done.4), channel_id=1, source_target_pairs={{0,2},{1,3},{2,0},{3,1},{4,6},{5,7},{6,4},{7,5},{8,10},{9,11},{10,... | collective-permute-start | bytes 1572872 | tf_op jit(solution)/shard_map/ppermute | solution.py:100
  80.8 37.5 %collective-permute-start.16 = (bf16[128,2048]{1,0:T(8,128)(2,1)}, bf16[128,2048]{1,0:T(8,128)(2,1)}, u32[]{:S(2)}, u32[]{:S(2)}) collective-permute-start(bf16[128,2048]{1,0:T(8,128)(2,1)} %copy-done.30), channel_id=1, source_target_pairs={{0,2},{1,3},{2,0},{3,1},{4,6},{5,7},{6,4},{7,5},{8,10},{9,11},{10,... | collective-permute-start | bytes 1572872 | tf_op jit(solution)/shard_map/ppermute | solution.py:100
  83.9 29.7 %collective-permute-start.19 = (f32[128,16]{0,1:T(8,128)S(1)}, f32[128,16]{0,1:T(8,128)S(1)}, u32[]{:S(2)}, u32[]{:S(2)}) collective-permute-start(f32[128,16]{0,1:T(8,128)S(1)} %collective-permute-done.5), channel_id=1, source_target_pairs={{0,4},{1,5},{2,6},{3,7},{4,0},{5,1},{6,2},{7,3},{8,12},{9,13},{10,... | collective-permute-start | bytes 24584 | tf_op jit(solution)/shard_map/ppermute | solution.py:100
  85.4 28.8 %collective-permute-start.15 = (f32[128,16]{0,1:T(8,128)S(1)}, f32[128,16]{0,1:T(8,128)S(1)}, u32[]{:S(2)}, u32[]{:S(2)}) collective-permute-start(f32[128,16]{0,1:T(8,128)S(1)} %collective-permute-done.5), channel_id=1, source_target_pairs={{0,2},{1,3},{2,0},{3,1},{4,6},{5,7},{6,4},{7,5},{8,10},{9,11},{10,... | collective-permute-start | bytes 24584 | tf_op jit(solution)/shard_map/ppermute | solution.py:100
  103.6 14.7 %collective-permute-start.18 = (bf16[128,2048]{1,0:T(8,128)(2,1)}, bf16[128,2048]{1,0:T(8,128)(2,1)}, u32[]{:S(2)}, u32[]{:S(2)}) collective-permute-start(bf16[128,2048]{1,0:T(8,128)(2,1)} %collective-permute-done.12), channel_id=1, source_target_pairs={{0,2},{1,3},{2,0},{3,1},{4,6},{5,7},{6,4},{7,5},{8,10},{9,11},{10,... | collective-permute-start | bytes 1572872 | tf_op jit(solution)/shard_map/ppermute | solution.py:100
  117.3 11.7 %collective-permute-start.24 = (f32[128,16]{0,1:T(8,128)S(1)}, f32[128,16]{0,1:T(8,128)S(1)}, u32[]{:S(2)}, u32[]{:S(2)}) collective-permute-start(f32[128,16]{0,1:T(8,128)S(1)} %collective-permute-done.5), channel_id=1, source_target_pairs={{0,1},{1,0},{2,3},{3,2},{4,5},{5,4},{6,7},{7,6},{8,9},{9,8},{10,11... | collective-permute-start | bytes 24584 | tf_op jit(solution)/shard_map/ppermute | solution.py:100
  117.8 11.3 %collective-permute-start.25 = (f32[128,16]{0,1:T(8,128)S(1)}, f32[128,16]{0,1:T(8,128)S(1)}, u32[]{:S(2)}, u32[]{:S(2)}) collective-permute-start(f32[128,16]{0,1:T(8,128)S(1)} %collective-permute-done.7), channel_id=1, source_target_pairs={{0,1},{1,0},{2,3},{3,2},{4,5},{5,4},{6,7},{7,6},{8,9},{9,8},{10,11... | collective-permute-start | bytes 24584 | tf_op jit(solution)/shard_map/ppermute | solution.py:100
  117.8 14.0 %collective-permute-start.26 = (f32[128,16]{0,1:T(8,128)S(1)}, f32[128,16]{0,1:T(8,128)S(1)}, u32[]{:S(2)}, u32[]{:S(2)}) collective-permute-start(f32[128,16]{0,1:T(8,128)S(1)} %collective-permute-done.19), channel_id=1, source_target_pairs={{0,1},{1,0},{2,3},{3,2},{4,5},{5,4},{6,7},{7,6},{8,9},{9,8},{10,11... | collective-permute-start | bytes 24584 | tf_op jit(solution)/shard_map/ppermute | solution.py:100
  118.3 13.5 %collective-permute-start.32 = (f32[128,16]{0,1:T(8,128)S(1)}, f32[128,16]{0,1:T(8,128)S(1)}, u32[]{:S(2)}, u32[]{:S(2)}) collective-permute-start(f32[128,16]{0,1:T(8,128)S(1)} %collective-permute-done.9), channel_id=1, source_target_pairs={{0,1},{1,0},{2,3},{3,2},{4,5},{5,4},{6,7},{7,6},{8,9},{9,8},{10,11... | collective-permute-start | bytes 24584 | tf_op jit(solution)/shard_map/ppermute | solution.py:100
  118.4 13.9 %collective-permute-start.33 = (f32[128,16]{0,1:T(8,128)S(1)}, f32[128,16]{0,1:T(8,128)S(1)}, u32[]{:S(2)}, u32[]{:S(2)}) collective-permute-start(f32[128,16]{0,1:T(8,128)S(1)} %collective-permute-done.15), channel_id=1, source_target_pairs={{0,1},{1,0},{2,3},{3,2},{4,5},{5,4},{6,7},{7,6},{8,9},{9,8},{10,11... | collective-permute-start | bytes 24584 | tf_op jit(solution)/shard_map/ppermute | solution.py:100
  131.8 11.6 %collective-permute-start.29 = (bf16[128,2048]{1,0:T(8,128)(2,1)}, bf16[128,2048]{1,0:T(8,128)(2,1)}, u32[]{:S(2)}, u32[]{:S(2)}) collective-permute-start(bf16[128,2048]{1,0:T(8,128)(2,1)} %collective-permute-done.14), channel_id=1, source_target_pairs={{0,1},{1,0},{2,3},{3,2},{4,5},{5,4},{6,7},{7,6},{8,9},{9,8},{10,11... | collective-permute-start | bytes 1572872 | tf_op jit(solution)/shard_map/ppermute | solution.py:100
  132.3 12.3 %collective-permute-start.30 = (bf16[128,2048]{1,0:T(8,128)(2,1)}, bf16[128,2048]{1,0:T(8,128)(2,1)}, u32[]{:S(2)}, u32[]{:S(2)}) collective-permute-start(bf16[128,2048]{1,0:T(8,128)(2,1)} %collective-permute-done.16), channel_id=1, source_target_pairs={{0,1},{1,0},{2,3},{3,2},{4,5},{5,4},{6,7},{7,6},{8,9},{9,8},{10,11... | collective-permute-start | bytes 1572872 | tf_op jit(solution)/shard_map/ppermute | solution.py:100
  132.4 13.3 %collective-permute-start.31 = (bf16[128,2048]{1,0:T(8,128)(2,1)}, bf16[128,2048]{1,0:T(8,128)(2,1)}, u32[]{:S(2)}, u32[]{:S(2)}) collective-permute-start(bf16[128,2048]{1,0:T(8,128)(2,1)} %collective-permute-done.18), channel_id=1, source_target_pairs={{0,1},{1,0},{2,3},{3,2},{4,5},{5,4},{6,7},{7,6},{8,9},{9,8},{10,11... | collective-permute-start | bytes 1572872 | tf_op jit(solution)/shard_map/ppermute | solution.py:100
  142.2 38.3 %collective-permute-start.38 = (bf16[128,2048]{1,0:T(8,128)(2,1)}, bf16[128,2048]{1,0:T(8,128)(2,1)}, u32[]{:S(2)}, u32[]{:S(2)}) collective-permute-start(bf16[128,2048]{1,0:T(8,128)(2,1)} %get-tuple-element.74), channel_id=1, source_target_pairs={{1,0},{0,1},{3,2},{2,3},{5,4},{4,5},{7,6},{6,7},{9,8},{8,9},{11,10... | collective-permute-start | bytes 1572872 | tf_op jit(solution)/shard_map/ppermute | solution.py:130
  166.1 16.0 %collective-permute-start.45 = (bf16[128,2048]{1,0:T(8,128)(2,1)}, bf16[128,2048]{1,0:T(8,128)(2,1)}, u32[]{:S(2)}, u32[]{:S(2)}) collective-permute-start(bf16[128,2048]{1,0:T(8,128)(2,1)} %get-tuple-element.72), channel_id=1, source_target_pairs={{1,0},{0,1},{3,2},{2,3},{5,4},{4,5},{7,6},{6,7},{9,8},{8,9},{11,10... | collective-permute-start | bytes 1572872 | tf_op jit(solution)/shard_map/ppermute | solution.py:130
  166.6 35.7 %collective-permute-start.42 = (bf16[128,2048]{1,0:T(8,128)(2,1)}, bf16[128,2048]{1,0:T(8,128)(2,1)}, u32[]{:S(2)}, u32[]{:S(2)}) collective-permute-start(bf16[128,2048]{1,0:T(8,128)(2,1)} %get-tuple-element.73), channel_id=1, source_target_pairs={{1,0},{0,1},{3,2},{2,3},{5,4},{4,5},{7,6},{6,7},{9,8},{8,9},{11,10... | collective-permute-start | bytes 1572872 | tf_op jit(solution)/shard_map/ppermute | solution.py:130
  171.2 15.0 %collective-permute-start.40 = (bf16[128,2048]{1,0:T(8,128)(2,1)}, bf16[128,2048]{1,0:T(8,128)(2,1)}, u32[]{:S(2)}, u32[]{:S(2)}) collective-permute-start(bf16[128,2048]{1,0:T(8,128)(2,1)} %get-tuple-element.61), channel_id=1, source_target_pairs={{2,0},{3,1},{0,2},{1,3},{6,4},{7,5},{4,6},{5,7},{10,8},{11,9},{8,1... | collective-permute-start | bytes 1572872 | tf_op jit(solution)/shard_map/ppermute | solution.py:130
  172.8 24.8 %collective-permute-start.47 = (bf16[128,2048]{1,0:T(8,128)(2,1)}, bf16[128,2048]{1,0:T(8,128)(2,1)}, u32[]{:S(2)}, u32[]{:S(2)}) collective-permute-start(bf16[128,2048]{1,0:T(8,128)(2,1)} %get-tuple-element.59), channel_id=1, source_target_pairs={{2,0},{3,1},{0,2},{1,3},{6,4},{7,5},{4,6},{5,7},{10,8},{11,9},{8,1... | collective-permute-start | bytes 1572872 | tf_op jit(solution)/shard_map/ppermute | solution.py:130
  180.5 28.2 %collective-permute-start.44 = (bf16[128,2048]{1,0:T(8,128)(2,1)}, bf16[128,2048]{1,0:T(8,128)(2,1)S(1)}, u32[]{:S(2)}, u32[]{:S(2)}) collective-permute-start(bf16[128,2048]{1,0:T(8,128)(2,1)} %get-tuple-element.60), channel_id=1, source_target_pairs={{2,0},{3,1},{0,2},{1,3},{6,4},{7,5},{4,6},{5,7},{10,8},{11,9},{8,1... | collective-permute-start | bytes 1572872 | tf_op jit(solution)/shard_map/ppermute | solution.py:130
  200.1 14.9 %collective-permute-start.48 = (bf16[128,2048]{1,0:T(8,128)(2,1)S(1)}, bf16[128,2048]{1,0:T(8,128)(2,1)S(1)}, u32[]{:S(2)}, u32[]{:S(2)}) collective-permute-start(bf16[128,2048]{1,0:T(8,128)(2,1)S(1)} %get-tuple-element.63), channel_id=1, source_target_pairs={{4,0},{5,1},{6,2},{7,3},{0,4},{1,5},{2,6},{3,7},{12,8},{13,9},{14,... | collective-permute-start | bytes 1572872 | tf_op jit(solution)/shard_map/ppermute | solution.py:130
  200.6 16.2 %collective-permute-start.27 = (bf16[128,2048]{1,0:T(8,128)(2,1)S(1)}, bf16[128,2048]{1,0:T(8,128)(2,1)S(1)}, u32[]{:S(2)}, u32[]{:S(2)}) collective-permute-start(bf16[128,2048]{1,0:T(8,128)(2,1)S(1)} %copy-done.20), channel_id=1, source_target_pairs={{1,0},{0,1},{3,2},{2,3},{5,4},{4,5},{7,6},{6,7},{9,8},{8,9},{11,10... | collective-permute-start | bytes 1572872 | tf_op jit(solution)/shard_map/ppermute | solution.py:130
  200.7 18.8 %collective-permute-start.37 = (bf16[128,2048]{1,0:T(8,128)(2,1)S(1)}, bf16[128,2048]{1,0:T(8,128)(2,1)S(1)}, u32[]{:S(2)}, u32[]{:S(2)}) collective-permute-start(bf16[128,2048]{1,0:T(8,128)(2,1)S(1)} %copy-done.16), channel_id=1, source_target_pairs={{2,0},{3,1},{0,2},{1,3},{6,4},{7,5},{4,6},{5,7},{10,8},{11,9},{8,1... | collective-permute-start | bytes 1572872 | tf_op jit(solution)/shard_map/ppermute | solution.py:130
  202.3 30.1 %collective-permute-start.41 = (bf16[128,2048]{1,0:T(8,128)(2,1)S(1)}, bf16[128,2048]{1,0:T(8,128)(2,1)S(1)}, u32[]{:S(2)}, u32[]{:S(2)}) collective-permute-start(bf16[128,2048]{1,0:T(8,128)(2,1)S(1)} %get-tuple-element.62), channel_id=1, source_target_pairs={{4,0},{5,1},{6,2},{7,3},{0,4},{1,5},{2,6},{3,7},{12,8},{13,9},{14,... | collective-permute-start | bytes 1572872 | tf_op jit(solution)/shard_map/ppermute | solution.py:130
  216.4 22.5 %collective-permute-start.49 = (bf16[128,2048]{1,0:T(8,128)(2,1)S(1)}, bf16[128,2048]{1,0:T(8,128)(2,1)S(1)}, u32[]{:S(2)}, u32[]{:S(2)}) collective-permute-start(bf16[128,2048]{1,0:T(8,128)(2,1)S(1)} %fusion.37), channel_id=1, source_target_pairs={{8,0},{9,1},{10,2},{11,3},{12,4},{13,5},{14,6},{15,7},{0,8},{1,9},... | collective-permute-start | bytes 1572872 | tf_op jit(solution)/shard_map/ppermute | solution.py:130
  (51 other events, 350.3 us)

commit v12 on v11

--- a/solution.py
+++ b/solution.py
@@ -82,22 +82,34 @@
         out_rows = out_rows.astype(jnp.bfloat16).astype(jnp.float32)
         return out_rows * weights[:, None]
 
+    every_table = weight_table[None]
+    ep_count = lax.axis_size("ep")
+    span = 1
+    while span < ep_count:
+        swapped = lax.ppermute(every_table, "ep", [(r, r ^ span) for r in range(ep_count)])
+        every_table = jnp.concatenate([every_table, swapped], axis=0)
+        span *= 2
+    origins = {0: np.arange(ep_count)}
     pieces = [((normed, weight_table), None, None)]
     groups = []
     low = 0
     tie_at = next((n + 1 for n, (_, ends) in enumerate(plan) if ends), 0)
     first_wave = [
-        [lax.ppermute(pieces[0][0], "ep", pairs) for pairs in pairs_list] for pairs_list, _ in plan
+        [(lax.ppermute(normed, "ep", pairs), None) for pairs in pairs_list] for pairs_list, _ in plan
     ]
     first_wave = lax.optimization_barrier(first_wave)
     for number, (pairs_list, ends) in enumerate(plan):
         grown = []
         for parent, (block, _, _) in enumerate(pieces):
             for slot, pairs in enumerate(pairs_list):
+                moved = np.zeros(ep_count, dtype=np.int64)
+                for source, target in pairs:
+                    moved[target] = origins[parent][source]
+                origins[len(pieces) + len(grown)] = moved
                 if parent == 0:
                     grown.append((first_wave[number][slot], parent, pairs))
                 else:
-                    grown.append((lax.ppermute(block, "ep", pairs), parent, pairs))
+                    grown.append(((lax.ppermute(block[0], "ep", pairs), None), parent, pairs))
         if number == tie_at:
             tied = lax.optimization_barrier((tuple(full), [piece[0] for piece in grown]))
             full = list(tied[0])
@@ -120,7 +132,14 @@
             ordered.append(members)
     for members in ordered:
         rows = jnp.concatenate([pieces[i][0][0] for i in members], axis=0)
-        table = jnp.concatenate([pieces[i][0][1] for i in members], axis=0)
+        tables = []
+        for i in members:
+            if i == 0:
+                tables.append(weight_table)
+            else:
+                place = jnp.bitwise_xor(jnp.asarray(origins[i], jnp.int32)[own_expert], own_expert)
+                tables.append(lax.dynamic_index_in_dim(every_table, place, 0, False))
+        table = jnp.concatenate(tables, axis=0)
         out = expert(rows, table)
         for offset, i in enumerate(members):
             partial[i] = out[offset * size:(offset + 1) * size]
@@ -135,7 +154,7 @@
 def gather_plan(mesh, shapes):
     kv_count, ep_count = mesh.devices.shape
     rows = ep_count * shapes[0][1] // kv_count
-    if EXP_DEV != 1 or shapes[12][0] != ep_count or rows > 4096:
+    if EXP_DEV != 1 or shapes[12][0] != ep_count or rows > 4096 or ep_count & (ep_count - 1):
         return None
     places = []
     for device in mesh.devices[0]:

time: 242 us -> 253 us (1.045); the launches traced: 240 us -> 249 us
  between operations: 1.31 us -> 9.97 us
  starting transfers between devices: 33.4 us -> 26.6 us
  matrix products: 48.1 us -> 53 us
  waiting for transfers between devices: 107 us -> 104 us
  local copies, waits for them, and re-layouts: 29.9 us -> 32.7 us
    ppermute x30 -> x19, starting transfers between devices: 19.1 us -> 8.94 us  [the longest x11 4.39 us: dense_moe(): grown.append(((lax.ppermute(block[0], 'ep', pairs), None), parent, pairs))]
    dynamic_slice x0 -> x15, local copies, waits for them, and re-layouts: none -> 8.39 us  [dense_moe(): jnp.asarray(origins[i], jnp.int32)[own_expert]]
    unnamed x81 -> x111, local copies, waits for them, and re-layouts: 19.5 us -> 15.1 us
    ppermute x30 -> x19, waiting for transfers between devices: 36 us -> 39.9 us  [the longest x4 16.9 us: dense_moe(): lax.ppermute(normed, 'ep', pairs)]
    ppermute x1, waiting for transfers between devices: 15.2 us -> 11.5 us  [full_weights(): other = lax.ppermute(packed, 'kv', [(0, 1), (1, 0)])]
    ppermute x15, starting transfers between devices: 9.38 us -> 12.8 us  [dense_moe(): sent = lax.ppermute(partial[index].astype(jnp.bfloat16), 'ep', back)]
  transfers between devices with their start and end apart: 50 -> 39, of which waited for: 16 -> 14; matrix products, arithmetic and copies ran while one was open for 35% -> 41% of each run, Pallas kernels for 0% -> 0%
where the time goes in v12:
time: 253 us; the launch traced here: 249 us
  waiting for transfers between devices  104 us (41%)
  matrix products  53 us (21%)
  local copies, waits for them, and re-layouts  32.7 us (13%)
  starting transfers between devices  26.6 us (11%)
  other arithmetic  22.3 us (9%)
  between operations  9.97 us (4%)
    ppermute x15, waiting for transfers between devices, dense_moe(): sent = lax.ppermute(partial[index].astype(jnp.bfloat16), 'ep', back)  46.5 us
    dot_general x4, matrix products, expert(): out_rows = jnp.dot(act, full[2], preferred_element_type=jnp.float32)  26.7 us
    ppermute x4, waiting for transfers between devices, dense_moe(): lax.ppermute(normed, 'ep', pairs)  16.9 us
    unnamed x111, local copies, waits for them, and re-layouts  15.1 us
    ppermute x15, starting transfers between devices, dense_moe(): sent = lax.ppermute(partial[index].astype(jnp.bfloat16), 'ep', back)  12.8 us
    ppermute x4, waiting for transfers between devices, dense_moe(): lax.ppermute(every_table, 'ep', [(r, r ^ span) for r in range(ep_count)])  12.6 us
    ppermute x1, waiting for transfers between devices, full_weights(): other = lax.ppermute(packed, 'kv', [(0, 1), (1, 0)])  11.5 us
    ppermute x11, waiting for transfers between devices, dense_moe(): grown.append(((lax.ppermute(block[0], 'ep', pairs), None), parent, pairs))  10.5 us
  transfers between devices with their start and end apart: 39, of which 14 were waited for; matrix products, arithmetic and copies ran while one was open for 41% of the time, Pallas kernels for 0%

profile of v12, /device:TPU:24, one launch (start us, length us, event | category | flops | bytes accessed | tf_op | source)
XLA Modules:
  0.0 248.6 jit_solution(3465451659400977227)
XLA Ops:
  4.8 3.7 %copy.119 = bf16[128,8,8,128]{3,2,1,0:T(8,128)(2,1)} copy(bf16[128,8,8,128]{3,1,2,0:T(8,128)(2,1)} %bitcast.139) | data formatting | bytes 4194304
  10.8 2.6 %bitcast_reduce_fusion.1 = (f32[128,8]{0,1:T(8,128)S(1)}, f32[8,1024,128]{2,1,0:T(8,128)S(1)}) fusion(pred[1024]{0:T(1024)(128)(4,1)S(1)} %add_compare_fusion, bf16[128,8,128]{2,1,0:T(8,128)(2,1)S(1)} %bitcast.149, bf16[1024,8,128]{2,1,0:T(8,128)(2,1)} %bitcast.143), kind=kOutput, calls=%fused_computation.4 | convolution fusion | flops 271580160 | bytes 6558720 | tf_op jit(solution)/shard_map/qhd,khd->qhk/dot_general | solution.py:279
  13.5 2.5 %fusion.10 = f32[8,128,128]{1,2,0:T(8,128)} fusion(f32[8,1024,128]{2,1,0:T(8,128)S(1)} %get-tuple-element.81, f32[128,8]{0,1:T(8,128)S(1)} %max.17, pred[1024]{0:T(1024)(128)(4,1)S(1)} %add_compare_fusion, bf16[1024,8,128]{2,1,0:T(8,128)(2,1)S(1)} %bitcast.141), kind=kOutput, calls=%fused_computation.25 | convolution fusion | flops 272629760 | bytes 6820864 | tf_op jit(solution)/shard_map/qhk,khd->qhd/dot_general | solution.py:291
  16.2 4.6 %fusion.2 = (f32[128,8]{0,1:T(8,128)S(1)}, f32[128,8]{0,1:T(8,128)S(1)}, f32[8,1024,128]{2,1,0:T(8,128)S(1)}) fusion(f32[8,1024,128]{2,1,0:T(8,128)} %copy-done.44, f32[128,8]{0,1:T(8,128)S(1)} %max.17, pred[1024]{0:T(1024)(128)(4,1)S(1)} %add_compare_fusion, bf16[128,8,128]{0,2,1:T(8,128)(2,1)} %bitcast.6, bf16[1024,8,128]{2,1,0:T(8,128)(2,1)} %bitcast.144), kind=kOutput, calls=%fused_computation.12 | convolution fusion | flops 275773440 | bytes 10761216 | tf_op jit(solution)/shard_map/qhd,khd->qhk/dot_general | solution.py:279
  29.3 6.1 %collective-permute-done.2 = bf16[128,8,128]{0,2,1:T(8,128)(2,1)S(1)} collective-permute-done((bf16[128,8,128]{0,2,1:T(8,128)(2,1)S(1)}, bf16[128,8,128]{0,2,1:T(8,128)(2,1)S(1)}, u32[]{:S(2)}, u32[]{:S(2)}) %collective-permute-start.2) | collective-permute-done | bytes 262176 | tf_op jit(solution)/shard_map/ppermute | solution.py:317
  37.0 3.4 %pad_maximum_fusion = bf16[3,2048,256]{2,1,0:T(8,128)(2,1)} fusion(bf16[1,2048,256]{2,1,0:T(8,128)(2,1)S(1)} %stack_reshape_squeeze.3, bf16[1,2048,256]{2,1,0:T(8,128)(2,1)S(1)} %copy-done.4, bf16[1,2048,256]{2,1,0:T(8,128)(2,1)} %param.42), kind=kLoop, calls=%fused_computation.16 | loop fusion | flops 3145728 | bytes 6291456 | tf_op jit(solution)/shard_map/stack | solution.py:53
  62.4 5.7 %collective-permute-done.4 = bf16[128,2048]{1,0:T(8,128)(2,1)} collective-permute-done((bf16[128,2048]{1,0:T(8,128)(2,1)}, bf16[128,2048]{1,0:T(8,128)(2,1)}, u32[]{:S(2)}, u32[]{:S(2)}) %collective-permute-start.4) | collective-permute-done | bytes 524320 | tf_op jit(solution)/shard_map/ppermute | solution.py:98
  68.1 11.2 %collective-permute-done.5 = bf16[128,2048]{1,0:T(8,128)(2,1)} collective-permute-done((bf16[128,2048]{1,0:T(8,128)(2,1)}, bf16[128,2048]{1,0:T(8,128)(2,1)}, u32[]{:S(2)}, u32[]{:S(2)}) %collective-permute-start.5) | collective-permute-done | bytes 524320 | tf_op jit(solution)/shard_map/ppermute | solution.py:98
  80.4 12.1 %collective-permute-done.16 = f32[8,128,16]{1,2,0:T(8,128)S(1)} collective-permute-done((f32[8,128,16]{1,2,0:T(8,128)S(1)}, f32[8,128,16]{1,2,0:T(8,128)S(1)}, u32[]{:S(2)}, u32[]{:S(2)}) %collective-permute-start.16) | collective-permute-done | bytes 65568 | tf_op jit(solution)/shard_map/ppermute | solution.py:89
  98.5 11.5 %collective-permute-done.9 = bf16[3,2048,256]{2,1,0:T(8,128)(2,1)} collective-permute-done((bf16[3,2048,256]{2,1,0:T(8,128)(2,1)}, bf16[3,2048,256]{2,1,0:T(8,128)(2,1)}, u32[]{:S(2)}, u32[]{:S(2)}) %collective-permute-start.9) | collective-permute-done | bytes 3145760 | tf_op jit(solution)/shard_map/ppermute | solution.py:54
  110.0 4.3 %select_bitcast_fusion.1 = (bf16[2048,256]{1,0:T(8,128)(2,1)}, bf16[2048,256]{1,0:T(8,128)(2,1)}, bf16[1,2048,256]{2,1,0:T(8,128)(2,1)}, bf16[2048,256]{1,0:T(8,128)(2,1)}, bf16[2048,256]{1,0:T(8,128)(2,1)}) fusion(bf16[1,2048,256]{2,1,0:T(8,128)(2,1)S(1)} %copy-done.4, pred[]{:T(512)S(6)} %eq.38, bf16[3,2048,256]{2,1,0:T(8,128)(2,1)} %collective-permute-done.9, ...), kind=kLoop, calls=%fused_computation.84 | loop fusion | flops 2097152 | bytes 10485761 | tf_op jit(solution)/shard_map/jit(_where)/select_n | solution.py:61
  119.9 9.9 %collective-permute-done.12 = bf16[128,2048]{1,0:T(8,128)(2,1)} collective-permute-done((bf16[128,2048]{1,0:T(8,128)(2,1)}, bf16[128,2048]{1,0:T(8,128)(2,1)}, u32[]{:S(2)}, u32[]{:S(2)}) %collective-permute-start.12) | collective-permute-done | bytes 524320 | tf_op jit(solution)/shard_map/ppermute | solution.py:112
  129.9 1.9 constant_dynamic-update-slice_fusion.12
  131.8 2.2 fusion.100
  134.0 6.3 %multiply_convert_fusion.1 = bf16[512,2048]{1,0:T(8,128)(2,1)} fusion(bf16[512,2048]{1,0:T(8,128)(2,1)S(1)} %pad_maximum_fusion.4, f32[512]{0:T(512)S(1)} %get-tuple-element.35, f32[512,512]{1,0:T(8,128)} %fusion.100, bf16[512,2048]{1,0:T(8,128)(2,1)} %copy-done.24, bf16[2048,512]{1,0:T(8,128)(2,1)} %get-tuple-element.26), kind=kOutput, calls=%fused_computation.8 | convolution fusion | flops 2153250816 | bytes 9439232 | tf_op jit(solution)/shard_map/dot_general | solution.py:81
  140.3 3.0 %fusion.90 = (bf16[128,2048]{1,0:T(8,128)(2,1)}, bf16[128,2048]{1,0:T(8,128)(2,1)}, bf16[128,2048]{1,0:T(8,128)(2,1)}, bf16[128,2048]{1,0:T(8,128)(2,1)}) fusion(bf16[512,2048]{1,0:T(8,128)(2,1)} %multiply_convert_fusion.1), kind=kLoop, calls=%fused_computation.176 | loop fusion | bytes 4194304 | tf_op jit(solution)/shard_map/slice | solution.py:145
  147.6 2.2 fusion.101
  151.1 2.3 fusion.102
  153.4 6.3 %multiply_convert_fusion = bf16[512,2048]{1,0:T(8,128)(2,1)} fusion(bf16[512,2048]{1,0:T(8,128)(2,1)S(1)} %pad_maximum_fusion.4, f32[512]{0:T(512)S(1)} %get-tuple-element.37, f32[512,512]{1,0:T(8,128)} %fusion.102, bf16[512,2048]{1,0:T(8,128)(2,1)} %copy-done.26, bf16[2048,512]{1,0:T(8,128)(2,1)} %get-tuple-element.26), kind=kOutput, calls=%fused_computation.6 | convolution fusion | flops 2153250816 | bytes 9439232 | tf_op jit(solution)/shard_map/dot_general | solution.py:81
  159.7 2.9 %fusion.91 = (bf16[128,2048]{1,0:T(8,128)(2,1)}, bf16[128,2048]{1,0:T(8,128)(2,1)}, bf16[128,2048]{1,0:T(8,128)(2,1)}, bf16[128,2048]{1,0:T(8,128)(2,1)}) fusion(bf16[512,2048]{1,0:T(8,128)(2,1)} %multiply_convert_fusion), kind=kLoop, calls=%fused_computation.177 | loop fusion | bytes 4194304 | tf_op jit(solution)/shard_map/slice | solution.py:145
  163.6 6.9 %convert_multiply_fusion = f32[512,2048]{1,0:T(8,128)} fusion(bf16[512,2048]{1,0:T(8,128)(2,1)S(1)} %pad_maximum_fusion.4, f32[512]{0:T(512)S(1)} %get-tuple-element.36, f32[512,512]{1,0:T(8,128)} %fusion.101, bf16[512,2048]{1,0:T(8,128)(2,1)} %copy-done.23, bf16[2048,512]{1,0:T(8,128)(2,1)} %get-tuple-element.26), kind=kOutput, calls=%fused_computation.7 | convolution fusion | flops 2152202240 | bytes 11536384 | tf_op jit(solution)/shard_map/dot_general | solution.py:81
  170.5 4.6 %fusion.56 = f32[512,512]{1,0:T(8,128)} fusion(bf16[2048,512]{1,0:T(8,128)(2,1)} %get-tuple-element.26, bf16[128,2048]{1,0:T(8,128)(2,1)} %collective-permute-done.8, bf16[128,2048]{1,0:T(8,128)(2,1)} %collective-permute-done.5, bf16[128,2048]{1,0:T(8,128)(2,1)} %collective-permute-done.4, bf16[128,2048]{1,0:T(8,128)(2,1)} %multiply_convert_fusion.6), kind=kOutput, calls=%fused_computation.101 | convolution fusion | flops 1082130432 | bytes 5242880 | tf_op jit(solution)/shard_map/dot_general | solution.py:79
  175.6 3.3 %fusion.41 = (bf16[128,2048]{1,0:T(8,128)(2,1)}, bf16[128,2048]{1,0:T(8,128)(2,1)}, bf16[128,2048]{1,0:T(8,128)(2,1)}, bf16[128,2048]{1,0:T(8,128)(2,1)}) fusion(f32[512,2048]{1,0:T(8,128)S(1)} %copy-done.3, bf16[128,2048]{1,0:T(8,128)(2,1)} %collective-permute-done.25, bf16[128,2048]{1,0:T(8,128)(2,1)} %collective-permute-done.35, ...), kind=kLoop, calls=%fused_computation.70 | loop fusion | flops 3145728 | bytes 8388608 | tf_op jit(solution)/shard_map/convert_element_type | solution.py:149
  181.0 7.2 %convert_multiply_fusion.1 = f32[512,2048]{1,0:T(8,128)} fusion(bf16[512,2048]{1,0:T(8,128)(2,1)S(1)} %pad_maximum_fusion.4, f32[512]{0:T(512)S(1)} %get-tuple-element.38, f32[512,512]{1,0:T(8,128)} %fusion.56, bf16[2048,512]{1,0:T(8,128)(2,1)} %copy-done.13, bf16[128,2048]{1,0:T(8,128)(2,1)} %collective-permute-done.8, ...), kind=kOutput, calls=%fused_computation.9 | convolution fusion | flops 2160590848 | bytes 11536384 | tf_op jit(solution)/shard_map/dot_general | solution.py:81
  189.8 4.2 %collective-permute-done.29 = bf16[128,2048]{1,0:T(8,128)(2,1)} collective-permute-done((bf16[128,2048]{1,0:T(8,128)(2,1)}, bf16[128,2048]{1,0:T(8,128)(2,1)}, u32[]{:S(2)}, u32[]{:S(2)}) %collective-permute-start.29) | collective-permute-done | bytes 524320 | tf_op jit(solution)/shard_map/ppermute | solution.py:149
  194.0 11.2 %collective-permute-done.36 = bf16[128,2048]{1,0:T(8,128)(2,1)} collective-permute-done((bf16[128,2048]{1,0:T(8,128)(2,1)}, bf16[128,2048]{1,0:T(8,128)(2,1)}, u32[]{:S(2)}, u32[]{:S(2)}) %collective-permute-start.36) | collective-permute-done | bytes 524320 | tf_op jit(solution)/shard_map/ppermute | solution.py:149
  205.2 2.6 %fusion.40 = (bf16[128,2048]{1,0:T(8,128)(2,1)S(1)}, bf16[128,2048]{1,0:T(8,128)(2,1)S(1)}) fusion(f32[512,2048]{1,0:T(8,128)} %convert_multiply_fusion.1, bf16[128,2048]{1,0:T(8,128)(2,1)} %collective-permute-done.29, bf16[128,2048]{1,0:T(8,128)(2,1)} %collective-permute-done.27, bf16[128,2048]{1,0:T(8,128)(2,1)} %collective-permute-done.36, ...), kind=kLoop, calls=%fused_computation.68 | loop fusion | flops 2621440 | bytes 5242880 | tf_op jit(solution)/shard_map/convert_element_type | solution.py:149
  211.5 4.8 %collective-permute-done.33 = bf16[128,2048]{1,0:T(8,128)(2,1)S(1)} collective-permute-done((bf16[128,2048]{1,0:T(8,128)(2,1)}, bf16[128,2048]{1,0:T(8,128)(2,1)S(1)}, u32[]{:S(2)}, u32[]{:S(2)}) %collective-permute-start.33) | collective-permute-done | bytes 524320 | tf_op jit(solution)/shard_map/ppermute | solution.py:149
  216.4 6.4 %collective-permute-done.37 = bf16[128,2048]{1,0:T(8,128)(2,1)S(1)} collective-permute-done((bf16[128,2048]{1,0:T(8,128)(2,1)S(1)}, bf16[128,2048]{1,0:T(8,128)(2,1)S(1)}, u32[]{:S(2)}, u32[]{:S(2)}) %collective-permute-start.37) | collective-permute-done | bytes 524320 | tf_op jit(solution)/shard_map/ppermute | solution.py:149
  224.1 3.4 %collective-permute-start.38 = (bf16[128,2048]{1,0:T(8,128)(2,1)S(1)}, bf16[128,2048]{1,0:T(8,128)(2,1)S(1)}, u32[]{:S(2)}, u32[]{:S(2)}) collective-permute-start(bf16[128,2048]{1,0:T(8,128)(2,1)S(1)} %fusion.37), channel_id=1, source_target_pairs={{8,0},{9,1},{10,2},{11,3},{12,4},{13,5},{14,6},{15,7},{0,8},{1,9},... | collective-permute-start | bytes 1572872 | tf_op jit(solution)/shard_map/ppermute | solution.py:149
  227.6 14.8 %collective-permute-done.30 = bf16[128,2048]{1,0:T(8,128)(2,1)S(1)} collective-permute-done((bf16[128,2048]{1,0:T(8,128)(2,1)S(1)}, bf16[128,2048]{1,0:T(8,128)(2,1)S(1)}, u32[]{:S(2)}, u32[]{:S(2)}) %collective-permute-start.30) | collective-permute-done | bytes 524320 | tf_op jit(solution)/shard_map/ppermute | solution.py:149
  242.4 5.0 %collective-permute-done.38 = bf16[128,2048]{1,0:T(8,128)(2,1)S(1)} collective-permute-done((bf16[128,2048]{1,0:T(8,128)(2,1)S(1)}, bf16[128,2048]{1,0:T(8,128)(2,1)S(1)}, u32[]{:S(2)}, u32[]{:S(2)}) %collective-permute-start.38) | collective-permute-done | bytes 524320 | tf_op jit(solution)/shard_map/ppermute | solution.py:149
  (225 shorter events, 59.4 us)
Async XLA Ops:
  1.8 14.4 %collective-permute-start = (bf16[128,1024]{0,1:T(8,128)(2,1)}, bf16[128,1024]{0,1:T(8,128)(2,1)}, u32[]{:S(2)}, u32[]{:S(2)}) collective-permute-start(bf16[128,1024]{0,1:T(8,128)(2,1)} %bitcast.5), channel_id=1, source_target_pairs={{0,16},{16,0},{1,17},{17,1},{2,18},{18,2},{3,19},{19,3},{4,20},{20... | collective-permute-start | bytes 786440 | tf_op jit(solution)/shard_map/ppermute | solution.py:307
  4.0 23.8 %collective-permute-start.13 = (f32[1,128,16]{1,2,0:T(8,128)S(1)}, f32[1,128,16]{1,2,0:T(8,128)S(1)}, u32[]{:S(2)}, u32[]{:S(2)}) collective-permute-start(f32[1,128,16]{1,2,0:T(8,128)S(1)} %bitcast.150), channel_id=1, source_target_pairs={{0,1},{1,0},{2,3},{3,2},{4,5},{5,4},{6,7},{7,6},{8,9},{9,8},{10,11... | collective-permute-start | bytes 24584 | tf_op jit(solution)/shard_map/ppermute | solution.py:89
  27.2 8.2 %collective-permute-start.2 = (bf16[128,8,128]{0,2,1:T(8,128)(2,1)S(1)}, bf16[128,8,128]{0,2,1:T(8,128)(2,1)S(1)}, u32[]{:S(2)}, u32[]{:S(2)}) collective-permute-start(bf16[128,8,128]{0,2,1:T(8,128)(2,1)S(1)} %fusion.30), channel_id=1, source_target_pairs={{0,16},{16,0},{1,17},{17,1},{2,18},{18,2},{3,19},{19,3},{4,20},{20... | collective-permute-start | bytes 786440 | tf_op jit(solution)/shard_map/ppermute | solution.py:317
  27.8 34.5 %collective-permute-start.14 = (f32[2,128,16]{1,2,0:T(8,128)S(1)}, f32[2,128,16]{1,2,0:T(8,128)S(1)}, u32[]{:S(2)}, u32[]{:S(2)}) collective-permute-start(f32[2,128,16]{1,2,0:T(8,128)S(1)} %pad_maximum_fusion.13), channel_id=1, source_target_pairs={{0,2},{1,3},{2,0},{3,1},{4,6},{5,7},{6,4},{7,5},{8,10},{9,11},{10,... | collective-permute-start | bytes 49160 | tf_op jit(solution)/shard_map/ppermute | solution.py:89
  40.5 69.5 %collective-permute-start.9 = (bf16[3,2048,256]{2,1,0:T(8,128)(2,1)}, bf16[3,2048,256]{2,1,0:T(8,128)(2,1)}, u32[]{:S(2)}, u32[]{:S(2)}) collective-permute-start(bf16[3,2048,256]{2,1,0:T(8,128)(2,1)} %pad_maximum_fusion), channel_id=1, source_target_pairs={{0,16},{16,0},{1,17},{17,1},{2,18},{18,2},{3,19},{19,3},{4,20},{20... | collective-permute-start | bytes 9437192 | tf_op jit(solution)/shard_map/ppermute | solution.py:54
  43.0 25.1 %collective-permute-start.4 = (bf16[128,2048]{1,0:T(8,128)(2,1)}, bf16[128,2048]{1,0:T(8,128)(2,1)}, u32[]{:S(2)}, u32[]{:S(2)}) collective-permute-start(bf16[128,2048]{1,0:T(8,128)(2,1)} %multiply_convert_fusion.6), channel_id=1, source_target_pairs={{0,8},{1,9},{2,10},{3,11},{4,12},{5,13},{6,14},{7,15},{8,0},{9,1},... | collective-permute-start | bytes 1572872 | tf_op jit(solution)/shard_map/ppermute | solution.py:98
  60.3 19.0 %collective-permute-start.5 = (bf16[128,2048]{1,0:T(8,128)(2,1)}, bf16[128,2048]{1,0:T(8,128)(2,1)}, u32[]{:S(2)}, u32[]{:S(2)}) collective-permute-start(bf16[128,2048]{1,0:T(8,128)(2,1)} %multiply_convert_fusion.6), channel_id=1, source_target_pairs={{0,4},{1,5},{2,6},{3,7},{4,0},{5,1},{6,2},{7,3},{8,12},{9,13},{10,... | collective-permute-start | bytes 1572872 | tf_op jit(solution)/shard_map/ppermute | solution.py:98
  60.6 18.7 %collective-permute-start.6 = (bf16[128,2048]{1,0:T(8,128)(2,1)}, bf16[128,2048]{1,0:T(8,128)(2,1)}, u32[]{:S(2)}, u32[]{:S(2)}) collective-permute-start(bf16[128,2048]{1,0:T(8,128)(2,1)} %multiply_convert_fusion.6), channel_id=1, source_target_pairs={{0,2},{1,3},{2,0},{3,1},{4,6},{5,7},{6,4},{7,5},{8,10},{9,11},{10,... | collective-permute-start | bytes 1572872 | tf_op jit(solution)/shard_map/ppermute | solution.py:98
  62.4 17.0 %collective-permute-start.7 = (bf16[128,2048]{1,0:T(8,128)(2,1)}, bf16[128,2048]{1,0:T(8,128)(2,1)S(1)}, u32[]{:S(2)}, u32[]{:S(2)}) collective-permute-start(bf16[128,2048]{1,0:T(8,128)(2,1)} %multiply_convert_fusion.6), channel_id=1, source_target_pairs={{0,1},{1,0},{2,3},{3,2},{4,5},{5,4},{6,7},{7,6},{8,9},{9,8},{10,11... | collective-permute-start | bytes 1572872 | tf_op jit(solution)/shard_map/ppermute | solution.py:98
  68.1 11.7 %collective-permute-start.15 = (f32[4,128,16]{1,2,0:T(8,128)S(1)}, f32[4,128,16]{1,2,0:T(8,128)S(1)}, u32[]{:S(2)}, u32[]{:S(2)}) collective-permute-start(f32[4,128,16]{1,2,0:T(8,128)S(1)} %pad_maximum_fusion.12), channel_id=1, source_target_pairs={{0,4},{1,5},{2,6},{3,7},{4,0},{5,1},{6,2},{7,3},{8,12},{9,13},{10,... | collective-permute-start | bytes 98312 | tf_op jit(solution)/shard_map/ppermute | solution.py:89
  79.3 15.5 %collective-permute-start.8 = (bf16[128,2048]{1,0:T(8,128)(2,1)}, bf16[128,2048]{1,0:T(8,128)(2,1)}, u32[]{:S(2)}, u32[]{:S(2)}) collective-permute-start(bf16[128,2048]{1,0:T(8,128)(2,1)} %collective-permute-done.4), channel_id=1, source_target_pairs={{0,4},{1,5},{2,6},{3,7},{4,0},{5,1},{6,2},{7,3},{8,12},{9,13},{10,... | collective-permute-start | bytes 1572872 | tf_op jit(solution)/shard_map/ppermute | solution.py:112
  79.8 12.7 %collective-permute-start.16 = (f32[8,128,16]{1,2,0:T(8,128)S(1)}, f32[8,128,16]{1,2,0:T(8,128)S(1)}, u32[]{:S(2)}, u32[]{:S(2)}) collective-permute-start(f32[8,128,16]{1,2,0:T(8,128)S(1)} %pad_maximum_fusion.11), channel_id=1, source_target_pairs={{0,8},{1,9},{2,10},{3,11},{4,12},{5,13},{6,14},{7,15},{8,0},{9,1},... | collective-permute-start | bytes 196616 | tf_op jit(solution)/shard_map/ppermute | solution.py:89
  80.4 14.4 %collective-permute-start.17 = (bf16[128,2048]{1,0:T(8,128)(2,1)}, bf16[128,2048]{1,0:T(8,128)(2,1)S(1)}, u32[]{:S(2)}, u32[]{:S(2)}) collective-permute-start(bf16[128,2048]{1,0:T(8,128)(2,1)} %collective-permute-done.4), channel_id=1, source_target_pairs={{0,1},{1,0},{2,3},{3,2},{4,5},{5,4},{6,7},{7,6},{8,9},{9,8},{10,11... | collective-permute-start | bytes 1572872 | tf_op jit(solution)/shard_map/ppermute | solution.py:112
  92.7 27.2 %collective-permute-start.10 = (bf16[128,2048]{1,0:T(8,128)(2,1)}, bf16[128,2048]{1,0:T(8,128)(2,1)}, u32[]{:S(2)}, u32[]{:S(2)}) collective-permute-start(bf16[128,2048]{1,0:T(8,128)(2,1)} %collective-permute-done.4), channel_id=1, source_target_pairs={{0,2},{1,3},{2,0},{3,1},{4,6},{5,7},{6,4},{7,5},{8,10},{9,11},{10,... | collective-permute-start | bytes 1572872 | tf_op jit(solution)/shard_map/ppermute | solution.py:112
  94.9 25.1 %collective-permute-start.11 = (bf16[128,2048]{1,0:T(8,128)(2,1)}, bf16[128,2048]{1,0:T(8,128)(2,1)}, u32[]{:S(2)}, u32[]{:S(2)}) collective-permute-start(bf16[128,2048]{1,0:T(8,128)(2,1)} %collective-permute-done.5), channel_id=1, source_target_pairs={{0,2},{1,3},{2,0},{3,1},{4,6},{5,7},{6,4},{7,5},{8,10},{9,11},{10,... | collective-permute-start | bytes 1572872 | tf_op jit(solution)/shard_map/ppermute | solution.py:112
  96.5 33.4 %collective-permute-start.12 = (bf16[128,2048]{1,0:T(8,128)(2,1)}, bf16[128,2048]{1,0:T(8,128)(2,1)}, u32[]{:S(2)}, u32[]{:S(2)}) collective-permute-start(bf16[128,2048]{1,0:T(8,128)(2,1)} %collective-permute-done.8), channel_id=1, source_target_pairs={{0,2},{1,3},{2,0},{3,1},{4,6},{5,7},{6,4},{7,5},{8,10},{9,11},{10,... | collective-permute-start | bytes 1572872 | tf_op jit(solution)/shard_map/ppermute | solution.py:112
  129.9 20.0 %collective-permute-start.21 = (bf16[128,2048]{1,0:T(8,128)(2,1)}, bf16[128,2048]{1,0:T(8,128)(2,1)}, u32[]{:S(2)}, u32[]{:S(2)}) collective-permute-start(bf16[128,2048]{1,0:T(8,128)(2,1)} %collective-permute-done.6), channel_id=1, source_target_pairs={{0,1},{1,0},{2,3},{3,2},{4,5},{5,4},{6,7},{7,6},{8,9},{9,8},{10,11... | collective-permute-start | bytes 1572872 | tf_op jit(solution)/shard_map/ppermute | solution.py:112
  143.3 44.9 %collective-permute-start.27 = (bf16[128,2048]{1,0:T(8,128)(2,1)}, bf16[128,2048]{1,0:T(8,128)(2,1)}, u32[]{:S(2)}, u32[]{:S(2)}) collective-permute-start(bf16[128,2048]{1,0:T(8,128)(2,1)} %get-tuple-element.58), channel_id=1, source_target_pairs={{1,0},{0,1},{3,2},{2,3},{5,4},{4,5},{7,6},{6,7},{9,8},{8,9},{11,10... | collective-permute-start | bytes 1572872 | tf_op jit(solution)/shard_map/ppermute | solution.py:149
  162.6 12.5 %collective-permute-start.25 = (bf16[128,2048]{1,0:T(8,128)(2,1)}, bf16[128,2048]{1,0:T(8,128)(2,1)}, u32[]{:S(2)}, u32[]{:S(2)}) collective-permute-start(bf16[128,2048]{1,0:T(8,128)(2,1)} %get-tuple-element.59), channel_id=1, source_target_pairs={{1,0},{0,1},{3,2},{2,3},{5,4},{4,5},{7,6},{6,7},{9,8},{8,9},{11,10... | collective-permute-start | bytes 1572872 | tf_op jit(solution)/shard_map/ppermute | solution.py:149
  163.0 12.5 %collective-permute-start.28 = (bf16[128,2048]{1,0:T(8,128)(2,1)}, bf16[128,2048]{1,0:T(8,128)(2,1)}, u32[]{:S(2)}, u32[]{:S(2)}) collective-permute-start(bf16[128,2048]{1,0:T(8,128)(2,1)} %get-tuple-element.62), channel_id=1, source_target_pairs={{1,0},{0,1},{3,2},{2,3},{5,4},{4,5},{7,6},{6,7},{9,8},{8,9},{11,10... | collective-permute-start | bytes 1572872 | tf_op jit(solution)/shard_map/ppermute | solution.py:149
  163.1 12.5 %collective-permute-start.32 = (bf16[128,2048]{1,0:T(8,128)(2,1)}, bf16[128,2048]{1,0:T(8,128)(2,1)}, u32[]{:S(2)}, u32[]{:S(2)}) collective-permute-start(bf16[128,2048]{1,0:T(8,128)(2,1)} %get-tuple-element.61), channel_id=1, source_target_pairs={{1,0},{0,1},{3,2},{2,3},{5,4},{4,5},{7,6},{6,7},{9,8},{8,9},{11,10... | collective-permute-start | bytes 1572872 | tf_op jit(solution)/shard_map/ppermute | solution.py:149
  163.5 12.1 %collective-permute-start.35 = (bf16[128,2048]{1,0:T(8,128)(2,1)}, bf16[128,2048]{1,0:T(8,128)(2,1)}, u32[]{:S(2)}, u32[]{:S(2)}) collective-permute-start(bf16[128,2048]{1,0:T(8,128)(2,1)} %get-tuple-element.60), channel_id=1, source_target_pairs={{1,0},{0,1},{3,2},{2,3},{5,4},{4,5},{7,6},{6,7},{9,8},{8,9},{11,10... | collective-permute-start | bytes 1572872 | tf_op jit(solution)/shard_map/ppermute | solution.py:149
  175.1 14.7 %collective-permute-start.34 = (bf16[128,2048]{1,0:T(8,128)(2,1)}, bf16[128,2048]{1,0:T(8,128)(2,1)}, u32[]{:S(2)}, u32[]{:S(2)}) collective-permute-start(bf16[128,2048]{1,0:T(8,128)(2,1)} %get-tuple-element.56), channel_id=1, source_target_pairs={{1,0},{0,1},{3,2},{2,3},{5,4},{4,5},{7,6},{6,7},{9,8},{8,9},{11,10... | collective-permute-start | bytes 1572872 | tf_op jit(solution)/shard_map/ppermute | solution.py:149
  175.5 35.3 %collective-permute-start.31 = (bf16[128,2048]{1,0:T(8,128)(2,1)}, bf16[128,2048]{1,0:T(8,128)(2,1)}, u32[]{:S(2)}, u32[]{:S(2)}) collective-permute-start(bf16[128,2048]{1,0:T(8,128)(2,1)} %get-tuple-element.57), channel_id=1, source_target_pairs={{1,0},{0,1},{3,2},{2,3},{5,4},{4,5},{7,6},{6,7},{9,8},{8,9},{11,10... | collective-permute-start | bytes 1572872 | tf_op jit(solution)/shard_map/ppermute | solution.py:149
  179.0 15.0 %collective-permute-start.29 = (bf16[128,2048]{1,0:T(8,128)(2,1)}, bf16[128,2048]{1,0:T(8,128)(2,1)}, u32[]{:S(2)}, u32[]{:S(2)}) collective-permute-start(bf16[128,2048]{1,0:T(8,128)(2,1)} %get-tuple-element.45), channel_id=1, source_target_pairs={{2,0},{3,1},{0,2},{1,3},{6,4},{7,5},{4,6},{5,7},{10,8},{11,9},{8,1... | collective-permute-start | bytes 1572872 | tf_op jit(solution)/shard_map/ppermute | solution.py:149
  180.5 24.8 %collective-permute-start.36 = (bf16[128,2048]{1,0:T(8,128)(2,1)}, bf16[128,2048]{1,0:T(8,128)(2,1)}, u32[]{:S(2)}, u32[]{:S(2)}) collective-permute-start(bf16[128,2048]{1,0:T(8,128)(2,1)} %get-tuple-element.43), channel_id=1, source_target_pairs={{2,0},{3,1},{0,2},{1,3},{6,4},{7,5},{4,6},{5,7},{10,8},{11,9},{8,1... | collective-permute-start | bytes 1572872 | tf_op jit(solution)/shard_map/ppermute | solution.py:149
  188.2 28.1 %collective-permute-start.33 = (bf16[128,2048]{1,0:T(8,128)(2,1)}, bf16[128,2048]{1,0:T(8,128)(2,1)S(1)}, u32[]{:S(2)}, u32[]{:S(2)}) collective-permute-start(bf16[128,2048]{1,0:T(8,128)(2,1)} %get-tuple-element.44), channel_id=1, source_target_pairs={{2,0},{3,1},{0,2},{1,3},{6,4},{7,5},{4,6},{5,7},{10,8},{11,9},{8,1... | collective-permute-start | bytes 1572872 | tf_op jit(solution)/shard_map/ppermute | solution.py:149
  207.8 14.9 %collective-permute-start.37 = (bf16[128,2048]{1,0:T(8,128)(2,1)S(1)}, bf16[128,2048]{1,0:T(8,128)(2,1)S(1)}, u32[]{:S(2)}, u32[]{:S(2)}) collective-permute-start(bf16[128,2048]{1,0:T(8,128)(2,1)S(1)} %get-tuple-element.47), channel_id=1, source_target_pairs={{4,0},{5,1},{6,2},{7,3},{0,4},{1,5},{2,6},{3,7},{12,8},{13,9},{14,... | collective-permute-start | bytes 1572872 | tf_op jit(solution)/shard_map/ppermute | solution.py:149
  209.4 18.2 %collective-permute-start.20 = (bf16[128,2048]{1,0:T(8,128)(2,1)S(1)}, bf16[128,2048]{1,0:T(8,128)(2,1)S(1)}, u32[]{:S(2)}, u32[]{:S(2)}) collective-permute-start(bf16[128,2048]{1,0:T(8,128)(2,1)S(1)} %copy-done.18), channel_id=1, source_target_pairs={{1,0},{0,1},{3,2},{2,3},{5,4},{4,5},{7,6},{6,7},{9,8},{8,9},{11,10... | collective-permute-start | bytes 1572872 | tf_op jit(solution)/shard_map/ppermute | solution.py:149
  209.4 18.2 %collective-permute-start.26 = (bf16[128,2048]{1,0:T(8,128)(2,1)S(1)}, bf16[128,2048]{1,0:T(8,128)(2,1)S(1)}, u32[]{:S(2)}, u32[]{:S(2)}) collective-permute-start(bf16[128,2048]{1,0:T(8,128)(2,1)S(1)} %copy-done.17), channel_id=1, source_target_pairs={{2,0},{3,1},{0,2},{1,3},{6,4},{7,5},{4,6},{5,7},{10,8},{11,9},{8,1... | collective-permute-start | bytes 1572872 | tf_op jit(solution)/shard_map/ppermute | solution.py:149
  210.9 31.5 %collective-permute-start.30 = (bf16[128,2048]{1,0:T(8,128)(2,1)S(1)}, bf16[128,2048]{1,0:T(8,128)(2,1)S(1)}, u32[]{:S(2)}, u32[]{:S(2)}) collective-permute-start(bf16[128,2048]{1,0:T(8,128)(2,1)S(1)} %get-tuple-element.46), channel_id=1, source_target_pairs={{4,0},{5,1},{6,2},{7,3},{0,4},{1,5},{2,6},{3,7},{12,8},{13,9},{14,... | collective-permute-start | bytes 1572872 | tf_op jit(solution)/shard_map/ppermute | solution.py:149
  224.1 23.2 %collective-permute-start.38 = (bf16[128,2048]{1,0:T(8,128)(2,1)S(1)}, bf16[128,2048]{1,0:T(8,128)(2,1)S(1)}, u32[]{:S(2)}, u32[]{:S(2)}) collective-permute-start(bf16[128,2048]{1,0:T(8,128)(2,1)S(1)} %fusion.37), channel_id=1, source_target_pairs={{8,0},{9,1},{10,2},{11,3},{12,4},{13,5},{14,6},{15,7},{0,8},{1,9},... | collective-permute-start | bytes 1572872 | tf_op jit(solution)/shard_map/ppermute | solution.py:149
  (53 other events, 417.3 us)

commit v13 on v8

--- a/solution.py
+++ b/solution.py
@@ -84,7 +84,13 @@
 
     pieces = [((normed, weight_table), None, None, -1)]
     waves = [[0]]
-    tie_at = min(2, len(plan) - 1)
+    axis_of = []
+    axis = 0
+    for _, ends in plan:
+        axis_of.append(axis)
+        axis += 1 if ends else 0
+    weight_stage = next((n for n, a in enumerate(axis_of) if a == 1), len(plan) - 1)
+    weights_tied = False
     while True:
         fresh = []
         for parent in waves[-1]:
@@ -95,32 +101,41 @@
         if not fresh:
             break
         blocks = [piece[0] for piece in fresh]
-        if len(waves) == tie_at + 1:
-            full, blocks = lax.optimization_barrier((tuple(full), blocks))
-            full = list(full)
-        else:
+        if len(waves) <= 2:
             blocks = lax.optimization_barrier(blocks)
+        elif not weights_tied:
+            spot = next((k for k, piece in enumerate(fresh) if piece[3] == weight_stage), None)
+            if spot is not None:
+                tied = lax.optimization_barrier((tuple(full), blocks[spot]))
+                full = list(tied[0])
+                blocks[spot] = tied[1]
+                weights_tied = True
         waves.append(list(range(len(pieces), len(pieces) + len(fresh))))
         pieces += [(b,) + piece[1:] for b, piece in zip(blocks, fresh)]
+    groups = {}
+    for index, piece in enumerate(pieces):
+        groups.setdefault(0 if index == 0 else axis_of[piece[3]], []).append(index)
+    member_lists = [members for _, members in sorted(groups.items())]
     partial = [None] * len(pieces)
     size = normed.shape[0]
-    groups = [[0] + waves[1]] + waves[2:] if len(waves) > 1 else [[0]]
-    for group in groups:
-        rows = jnp.concatenate([pieces[i][0][0] for i in group], axis=0)
-        table = jnp.concatenate([pieces[i][0][1] for i in group], axis=0)
+    ordered = []
+    for members in reversed(member_lists):
+        if len(members) >= 8:
+            half = len(members) // 2
+            ordered += [members[:half], members[half:]]
+        else:
+            ordered.append(members)
+    for members in ordered:
+        rows = jnp.concatenate([pieces[i][0][0] for i in members], axis=0)
+        table = jnp.concatenate([pieces[i][0][1] for i in members], axis=0)
         out = expert(rows, table)
-        for offset, i in enumerate(group):
+        for offset, i in enumerate(members):
             partial[i] = out[offset * size:(offset + 1) * size]
-    for wave in reversed(waves[1:]):
-        sent = []
-        for index in wave:
-            _, parent, pairs, _ = pieces[index]
-            back = [(target, source) for source, target in pairs]
-            sent.append(lax.ppermute(partial[index].astype(jnp.bfloat16), "ep", back))
-        sent = lax.optimization_barrier(sent)
-        for index, value in zip(wave, sent):
-            parent = pieces[index][1]
-            partial[parent] = partial[parent] + value.astype(jnp.float32)
+    for index in reversed(range(1, len(pieces))):
+        _, parent, pairs, _ = pieces[index]
+        back = [(target, source) for source, target in pairs]
+        sent = lax.ppermute(partial[index].astype(jnp.bfloat16), "ep", back)
+        partial[parent] = partial[parent] + sent.astype(jnp.float32)
     return partial[0], anchor
 
 

time: 269 us -> 270 us (level)
  starting transfers between devices: 37.5 us -> 29.5 us
  waiting for transfers between devices: 127 us -> 135 us
  local copies, waits for them, and re-layouts: 25 us -> 28.4 us
  matrix products: 52.2 us -> 49.1 us
    ppermute x15, waiting for transfers between devices: 39.2 us -> 52.1 us  [dense_moe(): sent = lax.ppermute(partial[index].astype(jnp.bfloat16), 'ep', back)]
    dot_general x4, matrix products: 31.3 us -> 26.4 us  [expert(): out_rows = jnp.dot(act, full[2], preferred_element_type=jnp.float32)]
    dot_general x4 -> x3, matrix products: 11.4 us -> 6.66 us  [expert(): gate_val = jnp.dot(rows, full[0], preferred_element_type=jnp.float32)]
    dot_general x0 -> x1, matrix products: none -> 4.57 us  [expert(): up_val = jnp.dot(rows, full[1], preferred_element_type=jnp.float32)]
    ppermute x15, starting transfers between devices: 11.6 us -> 7.39 us  [dense_moe(): sent = lax.ppermute(partial[index].astype(jnp.bfloat16), 'ep', back)]
    ppermute x30, starting transfers between devices: 21 us -> 17.3 us  [dense_moe(): fresh.append((lax.ppermute(block, 'ep', pairs), parent, pairs, stage))]
    ppermute x30, waiting for transfers between devices: 51.7 us -> 48.7 us  [dense_moe(): fresh.append((lax.ppermute(block, 'ep', pairs), parent, pairs, stage))]
    concatenate x2, other arithmetic: 3.18 us -> 0.48 us  [full_weights(): joined.append(jnp.concatenate([low, high], axis=axis))]
  transfers between devices with their start and end apart: 50 -> 50, of which waited for: 17 -> 17; matrix products, arithmetic and copies ran while one was open for 36% -> 34% of each run, Pallas kernels for 0% -> 0%
where the time goes in v13:
time: 270 us; the launch traced here: 266 us
  waiting for transfers between devices  135 us (50%)
  matrix products  49.1 us (18%)
  starting transfers between devices  29.5 us (11%)
  local copies, waits for them, and re-layouts  28.4 us (11%)
  other arithmetic  22.4 us (8%)
    ppermute x15, waiting for transfers between devices, dense_moe(): sent = lax.ppermute(partial[index].astype(jnp.bfloat16), 'ep', back)  52.1 us
    ppermute x30, waiting for transfers between devices, dense_moe(): fresh.append((lax.ppermute(block, 'ep', pairs), parent, pairs, stage))  48.7 us
    ppermute x1, waiting for transfers between devices, full_weights(): other = lax.ppermute(packed, 'kv', [(0, 1), (1, 0)])  26.6 us
    dot_general x4, matrix products, expert(): out_rows = jnp.dot(act, full[2], preferred_element_type=jnp.float32)  26.4 us
    ppermute x30, starting transfers between devices, dense_moe(): fresh.append((lax.ppermute(block, 'ep', pairs), parent, pairs, stage))  17.3 us
    unnamed x74, local copies, waits for them, and re-layouts  17 us
    convert_element_type x3, other arithmetic, dense_moe(): sent = lax.ppermute(partial[index].astype(jnp.bfloat16), 'ep', back)  8.56 us
    ppermute x3, waiting for transfers between devices, paired_attention(): lax.ppermute((far_top, far_denom, far_sum.astype(jnp.bfloat16)), 'kv', swap)  7.48 us
  transfers between devices with their start and end apart: 50, of which 17 were waited for; matrix products, arithmetic and copies ran while one was open for 34% of the time, Pallas kernels for 0%

profile of v13, /device:TPU:24, one launch (start us, length us, event | category | flops | bytes accessed | tf_op | source)
XLA Modules:
  0.0 265.7 jit_solution(6462922862503219101)
XLA Ops:
  4.2 3.7 %copy.104 = bf16[128,8,8,128]{3,2,1,0:T(8,128)(2,1)} copy(bf16[128,8,8,128]{3,1,2,0:T(8,128)(2,1)} %bitcast.92) | data formatting | bytes 4194304
  10.6 2.4 bitcast_reduce_fusion.1
  14.8 2.6 fusion.2
  25.7 6.4 %collective-permute-done.2 = bf16[128,8,128]{0,2,1:T(8,128)(2,1)S(1)} collective-permute-done((bf16[128,8,128]{0,2,1:T(8,128)(2,1)S(1)}, bf16[128,8,128]{0,2,1:T(8,128)(2,1)S(1)}, u32[]{:S(2)}, u32[]{:S(2)}) %collective-permute-start.2) | collective-permute-done | bytes 262176 | tf_op jit(solution)/shard_map/ppermute | solution.py:305
  36.5 2.6 collective-permute-start.5
  39.1 22.0 %collective-permute-done.5 = f32[128,16]{0,1:T(8,128)S(1)} collective-permute-done((f32[128,16]{0,1:T(8,128)S(1)}, f32[128,16]{0,1:T(8,128)S(1)}, u32[]{:S(2)}, u32[]{:S(2)}) %collective-permute-start.5) | collective-permute-done | bytes 8224 | tf_op jit(solution)/shard_map/ppermute | solution.py:100
  62.2 2.6 collective-permute-done.7
  66.3 3.5 %pad_maximum_fusion = bf16[3,2048,256]{2,1,0:T(8,128)(2,1)} fusion(bf16[1,2048,256]{2,1,0:T(8,128)(2,1)S(1)} %stack_reshape_squeeze.3, bf16[1,2048,256]{2,1,0:T(8,128)(2,1)} %param.28, bf16[1,2048,256]{2,1,0:T(8,128)(2,1)} %param.27), kind=kLoop, calls=%fused_computation.16 | loop fusion | flops 3145728 | bytes 6291456 | tf_op jit(solution)/shard_map/stack | solution.py:53
  74.6 8.5 %collective-permute-done.13 = f32[128,16]{0,1:T(8,128)S(1)} collective-permute-done((f32[128,16]{0,1:T(8,128)S(1)}, f32[128,16]{0,1:T(8,128)S(1)}, u32[]{:S(2)}, u32[]{:S(2)}) %collective-permute-start.13) | collective-permute-done | bytes 8224 | tf_op jit(solution)/shard_map/ppermute | solution.py:100
  84.4 2.4 collective-permute-done.19
  90.3 11.9 %collective-permute-done.18 = bf16[128,2048]{1,0:T(8,128)(2,1)S(1)} collective-permute-done((bf16[128,2048]{1,0:T(8,128)(2,1)}, bf16[128,2048]{1,0:T(8,128)(2,1)S(1)}, u32[]{:S(2)}, u32[]{:S(2)}) %collective-permute-start.18) | collective-permute-done | bytes 524320 | tf_op jit(solution)/shard_map/ppermute | solution.py:100
  112.2 26.6 %collective-permute-done.24 = bf16[3,2048,256]{2,1,0:T(8,128)(2,1)} collective-permute-done((bf16[3,2048,256]{2,1,0:T(8,128)(2,1)}, bf16[3,2048,256]{2,1,0:T(8,128)(2,1)}, u32[]{:S(2)}, u32[]{:S(2)}) %collective-permute-start.24) | collective-permute-done | bytes 3145760 | tf_op jit(solution)/shard_map/ppermute | solution.py:54
  138.8 4.3 %select_bitcast_fusion.1 = (bf16[2048,256]{1,0:T(8,128)(2,1)}, bf16[2048,256]{1,0:T(8,128)(2,1)}, bf16[1,2048,256]{2,1,0:T(8,128)(2,1)}, bf16[2048,256]{1,0:T(8,128)(2,1)}, bf16[2048,256]{1,0:T(8,128)(2,1)}) fusion(bf16[1,2048,256]{2,1,0:T(8,128)(2,1)S(1)} %copy-done.3, pred[]{:T(512)S(6)} %eq.42, bf16[3,2048,256]{2,1,0:T(8,128)(2,1)} %collective-permute-done.24, ...), kind=kLoop, calls=%fused_computation.84 | loop fusion | flops 2097152 | bytes 10485761 | tf_op jit(solution)/shard_map/jit(_where)/select_n | solution.py:61
  148.0 2.3 copy-done.26
  151.4 4.6 %fusion.56 = f32[512,512]{1,0:T(8,128)} fusion(bf16[2048,512]{1,0:T(8,128)(2,1)S(1)} %get-tuple-element.45, bf16[128,2048]{1,0:T(8,128)(2,1)} %collective-permute-done.12, bf16[128,2048]{1,0:T(8,128)(2,1)} %collective-permute-done.6, bf16[128,2048]{1,0:T(8,128)(2,1)} %collective-permute-done.4, bf16[128,2048]{1,0:T(8,128)(2,1)} %multiply_convert_fusion.6), kind=kOutput, calls=%fused_computation.101 | convolution fusion | flops 1082130432 | bytes 5242880 | tf_op jit(solution)/shard_map/dot_general | solution.py:79
  156.0 2.2 fusion.100
  158.2 2.2 fusion.101
  160.5 6.3 %multiply_convert_fusion.1 = bf16[512,2048]{1,0:T(8,128)(2,1)} fusion(bf16[512,2048]{1,0:T(8,128)(2,1)S(1)} %pad_maximum_fusion.4, f32[512]{0:T(512)S(1)} %get-tuple-element.63, f32[512,512]{1,0:T(8,128)} %fusion.100, bf16[512,2048]{1,0:T(8,128)(2,1)} %copy-done.23, bf16[2048,512]{1,0:T(8,128)(2,1)} %copy-done.13), kind=kOutput, calls=%fused_computation.8 | convolution fusion | flops 2153250816 | bytes 9439232 | tf_op jit(solution)/shard_map/dot_general | solution.py:81
  166.8 3.0 %fusion.90 = (bf16[128,2048]{1,0:T(8,128)(2,1)}, bf16[128,2048]{1,0:T(8,128)(2,1)}, bf16[128,2048]{1,0:T(8,128)(2,1)}, bf16[128,2048]{1,0:T(8,128)(2,1)}) fusion(bf16[512,2048]{1,0:T(8,128)(2,1)} %multiply_convert_fusion.1), kind=kLoop, calls=%fused_computation.153 | loop fusion | bytes 4194304 | tf_op jit(solution)/shard_map/slice | solution.py:133
  171.5 2.2 fusion.102
  173.7 6.3 %multiply_convert_fusion = bf16[512,2048]{1,0:T(8,128)(2,1)} fusion(f32[512]{0:T(512)S(1)} %get-tuple-element.65, bf16[512,2048]{1,0:T(8,128)(2,1)S(1)} %pad_maximum_fusion.4, f32[512,512]{1,0:T(8,128)} %fusion.102, bf16[512,2048]{1,0:T(8,128)(2,1)} %copy-done.22, bf16[2048,512]{1,0:T(8,128)(2,1)} %copy-done.13), kind=kOutput, calls=%fused_computation.6 | convolution fusion | flops 2153250816 | bytes 9439232 | tf_op jit(solution)/shard_map/dot_general | solution.py:81
  180.0 3.0 %fusion.91 = (bf16[128,2048]{1,0:T(8,128)(2,1)}, bf16[128,2048]{1,0:T(8,128)(2,1)}, bf16[128,2048]{1,0:T(8,128)(2,1)}, bf16[128,2048]{1,0:T(8,128)(2,1)}) fusion(bf16[512,2048]{1,0:T(8,128)(2,1)} %multiply_convert_fusion), kind=kLoop, calls=%fused_computation.154 | loop fusion | bytes 4194304 | tf_op jit(solution)/shard_map/slice | solution.py:133
  184.0 6.9 %convert_multiply_fusion = f32[512,2048]{1,0:T(8,128)} fusion(bf16[512,2048]{1,0:T(8,128)(2,1)S(1)} %pad_maximum_fusion.4, f32[512]{0:T(512)S(1)} %get-tuple-element.64, f32[512,512]{1,0:T(8,128)} %fusion.101, bf16[512,2048]{1,0:T(8,128)(2,1)} %copy-done.27, bf16[2048,512]{1,0:T(8,128)(2,1)} %copy-done.13), kind=kOutput, calls=%fused_computation.7 | convolution fusion | flops 2152202240 | bytes 11536384 | tf_op jit(solution)/shard_map/dot_general | solution.py:81
  191.4 4.6 %fusion.41 = (bf16[128,2048]{1,0:T(8,128)(2,1)}, bf16[128,2048]{1,0:T(8,128)(2,1)}, bf16[128,2048]{1,0:T(8,128)(2,1)}, bf16[128,2048]{1,0:T(8,128)(2,1)}) fusion(f32[512,2048]{1,0:T(8,128)} %convert_multiply_fusion, bf16[128,2048]{1,0:T(8,128)(2,1)} %collective-permute-done.28, bf16[128,2048]{1,0:T(8,128)(2,1)} %collective-permute-done.46, ...), kind=kLoop, calls=%fused_computation.70 | loop fusion | flops 3145728 | bytes 8388608 | tf_op jit(solution)/shard_map/convert_element_type | solution.py:137
  198.0 6.9 %convert_multiply_fusion.1 = f32[512,2048]{1,0:T(8,128)} fusion(bf16[512,2048]{1,0:T(8,128)(2,1)S(1)} %pad_maximum_fusion.4, f32[512]{0:T(512)S(1)} %get-tuple-element.66, f32[512,512]{1,0:T(8,128)} %fusion.56, bf16[2048,512]{1,0:T(8,128)(2,1)} %copy-done.11, bf16[128,2048]{1,0:T(8,128)(2,1)} %collective-permute-done.12, ...), kind=kOutput, calls=%fused_computation.9 | convolution fusion | flops 2160590848 | bytes 11536384 | tf_op jit(solution)/shard_map/dot_general | solution.py:81
  205.6 5.5 %collective-permute-done.40 = bf16[128,2048]{1,0:T(8,128)(2,1)} collective-permute-done((bf16[128,2048]{1,0:T(8,128)(2,1)}, bf16[128,2048]{1,0:T(8,128)(2,1)}, u32[]{:S(2)}, u32[]{:S(2)}) %collective-permute-start.40) | collective-permute-done | bytes 524320 | tf_op jit(solution)/shard_map/ppermute | solution.py:137
  211.1 11.2 %collective-permute-done.47 = bf16[128,2048]{1,0:T(8,128)(2,1)} collective-permute-done((bf16[128,2048]{1,0:T(8,128)(2,1)}, bf16[128,2048]{1,0:T(8,128)(2,1)}, u32[]{:S(2)}, u32[]{:S(2)}) %collective-permute-start.47) | collective-permute-done | bytes 524320 | tf_op jit(solution)/shard_map/ppermute | solution.py:137
  222.3 2.6 fusion.40
  227.6 5.8 %collective-permute-done.44 = bf16[128,2048]{1,0:T(8,128)(2,1)S(1)} collective-permute-done((bf16[128,2048]{1,0:T(8,128)(2,1)}, bf16[128,2048]{1,0:T(8,128)(2,1)S(1)}, u32[]{:S(2)}, u32[]{:S(2)}) %collective-permute-start.44) | collective-permute-done | bytes 524320 | tf_op jit(solution)/shard_map/ppermute | solution.py:137
  233.5 12.0 %collective-permute-done.48 = bf16[128,2048]{1,0:T(8,128)(2,1)S(1)} collective-permute-done((bf16[128,2048]{1,0:T(8,128)(2,1)S(1)}, bf16[128,2048]{1,0:T(8,128)(2,1)S(1)}, u32[]{:S(2)}, u32[]{:S(2)}) %collective-permute-start.48) | collective-permute-done | bytes 524320 | tf_op jit(solution)/shard_map/ppermute | solution.py:137
  246.9 7.2 %collective-permute-done.41 = bf16[128,2048]{1,0:T(8,128)(2,1)S(1)} collective-permute-done((bf16[128,2048]{1,0:T(8,128)(2,1)S(1)}, bf16[128,2048]{1,0:T(8,128)(2,1)S(1)}, u32[]{:S(2)}, u32[]{:S(2)}) %collective-permute-start.41) | collective-permute-done | bytes 524320 | tf_op jit(solution)/shard_map/ppermute | solution.py:137
  254.1 10.3 %collective-permute-done.49 = bf16[128,2048]{1,0:T(8,128)(2,1)S(1)} collective-permute-done((bf16[128,2048]{1,0:T(8,128)(2,1)S(1)}, bf16[128,2048]{1,0:T(8,128)(2,1)S(1)}, u32[]{:S(2)}, u32[]{:S(2)}) %collective-permute-start.49) | collective-permute-done | bytes 524320 | tf_op jit(solution)/shard_map/ppermute | solution.py:137
  (190 shorter events, 59.6 us)
Async XLA Ops:
  1.1 13.7 %collective-permute-start = (bf16[128,1024]{0,1:T(8,128)(2,1)S(1)}, bf16[128,1024]{0,1:T(8,128)(2,1)}, u32[]{:S(2)}, u32[]{:S(2)}) collective-permute-start(bf16[128,1024]{0,1:T(8,128)(2,1)S(1)} %bitcast.106), channel_id=1, source_target_pairs={{0,16},{16,0},{1,17},{17,1},{2,18},{18,2},{3,19},{19,3},{4,20},{20... | collective-permute-start | bytes 786440 | tf_op jit(solution)/shard_map/ppermute | solution.py:295
  3.4 33.1 %collective-permute-start.11 = (f32[128,16]{0,1:T(8,128)S(1)}, f32[128,16]{0,1:T(8,128)S(1)}, u32[]{:S(2)}, u32[]{:S(2)}) collective-permute-start(f32[128,16]{0,1:T(8,128)S(1)} %select_reduce_fusion), channel_id=1, source_target_pairs={{0,1},{1,0},{2,3},{3,2},{4,5},{5,4},{6,7},{7,6},{8,9},{9,8},{10,11... | collective-permute-start | bytes 24584 | tf_op jit(solution)/shard_map/ppermute | solution.py:100
  34.2 36.2 %collective-permute-start.10 = (bf16[128,2048]{1,0:T(8,128)(2,1)}, bf16[128,2048]{1,0:T(8,128)(2,1)}, u32[]{:S(2)}, u32[]{:S(2)}) collective-permute-start(bf16[128,2048]{1,0:T(8,128)(2,1)} %multiply_convert_fusion.6), channel_id=1, source_target_pairs={{0,1},{1,0},{2,3},{3,2},{4,5},{5,4},{6,7},{7,6},{8,9},{9,8},{10,11... | collective-permute-start | bytes 1572872 | tf_op jit(solution)/shard_map/ppermute | solution.py:100
  34.2 36.2 %collective-permute-start.4 = (bf16[128,2048]{1,0:T(8,128)(2,1)}, bf16[128,2048]{1,0:T(8,128)(2,1)}, u32[]{:S(2)}, u32[]{:S(2)}) collective-permute-start(bf16[128,2048]{1,0:T(8,128)(2,1)} %multiply_convert_fusion.6), channel_id=1, source_target_pairs={{0,8},{1,9},{2,10},{3,11},{4,12},{5,13},{6,14},{7,15},{8,0},{9,1},... | collective-permute-start | bytes 1572872 | tf_op jit(solution)/shard_map/ppermute | solution.py:100
  34.5 35.9 %collective-permute-start.6 = (bf16[128,2048]{1,0:T(8,128)(2,1)}, bf16[128,2048]{1,0:T(8,128)(2,1)}, u32[]{:S(2)}, u32[]{:S(2)}) collective-permute-start(bf16[128,2048]{1,0:T(8,128)(2,1)} %multiply_convert_fusion.6), channel_id=1, source_target_pairs={{0,4},{1,5},{2,6},{3,7},{4,0},{5,1},{6,2},{7,3},{8,12},{9,13},{10,... | collective-permute-start | bytes 1572872 | tf_op jit(solution)/shard_map/ppermute | solution.py:100
  35.0 35.4 %collective-permute-start.8 = (bf16[128,2048]{1,0:T(8,128)(2,1)}, bf16[128,2048]{1,0:T(8,128)(2,1)}, u32[]{:S(2)}, u32[]{:S(2)}) collective-permute-start(bf16[128,2048]{1,0:T(8,128)(2,1)} %multiply_convert_fusion.6), channel_id=1, source_target_pairs={{0,2},{1,3},{2,0},{3,1},{4,6},{5,7},{6,4},{7,5},{8,10},{9,11},{10,... | collective-permute-start | bytes 1572872 | tf_op jit(solution)/shard_map/ppermute | solution.py:100
  36.5 24.6 %collective-permute-start.5 = (f32[128,16]{0,1:T(8,128)S(1)}, f32[128,16]{0,1:T(8,128)S(1)}, u32[]{:S(2)}, u32[]{:S(2)}) collective-permute-start(f32[128,16]{0,1:T(8,128)S(1)} %select_reduce_fusion), channel_id=1, source_target_pairs={{0,8},{1,9},{2,10},{3,11},{4,12},{5,13},{6,14},{7,15},{8,0},{9,1},... | collective-permute-start | bytes 24584 | tf_op jit(solution)/shard_map/ppermute | solution.py:100
  69.9 68.9 %collective-permute-start.24 = (bf16[3,2048,256]{2,1,0:T(8,128)(2,1)}, bf16[3,2048,256]{2,1,0:T(8,128)(2,1)}, u32[]{:S(2)}, u32[]{:S(2)}) collective-permute-start(bf16[3,2048,256]{2,1,0:T(8,128)(2,1)} %pad_maximum_fusion), channel_id=1, source_target_pairs={{0,16},{16,0},{1,17},{17,1},{2,18},{18,2},{3,19},{19,3},{4,20},{20... | collective-permute-start | bytes 9437192 | tf_op jit(solution)/shard_map/ppermute | solution.py:54
  70.5 18.0 %collective-permute-start.12 = (bf16[128,2048]{1,0:T(8,128)(2,1)}, bf16[128,2048]{1,0:T(8,128)(2,1)}, u32[]{:S(2)}, u32[]{:S(2)}) collective-permute-start(bf16[128,2048]{1,0:T(8,128)(2,1)} %collective-permute-done.4), channel_id=1, source_target_pairs={{0,4},{1,5},{2,6},{3,7},{4,0},{5,1},{6,2},{7,3},{8,12},{9,13},{10,... | collective-permute-start | bytes 1572872 | tf_op jit(solution)/shard_map/ppermute | solution.py:100
  71.0 17.4 %collective-permute-start.14 = (bf16[128,2048]{1,0:T(8,128)(2,1)}, bf16[128,2048]{1,0:T(8,128)(2,1)S(1)}, u32[]{:S(2)}, u32[]{:S(2)}) collective-permute-start(bf16[128,2048]{1,0:T(8,128)(2,1)} %collective-permute-done.4), channel_id=1, source_target_pairs={{0,2},{1,3},{2,0},{3,1},{4,6},{5,7},{6,4},{7,5},{8,10},{9,11},{10,... | collective-permute-start | bytes 1572872 | tf_op jit(solution)/shard_map/ppermute | solution.py:100
  87.9 14.2 %collective-permute-start.18 = (bf16[128,2048]{1,0:T(8,128)(2,1)}, bf16[128,2048]{1,0:T(8,128)(2,1)S(1)}, u32[]{:S(2)}, u32[]{:S(2)}) collective-permute-start(bf16[128,2048]{1,0:T(8,128)(2,1)} %collective-permute-done.6), channel_id=1, source_target_pairs={{0,2},{1,3},{2,0},{3,1},{4,6},{5,7},{6,4},{7,5},{8,10},{9,11},{10,... | collective-permute-start | bytes 1572872 | tf_op jit(solution)/shard_map/ppermute | solution.py:100
  88.5 13.7 %collective-permute-start.20 = (bf16[128,2048]{1,0:T(8,128)(2,1)}, bf16[128,2048]{1,0:T(8,128)(2,1)}, u32[]{:S(2)}, u32[]{:S(2)}) collective-permute-start(bf16[128,2048]{1,0:T(8,128)(2,1)} %collective-permute-done.6), channel_id=1, source_target_pairs={{0,1},{1,0},{2,3},{3,2},{4,5},{5,4},{6,7},{7,6},{8,9},{9,8},{10,11... | collective-permute-start | bytes 1572872 | tf_op jit(solution)/shard_map/ppermute | solution.py:100
  88.5 13.7 %collective-permute-start.22 = (bf16[128,2048]{1,0:T(8,128)(2,1)}, bf16[128,2048]{1,0:T(8,128)(2,1)}, u32[]{:S(2)}, u32[]{:S(2)}) collective-permute-start(bf16[128,2048]{1,0:T(8,128)(2,1)} %collective-permute-done.8), channel_id=1, source_target_pairs={{0,1},{1,0},{2,3},{3,2},{4,5},{5,4},{6,7},{7,6},{8,9},{9,8},{10,11... | collective-permute-start | bytes 1572872 | tf_op jit(solution)/shard_map/ppermute | solution.py:100
  102.1 45.2 %collective-permute-start.25 = (bf16[128,2048]{1,0:T(8,128)(2,1)}, bf16[128,2048]{1,0:T(8,128)(2,1)}, u32[]{:S(2)}, u32[]{:S(2)}) collective-permute-start(bf16[128,2048]{1,0:T(8,128)(2,1)} %collective-permute-done.12), channel_id=1, source_target_pairs={{0,2},{1,3},{2,0},{3,1},{4,6},{5,7},{6,4},{7,5},{8,10},{9,11},{10,... | collective-permute-start | bytes 1572872 | tf_op jit(solution)/shard_map/ppermute | solution.py:100
  108.5 38.9 %collective-permute-start.26 = (f32[128,16]{0,1:T(8,128)S(1)}, f32[128,16]{0,1:T(8,128)S(1)}, u32[]{:S(2)}, u32[]{:S(2)}) collective-permute-start(f32[128,16]{0,1:T(8,128)S(1)} %collective-permute-done.13), channel_id=1, source_target_pairs={{0,2},{1,3},{2,0},{3,1},{4,6},{5,7},{6,4},{7,5},{8,10},{9,11},{10,... | collective-permute-start | bytes 24584 | tf_op jit(solution)/shard_map/ppermute | solution.py:100
  110.0 50.4 %collective-permute-start.35 = (f32[128,16]{0,1:T(8,128)S(1)}, f32[128,16]{0,1:T(8,128)S(1)}, u32[]{:S(2)}, u32[]{:S(2)}) collective-permute-start(f32[128,16]{0,1:T(8,128)S(1)} %collective-permute-done.13), channel_id=1, source_target_pairs={{0,1},{1,0},{2,3},{3,2},{4,5},{5,4},{6,7},{7,6},{8,9},{9,8},{10,11... | collective-permute-start | bytes 24584 | tf_op jit(solution)/shard_map/ppermute | solution.py:100
  110.2 50.3 %collective-permute-start.36 = (f32[128,16]{0,1:T(8,128)S(1)}, f32[128,16]{0,1:T(8,128)S(1)}, u32[]{:S(2)}, u32[]{:S(2)}) collective-permute-start(f32[128,16]{0,1:T(8,128)S(1)} %collective-permute-done.15), channel_id=1, source_target_pairs={{0,1},{1,0},{2,3},{3,2},{4,5},{5,4},{6,7},{7,6},{8,9},{9,8},{10,11... | collective-permute-start | bytes 24584 | tf_op jit(solution)/shard_map/ppermute | solution.py:100
  138.7 21.7 %collective-permute-start.37 = (f32[128,16]{0,1:T(8,128)S(1)}, f32[128,16]{0,1:T(8,128)S(1)}, u32[]{:S(2)}, u32[]{:S(2)}) collective-permute-start(f32[128,16]{0,1:T(8,128)S(1)} %collective-permute-done.19), channel_id=1, source_target_pairs={{0,1},{1,0},{2,3},{3,2},{4,5},{5,4},{6,7},{7,6},{8,9},{9,8},{10,11... | collective-permute-start | bytes 24584 | tf_op jit(solution)/shard_map/ppermute | solution.py:100
  147.4 23.0 %collective-permute-start.34 = (bf16[128,2048]{1,0:T(8,128)(2,1)}, bf16[128,2048]{1,0:T(8,128)(2,1)}, u32[]{:S(2)}, u32[]{:S(2)}) collective-permute-start(bf16[128,2048]{1,0:T(8,128)(2,1)} %collective-permute-done.25), channel_id=1, source_target_pairs={{0,1},{1,0},{2,3},{3,2},{4,5},{5,4},{6,7},{7,6},{8,9},{9,8},{10,11... | collective-permute-start | bytes 1572872 | tf_op jit(solution)/shard_map/ppermute | solution.py:100
  147.9 12.5 %collective-permute-start.38 = (f32[128,16]{0,1:T(8,128)S(1)}, f32[128,16]{0,1:T(8,128)S(1)}, u32[]{:S(2)}, u32[]{:S(2)}) collective-permute-start(f32[128,16]{0,1:T(8,128)S(1)} %collective-permute-done.26), channel_id=1, source_target_pairs={{0,1},{1,0},{2,3},{3,2},{4,5},{5,4},{6,7},{7,6},{8,9},{9,8},{10,11... | collective-permute-start | bytes 24584 | tf_op jit(solution)/shard_map/ppermute | solution.py:100
  169.9 21.0 %collective-permute-start.28 = (bf16[128,2048]{1,0:T(8,128)(2,1)}, bf16[128,2048]{1,0:T(8,128)(2,1)}, u32[]{:S(2)}, u32[]{:S(2)}) collective-permute-start(bf16[128,2048]{1,0:T(8,128)(2,1)} %get-tuple-element.86), channel_id=1, source_target_pairs={{1,0},{0,1},{3,2},{2,3},{5,4},{4,5},{7,6},{6,7},{9,8},{8,9},{11,10... | collective-permute-start | bytes 1572872 | tf_op jit(solution)/shard_map/ppermute | solution.py:137
  170.4 34.6 %collective-permute-start.30 = (bf16[128,2048]{1,0:T(8,128)(2,1)}, bf16[128,2048]{1,0:T(8,128)(2,1)}, u32[]{:S(2)}, u32[]{:S(2)}) collective-permute-start(bf16[128,2048]{1,0:T(8,128)(2,1)} %get-tuple-element.85), channel_id=1, source_target_pairs={{1,0},{0,1},{3,2},{2,3},{5,4},{4,5},{7,6},{6,7},{9,8},{8,9},{11,10... | collective-permute-start | bytes 1572872 | tf_op jit(solution)/shard_map/ppermute | solution.py:137
  190.9 35.0 %collective-permute-start.42 = (bf16[128,2048]{1,0:T(8,128)(2,1)}, bf16[128,2048]{1,0:T(8,128)(2,1)}, u32[]{:S(2)}, u32[]{:S(2)}) collective-permute-start(bf16[128,2048]{1,0:T(8,128)(2,1)} %get-tuple-element.84), channel_id=1, source_target_pairs={{1,0},{0,1},{3,2},{2,3},{5,4},{4,5},{7,6},{6,7},{9,8},{8,9},{11,10... | collective-permute-start | bytes 1572872 | tf_op jit(solution)/shard_map/ppermute | solution.py:137
  190.9 14.7 %collective-permute-start.45 = (bf16[128,2048]{1,0:T(8,128)(2,1)}, bf16[128,2048]{1,0:T(8,128)(2,1)}, u32[]{:S(2)}, u32[]{:S(2)}) collective-permute-start(bf16[128,2048]{1,0:T(8,128)(2,1)} %get-tuple-element.89), channel_id=1, source_target_pairs={{1,0},{0,1},{3,2},{2,3},{5,4},{4,5},{7,6},{6,7},{9,8},{8,9},{11,10... | collective-permute-start | bytes 1572872 | tf_op jit(solution)/shard_map/ppermute | solution.py:137
  196.0 15.1 %collective-permute-start.40 = (bf16[128,2048]{1,0:T(8,128)(2,1)}, bf16[128,2048]{1,0:T(8,128)(2,1)}, u32[]{:S(2)}, u32[]{:S(2)}) collective-permute-start(bf16[128,2048]{1,0:T(8,128)(2,1)} %get-tuple-element.73), channel_id=1, source_target_pairs={{2,0},{3,1},{0,2},{1,3},{6,4},{7,5},{4,6},{5,7},{10,8},{11,9},{8,1... | collective-permute-start | bytes 1572872 | tf_op jit(solution)/shard_map/ppermute | solution.py:137
  196.5 25.8 %collective-permute-start.47 = (bf16[128,2048]{1,0:T(8,128)(2,1)}, bf16[128,2048]{1,0:T(8,128)(2,1)}, u32[]{:S(2)}, u32[]{:S(2)}) collective-permute-start(bf16[128,2048]{1,0:T(8,128)(2,1)} %get-tuple-element.71), channel_id=1, source_target_pairs={{2,0},{3,1},{0,2},{1,3},{6,4},{7,5},{4,6},{5,7},{10,8},{11,9},{8,1... | collective-permute-start | bytes 1572872 | tf_op jit(solution)/shard_map/ppermute | solution.py:137
  205.0 28.5 %collective-permute-start.44 = (bf16[128,2048]{1,0:T(8,128)(2,1)}, bf16[128,2048]{1,0:T(8,128)(2,1)S(1)}, u32[]{:S(2)}, u32[]{:S(2)}) collective-permute-start(bf16[128,2048]{1,0:T(8,128)(2,1)} %get-tuple-element.72), channel_id=1, source_target_pairs={{2,0},{3,1},{0,2},{1,3},{6,4},{7,5},{4,6},{5,7},{10,8},{11,9},{8,1... | collective-permute-start | bytes 1572872 | tf_op jit(solution)/shard_map/ppermute | solution.py:137
  224.9 20.5 %collective-permute-start.48 = (bf16[128,2048]{1,0:T(8,128)(2,1)S(1)}, bf16[128,2048]{1,0:T(8,128)(2,1)S(1)}, u32[]{:S(2)}, u32[]{:S(2)}) collective-permute-start(bf16[128,2048]{1,0:T(8,128)(2,1)S(1)} %get-tuple-element.75), channel_id=1, source_target_pairs={{4,0},{5,1},{6,2},{7,3},{0,4},{1,5},{2,6},{3,7},{12,8},{13,9},{14,... | collective-permute-start | bytes 1572872 | tf_op jit(solution)/shard_map/ppermute | solution.py:137
  225.3 21.6 %collective-permute-start.27 = (bf16[128,2048]{1,0:T(8,128)(2,1)S(1)}, bf16[128,2048]{1,0:T(8,128)(2,1)S(1)}, u32[]{:S(2)}, u32[]{:S(2)}) collective-permute-start(bf16[128,2048]{1,0:T(8,128)(2,1)S(1)} %copy-done.17), channel_id=1, source_target_pairs={{1,0},{0,1},{3,2},{2,3},{5,4},{4,5},{7,6},{6,7},{9,8},{8,9},{11,10... | collective-permute-start | bytes 1572872 | tf_op jit(solution)/shard_map/ppermute | solution.py:137
  225.3 21.6 %collective-permute-start.29 = (bf16[128,2048]{1,0:T(8,128)(2,1)S(1)}, bf16[128,2048]{1,0:T(8,128)(2,1)S(1)}, u32[]{:S(2)}, u32[]{:S(2)}) collective-permute-start(bf16[128,2048]{1,0:T(8,128)(2,1)S(1)} %copy-done.16), channel_id=1, source_target_pairs={{2,0},{3,1},{0,2},{1,3},{6,4},{7,5},{4,6},{5,7},{10,8},{11,9},{8,1... | collective-permute-start | bytes 1572872 | tf_op jit(solution)/shard_map/ppermute | solution.py:137
  225.9 28.3 %collective-permute-start.41 = (bf16[128,2048]{1,0:T(8,128)(2,1)S(1)}, bf16[128,2048]{1,0:T(8,128)(2,1)S(1)}, u32[]{:S(2)}, u32[]{:S(2)}) collective-permute-start(bf16[128,2048]{1,0:T(8,128)(2,1)S(1)} %get-tuple-element.74), channel_id=1, source_target_pairs={{4,0},{5,1},{6,2},{7,3},{0,4},{1,5},{2,6},{3,7},{12,8},{13,9},{14,... | collective-permute-start | bytes 1572872 | tf_op jit(solution)/shard_map/ppermute | solution.py:137
  246.8 17.6 %collective-permute-start.49 = (bf16[128,2048]{1,0:T(8,128)(2,1)S(1)}, bf16[128,2048]{1,0:T(8,128)(2,1)S(1)}, u32[]{:S(2)}, u32[]{:S(2)}) collective-permute-start(bf16[128,2048]{1,0:T(8,128)(2,1)S(1)} %fusion.37), channel_id=1, source_target_pairs={{8,0},{9,1},{10,2},{11,3},{12,4},{13,5},{14,6},{15,7},{0,8},{1,9},... | collective-permute-start | bytes 1572872 | tf_op jit(solution)/shard_map/ppermute | solution.py:137
  (48 other events, 371.1 us)

commit v14 on v11

--- a/solution.py
+++ b/solution.py
@@ -99,9 +99,9 @@
                 else:
                     grown.append((lax.ppermute(block, "ep", pairs), parent, pairs))
         if number == tie_at:
-            tied = lax.optimization_barrier((tuple(full), [piece[0] for piece in grown]))
+            tied = lax.optimization_barrier((tuple(full), grown[-1][0]))
             full = list(tied[0])
-            grown = [(block, parent, pairs) for block, (_, parent, pairs) in zip(tied[1], grown)]
+            grown[-1] = (tied[1],) + grown[-1][1:]
         pieces = pieces + grown
         if ends:
             groups.append((low, len(pieces)))

time: 242 us -> 237 us (0.979); the launches traced: 240 us -> 233 us
  local copies, waits for them, and re-layouts: 29.9 us -> 23.8 us
  waiting for transfers between devices: 107 us -> 104 us
    ppermute x22, waiting for transfers between devices: 12.9 us -> 21.1 us  [dense_moe(): grown.append((lax.ppermute(block, 'ep', pairs), parent, pairs))]
    ppermute x1, waiting for transfers between devices: 15.2 us -> 7.33 us  [full_weights(): other = lax.ppermute(packed, 'kv', [(0, 1), (1, 0)])]
    unnamed x81 -> x94, local copies, waits for them, and re-layouts: 19.5 us -> 14.8 us
    dot_general x4, matrix products: 26.6 us -> 29.2 us  [expert(): out_rows = jnp.dot(act, full[2], preferred_element_type=jnp.float32)]
  transfers between devices with their start and end apart: 50 -> 50, of which waited for: 16 -> 15; matrix products, arithmetic and copies ran while one was open for 35% -> 37% of each run, Pallas kernels for 0% -> 0%
where the time goes in v14:
time: 237 us; the launch traced here: 233 us
  waiting for transfers between devices  104 us (44%)
  matrix products  48 us (20%)
  starting transfers between devices  32.9 us (14%)
  local copies, waits for them, and re-layouts  23.8 us (10%)
  other arithmetic  22.7 us (10%)
    ppermute x15, waiting for transfers between devices, dense_moe(): sent = lax.ppermute(partial[index].astype(jnp.bfloat16), 'ep', back)  47.3 us
    dot_general x4, matrix products, expert(): out_rows = jnp.dot(act, full[2], preferred_element_type=jnp.float32)  29.2 us
    ppermute x8, waiting for transfers between devices, dense_moe(): lax.ppermute(pieces[0][0], 'ep', pairs)  23.2 us
    ppermute x22, waiting for transfers between devices, dense_moe(): grown.append((lax.ppermute(block, 'ep', pairs), parent, pairs))  21.1 us
    unnamed x94, local copies, waits for them, and re-layouts  14.8 us
    ppermute x22, starting transfers between devices, dense_moe(): grown.append((lax.ppermute(block, 'ep', pairs), parent, pairs))  11 us
    ppermute x15, starting transfers between devices, dense_moe(): sent = lax.ppermute(partial[index].astype(jnp.bfloat16), 'ep', back)  9.89 us
    convert_element_type x3, other arithmetic, dense_moe(): sent = lax.ppermute(partial[index].astype(jnp.bfloat16), 'ep', back)  8.06 us
  transfers between devices with their start and end apart: 50, of which 15 were waited for; matrix products, arithmetic and copies ran while one was open for 37% of the time, Pallas kernels for 0%

profile of v14, /device:TPU:24, one launch (start us, length us, event | category | flops | bytes accessed | tf_op | source)
XLA Modules:
  0.0 232.7 jit_solution(5039263238192668450)
XLA Ops:
  4.6 3.7 %copy.104 = bf16[128,8,8,128]{3,2,1,0:T(8,128)(2,1)} copy(bf16[128,8,8,128]{3,1,2,0:T(8,128)(2,1)} %bitcast.92) | data formatting | bytes 4194304
  8.4 2.0 copy.103
  12.2 2.6 %bitcast_reduce_fusion.1 = (f32[128,8]{0,1:T(8,128)S(1)}, f32[8,1024,128]{2,1,0:T(8,128)S(1)}) fusion(pred[1024]{0:T(1024)(128)(4,1)S(1)} %add_compare_fusion, bf16[128,8,128]{2,1,0:T(8,128)(2,1)S(1)} %bitcast.102, bf16[1024,8,128]{2,1,0:T(8,128)(2,1)} %bitcast.96), kind=kOutput, calls=%fused_computation.4 | convolution fusion | flops 271580160 | bytes 6558720 | tf_op jit(solution)/shard_map/qhd,khd->qhk/dot_general | solution.py:260
  14.8 1.7 fusion.10
  20.0 1.7 fusion.8
  25.7 1.8 collective-permute-start.9
  27.5 3.8 %collective-permute-done.2 = bf16[128,8,128]{0,2,1:T(8,128)(2,1)S(1)} collective-permute-done((bf16[128,8,128]{0,2,1:T(8,128)(2,1)S(1)}, bf16[128,8,128]{0,2,1:T(8,128)(2,1)S(1)}, u32[]{:S(2)}, u32[]{:S(2)}) %collective-permute-start.2) | collective-permute-done | bytes 262176 | tf_op jit(solution)/shard_map/ppermute | solution.py:298
  33.4 3.5 %pad_maximum_fusion = bf16[3,2048,256]{2,1,0:T(8,128)(2,1)} fusion(bf16[1,2048,256]{2,1,0:T(8,128)(2,1)S(1)} %stack_reshape_squeeze.3, bf16[1,2048,256]{2,1,0:T(8,128)(2,1)} %param.28, bf16[1,2048,256]{2,1,0:T(8,128)(2,1)} %param.27), kind=kLoop, calls=%fused_computation.16 | loop fusion | flops 3145728 | bytes 6291456 | tf_op jit(solution)/shard_map/stack | solution.py:53
  37.8 2.7 %collective-permute-start.4 = (bf16[128,2048]{1,0:T(8,128)(2,1)S(1)}, bf16[128,2048]{1,0:T(8,128)(2,1)S(1)}, u32[]{:S(2)}, u32[]{:S(2)}) collective-permute-start(bf16[128,2048]{1,0:T(8,128)(2,1)S(1)} %multiply_convert_fusion.6), channel_id=1, source_target_pairs={{0,8},{1,9},{2,10},{3,11},{4,12},{5,13},{6,14},{7,15},{8,0},{9,1},... | collective-permute-start | bytes 1572872 | tf_op jit(solution)/shard_map/ppermute | solution.py:90
  42.4 21.8 %collective-permute-done.4 = bf16[128,2048]{1,0:T(8,128)(2,1)S(1)} collective-permute-done((bf16[128,2048]{1,0:T(8,128)(2,1)S(1)}, bf16[128,2048]{1,0:T(8,128)(2,1)S(1)}, u32[]{:S(2)}, u32[]{:S(2)}) %collective-permute-start.4) | collective-permute-done | bytes 524320 | tf_op jit(solution)/shard_map/ppermute | solution.py:90
  70.9 10.2 %collective-permute-done.12 = bf16[128,2048]{1,0:T(8,128)(2,1)} collective-permute-done((bf16[128,2048]{1,0:T(8,128)(2,1)}, bf16[128,2048]{1,0:T(8,128)(2,1)}, u32[]{:S(2)}, u32[]{:S(2)}) %collective-permute-start.12) | collective-permute-done | bytes 524320 | tf_op jit(solution)/shard_map/ppermute | solution.py:100
  82.4 10.0 %collective-permute-done.25 = bf16[128,2048]{1,0:T(8,128)(2,1)S(1)} collective-permute-done((bf16[128,2048]{1,0:T(8,128)(2,1)S(1)}, bf16[128,2048]{1,0:T(8,128)(2,1)S(1)}, u32[]{:S(2)}, u32[]{:S(2)}) %collective-permute-start.25) | collective-permute-done | bytes 524320 | tf_op jit(solution)/shard_map/ppermute | solution.py:100
  98.3 7.3 %collective-permute-done.13 = bf16[3,2048,256]{2,1,0:T(8,128)(2,1)} collective-permute-done((bf16[3,2048,256]{2,1,0:T(8,128)(2,1)}, bf16[3,2048,256]{2,1,0:T(8,128)(2,1)}, u32[]{:S(2)}, u32[]{:S(2)}) %collective-permute-start.13) | collective-permute-done | bytes 3145760 | tf_op jit(solution)/shard_map/ppermute | solution.py:54
  107.2 4.5 %select_bitcast_fusion.1 = (bf16[2048,256]{1,0:T(8,128)(2,1)}, bf16[2048,256]{1,0:T(8,128)(2,1)}, bf16[1,2048,256]{2,1,0:T(8,128)(2,1)}, bf16[2048,256]{1,0:T(8,128)(2,1)}, bf16[2048,256]{1,0:T(8,128)(2,1)}) fusion(bf16[1,2048,256]{2,1,0:T(8,128)(2,1)S(1)} %copy-done.3, pred[]{:T(512)S(6)} %eq.42, bf16[3,2048,256]{2,1,0:T(8,128)(2,1)} %collective-permute-done.13, ...), kind=kLoop, calls=%fused_computation.84 | loop fusion | flops 2097152 | bytes 10485761 | tf_op jit(solution)/shard_map/jit(_where)/select_n | solution.py:61
  118.9 2.2 fusion.100
  121.2 3.4 %fusion.56 = f32[512,512]{1,0:T(8,128)} fusion(bf16[2048,512]{1,0:T(8,128)(2,1)S(1)} %get-tuple-element.28, bf16[128,2048]{1,0:T(8,128)(2,1)} %collective-permute-done.12, bf16[128,2048]{1,0:T(8,128)(2,1)S(1)} %copy-done.38, bf16[128,2048]{1,0:T(8,128)(2,1)S(1)} %copy-done.35, bf16[128,2048]{1,0:T(8,128)(2,1)S(1)} %copy-done.20), kind=kOutput, calls=%fused_computation.101 | convolution fusion | flops 1082130432 | bytes 5242880 | tf_op jit(solution)/shard_map/dot_general | solution.py:79
  126.8 2.2 fusion.101
  129.2 7.0 %multiply_convert_fusion.1 = bf16[512,2048]{1,0:T(8,128)(2,1)} fusion(f32[512]{0:T(512)S(1)} %get-tuple-element.39, bf16[512,2048]{1,0:T(8,128)(2,1)} %pad_maximum_fusion.4, f32[512,512]{1,0:T(8,128)} %fusion.100, bf16[512,2048]{1,0:T(8,128)(2,1)} %copy-done.31, bf16[2048,512]{1,0:T(8,128)(2,1)} %copy-done.14), kind=kOutput, calls=%fused_computation.8 | convolution fusion | flops 2153250816 | bytes 9439232 | tf_op jit(solution)/shard_map/dot_general | solution.py:81
  136.2 3.1 %fusion.90 = (bf16[128,2048]{1,0:T(8,128)(2,1)}, bf16[128,2048]{1,0:T(8,128)(2,1)}, bf16[128,2048]{1,0:T(8,128)(2,1)}, bf16[128,2048]{1,0:T(8,128)(2,1)}) fusion(bf16[512,2048]{1,0:T(8,128)(2,1)} %multiply_convert_fusion.1), kind=kLoop, calls=%fused_computation.153 | loop fusion | bytes 4194304 | tf_op jit(solution)/shard_map/slice | solution.py:126
  141.1 6.7 %multiply_convert_fusion = bf16[512,2048]{1,0:T(8,128)(2,1)} fusion(bf16[512,2048]{1,0:T(8,128)(2,1)} %pad_maximum_fusion.4, f32[512]{0:T(512)S(1)} %get-tuple-element.41, f32[512,512]{1,0:T(8,128)S(1)} %fusion.102, bf16[512,2048]{1,0:T(8,128)(2,1)} %copy-done.27, bf16[2048,512]{1,0:T(8,128)(2,1)} %copy-done.14), kind=kOutput, calls=%fused_computation.6 | convolution fusion | flops 2153250816 | bytes 9439232 | tf_op jit(solution)/shard_map/dot_general | solution.py:81
  147.8 2.7 %fusion.91 = (bf16[128,2048]{1,0:T(8,128)(2,1)S(1)}, bf16[128,2048]{1,0:T(8,128)(2,1)}, bf16[128,2048]{1,0:T(8,128)(2,1)}, bf16[128,2048]{1,0:T(8,128)(2,1)}) fusion(bf16[512,2048]{1,0:T(8,128)(2,1)} %multiply_convert_fusion), kind=kLoop, calls=%fused_computation.154 | loop fusion | bytes 4194304 | tf_op jit(solution)/shard_map/slice | solution.py:126
  151.5 7.6 %convert_multiply_fusion = f32[512,2048]{1,0:T(8,128)} fusion(bf16[512,2048]{1,0:T(8,128)(2,1)} %pad_maximum_fusion.4, f32[512]{0:T(512)S(1)} %get-tuple-element.40, f32[512,512]{1,0:T(8,128)} %fusion.101, bf16[512,2048]{1,0:T(8,128)(2,1)} %copy-done.30, bf16[2048,512]{1,0:T(8,128)(2,1)} %copy-done.14), kind=kOutput, calls=%fused_computation.7 | convolution fusion | flops 2152202240 | bytes 11536384 | tf_op jit(solution)/shard_map/dot_general | solution.py:81
  160.1 4.4 %fusion.41 = (bf16[128,2048]{1,0:T(8,128)(2,1)S(1)}, bf16[128,2048]{1,0:T(8,128)(2,1)}, bf16[128,2048]{1,0:T(8,128)(2,1)S(1)}, bf16[128,2048]{1,0:T(8,128)(2,1)}) fusion(f32[512,2048]{1,0:T(8,128)} %convert_multiply_fusion, bf16[128,2048]{1,0:T(8,128)(2,1)} %copy-done.17, bf16[128,2048]{1,0:T(8,128)(2,1)} %collective-permute-done.46, ...), kind=kLoop, calls=%fused_computation.70 | loop fusion | flops 3145728 | bytes 8388608 | tf_op jit(solution)/shard_map/convert_element_type | solution.py:130
  166.6 8.0 %convert_multiply_fusion.1 = f32[512,2048]{1,0:T(8,128)} fusion(bf16[512,2048]{1,0:T(8,128)(2,1)} %pad_maximum_fusion.4, f32[512]{0:T(512)S(1)} %get-tuple-element.42, f32[512,512]{1,0:T(8,128)} %fusion.56, bf16[2048,512]{1,0:T(8,128)(2,1)} %copy-done.12, bf16[128,2048]{1,0:T(8,128)(2,1)} %collective-permute-done.12, bf16[128,2048]{1,0:T(8,128)(2,1)} %copy-done.36, ...), kind=kOutput, calls=%fused_computation.9 | convolution fusion | flops 2160590848 | bytes 11536384 | tf_op jit(solution)/shard_map/dot_general | solution.py:81
  175.2 4.5 %collective-permute-done.40 = bf16[128,2048]{1,0:T(8,128)(2,1)} collective-permute-done((bf16[128,2048]{1,0:T(8,128)(2,1)}, bf16[128,2048]{1,0:T(8,128)(2,1)}, u32[]{:S(2)}, u32[]{:S(2)}) %collective-permute-start.40) | collective-permute-done | bytes 524320 | tf_op jit(solution)/shard_map/ppermute | solution.py:130
  179.6 11.2 %collective-permute-done.47 = bf16[128,2048]{1,0:T(8,128)(2,1)} collective-permute-done((bf16[128,2048]{1,0:T(8,128)(2,1)}, bf16[128,2048]{1,0:T(8,128)(2,1)}, u32[]{:S(2)}, u32[]{:S(2)}) %collective-permute-start.47) | collective-permute-done | bytes 524320 | tf_op jit(solution)/shard_map/ppermute | solution.py:130
  190.9 2.3 fusion.40
  195.8 6.2 %collective-permute-done.44 = bf16[128,2048]{1,0:T(8,128)(2,1)S(1)} collective-permute-done((bf16[128,2048]{1,0:T(8,128)(2,1)S(1)}, bf16[128,2048]{1,0:T(8,128)(2,1)S(1)}, u32[]{:S(2)}, u32[]{:S(2)}) %collective-permute-start.44) | collective-permute-done | bytes 524320 | tf_op jit(solution)/shard_map/ppermute | solution.py:130
  202.0 6.1 %collective-permute-done.48 = bf16[128,2048]{1,0:T(8,128)(2,1)S(1)} collective-permute-done((bf16[128,2048]{1,0:T(8,128)(2,1)S(1)}, bf16[128,2048]{1,0:T(8,128)(2,1)S(1)}, u32[]{:S(2)}, u32[]{:S(2)}) %collective-permute-start.48) | collective-permute-done | bytes 524320 | tf_op jit(solution)/shard_map/ppermute | solution.py:130
  209.4 2.7 %collective-permute-start.49 = (bf16[128,2048]{1,0:T(8,128)(2,1)S(1)}, bf16[128,2048]{1,0:T(8,128)(2,1)S(1)}, u32[]{:S(2)}, u32[]{:S(2)}) collective-permute-start(bf16[128,2048]{1,0:T(8,128)(2,1)S(1)} %fusion.37), channel_id=1, source_target_pairs={{8,0},{9,1},{10,2},{11,3},{12,4},{13,5},{14,6},{15,7},{0,8},{1,9},... | collective-permute-start | bytes 1572872 | tf_op jit(solution)/shard_map/ppermute | solution.py:130
  212.6 15.0 %collective-permute-done.41 = bf16[128,2048]{1,0:T(8,128)(2,1)S(1)} collective-permute-done((bf16[128,2048]{1,0:T(8,128)(2,1)S(1)}, bf16[128,2048]{1,0:T(8,128)(2,1)S(1)}, u32[]{:S(2)}, u32[]{:S(2)}) %collective-permute-start.41) | collective-permute-done | bytes 524320 | tf_op jit(solution)/shard_map/ppermute | solution.py:130
  227.7 3.8 %collective-permute-done.49 = bf16[128,2048]{1,0:T(8,128)(2,1)S(1)} collective-permute-done((bf16[128,2048]{1,0:T(8,128)(2,1)S(1)}, bf16[128,2048]{1,0:T(8,128)(2,1)S(1)}, u32[]{:S(2)}, u32[]{:S(2)}) %collective-permute-start.49) | collective-permute-done | bytes 524320 | tf_op jit(solution)/shard_map/ppermute | solution.py:130
  (210 shorter events, 54.8 us)
Async XLA Ops:
  0.7 37.0 %collective-permute-start.11 = (f32[128,16]{0,1:T(8,128)S(1)}, f32[128,16]{0,1:T(8,128)S(1)}, u32[]{:S(2)}, u32[]{:S(2)}) collective-permute-start(f32[128,16]{0,1:T(8,128)S(1)} %select_reduce_fusion), channel_id=1, source_target_pairs={{0,1},{1,0},{2,3},{3,2},{4,5},{5,4},{6,7},{7,6},{8,9},{9,8},{10,11... | collective-permute-start | bytes 24584 | tf_op jit(solution)/shard_map/ppermute | solution.py:90
  0.8 37.0 %collective-permute-start.5 = (f32[128,16]{0,1:T(8,128)S(1)}, f32[128,16]{0,1:T(8,128)S(1)}, u32[]{:S(2)}, u32[]{:S(2)}) collective-permute-start(f32[128,16]{0,1:T(8,128)S(1)} %select_reduce_fusion), channel_id=1, source_target_pairs={{0,8},{1,9},{2,10},{3,11},{4,12},{5,13},{6,14},{7,15},{8,0},{9,1},... | collective-permute-start | bytes 24584 | tf_op jit(solution)/shard_map/ppermute | solution.py:90
  2.3 14.2 %collective-permute-start = (bf16[128,1024]{0,1:T(8,128)(2,1)S(1)}, bf16[128,1024]{0,1:T(8,128)(2,1)S(1)}, u32[]{:S(2)}, u32[]{:S(2)}) collective-permute-start(bf16[128,1024]{0,1:T(8,128)(2,1)S(1)} %bitcast.106), channel_id=1, source_target_pairs={{0,16},{16,0},{1,17},{17,1},{2,18},{18,2},{3,19},{19,3},{4,20},{20... | collective-permute-start | bytes 786440 | tf_op jit(solution)/shard_map/ppermute | solution.py:288
  25.5 14.9 %collective-permute-start.7 = (f32[128,16]{0,1:T(8,128)S(1)}, f32[128,16]{0,1:T(8,128)S(1)}, u32[]{:S(2)}, u32[]{:S(2)}) collective-permute-start(f32[128,16]{0,1:T(8,128)S(1)} %select_reduce_fusion), channel_id=1, source_target_pairs={{0,4},{1,5},{2,6},{3,7},{4,0},{5,1},{6,2},{7,3},{8,12},{9,13},{10,... | collective-permute-start | bytes 24584 | tf_op jit(solution)/shard_map/ppermute | solution.py:90
  25.7 15.2 %collective-permute-start.9 = (f32[128,16]{0,1:T(8,128)S(1)}, f32[128,16]{0,1:T(8,128)S(1)}, u32[]{:S(2)}, u32[]{:S(2)}) collective-permute-start(f32[128,16]{0,1:T(8,128)S(1)} %select_reduce_fusion), channel_id=1, source_target_pairs={{0,2},{1,3},{2,0},{3,1},{4,6},{5,7},{6,4},{7,5},{8,10},{9,11},{10,... | collective-permute-start | bytes 24584 | tf_op jit(solution)/shard_map/ppermute | solution.py:90
  36.9 68.7 %collective-permute-start.13 = (bf16[3,2048,256]{2,1,0:T(8,128)(2,1)}, bf16[3,2048,256]{2,1,0:T(8,128)(2,1)}, u32[]{:S(2)}, u32[]{:S(2)}) collective-permute-start(bf16[3,2048,256]{2,1,0:T(8,128)(2,1)} %pad_maximum_fusion), channel_id=1, source_target_pairs={{0,16},{16,0},{1,17},{17,1},{2,18},{18,2},{3,19},{19,3},{4,20},{20... | collective-permute-start | bytes 9437192 | tf_op jit(solution)/shard_map/ppermute | solution.py:54
  37.8 26.4 %collective-permute-start.4 = (bf16[128,2048]{1,0:T(8,128)(2,1)S(1)}, bf16[128,2048]{1,0:T(8,128)(2,1)S(1)}, u32[]{:S(2)}, u32[]{:S(2)}) collective-permute-start(bf16[128,2048]{1,0:T(8,128)(2,1)S(1)} %multiply_convert_fusion.6), channel_id=1, source_target_pairs={{0,8},{1,9},{2,10},{3,11},{4,12},{5,13},{6,14},{7,15},{8,0},{9,1},... | collective-permute-start | bytes 1572872 | tf_op jit(solution)/shard_map/ppermute | solution.py:90
  40.5 25.1 %collective-permute-start.6 = (bf16[128,2048]{1,0:T(8,128)(2,1)S(1)}, bf16[128,2048]{1,0:T(8,128)(2,1)S(1)}, u32[]{:S(2)}, u32[]{:S(2)}) collective-permute-start(bf16[128,2048]{1,0:T(8,128)(2,1)S(1)} %multiply_convert_fusion.6), channel_id=1, source_target_pairs={{0,4},{1,5},{2,6},{3,7},{4,0},{5,1},{6,2},{7,3},{8,12},{9,13},{10,... | collective-permute-start | bytes 1572872 | tf_op jit(solution)/shard_map/ppermute | solution.py:90
  40.9 24.7 %collective-permute-start.8 = (bf16[128,2048]{1,0:T(8,128)(2,1)S(1)}, bf16[128,2048]{1,0:T(8,128)(2,1)}, u32[]{:S(2)}, u32[]{:S(2)}) collective-permute-start(bf16[128,2048]{1,0:T(8,128)(2,1)S(1)} %multiply_convert_fusion.6), channel_id=1, source_target_pairs={{0,2},{1,3},{2,0},{3,1},{4,6},{5,7},{6,4},{7,5},{8,10},{9,11},{10,... | collective-permute-start | bytes 1572872 | tf_op jit(solution)/shard_map/ppermute | solution.py:90
  66.9 14.2 %collective-permute-start.12 = (bf16[128,2048]{1,0:T(8,128)(2,1)}, bf16[128,2048]{1,0:T(8,128)(2,1)}, u32[]{:S(2)}, u32[]{:S(2)}) collective-permute-start(bf16[128,2048]{1,0:T(8,128)(2,1)} %copy-done.34), channel_id=1, source_target_pairs={{0,4},{1,5},{2,6},{3,7},{4,0},{5,1},{6,2},{7,3},{8,12},{9,13},{10,... | collective-permute-start | bytes 1572872 | tf_op jit(solution)/shard_map/ppermute | solution.py:100
  67.3 15.0 %collective-permute-start.24 = (bf16[128,2048]{1,0:T(8,128)(2,1)}, bf16[128,2048]{1,0:T(8,128)(2,1)S(1)}, u32[]{:S(2)}, u32[]{:S(2)}) collective-permute-start(bf16[128,2048]{1,0:T(8,128)(2,1)} %copy-done.34), channel_id=1, source_target_pairs={{0,2},{1,3},{2,0},{3,1},{4,6},{5,7},{6,4},{7,5},{8,10},{9,11},{10,... | collective-permute-start | bytes 1572872 | tf_op jit(solution)/shard_map/ppermute | solution.py:100
  70.1 22.3 %collective-permute-start.25 = (bf16[128,2048]{1,0:T(8,128)(2,1)S(1)}, bf16[128,2048]{1,0:T(8,128)(2,1)S(1)}, u32[]{:S(2)}, u32[]{:S(2)}) collective-permute-start(bf16[128,2048]{1,0:T(8,128)(2,1)S(1)} %copy-done.37), channel_id=1, source_target_pairs={{0,2},{1,3},{2,0},{3,1},{4,6},{5,7},{6,4},{7,5},{8,10},{9,11},{10,... | collective-permute-start | bytes 1572872 | tf_op jit(solution)/shard_map/ppermute | solution.py:100
  70.7 21.7 %collective-permute-start.18 = (bf16[128,2048]{1,0:T(8,128)(2,1)S(1)}, bf16[128,2048]{1,0:T(8,128)(2,1)S(1)}, u32[]{:S(2)}, u32[]{:S(2)}) collective-permute-start(bf16[128,2048]{1,0:T(8,128)(2,1)S(1)} %copy-done.37), channel_id=1, source_target_pairs={{0,1},{1,0},{2,3},{3,2},{4,5},{5,4},{6,7},{7,6},{8,9},{9,8},{10,11... | collective-permute-start | bytes 1572872 | tf_op jit(solution)/shard_map/ppermute | solution.py:100
  81.1 13.8 %collective-permute-start.15 = (f32[128,16]{0,1:T(8,128)S(1)}, f32[128,16]{0,1:T(8,128)S(1)}, u32[]{:S(2)}, u32[]{:S(2)}) collective-permute-start(f32[128,16]{0,1:T(8,128)S(1)} %collective-permute-done.5), channel_id=1, source_target_pairs={{0,4},{1,5},{2,6},{3,7},{4,0},{5,1},{6,2},{7,3},{8,12},{9,13},{10,... | collective-permute-start | bytes 24584 | tf_op jit(solution)/shard_map/ppermute | solution.py:100
  82.3 10.7 %collective-permute-start.19 = (bf16[128,2048]{1,0:T(8,128)(2,1)}, bf16[128,2048]{1,0:T(8,128)(2,1)S(1)}, u32[]{:S(2)}, u32[]{:S(2)}) collective-permute-start(bf16[128,2048]{1,0:T(8,128)(2,1)} %collective-permute-done.12), channel_id=1, source_target_pairs={{0,1},{1,0},{2,3},{3,2},{4,5},{5,4},{6,7},{7,6},{8,9},{9,8},{10,11... | collective-permute-start | bytes 1572872 | tf_op jit(solution)/shard_map/ppermute | solution.py:100
  93.1 32.6 %collective-permute-start.26 = (f32[128,16]{0,1:T(8,128)S(1)}, f32[128,16]{0,1:T(8,128)S(1)}, u32[]{:S(2)}, u32[]{:S(2)}) collective-permute-start(f32[128,16]{0,1:T(8,128)S(1)} %collective-permute-done.5), channel_id=1, source_target_pairs={{0,2},{1,3},{2,0},{3,1},{4,6},{5,7},{6,4},{7,5},{8,10},{9,11},{10,... | collective-permute-start | bytes 24584 | tf_op jit(solution)/shard_map/ppermute | solution.py:100
  94.7 31.5 %collective-permute-start.20 = (f32[128,16]{0,1:T(8,128)S(1)}, f32[128,16]{0,1:T(8,128)S(1)}, u32[]{:S(2)}, u32[]{:S(2)}) collective-permute-start(f32[128,16]{0,1:T(8,128)S(1)} %collective-permute-done.5), channel_id=1, source_target_pairs={{0,1},{1,0},{2,3},{3,2},{4,5},{5,4},{6,7},{7,6},{8,9},{9,8},{10,11... | collective-permute-start | bytes 24584 | tf_op jit(solution)/shard_map/ppermute | solution.py:100
  94.9 30.9 %collective-permute-start.27 = (f32[128,16]{0,1:T(8,128)S(1)}, f32[128,16]{0,1:T(8,128)S(1)}, u32[]{:S(2)}, u32[]{:S(2)}) collective-permute-start(f32[128,16]{0,1:T(8,128)S(1)} %collective-permute-done.7), channel_id=1, source_target_pairs={{0,2},{1,3},{2,0},{3,1},{4,6},{5,7},{6,4},{7,5},{8,10},{9,11},{10,... | collective-permute-start | bytes 24584 | tf_op jit(solution)/shard_map/ppermute | solution.py:100
  96.1 21.2 %collective-permute-start.16 = (f32[128,16]{0,1:T(8,128)S(1)}, f32[128,16]{0,1:T(8,128)S(1)}, u32[]{:S(2)}, u32[]{:S(2)}) collective-permute-start(f32[128,16]{0,1:T(8,128)S(1)} %collective-permute-done.15), channel_id=1, source_target_pairs={{0,2},{1,3},{2,0},{3,1},{4,6},{5,7},{6,4},{7,5},{8,10},{9,11},{10,... | collective-permute-start | bytes 24584 | tf_op jit(solution)/shard_map/ppermute | solution.py:100
  105.7 11.6 %collective-permute-start.14 = (bf16[128,2048]{1,0:T(8,128)(2,1)}, bf16[128,2048]{1,0:T(8,128)(2,1)}, u32[]{:S(2)}, u32[]{:S(2)}) collective-permute-start(bf16[128,2048]{1,0:T(8,128)(2,1)} %collective-permute-done.12), channel_id=1, source_target_pairs={{0,2},{1,3},{2,0},{3,1},{4,6},{5,7},{6,4},{7,5},{8,10},{9,11},{10,... | collective-permute-start | bytes 1572872 | tf_op jit(solution)/shard_map/ppermute | solution.py:100
  117.3 11.7 %collective-permute-start.32 = (f32[128,16]{0,1:T(8,128)S(1)}, f32[128,16]{0,1:T(8,128)S(1)}, u32[]{:S(2)}, u32[]{:S(2)}) collective-permute-start(f32[128,16]{0,1:T(8,128)S(1)} %collective-permute-done.9), channel_id=1, source_target_pairs={{0,1},{1,0},{2,3},{3,2},{4,5},{5,4},{6,7},{7,6},{8,9},{9,8},{10,11... | collective-permute-start | bytes 24584 | tf_op jit(solution)/shard_map/ppermute | solution.py:100
  139.3 35.3 %collective-permute-start.38 = (bf16[128,2048]{1,0:T(8,128)(2,1)}, bf16[128,2048]{1,0:T(8,128)(2,1)S(1)}, u32[]{:S(2)}, u32[]{:S(2)}) collective-permute-start(bf16[128,2048]{1,0:T(8,128)(2,1)} %get-tuple-element.62), channel_id=1, source_target_pairs={{1,0},{0,1},{3,2},{2,3},{5,4},{4,5},{7,6},{6,7},{9,8},{8,9},{11,10... | collective-permute-start | bytes 1572872 | tf_op jit(solution)/shard_map/ppermute | solution.py:130
  159.1 16.0 %collective-permute-start.45 = (bf16[128,2048]{1,0:T(8,128)(2,1)}, bf16[128,2048]{1,0:T(8,128)(2,1)S(1)}, u32[]{:S(2)}, u32[]{:S(2)}) collective-permute-start(bf16[128,2048]{1,0:T(8,128)(2,1)} %get-tuple-element.60), channel_id=1, source_target_pairs={{1,0},{0,1},{3,2},{2,3},{5,4},{4,5},{7,6},{6,7},{9,8},{8,9},{11,10... | collective-permute-start | bytes 1572872 | tf_op jit(solution)/shard_map/ppermute | solution.py:130
  159.2 35.0 %collective-permute-start.42 = (bf16[128,2048]{1,0:T(8,128)(2,1)}, bf16[128,2048]{1,0:T(8,128)(2,1)}, u32[]{:S(2)}, u32[]{:S(2)}) collective-permute-start(bf16[128,2048]{1,0:T(8,128)(2,1)} %get-tuple-element.61), channel_id=1, source_target_pairs={{1,0},{0,1},{3,2},{2,3},{5,4},{4,5},{7,6},{6,7},{9,8},{8,9},{11,10... | collective-permute-start | bytes 1572872 | tf_op jit(solution)/shard_map/ppermute | solution.py:130
  164.6 15.1 %collective-permute-start.40 = (bf16[128,2048]{1,0:T(8,128)(2,1)}, bf16[128,2048]{1,0:T(8,128)(2,1)}, u32[]{:S(2)}, u32[]{:S(2)}) collective-permute-start(bf16[128,2048]{1,0:T(8,128)(2,1)} %get-tuple-element.49), channel_id=1, source_target_pairs={{2,0},{3,1},{0,2},{1,3},{6,4},{7,5},{4,6},{5,7},{10,8},{11,9},{8,1... | collective-permute-start | bytes 1572872 | tf_op jit(solution)/shard_map/ppermute | solution.py:130
  165.1 25.8 %collective-permute-start.47 = (bf16[128,2048]{1,0:T(8,128)(2,1)}, bf16[128,2048]{1,0:T(8,128)(2,1)}, u32[]{:S(2)}, u32[]{:S(2)}) collective-permute-start(bf16[128,2048]{1,0:T(8,128)(2,1)} %get-tuple-element.47), channel_id=1, source_target_pairs={{2,0},{3,1},{0,2},{1,3},{6,4},{7,5},{4,6},{5,7},{10,8},{11,9},{8,1... | collective-permute-start | bytes 1572872 | tf_op jit(solution)/shard_map/ppermute | solution.py:130
  174.6 27.4 %collective-permute-start.44 = (bf16[128,2048]{1,0:T(8,128)(2,1)S(1)}, bf16[128,2048]{1,0:T(8,128)(2,1)S(1)}, u32[]{:S(2)}, u32[]{:S(2)}) collective-permute-start(bf16[128,2048]{1,0:T(8,128)(2,1)S(1)} %get-tuple-element.48), channel_id=1, source_target_pairs={{2,0},{3,1},{0,2},{1,3},{6,4},{7,5},{4,6},{5,7},{10,8},{11,9},{8,1... | collective-permute-start | bytes 1572872 | tf_op jit(solution)/shard_map/ppermute | solution.py:130
  193.2 14.9 %collective-permute-start.48 = (bf16[128,2048]{1,0:T(8,128)(2,1)S(1)}, bf16[128,2048]{1,0:T(8,128)(2,1)S(1)}, u32[]{:S(2)}, u32[]{:S(2)}) collective-permute-start(bf16[128,2048]{1,0:T(8,128)(2,1)S(1)} %get-tuple-element.51), channel_id=1, source_target_pairs={{4,0},{5,1},{6,2},{7,3},{0,4},{1,5},{2,6},{3,7},{12,8},{13,9},{14,... | collective-permute-start | bytes 1572872 | tf_op jit(solution)/shard_map/ppermute | solution.py:130
  193.7 18.4 %collective-permute-start.23 = (bf16[128,2048]{1,0:T(8,128)(2,1)S(1)}, bf16[128,2048]{1,0:T(8,128)(2,1)S(1)}, u32[]{:S(2)}, u32[]{:S(2)}) collective-permute-start(bf16[128,2048]{1,0:T(8,128)(2,1)S(1)} %copy-done.22), channel_id=1, source_target_pairs={{1,0},{0,1},{3,2},{2,3},{5,4},{4,5},{7,6},{6,7},{9,8},{8,9},{11,10... | collective-permute-start | bytes 1572872 | tf_op jit(solution)/shard_map/ppermute | solution.py:130
  193.7 19.0 %collective-permute-start.37 = (bf16[128,2048]{1,0:T(8,128)(2,1)S(1)}, bf16[128,2048]{1,0:T(8,128)(2,1)S(1)}, u32[]{:S(2)}, u32[]{:S(2)}) collective-permute-start(bf16[128,2048]{1,0:T(8,128)(2,1)S(1)} %get-tuple-element.46), channel_id=1, source_target_pairs={{2,0},{3,1},{0,2},{1,3},{6,4},{7,5},{4,6},{5,7},{10,8},{11,9},{8,1... | collective-permute-start | bytes 1572872 | tf_op jit(solution)/shard_map/ppermute | solution.py:130
  194.2 33.5 %collective-permute-start.41 = (bf16[128,2048]{1,0:T(8,128)(2,1)S(1)}, bf16[128,2048]{1,0:T(8,128)(2,1)S(1)}, u32[]{:S(2)}, u32[]{:S(2)}) collective-permute-start(bf16[128,2048]{1,0:T(8,128)(2,1)S(1)} %get-tuple-element.50), channel_id=1, source_target_pairs={{4,0},{5,1},{6,2},{7,3},{0,4},{1,5},{2,6},{3,7},{12,8},{13,9},{14,... | collective-permute-start | bytes 1572872 | tf_op jit(solution)/shard_map/ppermute | solution.py:130
  209.4 22.0 %collective-permute-start.49 = (bf16[128,2048]{1,0:T(8,128)(2,1)S(1)}, bf16[128,2048]{1,0:T(8,128)(2,1)S(1)}, u32[]{:S(2)}, u32[]{:S(2)}) collective-permute-start(bf16[128,2048]{1,0:T(8,128)(2,1)S(1)} %fusion.37), channel_id=1, source_target_pairs={{8,0},{9,1},{10,2},{11,3},{12,4},{13,5},{14,6},{15,7},{0,8},{1,9},... | collective-permute-start | bytes 1572872 | tf_op jit(solution)/shard_map/ppermute | solution.py:130
  (58 other events, 325.0 us)

commit v15 on v14

--- a/solution.py
+++ b/solution.py
@@ -113,7 +113,7 @@
     ordered = []
     for low, high in reversed(groups):
         members = list(range(low, high))
-        if len(members) >= 8:
+        if len(members) >= 4:
             half = len(members) // 2
             ordered += [members[:half], members[half:]]
         else:

time: 237 us -> 249 us (1.051)
  matrix products: 48 us -> 57 us
  waiting for transfers between devices: 104 us -> 112 us
  starting transfers between devices: 32.9 us -> 29.9 us
    ppermute x1, waiting for transfers between devices: 7.33 us -> 16.8 us  [full_weights(): other = lax.ppermute(packed, 'kv', [(0, 1), (1, 0)])]
    dot_general x3 -> x5, matrix products: 5.69 us -> 11.5 us  [expert(): gate_val = jnp.dot(rows, full[0], preferred_element_type=jnp.float32)]
    ppermute x8, waiting for transfers between devices: 23.2 us -> 19 us  [dense_moe(): lax.ppermute(pieces[0][0], 'ep', pairs)]
    unnamed x94 -> x84, local copies, waits for them, and re-layouts: 14.8 us -> 11.9 us
    dot_general x4 -> x6, matrix products: 29.2 us -> 31.4 us  [expert(): out_rows = jnp.dot(act, full[2], preferred_element_type=jnp.float32)]
    convert_element_type x3 -> x4, other arithmetic: 8.06 us -> 6.66 us  [dense_moe(): sent = lax.ppermute(partial[index].astype(jnp.bfloat16), 'ep', back)]
  transfers between devices with their start and end apart: 50 -> 50, of which waited for: 15 -> 14; matrix products, arithmetic and copies ran while one was open for 37% -> 34% of each run, Pallas kernels for 0% -> 0%
where the time goes in v15:
time: 249 us; the launch traced here: 245 us
  waiting for transfers between devices  112 us (45%)
  matrix products  57 us (23%)
  starting transfers between devices  29.9 us (12%)
  local copies, waits for them, and re-layouts  23 us (9%)
  other arithmetic  21.8 us (9%)
    ppermute x15, waiting for transfers between devices, dense_moe(): sent = lax.ppermute(partial[index].astype(jnp.bfloat16), 'ep', back)  48.4 us
    dot_general x6, matrix products, expert(): out_rows = jnp.dot(act, full[2], preferred_element_type=jnp.float32)  31.4 us
    ppermute x22, waiting for transfers between devices, dense_moe(): grown.append((lax.ppermute(block, 'ep', pairs), parent, pairs))  22.8 us
    ppermute x8, waiting for transfers between devices, dense_moe(): lax.ppermute(pieces[0][0], 'ep', pairs)  19 us
    ppermute x1, waiting for transfers between devices, full_weights(): other = lax.ppermute(packed, 'kv', [(0, 1), (1, 0)])  16.8 us
    unnamed x84, local copies, waits for them, and re-layouts  11.9 us
    dot_general x5, matrix products, expert(): gate_val = jnp.dot(rows, full[0], preferred_element_type=jnp.float32)  11.5 us
    ppermute x22, starting transfers between devices, dense_moe(): grown.append((lax.ppermute(block, 'ep', pairs), parent, pairs))  9.85 us
  transfers between devices with their start and end apart: 50, of which 14 were waited for; matrix products, arithmetic and copies ran while one was open for 34% of the time, Pallas kernels for 0%

profile of v15, /device:TPU:24, one launch (start us, length us, event | category | flops | bytes accessed | tf_op | source)
XLA Modules:
  0.0 245.1 jit_solution(2023926558729483432)
XLA Ops:
  4.6 3.7 %copy.104 = bf16[128,8,8,128]{3,2,1,0:T(8,128)(2,1)} copy(bf16[128,8,8,128]{3,1,2,0:T(8,128)(2,1)} %bitcast.102) | data formatting | bytes 4194304
  10.9 2.4 bitcast_reduce_fusion.1
  13.4 1.8 fusion.18
  15.1 2.6 %fusion.2 = (f32[128,8]{0,1:T(8,128)S(1)}, f32[128,8]{0,1:T(8,128)S(1)}, f32[8,1024,128]{2,1,0:T(8,128)S(1)}) fusion(f32[8,1024,128]{2,1,0:T(8,128)S(1)} %get-tuple-element.72, f32[128,8]{0,1:T(8,128)S(1)} %max.17, pred[1024]{0:T(1024)(128)(4,1)S(1)} %add_compare_fusion, bf16[128,8,128]{0,2,1:T(8,128)(2,1)} %bitcast.6, bf16[1024,8,128]{2,1,0:T(8,128)(2,1)S(1)} %bitcast.107), kind=kOutput, calls=%fused_computation.10 | convolution fusion | flops 275773440 | bytes 10761216 | tf_op jit(solution)/shard_map/qhd,khd->qhk/dot_general | solution.py:260
  20.5 1.7 fusion.16
  26.2 1.8 collective-permute-start.9
  28.0 3.8 %collective-permute-done.2 = bf16[128,8,128]{0,2,1:T(8,128)(2,1)S(1)} collective-permute-done((bf16[128,8,128]{0,2,1:T(8,128)(2,1)S(1)}, bf16[128,8,128]{0,2,1:T(8,128)(2,1)S(1)}, u32[]{:S(2)}, u32[]{:S(2)}) %collective-permute-start.2) | collective-permute-done | bytes 262176 | tf_op jit(solution)/shard_map/ppermute | solution.py:298
  34.9 2.6 %collective-permute-start.4 = (bf16[128,2048]{1,0:T(8,128)(2,1)}, bf16[128,2048]{1,0:T(8,128)(2,1)}, u32[]{:S(2)}, u32[]{:S(2)}) collective-permute-start(bf16[128,2048]{1,0:T(8,128)(2,1)} %multiply_convert_fusion.4), channel_id=1, source_target_pairs={{0,8},{1,9},{2,10},{3,11},{4,12},{5,13},{6,14},{7,15},{8,0},{9,1},... | collective-permute-start | bytes 1572872 | tf_op jit(solution)/shard_map/ppermute | solution.py:90
  39.6 3.6 %pad_maximum_fusion = bf16[3,2048,256]{2,1,0:T(8,128)(2,1)} fusion(bf16[1,2048,256]{2,1,0:T(8,128)(2,1)S(1)} %stack_reshape_squeeze.3, bf16[1,2048,256]{2,1,0:T(8,128)(2,1)} %param.28, bf16[1,2048,256]{2,1,0:T(8,128)(2,1)} %param.27), kind=kLoop, calls=%fused_computation.14 | loop fusion | flops 3145728 | bytes 6291456 | tf_op jit(solution)/shard_map/stack | solution.py:53
  43.7 17.6 %collective-permute-done.4 = bf16[128,2048]{1,0:T(8,128)(2,1)} collective-permute-done((bf16[128,2048]{1,0:T(8,128)(2,1)}, bf16[128,2048]{1,0:T(8,128)(2,1)}, u32[]{:S(2)}, u32[]{:S(2)}) %collective-permute-start.4) | collective-permute-done | bytes 524320 | tf_op jit(solution)/shard_map/ppermute | solution.py:90
  67.7 20.8 %collective-permute-done.28 = bf16[128,2048]{1,0:T(8,128)(2,1)S(1)} collective-permute-done((bf16[128,2048]{1,0:T(8,128)(2,1)}, bf16[128,2048]{1,0:T(8,128)(2,1)S(1)}, u32[]{:S(2)}, u32[]{:S(2)}) %collective-permute-start.28) | collective-permute-done | bytes 524320 | tf_op jit(solution)/shard_map/ppermute | solution.py:100
  95.9 16.8 %collective-permute-done.12 = bf16[3,2048,256]{2,1,0:T(8,128)(2,1)} collective-permute-done((bf16[3,2048,256]{2,1,0:T(8,128)(2,1)}, bf16[3,2048,256]{2,1,0:T(8,128)(2,1)}, u32[]{:S(2)}, u32[]{:S(2)}) %collective-permute-start.12) | collective-permute-done | bytes 3145760 | tf_op jit(solution)/shard_map/ppermute | solution.py:54
  113.2 4.3 %select_bitcast_fusion.1 = (bf16[2048,256]{1,0:T(8,128)(2,1)}, bf16[2048,256]{1,0:T(8,128)(2,1)}, bf16[1,2048,256]{2,1,0:T(8,128)(2,1)}, bf16[2048,256]{1,0:T(8,128)(2,1)}, bf16[2048,256]{1,0:T(8,128)(2,1)}) fusion(bf16[1,2048,256]{2,1,0:T(8,128)(2,1)S(1)} %copy-done.2, pred[]{:T(512)S(6)} %eq.46, bf16[3,2048,256]{2,1,0:T(8,128)(2,1)} %collective-permute-done.12, ...), kind=kLoop, calls=%fused_computation.90 | loop fusion | flops 2097152 | bytes 10485761 | tf_op jit(solution)/shard_map/jit(_where)/select_n | solution.py:61
  123.1 2.0 collective-permute-done.14
  131.5 4.7 %fusion.9 = f32[256,2048]{1,0:T(8,128)} fusion(bf16[512,2048]{1,0:T(8,128)(2,1)S(1)} %pad_maximum_fusion.3, f32[256]{0:T(256)S(1)} %get-tuple-element.39, f32[256,512]{1,0:T(8,128)} %fusion.119, bf16[256,2048]{1,0:T(8,128)(2,1)} %copy-done.27, bf16[2048,512]{1,0:T(8,128)(2,1)} %get-tuple-element.27), kind=kOutput, calls=%fused_computation.24 | convolution fusion | flops 1076101120 | bytes 7865344 | tf_op jit(solution)/shard_map/dot_general | solution.py:81
  136.2 4.6 %fusion.13 = f32[256,2048]{1,0:T(8,128)} fusion(bf16[512,2048]{1,0:T(8,128)(2,1)S(1)} %pad_maximum_fusion.3, f32[256]{0:T(256)S(1)} %get-tuple-element.41, f32[256,512]{1,0:T(8,128)} %fusion.122, bf16[256,2048]{1,0:T(8,128)(2,1)} %copy-done.22, bf16[2048,512]{1,0:T(8,128)(2,1)} %get-tuple-element.27), kind=kOutput, calls=%fused_computation.28 | convolution fusion | flops 1076101120 | bytes 7865344 | tf_op jit(solution)/shard_map/dot_general | solution.py:81
  140.9 4.6 %fusion.11 = f32[256,2048]{1,0:T(8,128)} fusion(bf16[512,2048]{1,0:T(8,128)(2,1)S(1)} %pad_maximum_fusion.3, f32[256]{0:T(256)S(1)} %get-tuple-element.40, f32[256,512]{1,0:T(8,128)} %fusion.121, bf16[256,2048]{1,0:T(8,128)(2,1)} %copy-done.23, bf16[2048,512]{1,0:T(8,128)(2,1)} %get-tuple-element.27), kind=kOutput, calls=%fused_computation.26 | convolution fusion | flops 1076101120 | bytes 7865344 | tf_op jit(solution)/shard_map/dot_general | solution.py:81
  146.6 4.7 %fusion.118 = f32[512,512]{1,0:T(8,128)} fusion(bf16[512,2048]{1,0:T(8,128)(2,1)} %copy-done.32, bf16[2048,512]{1,0:T(8,128)(2,1)} %copy-done.14), kind=kOutput, calls=%fused_computation.182 | convolution fusion | flops 1073741824 | bytes 5242880 | tf_op jit(solution)/shard_map/dot_general | solution.py:78
  152.5 2.2 fusion.120
  154.7 6.3 %multiply_convert_fusion = bf16[512,2048]{1,0:T(8,128)(2,1)} fusion(bf16[512,2048]{1,0:T(8,128)(2,1)S(1)} %pad_maximum_fusion.3, f32[512]{0:T(512)S(1)} %get-tuple-element.44, f32[512,512]{1,0:T(8,128)} %fusion.120, bf16[512,2048]{1,0:T(8,128)(2,1)} %copy-done.31, bf16[2048,512]{1,0:T(8,128)(2,1)} %get-tuple-element.27), kind=kOutput, calls=%fused_computation.6 | convolution fusion | flops 2153250816 | bytes 9439232 | tf_op jit(solution)/shard_map/dot_general | solution.py:81
  161.1 2.9 %fusion.105 = (bf16[128,2048]{1,0:T(8,128)(2,1)}, bf16[128,2048]{1,0:T(8,128)(2,1)}, bf16[128,2048]{1,0:T(8,128)(2,1)}, bf16[128,2048]{1,0:T(8,128)(2,1)}) fusion(bf16[512,2048]{1,0:T(8,128)(2,1)} %multiply_convert_fusion), kind=kLoop, calls=%fused_computation.174 | loop fusion | bytes 4194304 | tf_op jit(solution)/shard_map/slice | solution.py:126
  164.5 6.3 %multiply_convert_fusion.1 = bf16[512,2048]{1,0:T(8,128)(2,1)} fusion(f32[512]{0:T(512)S(1)} %get-tuple-element.43, bf16[512,2048]{1,0:T(8,128)(2,1)S(1)} %pad_maximum_fusion.3, f32[512,512]{1,0:T(8,128)} %fusion.118, bf16[512,2048]{1,0:T(8,128)(2,1)} %copy-done.32, bf16[2048,512]{1,0:T(8,128)(2,1)} %get-tuple-element.27), kind=kOutput, calls=%fused_computation.7 | convolution fusion | flops 2153250816 | bytes 9439232 | tf_op jit(solution)/shard_map/dot_general | solution.py:81
  170.8 2.8 %fusion.104 = (bf16[128,2048]{1,0:T(8,128)(2,1)}, bf16[128,2048]{1,0:T(8,128)(2,1)S(1)}, bf16[128,2048]{1,0:T(8,128)(2,1)}, bf16[128,2048]{1,0:T(8,128)(2,1)S(1)}) fusion(bf16[512,2048]{1,0:T(8,128)(2,1)} %multiply_convert_fusion.1), kind=kLoop, calls=%fused_computation.173 | loop fusion | bytes 4194304 | tf_op jit(solution)/shard_map/slice | solution.py:126
  182.3 10.3 %collective-permute-done.40 = bf16[128,2048]{1,0:T(8,128)(2,1)S(1)} collective-permute-done((bf16[128,2048]{1,0:T(8,128)(2,1)S(1)}, bf16[128,2048]{1,0:T(8,128)(2,1)S(1)}, u32[]{:S(2)}, u32[]{:S(2)}) %collective-permute-start.40) | collective-permute-done | bytes 524320 | tf_op jit(solution)/shard_map/ppermute | solution.py:130
  192.6 11.2 %collective-permute-done.47 = bf16[128,2048]{1,0:T(8,128)(2,1)S(1)} collective-permute-done((bf16[128,2048]{1,0:T(8,128)(2,1)S(1)}, bf16[128,2048]{1,0:T(8,128)(2,1)S(1)}, u32[]{:S(2)}, u32[]{:S(2)}) %collective-permute-start.47) | collective-permute-done | bytes 524320 | tf_op jit(solution)/shard_map/ppermute | solution.py:130
  206.9 2.7 %fusion.55 = f32[256,512]{1,0:T(8,128)} fusion(bf16[2048,512]{1,0:T(8,128)(2,1)S(1)} %copy-done.16, bf16[128,2048]{1,0:T(8,128)(2,1)} %collective-permute-done.4, bf16[128,2048]{1,0:T(8,128)(2,1)} %multiply_convert_fusion.4), kind=kOutput, calls=%fused_computation.95 | convolution fusion | flops 538968064 | bytes 3670016 | tf_op jit(solution)/shard_map/dot_general | solution.py:79
  209.6 4.7 %fusion.7 = f32[256,2048]{1,0:T(8,128)} fusion(bf16[512,2048]{1,0:T(8,128)(2,1)S(1)} %pad_maximum_fusion.3, f32[256]{0:T(256)S(1)} %get-tuple-element.42, f32[256,512]{1,0:T(8,128)} %fusion.55, bf16[2048,512]{1,0:T(8,128)(2,1)} %copy-done.14, bf16[128,2048]{1,0:T(8,128)(2,1)} %collective-permute-done.4, bf16[128,2048]{1,0:T(8,128)(2,1)} %multiply_convert_fusion.4), kind=kOutput, calls=%fused_computation.22 | convolution fusion | flops 1078198272 | bytes 7865344 | tf_op jit(solution)/shard_map/dot_general | solution.py:81
  215.8 2.4 collective-permute-done.48
  218.1 2.0 fusion.45
  220.5 8.4 %collective-permute-done.37 = bf16[128,2048]{1,0:T(8,128)(2,1)S(1)} collective-permute-done((bf16[128,2048]{1,0:T(8,128)(2,1)}, bf16[128,2048]{1,0:T(8,128)(2,1)S(1)}, u32[]{:S(2)}, u32[]{:S(2)}) %collective-permute-start.37) | collective-permute-done | bytes 524320 | tf_op jit(solution)/shard_map/ppermute | solution.py:130
  228.9 8.7 %collective-permute-done.41 = bf16[128,2048]{1,0:T(8,128)(2,1)S(1)} collective-permute-done((bf16[128,2048]{1,0:T(8,128)(2,1)}, bf16[128,2048]{1,0:T(8,128)(2,1)S(1)}, u32[]{:S(2)}, u32[]{:S(2)}) %collective-permute-start.41) | collective-permute-done | bytes 524320 | tf_op jit(solution)/shard_map/ppermute | solution.py:130
  237.6 6.2 %collective-permute-done.49 = bf16[128,2048]{1,0:T(8,128)(2,1)S(1)} collective-permute-done((bf16[128,2048]{1,0:T(8,128)(2,1)S(1)}, bf16[128,2048]{1,0:T(8,128)(2,1)S(1)}, u32[]{:S(2)}, u32[]{:S(2)}) %collective-permute-start.49) | collective-permute-done | bytes 524320 | tf_op jit(solution)/shard_map/ppermute | solution.py:130
  (208 shorter events, 62.2 us)
Async XLA Ops:
  0.7 34.2 %collective-permute-start.11 = (f32[128,16]{0,1:T(8,128)S(1)}, f32[128,16]{0,1:T(8,128)S(1)}, u32[]{:S(2)}, u32[]{:S(2)}) collective-permute-start(f32[128,16]{0,1:T(8,128)S(1)} %select_reduce_fusion), channel_id=1, source_target_pairs={{0,1},{1,0},{2,3},{3,2},{4,5},{5,4},{6,7},{7,6},{8,9},{9,8},{10,11... | collective-permute-start | bytes 24584 | tf_op jit(solution)/shard_map/ppermute | solution.py:90
  0.8 36.8 %collective-permute-start.5 = (f32[128,16]{0,1:T(8,128)S(1)}, f32[128,16]{0,1:T(8,128)S(1)}, u32[]{:S(2)}, u32[]{:S(2)}) collective-permute-start(f32[128,16]{0,1:T(8,128)S(1)} %select_reduce_fusion), channel_id=1, source_target_pairs={{0,8},{1,9},{2,10},{3,11},{4,12},{5,13},{6,14},{7,15},{8,0},{9,1},... | collective-permute-start | bytes 24584 | tf_op jit(solution)/shard_map/ppermute | solution.py:90
  2.3 12.8 %collective-permute-start = (bf16[128,1024]{0,1:T(8,128)(2,1)S(1)}, bf16[128,1024]{0,1:T(8,128)(2,1)}, u32[]{:S(2)}, u32[]{:S(2)}) collective-permute-start(bf16[128,1024]{0,1:T(8,128)(2,1)S(1)} %bitcast.116), channel_id=1, source_target_pairs={{0,16},{16,0},{1,17},{17,1},{2,18},{18,2},{3,19},{19,3},{4,20},{20... | collective-permute-start | bytes 786440 | tf_op jit(solution)/shard_map/ppermute | solution.py:288
  26.0 12.0 %collective-permute-start.7 = (f32[128,16]{0,1:T(8,128)S(1)}, f32[128,16]{0,1:T(8,128)S(1)}, u32[]{:S(2)}, u32[]{:S(2)}) collective-permute-start(f32[128,16]{0,1:T(8,128)S(1)} %select_reduce_fusion), channel_id=1, source_target_pairs={{0,4},{1,5},{2,6},{3,7},{4,0},{5,1},{6,2},{7,3},{8,12},{9,13},{10,... | collective-permute-start | bytes 24584 | tf_op jit(solution)/shard_map/ppermute | solution.py:90
  26.2 16.9 %collective-permute-start.9 = (f32[128,16]{0,1:T(8,128)S(1)}, f32[128,16]{0,1:T(8,128)S(1)}, u32[]{:S(2)}, u32[]{:S(2)}) collective-permute-start(f32[128,16]{0,1:T(8,128)S(1)} %select_reduce_fusion), channel_id=1, source_target_pairs={{0,2},{1,3},{2,0},{3,1},{4,6},{5,7},{6,4},{7,5},{8,10},{9,11},{10,... | collective-permute-start | bytes 24584 | tf_op jit(solution)/shard_map/ppermute | solution.py:90
  34.9 26.4 %collective-permute-start.4 = (bf16[128,2048]{1,0:T(8,128)(2,1)}, bf16[128,2048]{1,0:T(8,128)(2,1)}, u32[]{:S(2)}, u32[]{:S(2)}) collective-permute-start(bf16[128,2048]{1,0:T(8,128)(2,1)} %multiply_convert_fusion.4), channel_id=1, source_target_pairs={{0,8},{1,9},{2,10},{3,11},{4,12},{5,13},{6,14},{7,15},{8,0},{9,1},... | collective-permute-start | bytes 1572872 | tf_op jit(solution)/shard_map/ppermute | solution.py:90
  37.6 25.1 %collective-permute-start.6 = (bf16[128,2048]{1,0:T(8,128)(2,1)}, bf16[128,2048]{1,0:T(8,128)(2,1)}, u32[]{:S(2)}, u32[]{:S(2)}) collective-permute-start(bf16[128,2048]{1,0:T(8,128)(2,1)} %multiply_convert_fusion.4), channel_id=1, source_target_pairs={{0,4},{1,5},{2,6},{3,7},{4,0},{5,1},{6,2},{7,3},{8,12},{9,13},{10,... | collective-permute-start | bytes 1572872 | tf_op jit(solution)/shard_map/ppermute | solution.py:90
  38.0 24.6 %collective-permute-start.8 = (bf16[128,2048]{1,0:T(8,128)(2,1)}, bf16[128,2048]{1,0:T(8,128)(2,1)}, u32[]{:S(2)}, u32[]{:S(2)}) collective-permute-start(bf16[128,2048]{1,0:T(8,128)(2,1)} %multiply_convert_fusion.4), channel_id=1, source_target_pairs={{0,2},{1,3},{2,0},{3,1},{4,6},{5,7},{6,4},{7,5},{8,10},{9,11},{10,... | collective-permute-start | bytes 1572872 | tf_op jit(solution)/shard_map/ppermute | solution.py:90
  43.1 69.6 %collective-permute-start.12 = (bf16[3,2048,256]{2,1,0:T(8,128)(2,1)}, bf16[3,2048,256]{2,1,0:T(8,128)(2,1)}, u32[]{:S(2)}, u32[]{:S(2)}) collective-permute-start(bf16[3,2048,256]{2,1,0:T(8,128)(2,1)} %pad_maximum_fusion), channel_id=1, source_target_pairs={{0,16},{16,0},{1,17},{17,1},{2,18},{18,2},{3,19},{19,3},{4,20},{20... | collective-permute-start | bytes 9437192 | tf_op jit(solution)/shard_map/ppermute | solution.py:54
  62.7 26.6 %collective-permute-start.24 = (bf16[128,2048]{1,0:T(8,128)(2,1)}, bf16[128,2048]{1,0:T(8,128)(2,1)S(1)}, u32[]{:S(2)}, u32[]{:S(2)}) collective-permute-start(bf16[128,2048]{1,0:T(8,128)(2,1)} %collective-permute-done.4), channel_id=1, source_target_pairs={{0,2},{1,3},{2,0},{3,1},{4,6},{5,7},{6,4},{7,5},{8,10},{9,11},{10,... | collective-permute-start | bytes 1572872 | tf_op jit(solution)/shard_map/ppermute | solution.py:100
  64.2 25.9 %collective-permute-start.13 = (bf16[128,2048]{1,0:T(8,128)(2,1)}, bf16[128,2048]{1,0:T(8,128)(2,1)}, u32[]{:S(2)}, u32[]{:S(2)}) collective-permute-start(bf16[128,2048]{1,0:T(8,128)(2,1)} %collective-permute-done.4), channel_id=1, source_target_pairs={{0,4},{1,5},{2,6},{3,7},{4,0},{5,1},{6,2},{7,3},{8,12},{9,13},{10,... | collective-permute-start | bytes 1572872 | tf_op jit(solution)/shard_map/ppermute | solution.py:100
  64.7 23.8 %collective-permute-start.28 = (bf16[128,2048]{1,0:T(8,128)(2,1)}, bf16[128,2048]{1,0:T(8,128)(2,1)S(1)}, u32[]{:S(2)}, u32[]{:S(2)}) collective-permute-start(bf16[128,2048]{1,0:T(8,128)(2,1)} %collective-permute-done.6), channel_id=1, source_target_pairs={{0,2},{1,3},{2,0},{3,1},{4,6},{5,7},{6,4},{7,5},{8,10},{9,11},{10,... | collective-permute-start | bytes 1572872 | tf_op jit(solution)/shard_map/ppermute | solution.py:100
  67.5 22.2 %collective-permute-start.17 = (bf16[128,2048]{1,0:T(8,128)(2,1)}, bf16[128,2048]{1,0:T(8,128)(2,1)S(1)}, u32[]{:S(2)}, u32[]{:S(2)}) collective-permute-start(bf16[128,2048]{1,0:T(8,128)(2,1)} %collective-permute-done.4), channel_id=1, source_target_pairs={{0,1},{1,0},{2,3},{3,2},{4,5},{5,4},{6,7},{7,6},{8,9},{9,8},{10,11... | collective-permute-start | bytes 1572872 | tf_op jit(solution)/shard_map/ppermute | solution.py:100
  91.9 38.9 %collective-permute-start.25 = (f32[128,16]{0,1:T(8,128)S(1)}, f32[128,16]{0,1:T(8,128)S(1)}, u32[]{:S(2)}, u32[]{:S(2)}) collective-permute-start(f32[128,16]{0,1:T(8,128)S(1)} %collective-permute-done.5), channel_id=1, source_target_pairs={{0,2},{1,3},{2,0},{3,1},{4,6},{5,7},{6,4},{7,5},{8,10},{9,11},{10,... | collective-permute-start | bytes 24584 | tf_op jit(solution)/shard_map/ppermute | solution.py:100
  93.6 51.9 %collective-permute-start.20 = (f32[128,16]{0,1:T(8,128)S(1)}, f32[128,16]{0,1:T(8,128)S(1)}, u32[]{:S(2)}, u32[]{:S(2)}) collective-permute-start(f32[128,16]{0,1:T(8,128)S(1)} %collective-permute-done.5), channel_id=1, source_target_pairs={{0,1},{1,0},{2,3},{3,2},{4,5},{5,4},{6,7},{7,6},{8,9},{9,8},{10,11... | collective-permute-start | bytes 24584 | tf_op jit(solution)/shard_map/ppermute | solution.py:100
  93.7 37.6 %collective-permute-start.33 = (f32[128,16]{0,1:T(8,128)S(1)}, f32[128,16]{0,1:T(8,128)S(1)}, u32[]{:S(2)}, u32[]{:S(2)}) collective-permute-start(f32[128,16]{0,1:T(8,128)S(1)} %collective-permute-done.7), channel_id=1, source_target_pairs={{0,2},{1,3},{2,0},{3,1},{4,6},{5,7},{6,4},{7,5},{8,10},{9,11},{10,... | collective-permute-start | bytes 24584 | tf_op jit(solution)/shard_map/ppermute | solution.py:100
  94.5 28.6 %collective-permute-start.16 = (f32[128,16]{0,1:T(8,128)S(1)}, f32[128,16]{0,1:T(8,128)S(1)}, u32[]{:S(2)}, u32[]{:S(2)}) collective-permute-start(f32[128,16]{0,1:T(8,128)S(1)} %collective-permute-done.15), channel_id=1, source_target_pairs={{0,2},{1,3},{2,0},{3,1},{4,6},{5,7},{6,4},{7,5},{8,10},{9,11},{10,... | collective-permute-start | bytes 24584 | tf_op jit(solution)/shard_map/ppermute | solution.py:100
  112.7 12.5 %collective-permute-start.14 = (bf16[128,2048]{1,0:T(8,128)(2,1)}, bf16[128,2048]{1,0:T(8,128)(2,1)}, u32[]{:S(2)}, u32[]{:S(2)}) collective-permute-start(bf16[128,2048]{1,0:T(8,128)(2,1)} %collective-permute-done.13), channel_id=1, source_target_pairs={{0,2},{1,3},{2,0},{3,1},{4,6},{5,7},{6,4},{7,5},{8,10},{9,11},{10,... | collective-permute-start | bytes 1572872 | tf_op jit(solution)/shard_map/ppermute | solution.py:100
  123.0 23.0 %collective-permute-start.21 = (f32[128,16]{0,1:T(8,128)S(1)}, f32[128,16]{0,1:T(8,128)S(1)}, u32[]{:S(2)}, u32[]{:S(2)}) collective-permute-start(f32[128,16]{0,1:T(8,128)S(1)} %collective-permute-done.7), channel_id=1, source_target_pairs={{0,1},{1,0},{2,3},{3,2},{4,5},{5,4},{6,7},{7,6},{8,9},{9,8},{10,11... | collective-permute-start | bytes 24584 | tf_op jit(solution)/shard_map/ppermute | solution.py:100
  125.1 21.0 %collective-permute-start.31 = (f32[128,16]{0,1:T(8,128)S(1)}, f32[128,16]{0,1:T(8,128)S(1)}, u32[]{:S(2)}, u32[]{:S(2)}) collective-permute-start(f32[128,16]{0,1:T(8,128)S(1)} %collective-permute-done.9), channel_id=1, source_target_pairs={{0,1},{1,0},{2,3},{3,2},{4,5},{5,4},{6,7},{7,6},{8,9},{9,8},{10,11... | collective-permute-start | bytes 24584 | tf_op jit(solution)/shard_map/ppermute | solution.py:100
  130.9 20.4 %collective-permute-start.22 = (f32[128,16]{0,1:T(8,128)S(1)}, f32[128,16]{0,1:T(8,128)S(1)}, u32[]{:S(2)}, u32[]{:S(2)}) collective-permute-start(f32[128,16]{0,1:T(8,128)S(1)} %collective-permute-done.15), channel_id=1, source_target_pairs={{0,1},{1,0},{2,3},{3,2},{4,5},{5,4},{6,7},{7,6},{8,9},{9,8},{10,11... | collective-permute-start | bytes 24584 | tf_op jit(solution)/shard_map/ppermute | solution.py:100
  131.4 20.0 %collective-permute-start.30 = (bf16[128,2048]{1,0:T(8,128)(2,1)}, bf16[128,2048]{1,0:T(8,128)(2,1)}, u32[]{:S(2)}, u32[]{:S(2)}) collective-permute-start(bf16[128,2048]{1,0:T(8,128)(2,1)} %collective-permute-done.14), channel_id=1, source_target_pairs={{0,1},{1,0},{2,3},{3,2},{4,5},{5,4},{6,7},{7,6},{8,9},{9,8},{10,11... | collective-permute-start | bytes 1572872 | tf_op jit(solution)/shard_map/ppermute | solution.py:100
  164.0 10.4 %collective-permute-start.39 = (bf16[128,2048]{1,0:T(8,128)(2,1)}, bf16[128,2048]{1,0:T(8,128)(2,1)}, u32[]{:S(2)}, u32[]{:S(2)}) collective-permute-start(bf16[128,2048]{1,0:T(8,128)(2,1)} %get-tuple-element.64), channel_id=1, source_target_pairs={{1,0},{0,1},{3,2},{2,3},{5,4},{4,5},{7,6},{6,7},{9,8},{8,9},{11,10... | collective-permute-start | bytes 1572872 | tf_op jit(solution)/shard_map/ppermute | solution.py:130
  164.1 10.5 %collective-permute-start.46 = (bf16[128,2048]{1,0:T(8,128)(2,1)}, bf16[128,2048]{1,0:T(8,128)(2,1)}, u32[]{:S(2)}, u32[]{:S(2)}) collective-permute-start(bf16[128,2048]{1,0:T(8,128)(2,1)} %get-tuple-element.62), channel_id=1, source_target_pairs={{1,0},{0,1},{3,2},{2,3},{5,4},{4,5},{7,6},{6,7},{9,8},{8,9},{11,10... | collective-permute-start | bytes 1572872 | tf_op jit(solution)/shard_map/ppermute | solution.py:130
  174.2 41.1 %collective-permute-start.42 = (bf16[128,2048]{1,0:T(8,128)(2,1)}, bf16[128,2048]{1,0:T(8,128)(2,1)}, u32[]{:S(2)}, u32[]{:S(2)}) collective-permute-start(bf16[128,2048]{1,0:T(8,128)(2,1)} %get-tuple-element.57), channel_id=1, source_target_pairs={{1,0},{0,1},{3,2},{2,3},{5,4},{4,5},{7,6},{6,7},{9,8},{8,9},{11,10... | collective-permute-start | bytes 1572872 | tf_op jit(solution)/shard_map/ppermute | solution.py:130
  177.8 14.8 %collective-permute-start.40 = (bf16[128,2048]{1,0:T(8,128)(2,1)S(1)}, bf16[128,2048]{1,0:T(8,128)(2,1)S(1)}, u32[]{:S(2)}, u32[]{:S(2)}) collective-permute-start(bf16[128,2048]{1,0:T(8,128)(2,1)S(1)} %get-tuple-element.67), channel_id=1, source_target_pairs={{2,0},{3,1},{0,2},{1,3},{6,4},{7,5},{4,6},{5,7},{10,8},{11,9},{8,1... | collective-permute-start | bytes 1572872 | tf_op jit(solution)/shard_map/ppermute | solution.py:130
  178.7 25.1 %collective-permute-start.47 = (bf16[128,2048]{1,0:T(8,128)(2,1)S(1)}, bf16[128,2048]{1,0:T(8,128)(2,1)S(1)}, u32[]{:S(2)}, u32[]{:S(2)}) collective-permute-start(bf16[128,2048]{1,0:T(8,128)(2,1)S(1)} %get-tuple-element.68), channel_id=1, source_target_pairs={{2,0},{3,1},{0,2},{1,3},{6,4},{7,5},{4,6},{5,7},{10,8},{11,9},{8,1... | collective-permute-start | bytes 1572872 | tf_op jit(solution)/shard_map/ppermute | solution.py:130
  181.4 34.4 %collective-permute-start.44 = (bf16[128,2048]{1,0:T(8,128)(2,1)}, bf16[128,2048]{1,0:T(8,128)(2,1)}, u32[]{:S(2)}, u32[]{:S(2)}) collective-permute-start(bf16[128,2048]{1,0:T(8,128)(2,1)} %get-tuple-element.60), channel_id=1, source_target_pairs={{2,0},{3,1},{0,2},{1,3},{6,4},{7,5},{4,6},{5,7},{10,8},{11,9},{8,1... | collective-permute-start | bytes 1572872 | tf_op jit(solution)/shard_map/ppermute | solution.py:130
  205.4 12.8 %collective-permute-start.48 = (bf16[128,2048]{1,0:T(8,128)(2,1)}, bf16[128,2048]{1,0:T(8,128)(2,1)}, u32[]{:S(2)}, u32[]{:S(2)}) collective-permute-start(bf16[128,2048]{1,0:T(8,128)(2,1)} %get-tuple-element.66), channel_id=1, source_target_pairs={{4,0},{5,1},{6,2},{7,3},{0,4},{1,5},{2,6},{3,7},{12,8},{13,9},{14,... | collective-permute-start | bytes 1572872 | tf_op jit(solution)/shard_map/ppermute | solution.py:130
  214.4 14.5 %collective-permute-start.37 = (bf16[128,2048]{1,0:T(8,128)(2,1)}, bf16[128,2048]{1,0:T(8,128)(2,1)S(1)}, u32[]{:S(2)}, u32[]{:S(2)}) collective-permute-start(bf16[128,2048]{1,0:T(8,128)(2,1)} %get-tuple-element.59), channel_id=1, source_target_pairs={{2,0},{3,1},{0,2},{1,3},{6,4},{7,5},{4,6},{5,7},{10,8},{11,9},{8,1... | collective-permute-start | bytes 1572872 | tf_op jit(solution)/shard_map/ppermute | solution.py:130
  215.3 22.4 %collective-permute-start.41 = (bf16[128,2048]{1,0:T(8,128)(2,1)}, bf16[128,2048]{1,0:T(8,128)(2,1)S(1)}, u32[]{:S(2)}, u32[]{:S(2)}) collective-permute-start(bf16[128,2048]{1,0:T(8,128)(2,1)} %get-tuple-element.65), channel_id=1, source_target_pairs={{4,0},{5,1},{6,2},{7,3},{0,4},{1,5},{2,6},{3,7},{12,8},{13,9},{14,... | collective-permute-start | bytes 1572872 | tf_op jit(solution)/shard_map/ppermute | solution.py:130
  220.1 23.8 %collective-permute-start.49 = (bf16[128,2048]{1,0:T(8,128)(2,1)S(1)}, bf16[128,2048]{1,0:T(8,128)(2,1)S(1)}, u32[]{:S(2)}, u32[]{:S(2)}) collective-permute-start(bf16[128,2048]{1,0:T(8,128)(2,1)S(1)} %fusion.45), channel_id=1, source_target_pairs={{8,0},{9,1},{10,2},{11,3},{12,4},{13,5},{14,6},{15,7},{0,8},{1,9},... | collective-permute-start | bytes 1572872 | tf_op jit(solution)/shard_map/ppermute | solution.py:130
  (53 other events, 353.1 us)

commit v16 on v14

--- a/solution.py
+++ b/solution.py
@@ -114,8 +114,8 @@
     for low, high in reversed(groups):
         members = list(range(low, high))
         if len(members) >= 8:
-            half = len(members) // 2
-            ordered += [members[:half], members[half:]]
+            part = len(members) // 4
+            ordered += [members[k:k + part] for k in range(0, len(members), part)]
         else:
             ordered.append(members)
     for members in ordered:

time: 237 us -> 250 us (1.055)
  matrix products: 48 us -> 59.1 us
  waiting for transfers between devices: 104 us -> 112 us
  starting transfers between devices: 32.9 us -> 26 us
  local copies, waits for them, and re-layouts: 23.8 us -> 28.5 us
    dot_general x3 -> x5, matrix products: 5.69 us -> 11.5 us  [expert(): gate_val = jnp.dot(rows, full[0], preferred_element_type=jnp.float32)]
    ppermute x22, waiting for transfers between devices: 21.1 us -> 26.3 us  [dense_moe(): grown.append((lax.ppermute(block, 'ep', pairs), parent, pairs))]
    ppermute x8, starting transfers between devices: 7.15 us -> 3.66 us  [dense_moe(): lax.ppermute(pieces[0][0], 'ep', pairs)]
    ppermute x15, waiting for transfers between devices: 47.3 us -> 50.4 us  [dense_moe(): sent = lax.ppermute(partial[index].astype(jnp.bfloat16), 'ep', back)]
    ppermute x1, waiting for transfers between devices: 7.33 us -> 4.34 us  [full_weights(): other = lax.ppermute(packed, 'kv', [(0, 1), (1, 0)])]
    ppermute x22, starting transfers between devices: 11 us -> 8.26 us  [dense_moe(): grown.append((lax.ppermute(block, 'ep', pairs), parent, pairs))]
    slice x2 -> x4, local copies, waits for them, and re-layouts: 5.84 us -> 8.4 us  [dense_moe(): partial[i] = out[offset * size:(offset + 1) * size]]
    dot_general x4 -> x6, matrix products: 29.2 us -> 31.1 us  [expert(): out_rows = jnp.dot(act, full[2], preferred_element_type=jnp.float32)]
  transfers between devices with their start and end apart: 50 -> 50, of which waited for: 15 -> 18; matrix products, arithmetic and copies ran while one was open for 37% -> 41% of each run, Pallas kernels for 0% -> 0%
where the time goes in v16:
time: 250 us; the launch traced here: 248 us
  waiting for transfers between devices  112 us (45%)
  matrix products  59.1 us (24%)
  local copies, waits for them, and re-layouts  28.5 us (11%)
  starting transfers between devices  26 us (10%)
  other arithmetic  20.9 us (8%)
    ppermute x15, waiting for transfers between devices, dense_moe(): sent = lax.ppermute(partial[index].astype(jnp.bfloat16), 'ep', back)  50.4 us
    dot_general x6, matrix products, expert(): out_rows = jnp.dot(act, full[2], preferred_element_type=jnp.float32)  31.1 us
    ppermute x22, waiting for transfers between devices, dense_moe(): grown.append((lax.ppermute(block, 'ep', pairs), parent, pairs))  26.3 us
    ppermute x8, waiting for transfers between devices, dense_moe(): lax.ppermute(pieces[0][0], 'ep', pairs)  25 us
    unnamed x78, local copies, waits for them, and re-layouts  14.7 us
    dot_general x5, matrix products, expert(): gate_val = jnp.dot(rows, full[0], preferred_element_type=jnp.float32)  11.5 us
    ppermute x15, starting transfers between devices, dense_moe(): sent = lax.ppermute(partial[index].astype(jnp.bfloat16), 'ep', back)  9.17 us
    slice x4, local copies, waits for them, and re-layouts, dense_moe(): partial[i] = out[offset * size:(offset + 1) * size]  8.4 us
  transfers between devices with their start and end apart: 50, of which 18 were waited for; matrix products, arithmetic and copies ran while one was open for 41% of the time, Pallas kernels for 0%

profile of v16, /device:TPU:24, one launch (start us, length us, event | category | flops | bytes accessed | tf_op | source)
XLA Modules:
  0.0 247.8 jit_solution(11222118675771048939)
XLA Ops:
  13.1 2.4 bitcast_reduce_fusion.1
  27.1 5.0 %collective-permute-done.2 = bf16[128,8,128]{0,2,1:T(8,128)(2,1)S(1)} collective-permute-done((bf16[128,8,128]{0,2,1:T(8,128)(2,1)S(1)}, bf16[128,8,128]{0,2,1:T(8,128)(2,1)S(1)}, u32[]{:S(2)}, u32[]{:S(2)}) %collective-permute-start.2) | collective-permute-done | bytes 262176 | tf_op jit(solution)/shard_map/ppermute | solution.py:298
  33.2 3.3 %multiply_reduce_fusion = (f32[128]{0:T(128)S(1)}, f32[128,2048]{1,0:T(8,128)S(1)}) fusion(bf16[128,1024]{0,1:T(8,128)(2,1)S(1)} %bitcast.113, bf16[1024,2048]{1,0:T(8,128)(2,1)} %param.23, bf16[1,128,2048]{2,1,0:T(8,128)(2,1)} %param.15), kind=kOutput, calls=%fused_computation.98 | convolution fusion | flops 538443648 | bytes 6029824 | tf_op jit(solution)/shard_map/dot_general | solution.py:344
  41.2 12.5 %collective-permute-done.8 = bf16[128,2048]{1,0:T(8,128)(2,1)} collective-permute-done((bf16[128,2048]{1,0:T(8,128)(2,1)S(1)}, bf16[128,2048]{1,0:T(8,128)(2,1)}, u32[]{:S(2)}, u32[]{:S(2)}) %collective-permute-start.8) | collective-permute-done | bytes 524320 | tf_op jit(solution)/shard_map/ppermute | solution.py:90
  53.8 10.1 %collective-permute-done.6 = bf16[128,2048]{1,0:T(8,128)(2,1)S(1)} collective-permute-done((bf16[128,2048]{1,0:T(8,128)(2,1)S(1)}, bf16[128,2048]{1,0:T(8,128)(2,1)S(1)}, u32[]{:S(2)}, u32[]{:S(2)}) %collective-permute-start.6) | collective-permute-done | bytes 524320 | tf_op jit(solution)/shard_map/ppermute | solution.py:90
  70.7 11.4 %collective-permute-done.21 = bf16[128,2048]{1,0:T(8,128)(2,1)S(1)} collective-permute-done((bf16[128,2048]{1,0:T(8,128)(2,1)}, bf16[128,2048]{1,0:T(8,128)(2,1)S(1)}, u32[]{:S(2)}, u32[]{:S(2)}) %collective-permute-start.21) | collective-permute-done | bytes 524320 | tf_op jit(solution)/shard_map/ppermute | solution.py:100
  82.1 10.8 %collective-permute-done.20 = bf16[128,2048]{1,0:T(8,128)(2,1)S(1)} collective-permute-done((bf16[128,2048]{1,0:T(8,128)(2,1)}, bf16[128,2048]{1,0:T(8,128)(2,1)S(1)}, u32[]{:S(2)}, u32[]{:S(2)}) %collective-permute-start.20) | collective-permute-done | bytes 524320 | tf_op jit(solution)/shard_map/ppermute | solution.py:100
  96.2 3.6 %collective-permute-done.15 = f32[128,16]{0,1:T(8,128)S(1)} collective-permute-done((f32[128,16]{0,1:T(8,128)S(1)}, f32[128,16]{0,1:T(8,128)S(1)}, u32[]{:S(2)}, u32[]{:S(2)}) %collective-permute-start.15) | collective-permute-done | bytes 8224 | tf_op jit(solution)/shard_map/ppermute | solution.py:100
  102.9 4.3 %collective-permute-done.13 = bf16[3,2048,256]{2,1,0:T(8,128)(2,1)} collective-permute-done((bf16[3,2048,256]{2,1,0:T(8,128)(2,1)}, bf16[3,2048,256]{2,1,0:T(8,128)(2,1)}, u32[]{:S(2)}, u32[]{:S(2)}) %collective-permute-start.13) | collective-permute-done | bytes 3145760 | tf_op jit(solution)/shard_map/ppermute | solution.py:54
  107.7 4.4 %select_bitcast_fusion.1 = (bf16[2048,256]{1,0:T(8,128)(2,1)}, bf16[2048,256]{1,0:T(8,128)(2,1)}, bf16[1,2048,256]{2,1,0:T(8,128)(2,1)}, bf16[2048,256]{1,0:T(8,128)(2,1)}, bf16[2048,256]{1,0:T(8,128)(2,1)}) fusion(bf16[1,2048,256]{2,1,0:T(8,128)(2,1)S(1)} %copy-done.3, pred[]{:T(512)S(6)} %eq.46, bf16[3,2048,256]{2,1,0:T(8,128)(2,1)} %collective-permute-done.13, ...), kind=kLoop, calls=%fused_computation.94 | loop fusion | flops 2097152 | bytes 10485761 | tf_op jit(solution)/shard_map/jit(_where)/select_n | solution.py:61
  122.5 2.2 fusion.125
  124.8 6.9 %convert_multiply_fusion = f32[512,2048]{1,0:T(8,128)} fusion(bf16[512,2048]{1,0:T(8,128)(2,1)S(1)} %pad_maximum_fusion.4, f32[512]{0:T(512)S(1)} %get-tuple-element.43, f32[512,512]{1,0:T(8,128)} %fusion.125, bf16[512,2048]{1,0:T(8,128)(2,1)} %copy-done.27, bf16[2048,512]{1,0:T(8,128)(2,1)} %get-tuple-element.28), kind=kOutput, calls=%fused_computation.6 | convolution fusion | flops 2152202240 | bytes 11536384 | tf_op jit(solution)/shard_map/dot_general | solution.py:81
  131.7 4.5 %fusion.66 = f32[512,512]{1,0:T(8,128)} fusion(bf16[2048,512]{1,0:T(8,128)(2,1)} %get-tuple-element.28, bf16[128,2048]{1,0:T(8,128)(2,1)} %collective-permute-done.12, bf16[128,2048]{1,0:T(8,128)(2,1)} %copy-done.29, bf16[128,2048]{1,0:T(8,128)(2,1)} %copy-done.30, bf16[128,2048]{1,0:T(8,128)(2,1)} %copy-done.18), kind=kOutput, calls=%fused_computation.113 | convolution fusion | flops 1082130432 | bytes 5242880 | tf_op jit(solution)/shard_map/dot_general | solution.py:79
  136.2 7.0 %convert_multiply_fusion.1 = f32[512,2048]{1,0:T(8,128)} fusion(bf16[512,2048]{1,0:T(8,128)(2,1)S(1)} %pad_maximum_fusion.4, f32[512]{0:T(512)S(1)} %get-tuple-element.44, f32[512,512]{1,0:T(8,128)} %fusion.66, bf16[2048,512]{1,0:T(8,128)(2,1)} %copy-done.13, bf16[128,2048]{1,0:T(8,128)(2,1)} %collective-permute-done.12, bf16[128,2048]{1,0:T(8,128)(2,1)} %copy-done.29, ...), kind=kOutput, calls=%fused_computation.7 | convolution fusion | flops 2160590848 | bytes 11536384 | tf_op jit(solution)/shard_map/dot_general | solution.py:81
  143.2 3.6 %fusion.126 = f32[256,512]{1,0:T(8,128)} fusion(bf16[256,2048]{1,0:T(8,128)(2,1)} %copy-done.22, bf16[2048,512]{1,0:T(8,128)(2,1)} %copy-done.13), kind=kOutput, calls=%fused_computation.188 | convolution fusion | flops 536870912 | bytes 3670016 | tf_op jit(solution)/shard_map/dot_general | solution.py:78
  148.9 4.3 %fusion.11 = bf16[256,2048]{1,0:T(8,128)(2,1)} fusion(bf16[512,2048]{1,0:T(8,128)(2,1)S(1)} %pad_maximum_fusion.4, f32[256]{0:T(256)S(1)} %get-tuple-element.40, f32[256,512]{1,0:T(8,128)} %fusion.126, bf16[256,2048]{1,0:T(8,128)(2,1)} %copy-done.22, bf16[2048,512]{1,0:T(8,128)(2,1)} %get-tuple-element.28), kind=kOutput, calls=%fused_computation.26 | convolution fusion | flops 1076625408 | bytes 6816768 | tf_op jit(solution)/shard_map/dot_general | solution.py:81
  153.3 2.4 fusion.109
  158.1 2.7 %fusion.128 = f32[256,512]{1,0:T(8,128)} fusion(bf16[256,2048]{1,0:T(8,128)(2,1)} %constant_dynamic-update-slice_fusion.10, bf16[2048,512]{1,0:T(8,128)(2,1)S(1)} %copy-done.15), kind=kOutput, calls=%fused_computation.190 | convolution fusion | flops 536870912 | bytes 3670016 | tf_op jit(solution)/shard_map/dot_general | solution.py:78
  160.9 4.3 %fusion.17 = bf16[256,2048]{1,0:T(8,128)(2,1)} fusion(bf16[512,2048]{1,0:T(8,128)(2,1)S(1)} %pad_maximum_fusion.4, f32[256]{0:T(256)S(1)} %get-tuple-element.42, f32[256,512]{1,0:T(8,128)} %fusion.128, bf16[256,2048]{1,0:T(8,128)(2,1)} %constant_dynamic-update-slice_fusion.10, bf16[2048,512]{1,0:T(8,128)(2,1)} %get-tuple-element.28), kind=kOutput, calls=%fused_computation.32 | convolution fusion | flops 1076625408 | bytes 6816768 | tf_op jit(solution)/shard_map/dot_general | solution.py:81
  165.2 2.4 fusion.111
  168.0 4.3 %fusion.14 = bf16[256,2048]{1,0:T(8,128)(2,1)} fusion(bf16[512,2048]{1,0:T(8,128)(2,1)S(1)} %pad_maximum_fusion.4, f32[256]{0:T(256)S(1)} %get-tuple-element.41, f32[256,512]{1,0:T(8,128)} %fusion.127, bf16[256,2048]{1,0:T(8,128)(2,1)} %copy-done.20, bf16[2048,512]{1,0:T(8,128)(2,1)} %get-tuple-element.28), kind=kOutput, calls=%fused_computation.29 | convolution fusion | flops 1076625408 | bytes 6816768 | tf_op jit(solution)/shard_map/dot_general | solution.py:81
  172.3 2.3 fusion.110
  175.2 4.8 %fusion.53 = (bf16[128,2048]{1,0:T(8,128)(2,1)}, bf16[128,2048]{1,0:T(8,128)(2,1)}, bf16[128,2048]{1,0:T(8,128)(2,1)}, bf16[128,2048]{1,0:T(8,128)(2,1)}) fusion(f32[512,2048]{1,0:T(8,128)} %convert_multiply_fusion, bf16[128,2048]{1,0:T(8,128)(2,1)} %collective-permute-done.28, bf16[128,2048]{1,0:T(8,128)(2,1)} %collective-permute-done.46, ...), kind=kLoop, calls=%fused_computation.82 | loop fusion | flops 3145728 | bytes 8388608 | tf_op jit(solution)/shard_map/convert_element_type | solution.py:130
  182.0 4.3 %fusion.8 = bf16[256,2048]{1,0:T(8,128)(2,1)} fusion(bf16[512,2048]{1,0:T(8,128)(2,1)S(1)} %pad_maximum_fusion.4, f32[256]{0:T(256)S(1)} %get-tuple-element.39, f32[256,512]{1,0:T(8,128)} %fusion.124, bf16[256,2048]{1,0:T(8,128)(2,1)} %copy-done.23, bf16[2048,512]{1,0:T(8,128)(2,1)} %get-tuple-element.28), kind=kOutput, calls=%fused_computation.23 | convolution fusion | flops 1076625408 | bytes 6816768 | tf_op jit(solution)/shard_map/dot_general | solution.py:81
  189.3 5.7 %collective-permute-done.47 = bf16[128,2048]{1,0:T(8,128)(2,1)} collective-permute-done((bf16[128,2048]{1,0:T(8,128)(2,1)}, bf16[128,2048]{1,0:T(8,128)(2,1)}, u32[]{:S(2)}, u32[]{:S(2)}) %collective-permute-start.47) | collective-permute-done | bytes 524320 | tf_op jit(solution)/shard_map/ppermute | solution.py:130
  195.0 11.2 %collective-permute-done.40 = bf16[128,2048]{1,0:T(8,128)(2,1)} collective-permute-done((bf16[128,2048]{1,0:T(8,128)(2,1)}, bf16[128,2048]{1,0:T(8,128)(2,1)}, u32[]{:S(2)}, u32[]{:S(2)}) %collective-permute-start.40) | collective-permute-done | bytes 524320 | tf_op jit(solution)/shard_map/ppermute | solution.py:130
  206.2 2.6 %fusion.52 = (bf16[128,2048]{1,0:T(8,128)(2,1)S(1)}, bf16[128,2048]{1,0:T(8,128)(2,1)S(1)}) fusion(f32[512,2048]{1,0:T(8,128)} %convert_multiply_fusion.1, bf16[128,2048]{1,0:T(8,128)(2,1)} %collective-permute-done.40, bf16[128,2048]{1,0:T(8,128)(2,1)} %collective-permute-done.34, bf16[128,2048]{1,0:T(8,128)(2,1)} %collective-permute-done.47, ...), kind=kLoop, calls=%fused_computation.80 | loop fusion | flops 2621440 | bytes 5242880 | tf_op jit(solution)/shard_map/convert_element_type | solution.py:130
  212.4 4.9 %collective-permute-done.44 = bf16[128,2048]{1,0:T(8,128)(2,1)S(1)} collective-permute-done((bf16[128,2048]{1,0:T(8,128)(2,1)S(1)}, bf16[128,2048]{1,0:T(8,128)(2,1)S(1)}, u32[]{:S(2)}, u32[]{:S(2)}) %collective-permute-start.44) | collective-permute-done | bytes 524320 | tf_op jit(solution)/shard_map/ppermute | solution.py:130
  217.3 6.4 %collective-permute-done.48 = bf16[128,2048]{1,0:T(8,128)(2,1)S(1)} collective-permute-done((bf16[128,2048]{1,0:T(8,128)(2,1)S(1)}, bf16[128,2048]{1,0:T(8,128)(2,1)S(1)}, u32[]{:S(2)}, u32[]{:S(2)}) %collective-permute-start.48) | collective-permute-done | bytes 524320 | tf_op jit(solution)/shard_map/ppermute | solution.py:130
  224.4 3.7 %collective-permute-done.29 = bf16[128,2048]{1,0:T(8,128)(2,1)S(1)} collective-permute-done((bf16[128,2048]{1,0:T(8,128)(2,1)S(1)}, bf16[128,2048]{1,0:T(8,128)(2,1)S(1)}, u32[]{:S(2)}, u32[]{:S(2)}) %collective-permute-start.29) | collective-permute-done | bytes 524320 | tf_op jit(solution)/shard_map/ppermute | solution.py:130
  228.1 13.9 %collective-permute-done.41 = bf16[128,2048]{1,0:T(8,128)(2,1)S(1)} collective-permute-done((bf16[128,2048]{1,0:T(8,128)(2,1)S(1)}, bf16[128,2048]{1,0:T(8,128)(2,1)S(1)}, u32[]{:S(2)}, u32[]{:S(2)}) %collective-permute-start.41) | collective-permute-done | bytes 524320 | tf_op jit(solution)/shard_map/ppermute | solution.py:130
  242.1 4.5 %collective-permute-done.49 = bf16[128,2048]{1,0:T(8,128)(2,1)S(1)} collective-permute-done((bf16[128,2048]{1,0:T(8,128)(2,1)S(1)}, bf16[128,2048]{1,0:T(8,128)(2,1)S(1)}, u32[]{:S(2)}, u32[]{:S(2)}) %collective-permute-start.49) | collective-permute-done | bytes 524320 | tf_op jit(solution)/shard_map/ppermute | solution.py:130
  (203 shorter events, 69.8 us)
Async XLA Ops:
  0.9 38.4 %collective-permute-start.11 = (f32[128,16]{0,1:T(8,128)S(1)}, f32[128,16]{0,1:T(8,128)S(1)}, u32[]{:S(2)}, u32[]{:S(2)}) collective-permute-start(f32[128,16]{0,1:T(8,128)S(1)} %select_reduce_fusion), channel_id=1, source_target_pairs={{0,1},{1,0},{2,3},{3,2},{4,5},{5,4},{6,7},{7,6},{8,9},{9,8},{10,11... | collective-permute-start | bytes 24584 | tf_op jit(solution)/shard_map/ppermute | solution.py:90
  0.9 38.4 %collective-permute-start.9 = (f32[128,16]{0,1:T(8,128)S(1)}, f32[128,16]{0,1:T(8,128)S(1)}, u32[]{:S(2)}, u32[]{:S(2)}) collective-permute-start(f32[128,16]{0,1:T(8,128)S(1)} %select_reduce_fusion), channel_id=1, source_target_pairs={{0,2},{1,3},{2,0},{3,1},{4,6},{5,7},{6,4},{7,5},{8,10},{9,11},{10,... | collective-permute-start | bytes 24584 | tf_op jit(solution)/shard_map/ppermute | solution.py:90
  3.7 13.7 %collective-permute-start = (bf16[128,1024]{0,1:T(8,128)(2,1)S(1)}, bf16[128,1024]{0,1:T(8,128)(2,1)S(1)}, u32[]{:S(2)}, u32[]{:S(2)}) collective-permute-start(bf16[128,1024]{0,1:T(8,128)(2,1)S(1)} %bitcast.116), channel_id=1, source_target_pairs={{0,16},{16,0},{1,17},{17,1},{2,18},{18,2},{3,19},{19,3},{4,20},{20... | collective-permute-start | bytes 786440 | tf_op jit(solution)/shard_map/ppermute | solution.py:288
  26.3 13.6 %collective-permute-start.7 = (f32[128,16]{0,1:T(8,128)S(1)}, f32[128,16]{0,1:T(8,128)S(1)}, u32[]{:S(2)}, u32[]{:S(2)}) collective-permute-start(f32[128,16]{0,1:T(8,128)S(1)} %select_reduce_fusion), channel_id=1, source_target_pairs={{0,4},{1,5},{2,6},{3,7},{4,0},{5,1},{6,2},{7,3},{8,12},{9,13},{10,... | collective-permute-start | bytes 24584 | tf_op jit(solution)/shard_map/ppermute | solution.py:90
  38.5 68.7 %collective-permute-start.13 = (bf16[3,2048,256]{2,1,0:T(8,128)(2,1)}, bf16[3,2048,256]{2,1,0:T(8,128)(2,1)}, u32[]{:S(2)}, u32[]{:S(2)}) collective-permute-start(bf16[3,2048,256]{2,1,0:T(8,128)(2,1)} %pad_maximum_fusion), channel_id=1, source_target_pairs={{0,16},{16,0},{1,17},{17,1},{2,18},{18,2},{3,19},{19,3},{4,20},{20... | collective-permute-start | bytes 9437192 | tf_op jit(solution)/shard_map/ppermute | solution.py:54
  39.3 14.4 %collective-permute-start.8 = (bf16[128,2048]{1,0:T(8,128)(2,1)S(1)}, bf16[128,2048]{1,0:T(8,128)(2,1)}, u32[]{:S(2)}, u32[]{:S(2)}) collective-permute-start(bf16[128,2048]{1,0:T(8,128)(2,1)S(1)} %multiply_convert_fusion.2), channel_id=1, source_target_pairs={{0,2},{1,3},{2,0},{3,1},{4,6},{5,7},{6,4},{7,5},{8,10},{9,11},{10,... | collective-permute-start | bytes 1572872 | tf_op jit(solution)/shard_map/ppermute | solution.py:90
  39.9 24.0 %collective-permute-start.6 = (bf16[128,2048]{1,0:T(8,128)(2,1)S(1)}, bf16[128,2048]{1,0:T(8,128)(2,1)S(1)}, u32[]{:S(2)}, u32[]{:S(2)}) collective-permute-start(bf16[128,2048]{1,0:T(8,128)(2,1)S(1)} %multiply_convert_fusion.2), channel_id=1, source_target_pairs={{0,4},{1,5},{2,6},{3,7},{4,0},{5,1},{6,2},{7,3},{8,12},{9,13},{10,... | collective-permute-start | bytes 1572872 | tf_op jit(solution)/shard_map/ppermute | solution.py:90
  40.4 25.9 %collective-permute-start.4 = (bf16[128,2048]{1,0:T(8,128)(2,1)S(1)}, bf16[128,2048]{1,0:T(8,128)(2,1)S(1)}, u32[]{:S(2)}, u32[]{:S(2)}) collective-permute-start(bf16[128,2048]{1,0:T(8,128)(2,1)S(1)} %multiply_convert_fusion.2), channel_id=1, source_target_pairs={{0,8},{1,9},{2,10},{3,11},{4,12},{5,13},{6,14},{7,15},{8,0},{9,1},... | collective-permute-start | bytes 1572872 | tf_op jit(solution)/shard_map/ppermute | solution.py:90
  67.1 15.0 %collective-permute-start.21 = (bf16[128,2048]{1,0:T(8,128)(2,1)}, bf16[128,2048]{1,0:T(8,128)(2,1)S(1)}, u32[]{:S(2)}, u32[]{:S(2)}) collective-permute-start(bf16[128,2048]{1,0:T(8,128)(2,1)} %copy-done.29), channel_id=1, source_target_pairs={{0,2},{1,3},{2,0},{3,1},{4,6},{5,7},{6,4},{7,5},{8,10},{9,11},{10,... | collective-permute-start | bytes 1572872 | tf_op jit(solution)/shard_map/ppermute | solution.py:100
  68.7 24.2 %collective-permute-start.20 = (bf16[128,2048]{1,0:T(8,128)(2,1)}, bf16[128,2048]{1,0:T(8,128)(2,1)S(1)}, u32[]{:S(2)}, u32[]{:S(2)}) collective-permute-start(bf16[128,2048]{1,0:T(8,128)(2,1)} %copy-done.30), channel_id=1, source_target_pairs={{0,2},{1,3},{2,0},{3,1},{4,6},{5,7},{6,4},{7,5},{8,10},{9,11},{10,... | collective-permute-start | bytes 1572872 | tf_op jit(solution)/shard_map/ppermute | solution.py:100
  70.5 22.5 %collective-permute-start.17 = (bf16[128,2048]{1,0:T(8,128)(2,1)S(1)}, bf16[128,2048]{1,0:T(8,128)(2,1)S(1)}, u32[]{:S(2)}, u32[]{:S(2)}) collective-permute-start(bf16[128,2048]{1,0:T(8,128)(2,1)S(1)} %copy-done.31), channel_id=1, source_target_pairs={{0,1},{1,0},{2,3},{3,2},{4,5},{5,4},{6,7},{7,6},{8,9},{9,8},{10,11... | collective-permute-start | bytes 1572872 | tf_op jit(solution)/shard_map/ppermute | solution.py:100
  70.6 23.0 %collective-permute-start.12 = (bf16[128,2048]{1,0:T(8,128)(2,1)S(1)}, bf16[128,2048]{1,0:T(8,128)(2,1)}, u32[]{:S(2)}, u32[]{:S(2)}) collective-permute-start(bf16[128,2048]{1,0:T(8,128)(2,1)S(1)} %copy-done.31), channel_id=1, source_target_pairs={{0,4},{1,5},{2,6},{3,7},{4,0},{5,1},{6,2},{7,3},{8,12},{9,13},{10,... | collective-permute-start | bytes 1572872 | tf_op jit(solution)/shard_map/ppermute | solution.py:100
  93.0 53.7 %collective-permute-start.32 = (f32[128,16]{0,1:T(8,128)S(1)}, f32[128,16]{0,1:T(8,128)S(1)}, u32[]{:S(2)}, u32[]{:S(2)}) collective-permute-start(f32[128,16]{0,1:T(8,128)S(1)} %collective-permute-done.7), channel_id=1, source_target_pairs={{0,1},{1,0},{2,3},{3,2},{4,5},{5,4},{6,7},{7,6},{8,9},{9,8},{10,11... | collective-permute-start | bytes 24584 | tf_op jit(solution)/shard_map/ppermute | solution.py:100
  93.7 23.9 %collective-permute-start.23 = (f32[128,16]{0,1:T(8,128)S(1)}, f32[128,16]{0,1:T(8,128)S(1)}, u32[]{:S(2)}, u32[]{:S(2)}) collective-permute-start(f32[128,16]{0,1:T(8,128)S(1)} %collective-permute-done.7), channel_id=1, source_target_pairs={{0,2},{1,3},{2,0},{3,1},{4,6},{5,7},{6,4},{7,5},{8,10},{9,11},{10,... | collective-permute-start | bytes 24584 | tf_op jit(solution)/shard_map/ppermute | solution.py:100
  99.8 17.9 %collective-permute-start.22 = (f32[128,16]{0,1:T(8,128)S(1)}, f32[128,16]{0,1:T(8,128)S(1)}, u32[]{:S(2)}, u32[]{:S(2)}) collective-permute-start(f32[128,16]{0,1:T(8,128)S(1)} %collective-permute-done.5), channel_id=1, source_target_pairs={{0,2},{1,3},{2,0},{3,1},{4,6},{5,7},{6,4},{7,5},{8,10},{9,11},{10,... | collective-permute-start | bytes 24584 | tf_op jit(solution)/shard_map/ppermute | solution.py:100
  100.3 17.9 %collective-permute-start.16 = (f32[128,16]{0,1:T(8,128)S(1)}, f32[128,16]{0,1:T(8,128)S(1)}, u32[]{:S(2)}, u32[]{:S(2)}) collective-permute-start(f32[128,16]{0,1:T(8,128)S(1)} %collective-permute-done.15), channel_id=1, source_target_pairs={{0,2},{1,3},{2,0},{3,1},{4,6},{5,7},{6,4},{7,5},{8,10},{9,11},{10,... | collective-permute-start | bytes 24584 | tf_op jit(solution)/shard_map/ppermute | solution.py:100
  117.7 31.1 %collective-permute-start.18 = (f32[128,16]{0,1:T(8,128)S(1)}, f32[128,16]{0,1:T(8,128)S(1)}, u32[]{:S(2)}, u32[]{:S(2)}) collective-permute-start(f32[128,16]{0,1:T(8,128)S(1)} %collective-permute-done.5), channel_id=1, source_target_pairs={{0,1},{1,0},{2,3},{3,2},{4,5},{5,4},{6,7},{7,6},{8,9},{9,8},{10,11... | collective-permute-start | bytes 24584 | tf_op jit(solution)/shard_map/ppermute | solution.py:100
  117.7 29.0 %collective-permute-start.26 = (f32[128,16]{0,1:T(8,128)S(1)}, f32[128,16]{0,1:T(8,128)S(1)}, u32[]{:S(2)}, u32[]{:S(2)}) collective-permute-start(f32[128,16]{0,1:T(8,128)S(1)} %collective-permute-done.9), channel_id=1, source_target_pairs={{0,1},{1,0},{2,3},{3,2},{4,5},{5,4},{6,7},{7,6},{8,9},{9,8},{10,11... | collective-permute-start | bytes 24584 | tf_op jit(solution)/shard_map/ppermute | solution.py:100
  118.2 30.6 %collective-permute-start.37 = (f32[128,16]{0,1:T(8,128)S(1)}, f32[128,16]{0,1:T(8,128)S(1)}, u32[]{:S(2)}, u32[]{:S(2)}) collective-permute-start(f32[128,16]{0,1:T(8,128)S(1)} %collective-permute-done.23), channel_id=1, source_target_pairs={{0,1},{1,0},{2,3},{3,2},{4,5},{5,4},{6,7},{7,6},{8,9},{9,8},{10,11... | collective-permute-start | bytes 24584 | tf_op jit(solution)/shard_map/ppermute | solution.py:100
  118.8 30.0 %collective-permute-start.27 = (f32[128,16]{0,1:T(8,128)S(1)}, f32[128,16]{0,1:T(8,128)S(1)}, u32[]{:S(2)}, u32[]{:S(2)}) collective-permute-start(f32[128,16]{0,1:T(8,128)S(1)} %collective-permute-done.22), channel_id=1, source_target_pairs={{0,1},{1,0},{2,3},{3,2},{4,5},{5,4},{6,7},{7,6},{8,9},{9,8},{10,11... | collective-permute-start | bytes 24584 | tf_op jit(solution)/shard_map/ppermute | solution.py:100
  155.7 19.4 %collective-permute-start.28 = (bf16[128,2048]{1,0:T(8,128)(2,1)}, bf16[128,2048]{1,0:T(8,128)(2,1)}, u32[]{:S(2)}, u32[]{:S(2)}) collective-permute-start(bf16[128,2048]{1,0:T(8,128)(2,1)} %get-tuple-element.65), channel_id=1, source_target_pairs={{1,0},{0,1},{3,2},{2,3},{5,4},{4,5},{7,6},{6,7},{9,8},{8,9},{11,10... | collective-permute-start | bytes 1572872 | tf_op jit(solution)/shard_map/ppermute | solution.py:130
  156.1 19.0 %collective-permute-start.43 = (bf16[128,2048]{1,0:T(8,128)(2,1)}, bf16[128,2048]{1,0:T(8,128)(2,1)}, u32[]{:S(2)}, u32[]{:S(2)}) collective-permute-start(bf16[128,2048]{1,0:T(8,128)(2,1)} %get-tuple-element.66), channel_id=1, source_target_pairs={{1,0},{0,1},{3,2},{2,3},{5,4},{4,5},{7,6},{6,7},{9,8},{8,9},{11,10... | collective-permute-start | bytes 1572872 | tf_op jit(solution)/shard_map/ppermute | solution.py:130
  175.1 14.2 %collective-permute-start.45 = (bf16[128,2048]{1,0:T(8,128)(2,1)}, bf16[128,2048]{1,0:T(8,128)(2,1)}, u32[]{:S(2)}, u32[]{:S(2)}) collective-permute-start(bf16[128,2048]{1,0:T(8,128)(2,1)} %get-tuple-element.68), channel_id=1, source_target_pairs={{1,0},{0,1},{3,2},{2,3},{5,4},{4,5},{7,6},{6,7},{9,8},{8,9},{11,10... | collective-permute-start | bytes 1572872 | tf_op jit(solution)/shard_map/ppermute | solution.py:130
  179.9 15.0 %collective-permute-start.47 = (bf16[128,2048]{1,0:T(8,128)(2,1)}, bf16[128,2048]{1,0:T(8,128)(2,1)}, u32[]{:S(2)}, u32[]{:S(2)}) collective-permute-start(bf16[128,2048]{1,0:T(8,128)(2,1)} %get-tuple-element.49), channel_id=1, source_target_pairs={{2,0},{3,1},{0,2},{1,3},{6,4},{7,5},{4,6},{5,7},{10,8},{11,9},{8,1... | collective-permute-start | bytes 1572872 | tf_op jit(solution)/shard_map/ppermute | solution.py:130
  181.4 24.8 %collective-permute-start.40 = (bf16[128,2048]{1,0:T(8,128)(2,1)}, bf16[128,2048]{1,0:T(8,128)(2,1)}, u32[]{:S(2)}, u32[]{:S(2)}) collective-permute-start(bf16[128,2048]{1,0:T(8,128)(2,1)} %get-tuple-element.51), channel_id=1, source_target_pairs={{2,0},{3,1},{0,2},{1,3},{6,4},{7,5},{4,6},{5,7},{10,8},{11,9},{8,1... | collective-permute-start | bytes 1572872 | tf_op jit(solution)/shard_map/ppermute | solution.py:130
  187.6 23.3 %collective-permute-start.42 = (bf16[128,2048]{1,0:T(8,128)(2,1)S(1)}, bf16[128,2048]{1,0:T(8,128)(2,1)S(1)}, u32[]{:S(2)}, u32[]{:S(2)}) collective-permute-start(bf16[128,2048]{1,0:T(8,128)(2,1)S(1)} %get-tuple-element.64), channel_id=1, source_target_pairs={{1,0},{0,1},{3,2},{2,3},{5,4},{4,5},{7,6},{6,7},{9,8},{8,9},{11,10... | collective-permute-start | bytes 1572872 | tf_op jit(solution)/shard_map/ppermute | solution.py:130
  187.7 29.6 %collective-permute-start.44 = (bf16[128,2048]{1,0:T(8,128)(2,1)S(1)}, bf16[128,2048]{1,0:T(8,128)(2,1)S(1)}, u32[]{:S(2)}, u32[]{:S(2)}) collective-permute-start(bf16[128,2048]{1,0:T(8,128)(2,1)S(1)} %copy-done.17), channel_id=1, source_target_pairs={{2,0},{3,1},{0,2},{1,3},{6,4},{7,5},{4,6},{5,7},{10,8},{11,9},{8,1... | collective-permute-start | bytes 1572872 | tf_op jit(solution)/shard_map/ppermute | solution.py:130
  208.8 14.9 %collective-permute-start.48 = (bf16[128,2048]{1,0:T(8,128)(2,1)S(1)}, bf16[128,2048]{1,0:T(8,128)(2,1)S(1)}, u32[]{:S(2)}, u32[]{:S(2)}) collective-permute-start(bf16[128,2048]{1,0:T(8,128)(2,1)S(1)} %get-tuple-element.53), channel_id=1, source_target_pairs={{4,0},{5,1},{6,2},{7,3},{0,4},{1,5},{2,6},{3,7},{12,8},{13,9},{14,... | collective-permute-start | bytes 1572872 | tf_op jit(solution)/shard_map/ppermute | solution.py:130
  209.3 15.1 %collective-permute-start.19 = (bf16[128,2048]{1,0:T(8,128)(2,1)S(1)}, bf16[128,2048]{1,0:T(8,128)(2,1)S(1)}, u32[]{:S(2)}, u32[]{:S(2)}) collective-permute-start(bf16[128,2048]{1,0:T(8,128)(2,1)S(1)} %get-tuple-element.63), channel_id=1, source_target_pairs={{1,0},{0,1},{3,2},{2,3},{5,4},{4,5},{7,6},{6,7},{9,8},{8,9},{11,10... | collective-permute-start | bytes 1572872 | tf_op jit(solution)/shard_map/ppermute | solution.py:130
  209.3 18.8 %collective-permute-start.29 = (bf16[128,2048]{1,0:T(8,128)(2,1)S(1)}, bf16[128,2048]{1,0:T(8,128)(2,1)S(1)}, u32[]{:S(2)}, u32[]{:S(2)}) collective-permute-start(bf16[128,2048]{1,0:T(8,128)(2,1)S(1)} %copy-done.16), channel_id=1, source_target_pairs={{2,0},{3,1},{0,2},{1,3},{6,4},{7,5},{4,6},{5,7},{10,8},{11,9},{8,1... | collective-permute-start | bytes 1572872 | tf_op jit(solution)/shard_map/ppermute | solution.py:130
  210.9 31.2 %collective-permute-start.41 = (bf16[128,2048]{1,0:T(8,128)(2,1)S(1)}, bf16[128,2048]{1,0:T(8,128)(2,1)S(1)}, u32[]{:S(2)}, u32[]{:S(2)}) collective-permute-start(bf16[128,2048]{1,0:T(8,128)(2,1)S(1)} %get-tuple-element.52), channel_id=1, source_target_pairs={{4,0},{5,1},{6,2},{7,3},{0,4},{1,5},{2,6},{3,7},{12,8},{13,9},{14,... | collective-permute-start | bytes 1572872 | tf_op jit(solution)/shard_map/ppermute | solution.py:130
  224.1 22.5 %collective-permute-start.49 = (bf16[128,2048]{1,0:T(8,128)(2,1)S(1)}, bf16[128,2048]{1,0:T(8,128)(2,1)S(1)}, u32[]{:S(2)}, u32[]{:S(2)}) collective-permute-start(bf16[128,2048]{1,0:T(8,128)(2,1)S(1)} %fusion.49), channel_id=1, source_target_pairs={{8,0},{9,1},{10,2},{11,3},{12,4},{13,5},{14,6},{15,7},{0,8},{1,9},... | collective-permute-start | bytes 1572872 | tf_op jit(solution)/shard_map/ppermute | solution.py:130
  (51 other events, 334.3 us)
